TPU v7x, 32 devices: a whole 2x2x4 slice. The times are simulated.
32 devices in a mesh: gx: 8 (over y, x, core), gy: 4 (over z).
Axes of the slice: x: 2, y: 2, z: 4, core: 2. Of those that a mesh axis runs over, the one named last changes fastest.
Arguments:
- temp_start: float32 [8, 1024, 2048], P(None, ('gx', 'gy')), may hold values from -6 to 6
- heat_input: float32 [8, 1024, 2048], P(None, ('gx', 'gy')), may hold values from -3 to 3
- lateral: float32 [8], replicated, may hold values from 0.03 to 0.15
- vertical: float32 [7], replicated, may hold values from 0.03 to 0.15
- weighting: float32 [8], replicated, may hold values from -1 to 1
- modulus: float32 [1024, 2048], P('gx', 'gy'), may hold values from 0.3 to 3
- warp_prev: float32 [1024, 2048], P('gx', 'gy'), may hold values from -6 to 6
- joint_cell: int32 [65536], P(('gx', 'gy')), may hold values from 0 to 65535
- joint_owner: int32 [65536, 1], P(('gx', 'gy')), may hold values from 0 to 31; in each aligned block of 2048 rows (0 to 2047, 2048 to 4095, ...) at most 192 rows name the same one
- joint_strain: float32 [2, 32, 6144], P(None, ('gx', 'gy')), may hold values from -4 to 4
- joint_resist: float32 [32, 6144], P(('gx', 'gy')), may hold values from 1 to 2
Outputs:
- warpage: float32 [1024, 2048], P('gx', 'gy')
- strain_next: float32 [2, 32, 6144], P(None, ('gx', 'gy'))
- resist_next: float32 [32, 6144], P(('gx', 'gy'))
Inputs may be any that keep to these rules, and one draw needn't show every extreme that they name: `joint_owner`: among the 2048 joints of one device at most 192 have the same owner, and on some device exactly 192 do.
All inputs are finite; a program needn't handle non-finite values.
Results may differ from a plain program's by a relative error of at most 0.0003.
Values sent between devices are 32-bit elements; how exact they have to be, the bound alone decides.
No kernel may reach another device: no remote copies, remote signals or barrier semaphores. Data moves between devices by JAX's collectives and lax.ppermute only.
A program may use at most 320 MiB of HBM per device.

v0:
```python
import jax
import jax.numpy as jnp
from jax import lax
from jax.sharding import PartitionSpec as P

STEPS = 2
SWEEPS = 3


stiffness = 0.2
shear_mod = 0.6
rate_scale = 0.5
sat_level = 2.5
sat_power = 0.3
harden = 2.0


def with_halo(array, sides, width):
    for axis, dim in sides:
        count, length = (lax.axis_size(axis), array.shape[dim])
        up = [(i, (i + 1) % count) for i in range(count - 1)]
        down = [(j, i) for i, j in up]
        last = lax.slice_in_dim(array, length - width, length, axis=dim)
        leading = lax.slice_in_dim(array, 0, width, axis=dim)
        before = lax.ppermute(last, axis, up)
        after = lax.ppermute(leading, axis, down)
        array = jnp.concatenate([before, array, after], axis=dim)
    return array


def thermal_step(ext, heat_rows, lateral, vertical):
    cols = jnp.pad(ext, ((0, 0), (0, 0), (1, 1)))
    center = ext[:, 1:-1]
    lap = ext[:, 2:] + ext[:, :-2] + cols[:, 1:-1, 2:] + cols[:, 1:-1, :-2] - 4.0 * center
    flux = vertical[:, None, None] * (center[1:] - center[:-1])
    vert = jnp.pad(flux, ((0, 1), (0, 0), (0, 0))) - jnp.pad(flux, ((1, 0), (0, 0), (0, 0)))
    return center + lateral[:, None, None] * lap + vert + heat_rows


def moment_of(field, weighting):
    total = weighting[0] * field[0]
    for layer in range(1, field.shape[0]):
        total = total + weighting[layer] * field[layer]
    return total


def sweep(w_pad, e_pad, load):
    center = e_pad[1:-1, 1:-1]
    e_up = 0.5 * (center + e_pad[:-2, 1:-1])
    e_down = 0.5 * (center + e_pad[2:, 1:-1])
    e_left = 0.5 * (center + e_pad[1:-1, :-2])
    e_right = 0.5 * (center + e_pad[1:-1, 2:])
    numer = (
        load
        + e_up * w_pad[:-2, 1:-1]
        + e_down * w_pad[2:, 1:-1]
        + e_left * w_pad[1:-1, :-2]
        + e_right * w_pad[1:-1, 2:]
    )
    denom = stiffness + e_up + e_down + e_left + e_right
    return numer / denom


def anand(strain, resist, recv):
    total, inelastic = (strain[0], strain[1])
    increment, theta, live = (recv[0], recv[1], recv[2])
    total_new = total + increment
    arrhen = jnp.exp(2.0 - 2.0 / (1.0 + 0.1 * theta * theta))
    hyper = jnp.sinh(shear_mod * (total_new - inelastic) / resist)
    rate = rate_scale * arrhen * hyper * jnp.abs(hyper)
    inelastic_new = inelastic + rate
    target = sat_level * jnp.power(1.0 + jnp.abs(rate) / arrhen, sat_power)
    resist_new = resist + harden * (1.0 - resist / target) * jnp.abs(rate)
    keep = live > 0.5
    strain_out = jnp.stack(
        [jnp.where(keep, total_new, total), jnp.where(keep, inelastic_new, inelastic)]
    )
    return (strain_out, jnp.where(keep, resist_new, resist))


def body(
    temp_start,
    heat_input,
    lateral,
    vertical,
    weighting,
    modulus,
    warp_prev,
    joint_cell,
    joint_owner,
    joint_strain,
    joint_resist,
):
    devices = lax.axis_size(("gx", "gy"))
    temp = temp_start
    for step in range(STEPS):
        ext = with_halo(temp, ((("gx", "gy"), 1),), 1)
        temp = thermal_step(ext, heat_input, lateral, vertical)
    relayed = lax.all_to_all(temp, "gy", split_axis=2, concat_axis=1, tiled=True)
    load = moment_of(relayed, weighting)
    top = relayed[-1]
    e_pad = with_halo(modulus, (("gx", 0), ("gy", 1)), 1)
    warp = warp_prev
    for step in range(SWEEPS):
        w_pad = with_halo(warp, (("gx", 0), ("gy", 1)), 1)
        warp = sweep(w_pad, e_pad, load)
    capacity = joint_resist.shape[1] // devices
    owners = joint_owner[:, 0]
    increment = warp.reshape(-1)[joint_cell] - warp_prev.reshape(-1)[joint_cell]
    theta = top.reshape(-1)[joint_cell]
    values = jnp.stack([increment, theta, jnp.ones_like(theta)])
    onehot = (owners[:, None] == jnp.arange(devices, dtype=jnp.int32)[None, :]).astype(jnp.int32)
    ranks = jnp.sum(jnp.cumsum(onehot, axis=0) * onehot, axis=1) - 1
    slots = owners * capacity + ranks
    outgoing = jnp.zeros((3, devices * capacity), jnp.float32).at[:, slots].set(values)
    incoming = lax.all_to_all(outgoing, ("gx", "gy"), split_axis=1, concat_axis=1, tiled=True)
    strain_next, resist_next = anand(joint_strain, joint_resist, incoming[:, None, :])
    return (warp, strain_next, resist_next)


def solution(mesh):
    return jax.shard_map(
        body,
        mesh=mesh,
        in_specs=(
            P(None, ("gx", "gy"), None),
            P(None, ("gx", "gy"), None),
            P(),
            P(),
            P(),
            P("gx", "gy"),
            P("gx", "gy"),
            P(("gx", "gy")),
            P(("gx", "gy"), None),
            P(None, ("gx", "gy"), None),
            P(("gx", "gy"), None),
        ),
        out_specs=(P("gx", "gy"), P(None, ("gx", "gy"), None), P(("gx", "gy"), None)),
        check_vma=False,
    )
```

profile of v0, /device:TPU:0, one launch (start us, length us, event | category | flops | bytes accessed | tf_op | source)
XLA Modules:
  0.0 217.0 jit_solution(10733385116861195216)
XLA Ops:
  4.8 5.6 %collective-permute-start.1 = (f32[8,1,2048]{2,0,1:T(8,128)S(1)}, f32[8,1,2048]{2,0,1:T(8,128)S(1)}, u32[]{:S(2)}, u32[]{:S(2)}) collective-permute-start(f32[8,1,2048]{2,0,1:T(8,128)S(1)} %get-tuple-element.11), channel_id=1, source_target_pairs={{0,1},{1,2},{2,3},{3,4},{4,5},{5,6},{6,7},{7,8},{8,9},{9,10},{10,1... | collective-permute-start | bytes 196616 | tf_op jit(solution)/shard_map/ppermute | solution.py:25
  17.0 5.0 %collective-permute-start.3 = (f32[8,1,2048]{2,0,1:T(8,128)S(1)}, f32[8,1,2048]{2,0,1:T(8,128)S(1)}, u32[]{:S(2)}, u32[]{:S(2)}) collective-permute-start(f32[8,1,2048]{2,0,1:T(8,128)S(1)} %get-tuple-element.9), channel_id=1, source_target_pairs={{0,1},{1,2},{2,3},{3,4},{4,5},{5,6},{6,7},{7,8},{8,9},{9,10},{10,1... | collective-permute-start | bytes 196616 | tf_op jit(solution)/shard_map/ppermute | solution.py:25
  27.2 4.9 %copy.63 = f32[8,32,2048]{1,0,2:T(8,128)} copy(f32[8,32,2048]{2,0,1:T(8,128)S(1)} %fusion.6) | data formatting | bytes 4194304 | tf_op jit(solution)/shard_map/add | solution.py:37
  32.1 7.1 %reshape.264 = f32[4,1,131072]{2,1,0:T(1,128)} reshape(f32[2048,8,32]{2,1,0:T(8,128)} %bitcast.70) | data formatting | bytes 4194304
  39.2 8.6 %all-to-all-start = ((f32[4,1,131072]{2,1,0:T(1,128)}), f32[4,1,131072]{2,1,0:T(1,128)S(1)}, u32[]{:S(2)}, u32[]{:S(2)}) async-start(f32[4,1,131072]{2,1,0:T(1,128)} %reshape.264), calls=%async_computation | async-start | bytes 4194304 | tf_op jit(solution)/shard_map/all_to_all | solution.py:99
  47.8 4.4 %collective-permute-start.4 = (f32[1,512]{1,0:T(1,128)S(1)}, f32[1,512]{1,0:T(1,128)S(1)}, u32[]{:S(2)}, u32[]{:S(2)}) collective-permute-start(f32[1,512]{1,0:T(1,128)S(1)} %get-tuple-element.26), channel_id=1, source_target_pairs={{0,4},{4,8},{8,12},{12,16},{16,20},{20,24},{24,28},{1,5},{5,9},{9,... | collective-permute-start | bytes 6152 | tf_op jit(solution)/shard_map/ppermute | solution.py:25
  53.6 5.2 %collective-permute-start.5 = (f32[1,512]{1,0:T(1,128)S(1)}, f32[1,512]{1,0:T(1,128)S(1)}, u32[]{:S(2)}, u32[]{:S(2)}) collective-permute-start(f32[1,512]{1,0:T(1,128)S(1)} %get-tuple-element.27), channel_id=1, source_target_pairs={{0,4},{4,8},{8,12},{12,16},{16,20},{20,24},{24,28},{1,5},{5,9},{9,... | collective-permute-start | bytes 6152 | tf_op jit(solution)/shard_map/ppermute | solution.py:25
  60.2 9.1 %reduce-window.6 = s32[32,16,128]{2,1,0:T(8,128)S(1)} reduce-window(s32[32,16,128]{2,1,0:T(8,128)S(1)} %fusion.61, s32[]{:T(128)} %constant.6.clone.1), window={size=1x1x128 pad=0_0x0_0x127_0}, to_apply=%region_0.1 | reduce-window | flops 8323072 | bytes 524292 | tf_op jit(solution)/shard_map/reduce-window
  72.2 4.5 %collective-permute-start.8 = (f32[130,1]{1,0:T(8,128)S(1)}, f32[130,1]{1,0:T(8,128)S(1)}, u32[]{:S(2)}, u32[]{:S(2)}) collective-permute-start(f32[130,1]{1,0:T(8,128)S(1)} %get-tuple-element.18), channel_id=1, source_target_pairs={{0,1},{1,2},{2,3},{4,5},{5,6},{6,7},{8,9},{9,10},{10,11},{12,13},{... | collective-permute-start | bytes 1568 | tf_op jit(solution)/shard_map/ppermute | solution.py:25
  78.7 5.2 %collective-permute-start.9 = (f32[130,1]{1,0:T(8,128)S(1)}, f32[130,1]{1,0:T(8,128)}, u32[]{:S(2)}, u32[]{:S(2)}) collective-permute-start(f32[130,1]{1,0:T(8,128)S(1)} %get-tuple-element.19), channel_id=1, source_target_pairs={{0,1},{1,2},{2,3},{4,5},{5,6},{6,7},{8,9},{9,10},{10,11},{12,13},{... | collective-permute-start | bytes 1568 | tf_op jit(solution)/shard_map/ppermute | solution.py:25
  83.9 12.6 %all-to-all-done = f32[4,1,131072]{2,1,0:T(1,128)S(1)} async-done(((f32[4,1,131072]{2,1,0:T(1,128)}), f32[4,1,131072]{2,1,0:T(1,128)S(1)}, u32[]{:S(2)}, u32[]{:S(2)}) %all-to-all-start) | async-done | bytes 2097184 | tf_op jit(solution)/shard_map/all_to_all | solution.py:99
  98.3 7.7 %reduce.8 = f32[4,131072]{1,0:T(4,128)S(1)} reduce(f32[4,1,131072]{2,1,0:T(1,128)} %copy-done.1, f32[]{:T(128)} %broadcast.270), dimensions={1}, to_apply=%all_to_all.17.reduce_sub_computation | reduce | bytes 4194308 | tf_op jit(solution)/shard_map/all_to_all | solution.py:99
  106.0 6.2 %reshape.265 = f32[2048,8,32]{2,1,0:T(8,128)} reshape(f32[4,131072]{1,0:T(4,128)S(1)} %reduce.8) | data formatting | bytes 4194304
  112.2 5.1 %copy.64 = f32[8,32,4,512]{3,1,2,0:T(8,128)S(1)} copy(f32[8,32,4,512]{1,0,3,2:T(8,128)} %bitcast.71) | data formatting | bytes 4194304 | tf_op jit(solution)/shard_map/all_to_all | solution.py:99
  117.3 5.2 %fusion.72 = (f32[1,4,32,512]{3,2,1,0:T(8,128)S(1)}, f32[1,4,32,512]{3,2,1,0:T(8,128)S(1)}) fusion(f32[8,4,32,512]{3,2,1,0:T(8,128)S(1)} %bitcast.73, f32[]{:T(128)} %bitcast.9, f32[]{:T(128)} %bitcast.8, f32[]{:T(128)} %bitcast.7, f32[]{:T(128)} %bitcast.6, f32[]{:T(128)} %bitcast.5, f32[]{:T(128)} %bitcast.4, f32[]{:T(128)} %bitcast.3, f32[]{:T(128)} %bitcast), kind=kLoop, calls=%fused_computation.165 | loop fusion | flops 983040 | bytes 2621472 | tf_op jit(solution)/shard_map/slice | solution.py:43
  123.9 3.7 %collective-permute-start.12 = (f32[1,512]{1,0:T(1,128)S(1)}, f32[1,512]{1,0:T(1,128)S(1)}, u32[]{:S(2)}, u32[]{:S(2)}) collective-permute-start(f32[1,512]{1,0:T(1,128)S(1)} %get-tuple-element.23), channel_id=1, source_target_pairs={{0,4},{4,8},{8,12},{12,16},{16,20},{20,24},{24,28},{1,5},{5,9},{9,... | collective-permute-start | bytes 6152 | tf_op jit(solution)/shard_map/ppermute | solution.py:25
  128.9 4.2 %collective-permute-done.13 = f32[1,512]{1,0:T(1,128)S(1)} collective-permute-done((f32[1,512]{1,0:T(1,128)S(1)}, f32[1,512]{1,0:T(1,128)S(1)}, u32[]{:S(2)}, u32[]{:S(2)}) %collective-permute-start.13) | collective-permute-done | bytes 2080 | tf_op jit(solution)/shard_map/ppermute | solution.py:26
  136.4 4.3 %collective-permute-done.15 = f32[130,1]{1,0:T(8,128)S(1)} collective-permute-done((f32[130,1]{1,0:T(8,128)S(1)}, f32[130,1]{1,0:T(8,128)S(1)}, u32[]{:S(2)}, u32[]{:S(2)}) %collective-permute-start.15) | collective-permute-done | bytes 552 | tf_op jit(solution)/shard_map/ppermute | solution.py:26
  145.6 11.8 %gather_fusion.1 = f32[2048]{0:T(1024)S(1)} fusion(f32[65536]{0:T(1024)S(1)} %bitcast.69, s32[2048]{0:T(1024)S(1)} %fusion.71), kind=kCustom, calls=%fused_computation.1 | custom fusion | bytes 24576 | tf_op jit(solution)/shard_map/gather | solution.py:109
  157.5 3.6 %collective-permute-start.18 = (f32[130,1]{1,0:T(8,128)S(1)}, f32[130,1]{1,0:T(8,128)S(1)}, u32[]{:S(2)}, u32[]{:S(2)}) collective-permute-start(f32[130,1]{1,0:T(8,128)S(1)} %get-tuple-element.13), channel_id=1, source_target_pairs={{0,1},{1,2},{2,3},{4,5},{5,6},{6,7},{8,9},{9,10},{10,11},{12,13},{... | collective-permute-start | bytes 1568 | tf_op jit(solution)/shard_map/ppermute | solution.py:25
  162.8 11.8 %gather_fusion.2 = f32[2048]{0:T(1024)S(1)} fusion(f32[65536]{0:T(1024)S(1)} %bitcast.67, s32[2048]{0:T(1024)S(1)} %fusion.71), kind=kCustom, calls=%fused_computation.2 | custom fusion | bytes 24576 | tf_op jit(solution)/shard_map/gather | solution.py:110
  175.2 11.8 %gather_fusion = f32[2048]{0:T(1024)S(1)} fusion(f32[65536]{0:T(1024)S(1)} %bitcast.68, s32[2048]{0:T(1024)S(1)} %fusion.71), kind=kCustom, calls=%fused_computation | custom fusion | bytes 24576 | tf_op jit(solution)/shard_map/gather | solution.py:109
  188.4 6.7 %scatter_custom_fusion = f32[3,6144]{0,1:T(8,128)S(1)} fusion(s32[2048]{0:T(1024)} %bitcast.85, f32[2048,3]{1,0:T(8,128)} %copy.67, f32[]{:T(128)} %constant.16.clone.1), kind=kCustom, calls=%fused_computation.35 | custom fusion | bytes 74240 | tf_op jit(solution)/shard_map/scatter | solution.py:115
  196.6 17.7 %all_to_all.24 = f32[3,32,192]{2,0,1:T(4,128)S(1)} all-to-all(f32[3,32,192]{2,0,1:T(4,128)S(1)} %copy.68), channel_id=1, replica_groups=mesh['gx'=8,'gy'=4] {'gx','gy'}, dimensions={1} | all-to-all | bytes 147456 | tf_op jit(solution)/shard_map/all_to_all | solution.py:116
  (104 shorter events, 43.7 us)
Async XLA Ops:
  3.5 7.3 %collective-permute-start = (f32[8,1,2048]{2,0,1:T(8,128)S(1)}, f32[8,1,2048]{2,0,1:T(8,128)S(1)}, u32[]{:S(2)}, u32[]{:S(2)}) collective-permute-start(f32[8,1,2048]{2,0,1:T(8,128)S(1)} %get-tuple-element.12), channel_id=1, source_target_pairs={{1,0},{2,1},{3,2},{4,3},{5,4},{6,5},{7,6},{8,7},{9,8},{10,9},{11,1... | collective-permute-start | bytes 196616 | tf_op jit(solution)/shard_map/ppermute | solution.py:26
  4.8 7.6 %collective-permute-start.1 = (f32[8,1,2048]{2,0,1:T(8,128)S(1)}, f32[8,1,2048]{2,0,1:T(8,128)S(1)}, u32[]{:S(2)}, u32[]{:S(2)}) collective-permute-start(f32[8,1,2048]{2,0,1:T(8,128)S(1)} %get-tuple-element.11), channel_id=1, source_target_pairs={{0,1},{1,2},{2,3},{3,4},{4,5},{5,6},{6,7},{7,8},{8,9},{9,10},{10,1... | collective-permute-start | bytes 196616 | tf_op jit(solution)/shard_map/ppermute | solution.py:25
  15.7 6.7 %collective-permute-start.2 = (f32[8,1,2048]{2,0,1:T(8,128)S(1)}, f32[8,1,2048]{2,0,1:T(8,128)S(1)}, u32[]{:S(2)}, u32[]{:S(2)}) collective-permute-start(f32[8,1,2048]{2,0,1:T(8,128)S(1)} %get-tuple-element.10), channel_id=1, source_target_pairs={{1,0},{2,1},{3,2},{4,3},{5,4},{6,5},{7,6},{8,7},{9,8},{10,9},{11,1... | collective-permute-start | bytes 196616 | tf_op jit(solution)/shard_map/ppermute | solution.py:26
  17.0 6.9 %collective-permute-start.3 = (f32[8,1,2048]{2,0,1:T(8,128)S(1)}, f32[8,1,2048]{2,0,1:T(8,128)S(1)}, u32[]{:S(2)}, u32[]{:S(2)}) collective-permute-start(f32[8,1,2048]{2,0,1:T(8,128)S(1)} %get-tuple-element.9), channel_id=1, source_target_pairs={{0,1},{1,2},{2,3},{3,4},{4,5},{5,6},{6,7},{7,8},{8,9},{9,10},{10,1... | collective-permute-start | bytes 196616 | tf_op jit(solution)/shard_map/ppermute | solution.py:25
  39.2 20.9 %copy-start.6 = (s32[2048,1]{0,1:T(1,128)S(1)}, s32[2048,1]{0,1:T(1,128)}, u32[]{:S(2)}) copy-start(s32[2048,1]{0,1:T(1,128)} %param.19) | copy-start | bytes 24580
  39.2 57.2 %all-to-all-start = ((f32[4,1,131072]{2,1,0:T(1,128)}), f32[4,1,131072]{2,1,0:T(1,128)S(1)}, u32[]{:S(2)}, u32[]{:S(2)}) async-start(f32[4,1,131072]{2,1,0:T(1,128)} %reshape.264), calls=%async_computation | async-start | bytes 4194304 | tf_op jit(solution)/shard_map/all_to_all | solution.py:99
  47.8 22.3 %copy-start.7 = (f32[8]{0:T(128)S(1)}, f32[8]{0:T(128)}, u32[]{:S(2)}) copy-start(f32[8]{0:T(128)} %param.15) | copy-start | bytes 100
  47.8 22.9 %collective-permute-start.4 = (f32[1,512]{1,0:T(1,128)S(1)}, f32[1,512]{1,0:T(1,128)S(1)}, u32[]{:S(2)}, u32[]{:S(2)}) collective-permute-start(f32[1,512]{1,0:T(1,128)S(1)} %get-tuple-element.26), channel_id=1, source_target_pairs={{0,4},{4,8},{8,12},{12,16},{16,20},{20,24},{24,28},{1,5},{5,9},{9,... | collective-permute-start | bytes 6152 | tf_op jit(solution)/shard_map/ppermute | solution.py:25
  52.3 18.5 %collective-permute-start.6 = (f32[1,512]{1,0:T(1,128)S(1)}, f32[1,512]{1,0:T(1,128)S(1)}, u32[]{:S(2)}, u32[]{:S(2)}) collective-permute-start(f32[1,512]{1,0:T(1,128)S(1)} %get-tuple-element.25), channel_id=1, source_target_pairs={{4,0},{8,4},{12,8},{16,12},{20,16},{24,20},{28,24},{5,1},{9,5},{13... | collective-permute-start | bytes 6152 | tf_op jit(solution)/shard_map/ppermute | solution.py:26
  53.6 23.1 %collective-permute-start.5 = (f32[1,512]{1,0:T(1,128)S(1)}, f32[1,512]{1,0:T(1,128)S(1)}, u32[]{:S(2)}, u32[]{:S(2)}) collective-permute-start(f32[1,512]{1,0:T(1,128)S(1)} %get-tuple-element.27), channel_id=1, source_target_pairs={{0,4},{4,8},{8,12},{12,16},{16,20},{20,24},{24,28},{1,5},{5,9},{9,... | collective-permute-start | bytes 6152 | tf_op jit(solution)/shard_map/ppermute | solution.py:25
  58.8 17.9 %collective-permute-start.7 = (f32[1,512]{1,0:T(1,128)S(1)}, f32[1,512]{1,0:T(1,128)S(1)}, u32[]{:S(2)}, u32[]{:S(2)}) collective-permute-start(f32[1,512]{1,0:T(1,128)S(1)} %get-tuple-element.28), channel_id=1, source_target_pairs={{4,0},{8,4},{12,8},{16,12},{20,16},{24,20},{28,24},{5,1},{9,5},{13... | collective-permute-start | bytes 6152 | tf_op jit(solution)/shard_map/ppermute | solution.py:26
  70.9 51.6 %collective-permute-start.10 = (f32[130,1]{1,0:T(8,128)S(1)}, f32[130,1]{1,0:T(8,128)S(1)}, u32[]{:S(2)}, u32[]{:S(2)}) collective-permute-start(f32[130,1]{1,0:T(8,128)S(1)} %get-tuple-element.17), channel_id=1, source_target_pairs={{1,0},{2,1},{3,2},{5,4},{6,5},{7,6},{9,8},{10,9},{11,10},{13,12},{... | collective-permute-start | bytes 1568 | tf_op jit(solution)/shard_map/ppermute | solution.py:26
  72.2 50.3 %collective-permute-start.8 = (f32[130,1]{1,0:T(8,128)S(1)}, f32[130,1]{1,0:T(8,128)S(1)}, u32[]{:S(2)}, u32[]{:S(2)}) collective-permute-start(f32[130,1]{1,0:T(8,128)S(1)} %get-tuple-element.18), channel_id=1, source_target_pairs={{0,1},{1,2},{2,3},{4,5},{5,6},{6,7},{8,9},{9,10},{10,11},{12,13},{... | collective-permute-start | bytes 1568 | tf_op jit(solution)/shard_map/ppermute | solution.py:25
  77.4 45.1 %collective-permute-start.11 = (f32[130,1]{1,0:T(8,128)}, f32[130,1]{1,0:T(8,128)}, u32[]{:S(2)}, u32[]{:S(2)}) collective-permute-start(f32[130,1]{1,0:T(8,128)} %get-tuple-element.20), channel_id=1, source_target_pairs={{1,0},{2,1},{3,2},{5,4},{6,5},{7,6},{9,8},{10,9},{11,10},{13,12},{... | collective-permute-start | bytes 1568 | tf_op jit(solution)/shard_map/ppermute | solution.py:26
  78.7 43.8 %collective-permute-start.9 = (f32[130,1]{1,0:T(8,128)S(1)}, f32[130,1]{1,0:T(8,128)}, u32[]{:S(2)}, u32[]{:S(2)}) collective-permute-start(f32[130,1]{1,0:T(8,128)S(1)} %get-tuple-element.19), channel_id=1, source_target_pairs={{0,1},{1,2},{2,3},{4,5},{5,6},{6,7},{8,9},{9,10},{10,11},{12,13},{... | collective-permute-start | bytes 1568 | tf_op jit(solution)/shard_map/ppermute | solution.py:25
  122.5 23.0 %copy-start.9 = (s32[2048]{0:T(1024)S(1)}, s32[2048]{0:T(1024)}, u32[]{:S(2)}) copy-start(s32[2048]{0:T(1024)} %param.18) | copy-start | bytes 24580
  123.9 5.0 %collective-permute-start.12 = (f32[1,512]{1,0:T(1,128)S(1)}, f32[1,512]{1,0:T(1,128)S(1)}, u32[]{:S(2)}, u32[]{:S(2)}) collective-permute-start(f32[1,512]{1,0:T(1,128)S(1)} %get-tuple-element.23), channel_id=1, source_target_pairs={{0,4},{4,8},{8,12},{12,16},{16,20},{20,24},{24,28},{1,5},{5,9},{9,... | collective-permute-start | bytes 6152 | tf_op jit(solution)/shard_map/ppermute | solution.py:25
  127.6 5.5 %collective-permute-start.13 = (f32[1,512]{1,0:T(1,128)S(1)}, f32[1,512]{1,0:T(1,128)S(1)}, u32[]{:S(2)}, u32[]{:S(2)}) collective-permute-start(f32[1,512]{1,0:T(1,128)S(1)} %get-tuple-element.24), channel_id=1, source_target_pairs={{4,0},{8,4},{12,8},{16,12},{20,16},{24,20},{28,24},{5,1},{9,5},{13... | collective-permute-start | bytes 6152 | tf_op jit(solution)/shard_map/ppermute | solution.py:26
  133.2 3.2 %collective-permute-start.14 = (f32[130,1]{1,0:T(8,128)S(1)}, f32[130,1]{1,0:T(8,128)S(1)}, u32[]{:S(2)}, u32[]{:S(2)}) collective-permute-start(f32[130,1]{1,0:T(8,128)S(1)} %get-tuple-element.15), channel_id=1, source_target_pairs={{0,1},{1,2},{2,3},{4,5},{5,6},{6,7},{8,9},{9,10},{10,11},{12,13},{... | collective-permute-start | bytes 1568 | tf_op jit(solution)/shard_map/ppermute | solution.py:25
  134.5 6.2 %collective-permute-start.15 = (f32[130,1]{1,0:T(8,128)S(1)}, f32[130,1]{1,0:T(8,128)S(1)}, u32[]{:S(2)}, u32[]{:S(2)}) collective-permute-start(f32[130,1]{1,0:T(8,128)S(1)} %get-tuple-element.16), channel_id=1, source_target_pairs={{1,0},{2,1},{3,2},{5,4},{6,5},{7,6},{9,8},{10,9},{11,10},{13,12},{... | collective-permute-start | bytes 1568 | tf_op jit(solution)/shard_map/ppermute | solution.py:26
  141.1 16.3 %collective-permute-start.16 = (f32[1,512]{1,0:T(1,128)S(1)}, f32[1,512]{1,0:T(1,128)S(1)}, u32[]{:S(2)}, u32[]{:S(2)}) collective-permute-start(f32[1,512]{1,0:T(1,128)S(1)} %get-tuple-element.21), channel_id=1, source_target_pairs={{0,4},{4,8},{8,12},{12,16},{16,20},{20,24},{24,28},{1,5},{5,9},{9,... | collective-permute-start | bytes 6152 | tf_op jit(solution)/shard_map/ppermute | solution.py:25
  144.2 13.2 %collective-permute-start.17 = (f32[1,512]{1,0:T(1,128)S(1)}, f32[1,512]{1,0:T(1,128)S(1)}, u32[]{:S(2)}, u32[]{:S(2)}) collective-permute-start(f32[1,512]{1,0:T(1,128)S(1)} %get-tuple-element.22), channel_id=1, source_target_pairs={{4,0},{8,4},{12,8},{16,12},{20,16},{24,20},{28,24},{5,1},{9,5},{13... | collective-permute-start | bytes 6152 | tf_op jit(solution)/shard_map/ppermute | solution.py:26
  157.5 17.1 %collective-permute-start.18 = (f32[130,1]{1,0:T(8,128)S(1)}, f32[130,1]{1,0:T(8,128)S(1)}, u32[]{:S(2)}, u32[]{:S(2)}) collective-permute-start(f32[130,1]{1,0:T(8,128)S(1)} %get-tuple-element.13), channel_id=1, source_target_pairs={{0,1},{1,2},{2,3},{4,5},{5,6},{6,7},{8,9},{9,10},{10,11},{12,13},{... | collective-permute-start | bytes 1568 | tf_op jit(solution)/shard_map/ppermute | solution.py:25
  161.2 13.5 %collective-permute-start.19 = (f32[130,1]{1,0:T(8,128)S(1)}, f32[130,1]{1,0:T(8,128)S(1)}, u32[]{:S(2)}, u32[]{:S(2)}) collective-permute-start(f32[130,1]{1,0:T(8,128)S(1)} %get-tuple-element.14), channel_id=1, source_target_pairs={{1,0},{2,1},{3,2},{5,4},{6,5},{7,6},{9,8},{10,9},{11,10},{13,12},{... | collective-permute-start | bytes 1568 | tf_op jit(solution)/shard_map/ppermute | solution.py:26
  (9 other events, 90.5 us)
where the time goes:
time: 218 us; the launch traced here: 217 us
  local copies, waits for them, and re-layouts  75 us (34%)
  starting transfers between devices  63.5 us (29%)
  other arithmetic  35.5 us (16%)
  waiting for transfers between devices  24.1 us (11%)
  blocking collectives  17.7 us (8%)
    ppermute x10, starting transfers between devices, with_halo(): before = lax.ppermute(last, axis, up)  41.7 us
    gather x2, local copies, waits for them, and re-layouts, body(): increment = warp.reshape(-1)[joint_cell] - warp_prev.reshape(-1)[joint_cell]  23.6 us
    all_to_all x1, blocking collectives, body(): lax.all_to_all(outgoing, ('gx', 'gy'), split_axis=1, concat_axis=1, tiled...  17.7 us
    unnamed x30, local copies, waits for them, and re-layouts  17.7 us
    ppermute x10, starting transfers between devices, with_halo(): after = lax.ppermute(leading, axis, down)  13.1 us
    all_to_all x1, waiting for transfers between devices, body(): lax.all_to_all(temp, 'gy', split_axis=2, concat_axis=1, tiled=True)  12.6 us
    gather x1, local copies, waits for them, and re-layouts, body(): theta = top.reshape(-1)[joint_cell]  11.8 us
    another operation x3, other arithmetic  9.41 us
  transfers between devices with their start and end apart: 21, of which 5 were waited for; matrix products, arithmetic and copies ran while one was open for 28% of the time, Pallas kernels for 0%

commit v1 on v0

--- a/solution.py
+++ b/solution.py
@@ -14,16 +14,22 @@
 sat_power = 0.3
 harden = 2.0
 
+FLAT = ("gx", "gy")
+
+
+def exchange(last, leading, axis):
+    count = lax.axis_size(axis)
+    up = [(i, i + 1) for i in range(count - 1)]
+    down = [(j, i) for i, j in up]
+    return lax.ppermute(last, axis, up), lax.ppermute(leading, axis, down)
+
 
 def with_halo(array, sides, width):
     for axis, dim in sides:
-        count, length = (lax.axis_size(axis), array.shape[dim])
-        up = [(i, (i + 1) % count) for i in range(count - 1)]
-        down = [(j, i) for i, j in up]
+        length = array.shape[dim]
         last = lax.slice_in_dim(array, length - width, length, axis=dim)
         leading = lax.slice_in_dim(array, 0, width, axis=dim)
-        before = lax.ppermute(last, axis, up)
-        after = lax.ppermute(leading, axis, down)
+        before, after = exchange(last, leading, axis)
         array = jnp.concatenate([before, array, after], axis=dim)
     return array
 
@@ -78,6 +84,67 @@
     return (strain_out, jnp.where(keep, resist_new, resist))
 
 
+def thermal(temp, heat, lateral, vertical):
+    devices = lax.axis_size(FLAT)
+    t = lax.axis_index(FLAT)
+    rows = temp.shape[1]
+    h = STEPS
+    last = jnp.concatenate([temp[:, rows - h:], heat[:, rows - (h - 1):]], axis=1)
+    leading = jnp.concatenate([temp[:, :h], heat[:, : h - 1]], axis=1)
+    before, after = exchange(last, leading, FLAT)
+    ext = jnp.concatenate([before[:, :h], temp, after[:, :h]], axis=1)
+    heat_ext = jnp.concatenate([before[:, h:], heat, after[:, h:]], axis=1)
+    for step in range(1, STEPS + 1):
+        r = STEPS - step
+        heat_rows = heat_ext[:, h - 1 - r: h - 1 - r + rows + 2 * r]
+        ext = thermal_step(ext, heat_rows, lateral, vertical)
+        if r > 0:
+            g = t * rows + jnp.arange(-r, rows + r)
+            inside = (g >= 0) & (g < devices * rows)
+            ext = jnp.where(inside[None, :, None], ext, 0.0)
+    return ext
+
+
+def relay(load, top, width):
+    n_gy = lax.axis_size("gy")
+    rows, cols = load.shape
+    cm = cols // n_gy
+    before, after = exchange(load[rows - width:], load[:width], FLAT)
+    load_ext = jnp.concatenate([before, load, after], axis=0)
+    lp = jnp.pad(load_ext, ((0, 0), (width, width)))
+    tp = jnp.pad(top, ((width, width), (width, width)))
+    both = jnp.stack([lp, tp])
+    send = jnp.stack([both[:, :, k * cm: k * cm + cm + 2 * width] for k in range(n_gy)])
+    recv = lax.all_to_all(send, "gy", split_axis=0, concat_axis=0, tiled=True)
+    parts = []
+    for k in range(n_gy):
+        lo = 0 if k == 0 else width
+        hi = rows + 2 * width if k == n_gy - 1 else rows + width
+        parts.append(recv[k, 0, lo:hi])
+    load_m = jnp.concatenate(parts, axis=0)
+    top_m = jnp.concatenate(
+        [recv[k, 1, width: rows + width, width: cm + width] for k in range(n_gy)], axis=0
+    )
+    return load_m, top_m
+
+
+def joint_ranks(owners, devices):
+    count = owners.shape[0]
+    block = 128 if count % 128 == 0 else count
+    nb = count // block
+    onehot = (owners[:, None] == jnp.arange(devices, dtype=jnp.int32)[None, :]).astype(jnp.float32)
+    oh = onehot.reshape(nb, block, devices)
+    ar = jnp.arange(block)
+    tri = (ar[:, None] >= ar[None, :]).astype(jnp.float32)
+    within = jnp.einsum("ij,bjd->bid", tri, oh, precision=lax.Precision.HIGHEST)
+    totals = within[:, -1, :]
+    ab = jnp.arange(nb)
+    stri = (ab[:, None] > ab[None, :]).astype(jnp.float32)
+    offs = jnp.dot(stri, totals, precision=lax.Precision.HIGHEST)
+    cum = (within + offs[:, None, :]).reshape(count, devices)
+    return jnp.sum(cum * onehot, axis=1).astype(jnp.int32) - 1
+
+
 def body(
     temp_start,
     heat_input,
@@ -91,29 +158,40 @@
     joint_strain,
     joint_resist,
 ):
-    devices = lax.axis_size(("gx", "gy"))
-    temp = temp_start
-    for step in range(STEPS):
-        ext = with_halo(temp, ((("gx", "gy"), 1),), 1)
-        temp = thermal_step(ext, heat_input, lateral, vertical)
-    relayed = lax.all_to_all(temp, "gy", split_axis=2, concat_axis=1, tiled=True)
-    load = moment_of(relayed, weighting)
-    top = relayed[-1]
-    e_pad = with_halo(modulus, (("gx", 0), ("gy", 1)), 1)
-    warp = warp_prev
-    for step in range(SWEEPS):
-        w_pad = with_halo(warp, (("gx", 0), ("gy", 1)), 1)
-        warp = sweep(w_pad, e_pad, load)
+    devices = lax.axis_size(FLAT)
+    n_gx, n_gy = lax.axis_size("gx"), lax.axis_size("gy")
+    gi, gj = lax.axis_index("gx"), lax.axis_index("gy")
+    rm, cm = warp_prev.shape
+
+    wm = with_halo(jnp.stack([warp_prev, modulus]), (("gx", 1), ("gy", 2)), SWEEPS)
+    owners = joint_owner[:, 0]
     capacity = joint_resist.shape[1] // devices
-    owners = joint_owner[:, 0]
-    increment = warp.reshape(-1)[joint_cell] - warp_prev.reshape(-1)[joint_cell]
-    theta = top.reshape(-1)[joint_cell]
-    values = jnp.stack([increment, theta, jnp.ones_like(theta)])
-    onehot = (owners[:, None] == jnp.arange(devices, dtype=jnp.int32)[None, :]).astype(jnp.int32)
-    ranks = jnp.sum(jnp.cumsum(onehot, axis=0) * onehot, axis=1) - 1
-    slots = owners * capacity + ranks
+    slots = owners * capacity + joint_ranks(owners, devices)
+
+    temp = thermal(temp_start, heat_input, lateral, vertical)
+    load_t = moment_of(temp, weighting)
+    load, top = relay(load_t, temp[-1], SWEEPS - 1)
+
+    warp = wm[0]
+    mod_ext = wm[1]
+    for step in range(1, SWEEPS + 1):
+        r = SWEEPS - step
+        off = SWEEPS - (r + 1)
+        e_pad = mod_ext[off: off + rm + 2 * r + 2, off: off + cm + 2 * r + 2]
+        lo = SWEEPS - 1 - r
+        ld = load[lo: lo + rm + 2 * r, lo: lo + cm + 2 * r]
+        warp = sweep(warp, e_pad, ld)
+        if r > 0:
+            gr = gi * rm + jnp.arange(-r, rm + r)
+            gc = gj * cm + jnp.arange(-r, cm + r)
+            inside = ((gr >= 0) & (gr < n_gx * rm))[:, None] & ((gc >= 0) & (gc < n_gy * cm))[None, :]
+            warp = jnp.where(inside, warp, 0.0)
+
+    fields = jnp.stack([(warp - warp_prev).reshape(-1), top.reshape(-1)])
+    picked = fields[:, joint_cell]
+    values = jnp.concatenate([picked, jnp.ones_like(picked[:1])], axis=0)
     outgoing = jnp.zeros((3, devices * capacity), jnp.float32).at[:, slots].set(values)
-    incoming = lax.all_to_all(outgoing, ("gx", "gy"), split_axis=1, concat_axis=1, tiled=True)
+    incoming = lax.all_to_all(outgoing, FLAT, split_axis=1, concat_axis=1, tiled=True)
     strain_next, resist_next = anand(joint_strain, joint_resist, incoming[:, None, :])
     return (warp, strain_next, resist_next)
 
@@ -123,18 +201,18 @@
         body,
         mesh=mesh,
         in_specs=(
-            P(None, ("gx", "gy"), None),
-            P(None, ("gx", "gy"), None),
+            P(None, FLAT, None),
+            P(None, FLAT, None),
             P(),
             P(),
             P(),
             P("gx", "gy"),
             P("gx", "gy"),
-            P(("gx", "gy")),
-            P(("gx", "gy"), None),
-            P(None, ("gx", "gy"), None),
-            P(("gx", "gy"), None),
+            P(FLAT),
+            P(FLAT, None),
+            P(None, FLAT, None),
+            P(FLAT, None),
         ),
-        out_specs=(P("gx", "gy"), P(None, ("gx", "gy"), None), P(("gx", "gy"), None)),
+        out_specs=(P("gx", "gy"), P(None, FLAT, None), P(FLAT, None)),
         check_vma=False,
     )

time: 218 us -> 137 us (0.63)
  starting transfers between devices: 63.5 us -> 26.7 us
  local copies, waits for them, and re-layouts: 75 us -> 51 us
  other arithmetic: 35.5 us -> 20.7 us
  waiting for transfers between devices: 24.1 us -> 20.8 us
  blocking collectives: 17.7 us -> 15.4 us
    ppermute x20 -> x8, starting transfers between devices: 54.9 us -> 21.4 us  [exchange(): return (lax.ppermute(last, axis, up), lax.ppermute(leading, axis, down))]
    gather x3 -> x1, local copies, waits for them, and re-layouts: 35.3 us -> 18.2 us  [body(): picked = fields[:, joint_cell]]
    unnamed x30 -> x22, local copies, waits for them, and re-layouts: 17.7 us -> 1.59 us
    another operation x3, local copies, waits for them, and re-layouts: 1.69 us -> 16.2 us  [the longest x1 15.6 us: body(): fields = jnp.stack([(warp - warp_prev).reshape(-1), top.reshape(-1)])]
    all_to_all x1, waiting for transfers between devices: 12.6 us -> 4.28 us  [relay(): recv = lax.all_to_all(send, 'gy', split_axis=0, concat_axis=0, tiled=True)]
    all_to_all x1 -> x0, other arithmetic: 7.72 us -> none  [body(): lax.all_to_all(temp, 'gy', split_axis=2, concat_axis=1, tiled=True)]
    another operation x4, other arithmetic: 9.48 us -> 2.56 us  [the longest x2 1.89 us: relay(): jnp.stack([both[:, :, k * cm:k * cm + cm + 2 * width] for k in range(n_gy)])]
    all_to_all x3 -> x1, local copies, waits for them, and re-layouts: 7.11 us -> 1.47 us  [body(): lax.all_to_all(outgoing, FLAT, split_axis=1, concat_axis=1, tiled=True)]
  transfers between devices with their start and end apart: 21 -> 9, of which waited for: 5 -> 4; matrix products, arithmetic and copies ran while one was open for 28% -> 14% of each run, Pallas kernels for 0% -> 0%
where the time goes in v1:
time: 137 us
  local copies, waits for them, and re-layouts  51 us (37%)
  starting transfers between devices  26.7 us (19%)
  waiting for transfers between devices  20.8 us (15%)
  other arithmetic  20.7 us (15%)
  blocking collectives  15.4 us (11%)
    ppermute x8, starting transfers between devices, exchange(): return (lax.ppermute(last, axis, up), lax.ppermute(leading, axis, down))  21.4 us
    gather x1, local copies, waits for them, and re-layouts, body(): picked = fields[:, joint_cell]  18.2 us
    ppermute x8, waiting for transfers between devices, exchange(): return (lax.ppermute(last, axis, up), lax.ppermute(leading, axis, down))  16.5 us
    another operation x1, local copies, waits for them, and re-layouts, body(): fields = jnp.stack([(warp - warp_prev).reshape(-1), top.reshape(-1)])  15.6 us
    all_to_all x1, blocking collectives, body(): lax.all_to_all(outgoing, FLAT, split_axis=1, concat_axis=1, tiled=True)  15.4 us
    scatter x1, local copies, waits for them, and re-layouts, body(): jnp.zeros((3, devices * capacity), jnp.float32).at[:, slots].set(values)  6.81 us
    all_to_all x1, starting transfers between devices, relay(): recv = lax.all_to_all(send, 'gy', split_axis=0, concat_axis=0, tiled=True)  5.38 us
    add x1, other arithmetic, moment_of(): total = total + weighting[layer] * field[layer]  5.21 us
  transfers between devices with their start and end apart: 9, of which 4 were waited for; matrix products, arithmetic and copies ran while one was open for 14% of the time, Pallas kernels for 0%

profile of v1, /device:TPU:0, one launch (start us, length us, event | category | flops | bytes accessed | tf_op | source)
XLA Modules:
  0.0 136.8 jit_solution(4110263155972718763)
XLA Ops:
  0.7 1.4 %fusion.88 = (f32[8,2,2048]{2,1,0:T(2,128)S(1)}, f32[8,2,2048]{2,1,0:T(2,128)S(1)}) fusion(f32[8,32,2048]{2,1,0:T(8,128)} %param.11), kind=kLoop, calls=%fused_computation.191 | loop fusion | bytes 524288 | tf_op jit(solution)/shard_map/slice | solution.py:92
  2.1 1.3 fusion.89
  3.5 5.0 %collective-permute-start = (f32[8,3,2048]{2,1,0:T(4,128)S(1)}, f32[8,3,2048]{2,1,0:T(4,128)S(1)}, u32[]{:S(2)}, u32[]{:S(2)}) collective-permute-start(f32[8,3,2048]{2,1,0:T(4,128)S(1)} %pad_maximum_fusion.5), channel_id=1, source_target_pairs={{0,1},{1,2},{2,3},{3,4},{4,5},{5,6},{6,7},{7,8},{8,9},{9,10},{10,1... | collective-permute-start | bytes 589832 | tf_op jit(solution)/shard_map/ppermute | solution.py:24
  8.6 1.3 collective-permute-start.1
  10.7 4.7 %collective-permute-start.4 = (f32[2,3,512]{2,1,0:T(4,128)S(1)}, f32[2,3,512]{2,1,0:T(4,128)S(1)}, u32[]{:S(2)}, u32[]{:S(2)}) collective-permute-start(f32[2,3,512]{2,1,0:T(4,128)S(1)} %get-tuple-element.31), channel_id=1, source_target_pairs={{0,4},{4,8},{8,12},{12,16},{16,20},{20,24},{24,28},{1,5},{5,9},{9,... | collective-permute-start | bytes 36872 | tf_op jit(solution)/shard_map/ppermute | solution.py:24
  15.4 1.3 collective-permute-start.5
  16.7 1.6 %fusion.94 = (f32[1]{0:T(128)}, f32[1]{0:T(128)}, f32[1]{0:T(128)}, f32[1]{0:T(128)}, f32[1]{0:T(128)}, /*index=5*/f32[1]{0:T(128)}, f32[1]{0:T(128)}, f32[1]{0:T(128)}) fusion(f32[8]{0:T(128)} %param.15), kind=kLoop, calls=%fused_computation.197 | loop fusion | bytes 64 | tf_op jit(solution)/shard_map/slice | solution.py:47
  19.9 3.4 %collective-permute-done.1 = f32[8,3,2048]{2,1,0:T(4,128)S(1)} collective-permute-done((f32[8,3,2048]{2,1,0:T(4,128)S(1)}, f32[8,3,2048]{2,1,0:T(4,128)S(1)}, u32[]{:S(2)}, u32[]{:S(2)}) %collective-permute-start.1) | collective-permute-done | bytes 196640 | tf_op jit(solution)/shard_map/ppermute | solution.py:24
  25.3 3.0 %fusion.7 = f32[8,34,2048]{2,1,0:T(8,128)S(1)} fusion(f32[8,36,2048]{2,1,0:T(8,128)S(1)} %pad_maximum_fusion, f32[8,2,2048]{2,1,0:T(2,128)S(1)} %slice.403, f32[8,32,2048]{2,1,0:T(8,128)S(1)} %copy-done, f32[8,2,2048]{2,1,0:T(2,128)S(1)} %slice.402, f32[8,1,2048]{2,1,0:T(1,128)S(1)} %slice.408, f32[8,32,2048]{2,1,0:T(8,128)S(1)} %copy-done.1, ...), kind=kLoop, calls=%fused_computation.13 | loop fusion | flops 8355840 | bytes 14353408 | tf_op jit(solution)/shard_map/jit(_where)/select_n | solution.py:104
  28.8 1.9 %fusion.15 = f32[8,32,2048]{2,1,0:T(8,128)S(1)} fusion(f32[8,32,2048]{2,1,0:T(8,128)S(1)} %copy-done.1, f32[8,34,2048]{2,1,0:T(8,128)S(1)} %fusion.7, f32[7,32,2048]{2,1,0:T(8,128)S(1)} %fusion.16, f32[8]{0:T(128)S(1)} %copy-done.9), kind=kLoop, calls=%fused_computation.24 | loop fusion | flops 5242880 | bytes 14942720 | tf_op jit(solution)/shard_map/add | solution.py:43
  30.7 5.2 %fusion.54 = f32[32,2048]{1,0:T(8,128)S(1)} fusion(f32[8,32,2048]{2,1,0:T(8,128)S(1)} %fusion.15, f32[]{:T(128)} %bitcast.8, f32[]{:T(128)} %bitcast.6, f32[]{:T(128)} %bitcast.5, f32[]{:T(128)} %bitcast.4, f32[]{:T(128)} %bitcast.3, f32[]{:T(128)} %bitcast.2, f32[]{:T(128)} %bitcast.1, f32[]{:T(128)} %bitcast), kind=kLoop, calls=%fused_computation.109 | loop fusion | flops 983040 | bytes 2359328 | tf_op jit(solution)/shard_map/add | solution.py:49
  35.9 2.5 %collective-permute-start.2 = (f32[2,2048]{1,0:T(2,128)S(1)}, f32[2,2048]{1,0:T(2,128)S(1)}, u32[]{:S(2)}, u32[]{:S(2)}) collective-permute-start(f32[2,2048]{1,0:T(2,128)S(1)} %get-tuple-element.33), channel_id=1, source_target_pairs={{0,1},{1,2},{2,3},{3,4},{4,5},{5,6},{6,7},{7,8},{8,9},{9,10},{10,1... | collective-permute-start | bytes 49160 | tf_op jit(solution)/shard_map/ppermute | solution.py:24
  40.1 3.9 %collective-permute-done.3 = f32[2,2048]{1,0:T(2,128)S(1)} collective-permute-done((f32[2,2048]{1,0:T(2,128)S(1)}, f32[2,2048]{1,0:T(2,128)S(1)}, u32[]{:S(2)}, u32[]{:S(2)}) %collective-permute-start.3) | collective-permute-done | bytes 16416 | tf_op jit(solution)/shard_map/ppermute | solution.py:24
  46.5 5.4 %all-to-all-start = ((f32[4,2,36,516]{3,1,2,0:T(2,128)}), f32[4,2,36,516]{3,1,2,0:T(2,128)S(1)}, u32[]{:S(2)}, u32[]{:S(2)}) async-start(f32[4,2,36,516]{3,1,2,0:T(2,128)} %pad_maximum_fusion.1), calls=%async_computation | async-start | bytes 1474560 | tf_op jit(solution)/shard_map/all_to_all | solution.py:118
  52.1 3.9 %collective-permute-start.6 = (f32[2,134,3]{2,1,0:T(8,128)S(1)}, f32[2,134,3]{2,1,0:T(8,128)S(1)}, u32[]{:S(2)}, u32[]{:S(2)}) collective-permute-start(f32[2,134,3]{2,1,0:T(8,128)S(1)} %get-tuple-element.29), channel_id=1, source_target_pairs={{0,1},{1,2},{2,3},{4,5},{5,6},{6,7},{8,9},{9,10},{10,11},{12,13},{... | collective-permute-start | bytes 9656 | tf_op jit(solution)/shard_map/ppermute | solution.py:24
  56.0 1.5 %collective-permute-start.7 = (f32[2,134,3]{2,1,0:T(8,128)S(1)}, f32[2,134,3]{2,1,0:T(8,128)S(1)}, u32[]{:S(2)}, u32[]{:S(2)}) collective-permute-start(f32[2,134,3]{2,1,0:T(8,128)S(1)} %get-tuple-element.30), channel_id=1, source_target_pairs={{1,0},{2,1},{3,2},{5,4},{6,5},{7,6},{9,8},{10,9},{11,10},{13,12},{... | collective-permute-start | bytes 9656 | tf_op jit(solution)/shard_map/ppermute | solution.py:24
  57.5 9.2 %collective-permute-done.6 = f32[2,134,3]{2,1,0:T(8,128)S(1)} collective-permute-done((f32[2,134,3]{2,1,0:T(8,128)S(1)}, f32[2,134,3]{2,1,0:T(8,128)S(1)}, u32[]{:S(2)}, u32[]{:S(2)}) %collective-permute-start.6) | collective-permute-done | bytes 3248 | tf_op jit(solution)/shard_map/ppermute | solution.py:24
  67.1 4.3 %all-to-all-done = f32[4,2,36,516]{3,1,2,0:T(2,128)S(1)} async-done(((f32[4,2,36,516]{3,1,2,0:T(2,128)}), f32[4,2,36,516]{3,1,2,0:T(2,128)S(1)}, u32[]{:S(2)}, u32[]{:S(2)}) %all-to-all-start) | async-done | bytes 594464 | tf_op jit(solution)/shard_map/all_to_all | solution.py:118
  74.4 1.4 %subtract_bitcast_fusion = (f32[1,1,128,512]{3,2,1,0:T(8,128)S(1)}, f32[128,512]{1,0:T(8,128)}) fusion(f32[128,512]{1,0:T(8,128)S(1)} %copy-done.2, f32[130,514]{1,0:T(8,128)S(1)} %fusion.23, f32[134,518]{1,0:T(8,128)S(1)} %get-tuple-element.23, f32[132,516]{1,0:T(8,128)S(1)} %get-tuple-element.10), kind=kLoop, calls=%fused_computation.124 | loop fusion | flops 1441792 | bytes 3407872
  76.6 15.6 %copy.24 = f32[2,65536]{0,1:T(8,128)} copy(f32[2,65536]{1,0:T(2,128)S(1)} %pad_maximum_fusion.3) | data formatting | bytes 1048576 | tf_op jit(solution)/shard_map/stack | solution.py:190
  92.2 18.2 %gather_fusion = f32[2048,2]{1,0:T(8,128)} fusion(f32[2,65536]{0,1:T(8,128)} %copy.24, s32[2048]{0:T(1024)S(1)} %fusion.79), kind=kCustom, calls=%fused_computation | custom fusion | bytes 40960 | tf_op jit(solution)/shard_map/gather | solution.py:191
  110.4 6.8 %scatter_custom_fusion = f32[3,6144]{0,1:T(8,128)S(1)} fusion(s32[2048]{0:T(1024)S(1)} %bitcast.102, f32[]{:T(128)} %constant.34.clone.1, f32[2,2048]{0,1:T(8,128)} %bitcast.96, f32[]{:T(128)} %constant.45.clone.1), kind=kCustom, calls=%fused_computation.28 | custom fusion | bytes 90120 | tf_op jit(solution)/shard_map/scatter | solution.py:193
  117.2 1.5 %copy.25 = f32[3,32,192]{2,0,1:T(4,128)S(1)} copy(f32[3,32,192]{0,2,1:T(8,128)S(1)} %bitcast.89) | data formatting | bytes 147456 | tf_op jit(solution)/shard_map/all_to_all | solution.py:194
  118.7 15.4 %all_to_all.14 = f32[3,32,192]{2,0,1:T(4,128)S(1)} all-to-all(f32[3,32,192]{2,0,1:T(4,128)S(1)} %copy.25), channel_id=1, replica_groups=mesh['gx'=8,'gy'=4] {'gx','gy'}, dimensions={1} | all-to-all | bytes 147456 | tf_op jit(solution)/shard_map/all_to_all | solution.py:194
  (83 shorter events, 16.0 us)
Async XLA Ops:
  0.6 22.7 %copy-start = (f32[8,32,2048]{2,1,0:T(8,128)S(1)}, f32[8,32,2048]{2,1,0:T(8,128)}, u32[]{:S(2)}) copy-start(f32[8,32,2048]{2,1,0:T(8,128)} %param.11) | copy-start | bytes 6291460
  0.6 19.0 %copy-start.5 = (s32[2048,1]{0,1:T(1,128)S(1)}, s32[2048,1]{0,1:T(1,128)}, u32[]{:S(2)}) copy-start(s32[2048,1]{0,1:T(1,128)} %param.19) | copy-start | bytes 24580
  0.7 19.2 %copy-start.7 = (s32[2048]{0:T(1024)S(1)}, s32[2048]{0:T(1024)}, u32[]{:S(2)}) copy-start(s32[2048]{0:T(1024)} %param.18) | copy-start | bytes 24580
  3.5 16.3 %collective-permute-start = (f32[8,3,2048]{2,1,0:T(4,128)S(1)}, f32[8,3,2048]{2,1,0:T(4,128)S(1)}, u32[]{:S(2)}, u32[]{:S(2)}) collective-permute-start(f32[8,3,2048]{2,1,0:T(4,128)S(1)} %pad_maximum_fusion.5), channel_id=1, source_target_pairs={{0,1},{1,2},{2,3},{3,4},{4,5},{5,6},{6,7},{7,8},{8,9},{9,10},{10,1... | collective-permute-start | bytes 589832 | tf_op jit(solution)/shard_map/ppermute | solution.py:24
  8.6 14.6 %collective-permute-start.1 = (f32[8,3,2048]{2,1,0:T(4,128)S(1)}, f32[8,3,2048]{2,1,0:T(4,128)S(1)}, u32[]{:S(2)}, u32[]{:S(2)}) collective-permute-start(f32[8,3,2048]{2,1,0:T(4,128)S(1)} %pad_maximum_fusion.6), channel_id=1, source_target_pairs={{1,0},{2,1},{3,2},{4,3},{5,4},{6,5},{7,6},{8,7},{9,8},{10,9},{11,1... | collective-permute-start | bytes 589832 | tf_op jit(solution)/shard_map/ppermute | solution.py:24
  10.7 41.2 %collective-permute-start.4 = (f32[2,3,512]{2,1,0:T(4,128)S(1)}, f32[2,3,512]{2,1,0:T(4,128)S(1)}, u32[]{:S(2)}, u32[]{:S(2)}) collective-permute-start(f32[2,3,512]{2,1,0:T(4,128)S(1)} %get-tuple-element.31), channel_id=1, source_target_pairs={{0,4},{4,8},{8,12},{12,16},{16,20},{20,24},{24,28},{1,5},{5,9},{9,... | collective-permute-start | bytes 36872 | tf_op jit(solution)/shard_map/ppermute | solution.py:24
  15.4 36.5 %collective-permute-start.5 = (f32[2,3,512]{2,1,0:T(4,128)S(1)}, f32[2,3,512]{2,1,0:T(4,128)S(1)}, u32[]{:S(2)}, u32[]{:S(2)}) collective-permute-start(f32[2,3,512]{2,1,0:T(4,128)S(1)} %get-tuple-element.32), channel_id=1, source_target_pairs={{4,0},{8,4},{12,8},{16,12},{20,16},{24,20},{28,24},{5,1},{9,5},{13... | collective-permute-start | bytes 36872 | tf_op jit(solution)/shard_map/ppermute | solution.py:24
  19.9 3.8 %copy-start.8 = (f32[7]{0:T(128)S(1)}, f32[7]{0:T(128)}, u32[]{:S(2)}) copy-start(f32[7]{0:T(128)} %param.14) | copy-start | bytes 88
  23.7 1.6 %copy-start.1 = (f32[8,32,2048]{2,1,0:T(8,128)S(1)}, f32[8,32,2048]{2,1,0:T(8,128)}, u32[]{:S(2)}) copy-start(f32[8,32,2048]{2,1,0:T(8,128)} %param.12) | copy-start | bytes 6291460
  23.8 1.6 %copy-start.9 = (f32[8]{0:T(128)S(1)}, f32[8]{0:T(128)}, u32[]{:S(2)}) copy-start(f32[8]{0:T(128)} %param.13) | copy-start | bytes 100
  35.9 4.2 %collective-permute-start.2 = (f32[2,2048]{1,0:T(2,128)S(1)}, f32[2,2048]{1,0:T(2,128)S(1)}, u32[]{:S(2)}, u32[]{:S(2)}) collective-permute-start(f32[2,2048]{1,0:T(2,128)S(1)} %get-tuple-element.33), channel_id=1, source_target_pairs={{0,1},{1,2},{2,3},{3,4},{4,5},{5,6},{6,7},{7,8},{8,9},{9,10},{10,1... | collective-permute-start | bytes 49160 | tf_op jit(solution)/shard_map/ppermute | solution.py:24
  38.4 5.6 %collective-permute-start.3 = (f32[2,2048]{1,0:T(2,128)S(1)}, f32[2,2048]{1,0:T(2,128)S(1)}, u32[]{:S(2)}, u32[]{:S(2)}) collective-permute-start(f32[2,2048]{1,0:T(2,128)S(1)} %get-tuple-element.34), channel_id=1, source_target_pairs={{1,0},{2,1},{3,2},{4,3},{5,4},{6,5},{7,6},{8,7},{9,8},{10,9},{11,1... | collective-permute-start | bytes 49160 | tf_op jit(solution)/shard_map/ppermute | solution.py:24
  44.2 7.7 %copy-start.2 = (f32[128,512]{1,0:T(8,128)S(1)}, f32[128,512]{1,0:T(8,128)}, u32[]{:S(2)}) copy-start(f32[128,512]{1,0:T(8,128)} %param.17) | copy-start | bytes 786436
  44.2 7.7 %copy-start.3 = (f32[128,512]{1,0:T(8,128)S(1)}, f32[128,512]{1,0:T(8,128)}, u32[]{:S(2)}) copy-start(f32[128,512]{1,0:T(8,128)} %param.16) | copy-start | bytes 786436
  46.5 24.8 %all-to-all-start = ((f32[4,2,36,516]{3,1,2,0:T(2,128)}), f32[4,2,36,516]{3,1,2,0:T(2,128)S(1)}, u32[]{:S(2)}, u32[]{:S(2)}) async-start(f32[4,2,36,516]{3,1,2,0:T(2,128)} %pad_maximum_fusion.1), calls=%async_computation | async-start | bytes 1474560 | tf_op jit(solution)/shard_map/all_to_all | solution.py:118
  52.1 14.6 %collective-permute-start.6 = (f32[2,134,3]{2,1,0:T(8,128)S(1)}, f32[2,134,3]{2,1,0:T(8,128)S(1)}, u32[]{:S(2)}, u32[]{:S(2)}) collective-permute-start(f32[2,134,3]{2,1,0:T(8,128)S(1)} %get-tuple-element.29), channel_id=1, source_target_pairs={{0,1},{1,2},{2,3},{4,5},{5,6},{6,7},{8,9},{9,10},{10,11},{12,13},{... | collective-permute-start | bytes 9656 | tf_op jit(solution)/shard_map/ppermute | solution.py:24
  56.0 10.7 %collective-permute-start.7 = (f32[2,134,3]{2,1,0:T(8,128)S(1)}, f32[2,134,3]{2,1,0:T(8,128)S(1)}, u32[]{:S(2)}, u32[]{:S(2)}) collective-permute-start(f32[2,134,3]{2,1,0:T(8,128)S(1)} %get-tuple-element.30), channel_id=1, source_target_pairs={{1,0},{2,1},{3,2},{5,4},{6,5},{7,6},{9,8},{10,9},{11,10},{13,12},{... | collective-permute-start | bytes 9656 | tf_op jit(solution)/shard_map/ppermute | solution.py:24
  117.2 17.7 %copy-start.4 = (f32[2,1,6144]{2,1,0:T(1,128)S(1)}, f32[2,1,6144]{2,1,0:T(1,128)}, u32[]{:S(2)}) copy-start(f32[2,1,6144]{2,1,0:T(1,128)} %param.20) | copy-start | bytes 147460
  117.2 17.7 %copy-start.6 = (f32[1,6144]{1,0:T(1,128)S(1)}, f32[1,6144]{1,0:T(1,128)}, u32[]{:S(2)}) copy-start(f32[1,6144]{1,0:T(1,128)} %param.21) | copy-start | bytes 73732

commit v2 on v1

--- a/solution.py
+++ b/solution.py
@@ -2,6 +2,7 @@
 import jax.numpy as jnp
 from jax import lax
 from jax.sharding import PartitionSpec as P
+from jax.experimental import pallas as pl
 
 STEPS = 2
 SWEEPS = 3
@@ -145,6 +146,49 @@
     return jnp.sum(cum * onehot, axis=1).astype(jnp.int32) - 1
 
 
+def pick_kernel(rc_ref, parts_ref, out_ref):
+    rc = rc_ref[...]
+    rows = rc[:, 0:1]
+    cols = rc[:, 1:2]
+    block = rc.shape[0]
+    _, rm, width = parts_ref.shape
+    fields = out_ref.shape[1]
+    cm = width // fields
+    hit = rows == lax.broadcasted_iota(jnp.int32, (block, rm), 1)
+    onehot = jnp.where(hit, 1.0, 0.0).astype(jnp.bfloat16)
+    acc = jnp.dot(onehot, parts_ref[0], preferred_element_type=jnp.float32)
+    acc = acc + jnp.dot(onehot, parts_ref[1], preferred_element_type=jnp.float32)
+    acc = acc + jnp.dot(onehot, parts_ref[2], preferred_element_type=jnp.float32)
+    lane = cols == lax.broadcasted_iota(jnp.int32, (block, cm), 1)
+    for f in range(fields):
+        seg = acc[:, f * cm: (f + 1) * cm]
+        out_ref[:, f: f + 1] = jnp.sum(jnp.where(lane, seg, 0.0), axis=1, keepdims=True)
+
+
+def pick_cells(fields, cells):
+    count = cells.shape[0]
+    nf, rm, cm = fields.shape
+    wide = jnp.concatenate(list(fields), axis=1)
+    hi = lax.reduce_precision(wide, exponent_bits=8, mantissa_bits=7)
+    rest = wide - hi
+    mid = lax.reduce_precision(rest, exponent_bits=8, mantissa_bits=7)
+    lo = rest - mid
+    parts = jnp.stack([hi, mid, lo]).astype(jnp.bfloat16)
+    rc = jnp.stack([cells // cm, cells % cm], axis=1).astype(jnp.int32)
+    block = 256 if count % 256 == 0 else count
+    picked = pl.pallas_call(
+        pick_kernel,
+        grid=(count // block,),
+        in_specs=[
+            pl.BlockSpec((block, 2), lambda i: (i, 0)),
+            pl.BlockSpec((3, rm, nf * cm), lambda i: (0, 0, 0)),
+        ],
+        out_specs=pl.BlockSpec((block, nf), lambda i: (i, 0)),
+        out_shape=jax.ShapeDtypeStruct((count, nf), jnp.float32),
+    )(rc, parts)
+    return picked.T
+
+
 def body(
     temp_start,
     heat_input,
@@ -187,8 +231,7 @@
             inside = ((gr >= 0) & (gr < n_gx * rm))[:, None] & ((gc >= 0) & (gc < n_gy * cm))[None, :]
             warp = jnp.where(inside, warp, 0.0)
 
-    fields = jnp.stack([(warp - warp_prev).reshape(-1), top.reshape(-1)])
-    picked = fields[:, joint_cell]
+    picked = pick_cells(jnp.stack([warp - warp_prev, top]), joint_cell)
     values = jnp.concatenate([picked, jnp.ones_like(picked[:1])], axis=0)
     outgoing = jnp.zeros((3, devices * capacity), jnp.float32).at[:, slots].set(values)
     incoming = lax.all_to_all(outgoing, FLAT, split_axis=1, concat_axis=1, tiled=True)

time: 137 us -> 113 us (0.82)
  local copies, waits for them, and re-layouts: 51 us -> 18 us
  Pallas kernels: 0 us -> 8.21 us
  waiting for transfers between devices: 20.8 us -> 18.7 us
    gather x1 -> x0, local copies, waits for them, and re-layouts: 18.2 us -> none  [body(): picked = fields[:, joint_cell]]
    another operation x1, local copies, waits for them, and re-layouts: 15.6 us -> 1.37 us  [pick_cells(): rc = jnp.stack([cells // cm, cells % cm], axis=1).astype(jnp.int32)]
    pallas_call x0 -> x1, Pallas kernels: none -> 8.21 us  [pick_cells(): pl.pallas_call(pick_kernel, grid=(count // block,), in_specs=[pl.BlockSpe...]
    ppermute x8, waiting for transfers between devices: 16.5 us -> 14.3 us  [exchange(): return (lax.ppermute(last, axis, up), lax.ppermute(leading, axis, down))]
    unnamed x2 -> x0, other arithmetic: 1.44 us -> none
    concatenate x0 -> x2, other arithmetic: none -> 1.44 us  [pick_cells(): wide = jnp.concatenate(list(fields), axis=1)]
  transfers between devices with their start and end apart: 9 -> 9, of which waited for: 4 -> 4; matrix products, arithmetic and copies ran while one was open for 14% -> 19% of each run, Pallas kernels for 0% -> 0%
where the time goes in v2:
time: 113 us; the launch traced here: 112 us
  starting transfers between devices  27.2 us (24%)
  other arithmetic  22 us (19%)
  waiting for transfers between devices  18.7 us (17%)
  local copies, waits for them, and re-layouts  18 us (16%)
  blocking collectives  15.7 us (14%)
  Pallas kernels  8.21 us (7%)
  between operations  1.22 us (1%)
    ppermute x8, starting transfers between devices, exchange(): return (lax.ppermute(last, axis, up), lax.ppermute(leading, axis, down))  21.4 us
    all_to_all x1, blocking collectives, body(): lax.all_to_all(outgoing, FLAT, split_axis=1, concat_axis=1, tiled=True)  15.7 us
    ppermute x8, waiting for transfers between devices, exchange(): return (lax.ppermute(last, axis, up), lax.ppermute(leading, axis, down))  14.3 us
    pallas_call x1, Pallas kernels, pick_cells(): pl.pallas_call(pick_kernel, grid=(count // block,), in_specs=[pl.BlockSpe...  8.21 us
    scatter x1, local copies, waits for them, and re-layouts, body(): jnp.zeros((3, devices * capacity), jnp.float32).at[:, slots].set(values)  6.81 us
    all_to_all x1, starting transfers between devices, relay(): recv = lax.all_to_all(send, 'gy', split_axis=0, concat_axis=0, tiled=True)  5.83 us
    add x1, other arithmetic, moment_of(): total = total + weighting[layer] * field[layer]  5.25 us
    all_to_all x1, waiting for transfers between devices, relay(): recv = lax.all_to_all(send, 'gy', split_axis=0, concat_axis=0, tiled=True)  4.42 us
  transfers between devices with their start and end apart: 9, of which 4 were waited for; matrix products, arithmetic and copies ran while one was open for 19% of the time, Pallas kernels for 0%

profile of v2, /device:TPU:0, one launch (start us, length us, event | category | flops | bytes accessed | tf_op | source)
XLA Modules:
  0.0 112.0 jit_solution(14945765473336084310)
XLA Ops:
  0.7 1.4 %fusion.90 = (f32[8,2,2048]{2,1,0:T(2,128)S(1)}, f32[8,2,2048]{2,1,0:T(2,128)S(1)}) fusion(f32[8,32,2048]{2,1,0:T(8,128)} %param.11), kind=kLoop, calls=%fused_computation.203 | loop fusion | bytes 524288 | tf_op jit(solution)/shard_map/slice | solution.py:93
  2.1 1.3 %fusion.91 = (f32[8,1,2048]{2,1,0:T(1,128)S(1)}, f32[8,1,2048]{2,1,0:T(1,128)S(1)}) fusion(f32[8,32,2048]{2,1,0:T(8,128)} %param.12), kind=kLoop, calls=%fused_computation.204 | loop fusion | bytes 262144 | tf_op jit(solution)/shard_map/slice | solution.py:93
  3.5 5.0 %collective-permute-start = (f32[8,3,2048]{2,1,0:T(4,128)S(1)}, f32[8,3,2048]{2,1,0:T(4,128)S(1)}, u32[]{:S(2)}, u32[]{:S(2)}) collective-permute-start(f32[8,3,2048]{2,1,0:T(4,128)S(1)} %pad_maximum_fusion.6), channel_id=1, source_target_pairs={{0,1},{1,2},{2,3},{3,4},{4,5},{5,6},{6,7},{7,8},{8,9},{9,10},{10,1... | collective-permute-start | bytes 589832 | tf_op jit(solution)/shard_map/ppermute | solution.py:25
  8.6 1.3 %collective-permute-start.1 = (f32[8,3,2048]{2,1,0:T(4,128)S(1)}, f32[8,3,2048]{2,1,0:T(4,128)S(1)}, u32[]{:S(2)}, u32[]{:S(2)}) collective-permute-start(f32[8,3,2048]{2,1,0:T(4,128)S(1)} %pad_maximum_fusion.7), channel_id=1, source_target_pairs={{1,0},{2,1},{3,2},{4,3},{5,4},{6,5},{7,6},{8,7},{9,8},{10,9},{11,1... | collective-permute-start | bytes 589832 | tf_op jit(solution)/shard_map/ppermute | solution.py:25
  10.7 4.7 %collective-permute-start.4 = (f32[2,3,512]{2,1,0:T(4,128)S(1)}, f32[2,3,512]{2,1,0:T(4,128)S(1)}, u32[]{:S(2)}, u32[]{:S(2)}) collective-permute-start(f32[2,3,512]{2,1,0:T(4,128)S(1)} %get-tuple-element.34), channel_id=1, source_target_pairs={{0,4},{4,8},{8,12},{12,16},{16,20},{20,24},{24,28},{1,5},{5,9},{9,... | collective-permute-start | bytes 36872 | tf_op jit(solution)/shard_map/ppermute | solution.py:25
  15.4 1.3 %collective-permute-start.5 = (f32[2,3,512]{2,1,0:T(4,128)S(1)}, f32[2,3,512]{2,1,0:T(4,128)S(1)}, u32[]{:S(2)}, u32[]{:S(2)}) collective-permute-start(f32[2,3,512]{2,1,0:T(4,128)S(1)} %get-tuple-element.35), channel_id=1, source_target_pairs={{4,0},{8,4},{12,8},{16,12},{20,16},{24,20},{28,24},{5,1},{9,5},{13... | collective-permute-start | bytes 36872 | tf_op jit(solution)/shard_map/ppermute | solution.py:25
  16.7 1.6 %fusion.96 = (f32[1]{0:T(128)}, f32[1]{0:T(128)}, f32[1]{0:T(128)}, f32[1]{0:T(128)}, f32[1]{0:T(128)}, /*index=5*/f32[1]{0:T(128)}, f32[1]{0:T(128)}, f32[1]{0:T(128)}) fusion(f32[8]{0:T(128)} %param.15), kind=kLoop, calls=%fused_computation.209 | loop fusion | bytes 64 | tf_op jit(solution)/shard_map/slice | solution.py:48
  20.6 2.7 %collective-permute-done.1 = f32[8,3,2048]{2,1,0:T(4,128)S(1)} collective-permute-done((f32[8,3,2048]{2,1,0:T(4,128)S(1)}, f32[8,3,2048]{2,1,0:T(4,128)S(1)}, u32[]{:S(2)}, u32[]{:S(2)}) %collective-permute-start.1) | collective-permute-done | bytes 196640 | tf_op jit(solution)/shard_map/ppermute | solution.py:25
  25.3 3.0 %fusion.7 = f32[8,34,2048]{2,1,0:T(8,128)S(1)} fusion(f32[8,36,2048]{2,1,0:T(8,128)S(1)} %pad_maximum_fusion, f32[8,2,2048]{2,1,0:T(2,128)S(1)} %slice.401, f32[8,32,2048]{2,1,0:T(8,128)S(1)} %copy-done, f32[8,2,2048]{2,1,0:T(2,128)S(1)} %slice.400, f32[8,1,2048]{2,1,0:T(1,128)S(1)} %slice.406, f32[8,32,2048]{2,1,0:T(8,128)S(1)} %copy-done.1, ...), kind=kLoop, calls=%fused_computation.12 | loop fusion | flops 8355840 | bytes 14353408 | tf_op jit(solution)/shard_map/jit(_where)/select_n | solution.py:105
  28.8 1.9 %fusion.15 = f32[8,32,2048]{2,1,0:T(8,128)S(1)} fusion(f32[8,32,2048]{2,1,0:T(8,128)S(1)} %copy-done.1, f32[8,34,2048]{2,1,0:T(8,128)S(1)} %fusion.7, f32[7,32,2048]{2,1,0:T(8,128)S(1)} %fusion.16, f32[8]{0:T(128)S(1)} %copy-done.8), kind=kLoop, calls=%fused_computation.23 | loop fusion | flops 5242880 | bytes 14942720 | tf_op jit(solution)/shard_map/add | solution.py:44
  30.7 5.3 %fusion.55 = f32[32,2048]{1,0:T(8,128)S(1)} fusion(f32[8,32,2048]{2,1,0:T(8,128)S(1)} %fusion.15, f32[]{:T(128)} %bitcast.8, f32[]{:T(128)} %bitcast.6, f32[]{:T(128)} %bitcast.5, f32[]{:T(128)} %bitcast.4, f32[]{:T(128)} %bitcast.3, f32[]{:T(128)} %bitcast.2, f32[]{:T(128)} %bitcast.1, f32[]{:T(128)} %bitcast), kind=kLoop, calls=%fused_computation.114 | loop fusion | flops 983040 | bytes 2359328 | tf_op jit(solution)/shard_map/add | solution.py:50
  36.0 2.5 %collective-permute-start.2 = (f32[2,2048]{1,0:T(2,128)S(1)}, f32[2,2048]{1,0:T(2,128)S(1)}, u32[]{:S(2)}, u32[]{:S(2)}) collective-permute-start(f32[2,2048]{1,0:T(2,128)S(1)} %get-tuple-element.36), channel_id=1, source_target_pairs={{0,1},{1,2},{2,3},{3,4},{4,5},{5,6},{6,7},{7,8},{8,9},{9,10},{10,1... | collective-permute-start | bytes 49160 | tf_op jit(solution)/shard_map/ppermute | solution.py:25
  40.2 3.9 %collective-permute-done.3 = f32[2,2048]{1,0:T(2,128)S(1)} collective-permute-done((f32[2,2048]{1,0:T(2,128)S(1)}, f32[2,2048]{1,0:T(2,128)S(1)}, u32[]{:S(2)}, u32[]{:S(2)}) %collective-permute-start.3) | collective-permute-done | bytes 16416 | tf_op jit(solution)/shard_map/ppermute | solution.py:25
  46.5 5.8 %all-to-all-start = ((f32[4,2,36,516]{3,1,2,0:T(2,128)}), f32[4,2,36,516]{3,1,2,0:T(2,128)S(1)}, u32[]{:S(2)}, u32[]{:S(2)}) async-start(f32[4,2,36,516]{3,1,2,0:T(2,128)} %pad_maximum_fusion.2), calls=%async_computation | async-start | bytes 1474560 | tf_op jit(solution)/shard_map/all_to_all | solution.py:119
  52.6 3.9 %collective-permute-start.6 = (f32[2,134,3]{2,1,0:T(8,128)S(1)}, f32[2,134,3]{2,1,0:T(8,128)S(1)}, u32[]{:S(2)}, u32[]{:S(2)}) collective-permute-start(f32[2,134,3]{2,1,0:T(8,128)S(1)} %get-tuple-element.29), channel_id=1, source_target_pairs={{0,1},{1,2},{2,3},{4,5},{5,6},{6,7},{8,9},{9,10},{10,11},{12,13},{... | collective-permute-start | bytes 9656 | tf_op jit(solution)/shard_map/ppermute | solution.py:25
  56.5 1.5 %collective-permute-start.7 = (f32[2,134,3]{2,1,0:T(8,128)S(1)}, f32[2,134,3]{2,1,0:T(8,128)S(1)}, u32[]{:S(2)}, u32[]{:S(2)}) collective-permute-start(f32[2,134,3]{2,1,0:T(8,128)S(1)} %get-tuple-element.30), channel_id=1, source_target_pairs={{1,0},{2,1},{3,2},{5,4},{6,5},{7,6},{9,8},{10,9},{11,10},{13,12},{... | collective-permute-start | bytes 9656 | tf_op jit(solution)/shard_map/ppermute | solution.py:25
  58.0 1.4 %copy.26.rc_ref = s32[2048,2]{1,0:T(8,128)} copy(s32[2048,2]{0,1:T(2,128)S(1)} %pad_add_fusion) | data formatting | bytes 32768 | tf_op jit(solution)/shard_map/stack | solution.py:177
  59.4 7.7 %collective-permute-done.6 = f32[2,134,3]{2,1,0:T(8,128)S(1)} collective-permute-done((f32[2,134,3]{2,1,0:T(8,128)S(1)}, f32[2,134,3]{2,1,0:T(8,128)S(1)}, u32[]{:S(2)}, u32[]{:S(2)}) %collective-permute-start.6) | collective-permute-done | bytes 3248 | tf_op jit(solution)/shard_map/ppermute | solution.py:25
  67.4 4.4 %all-to-all-done = f32[4,2,36,516]{3,1,2,0:T(2,128)S(1)} async-done(((f32[4,2,36,516]{3,1,2,0:T(2,128)}), f32[4,2,36,516]{3,1,2,0:T(2,128)S(1)}, u32[]{:S(2)}, u32[]{:S(2)}) %all-to-all-start) | async-done | bytes 594464 | tf_op jit(solution)/shard_map/all_to_all | solution.py:119
  73.8 1.4 %subtract_bitcast_fusion = (f32[1,128,512]{2,1,0:T(8,128)S(1)}, f32[128,512]{1,0:T(8,128)}) fusion(f32[128,512]{1,0:T(8,128)S(1)} %copy-done.2, f32[130,514]{1,0:T(8,128)S(1)} %fusion.24, f32[134,518]{1,0:T(8,128)S(1)} %get-tuple-element.23, f32[132,516]{1,0:T(8,128)S(1)} %get-tuple-element.10), kind=kLoop, calls=%fused_computation.129 | loop fusion | flops 1441792 | bytes 3407872 | tf_op jit(solution)/shard_map/concatenate | solution.py:171
  77.2 8.2 %shard_map.130 = f32[2048,2]{1,0:T(8,128)} custom-call(s32[2048,2]{1,0:T(8,128)} %copy.26.rc_ref, bf16[3,128,1024]{2,1,0:T(8,128)(2,1)} %pad_maximum_fusion.1.parts_ref), custom_call_target="tpu_custom_call" | custom-call | tf_op jit(solution)/shard_map/pallas_call | solution.py:179
  85.4 6.8 %scatter_custom_fusion = f32[3,6144]{0,1:T(8,128)S(1)} fusion(s32[2048]{0:T(1024)S(1)} %bitcast.100, f32[]{:T(128)} %constant.36.clone.1, f32[2,2048]{0,1:T(8,128)} %bitcast.88, f32[]{:T(128)} %constant.23.clone.1), kind=kCustom, calls=%fused_computation.27 | custom fusion | bytes 90120 | tf_op jit(solution)/shard_map/scatter | solution.py:236
  92.2 1.5 %copy.27 = f32[3,32,192]{2,0,1:T(4,128)S(1)} copy(f32[3,32,192]{0,2,1:T(8,128)S(1)} %bitcast.87) | data formatting | bytes 147456 | tf_op jit(solution)/shard_map/all_to_all | solution.py:237
  93.7 15.7 %all_to_all.14 = f32[3,32,192]{2,0,1:T(4,128)S(1)} all-to-all(f32[3,32,192]{2,0,1:T(4,128)S(1)} %copy.27), channel_id=1, replica_groups=mesh['gx'=8,'gy'=4] {'gx','gy'}, dimensions={1} | all-to-all | bytes 147456 | tf_op jit(solution)/shard_map/all_to_all | solution.py:237
  (81 shorter events, 16.8 us)
Async XLA Ops:
  0.6 22.7 %copy-start = (f32[8,32,2048]{2,1,0:T(8,128)S(1)}, f32[8,32,2048]{2,1,0:T(8,128)}, u32[]{:S(2)}) copy-start(f32[8,32,2048]{2,1,0:T(8,128)} %param.11) | copy-start | bytes 6291460
  0.6 19.7 %copy-start.5 = (s32[2048,1]{0,1:T(1,128)S(1)}, s32[2048,1]{0,1:T(1,128)}, u32[]{:S(2)}) copy-start(s32[2048,1]{0,1:T(1,128)} %param.19) | copy-start | bytes 24580
  3.5 17.0 %collective-permute-start = (f32[8,3,2048]{2,1,0:T(4,128)S(1)}, f32[8,3,2048]{2,1,0:T(4,128)S(1)}, u32[]{:S(2)}, u32[]{:S(2)}) collective-permute-start(f32[8,3,2048]{2,1,0:T(4,128)S(1)} %pad_maximum_fusion.6), channel_id=1, source_target_pairs={{0,1},{1,2},{2,3},{3,4},{4,5},{5,6},{6,7},{7,8},{8,9},{9,10},{10,1... | collective-permute-start | bytes 589832 | tf_op jit(solution)/shard_map/ppermute | solution.py:25
  8.6 14.6 %collective-permute-start.1 = (f32[8,3,2048]{2,1,0:T(4,128)S(1)}, f32[8,3,2048]{2,1,0:T(4,128)S(1)}, u32[]{:S(2)}, u32[]{:S(2)}) collective-permute-start(f32[8,3,2048]{2,1,0:T(4,128)S(1)} %pad_maximum_fusion.7), channel_id=1, source_target_pairs={{1,0},{2,1},{3,2},{4,3},{5,4},{6,5},{7,6},{8,7},{9,8},{10,9},{11,1... | collective-permute-start | bytes 589832 | tf_op jit(solution)/shard_map/ppermute | solution.py:25
  10.7 41.7 %collective-permute-start.4 = (f32[2,3,512]{2,1,0:T(4,128)S(1)}, f32[2,3,512]{2,1,0:T(4,128)S(1)}, u32[]{:S(2)}, u32[]{:S(2)}) collective-permute-start(f32[2,3,512]{2,1,0:T(4,128)S(1)} %get-tuple-element.34), channel_id=1, source_target_pairs={{0,4},{4,8},{8,12},{12,16},{16,20},{20,24},{24,28},{1,5},{5,9},{9,... | collective-permute-start | bytes 36872 | tf_op jit(solution)/shard_map/ppermute | solution.py:25
  15.4 37.0 %collective-permute-start.5 = (f32[2,3,512]{2,1,0:T(4,128)S(1)}, f32[2,3,512]{2,1,0:T(4,128)S(1)}, u32[]{:S(2)}, u32[]{:S(2)}) collective-permute-start(f32[2,3,512]{2,1,0:T(4,128)S(1)} %get-tuple-element.35), channel_id=1, source_target_pairs={{4,0},{8,4},{12,8},{16,12},{20,16},{24,20},{28,24},{5,1},{9,5},{13... | collective-permute-start | bytes 36872 | tf_op jit(solution)/shard_map/ppermute | solution.py:25
  20.6 3.1 %copy-start.7 = (f32[7]{0:T(128)S(1)}, f32[7]{0:T(128)}, u32[]{:S(2)}) copy-start(f32[7]{0:T(128)} %param.14) | copy-start | bytes 88
  23.7 1.6 %copy-start.1 = (f32[8,32,2048]{2,1,0:T(8,128)S(1)}, f32[8,32,2048]{2,1,0:T(8,128)}, u32[]{:S(2)}) copy-start(f32[8,32,2048]{2,1,0:T(8,128)} %param.12) | copy-start | bytes 6291460
  23.8 1.6 %copy-start.8 = (f32[8]{0:T(128)S(1)}, f32[8]{0:T(128)}, u32[]{:S(2)}) copy-start(f32[8]{0:T(128)} %param.13) | copy-start | bytes 100
  36.0 4.2 %collective-permute-start.2 = (f32[2,2048]{1,0:T(2,128)S(1)}, f32[2,2048]{1,0:T(2,128)S(1)}, u32[]{:S(2)}, u32[]{:S(2)}) collective-permute-start(f32[2,2048]{1,0:T(2,128)S(1)} %get-tuple-element.36), channel_id=1, source_target_pairs={{0,1},{1,2},{2,3},{3,4},{4,5},{5,6},{6,7},{7,8},{8,9},{9,10},{10,1... | collective-permute-start | bytes 49160 | tf_op jit(solution)/shard_map/ppermute | solution.py:25
  38.4 5.6 %collective-permute-start.3 = (f32[2,2048]{1,0:T(2,128)S(1)}, f32[2,2048]{1,0:T(2,128)S(1)}, u32[]{:S(2)}, u32[]{:S(2)}) collective-permute-start(f32[2,2048]{1,0:T(2,128)S(1)} %get-tuple-element.37), channel_id=1, source_target_pairs={{1,0},{2,1},{3,2},{4,3},{5,4},{6,5},{7,6},{8,7},{9,8},{10,9},{11,1... | collective-permute-start | bytes 49160 | tf_op jit(solution)/shard_map/ppermute | solution.py:25
  44.3 8.2 %copy-start.2 = (f32[128,512]{1,0:T(8,128)S(1)}, f32[128,512]{1,0:T(8,128)}, u32[]{:S(2)}) copy-start(f32[128,512]{1,0:T(8,128)} %param.17) | copy-start | bytes 786436
  44.3 8.2 %copy-start.3 = (f32[128,512]{1,0:T(8,128)S(1)}, f32[128,512]{1,0:T(8,128)}, u32[]{:S(2)}) copy-start(f32[128,512]{1,0:T(8,128)} %param.16) | copy-start | bytes 786436
  46.5 25.3 %all-to-all-start = ((f32[4,2,36,516]{3,1,2,0:T(2,128)}), f32[4,2,36,516]{3,1,2,0:T(2,128)S(1)}, u32[]{:S(2)}, u32[]{:S(2)}) async-start(f32[4,2,36,516]{3,1,2,0:T(2,128)} %pad_maximum_fusion.2), calls=%async_computation | async-start | bytes 1474560 | tf_op jit(solution)/shard_map/all_to_all | solution.py:119
  52.6 14.5 %collective-permute-start.6 = (f32[2,134,3]{2,1,0:T(8,128)S(1)}, f32[2,134,3]{2,1,0:T(8,128)S(1)}, u32[]{:S(2)}, u32[]{:S(2)}) collective-permute-start(f32[2,134,3]{2,1,0:T(8,128)S(1)} %get-tuple-element.29), channel_id=1, source_target_pairs={{0,1},{1,2},{2,3},{4,5},{5,6},{6,7},{8,9},{9,10},{10,11},{12,13},{... | collective-permute-start | bytes 9656 | tf_op jit(solution)/shard_map/ppermute | solution.py:25
  56.5 10.5 %collective-permute-start.7 = (f32[2,134,3]{2,1,0:T(8,128)S(1)}, f32[2,134,3]{2,1,0:T(8,128)S(1)}, u32[]{:S(2)}, u32[]{:S(2)}) collective-permute-start(f32[2,134,3]{2,1,0:T(8,128)S(1)} %get-tuple-element.30), channel_id=1, source_target_pairs={{1,0},{2,1},{3,2},{5,4},{6,5},{7,6},{9,8},{10,9},{11,10},{13,12},{... | collective-permute-start | bytes 9656 | tf_op jit(solution)/shard_map/ppermute | solution.py:25
  92.2 17.9 %copy-start.4 = (f32[2,1,6144]{2,1,0:T(1,128)S(1)}, f32[2,1,6144]{2,1,0:T(1,128)}, u32[]{:S(2)}) copy-start(f32[2,1,6144]{2,1,0:T(1,128)} %param.20) | copy-start | bytes 147460
  92.2 17.9 %copy-start.6 = (f32[1,6144]{1,0:T(1,128)S(1)}, f32[1,6144]{1,0:T(1,128)}, u32[]{:S(2)}) copy-start(f32[1,6144]{1,0:T(1,128)} %param.21) | copy-start | bytes 73732

commit v3 on v2

--- a/solution.py
+++ b/solution.py
@@ -85,34 +85,58 @@
     return (strain_out, jnp.where(keep, resist_new, resist))
 
 
-def thermal(temp, heat, lateral, vertical):
+def thermal(temp, heat, lateral, vertical, extra):
     devices = lax.axis_size(FLAT)
     t = lax.axis_index(FLAT)
     rows = temp.shape[1]
-    h = STEPS
-    last = jnp.concatenate([temp[:, rows - h:], heat[:, rows - (h - 1):]], axis=1)
-    leading = jnp.concatenate([temp[:, :h], heat[:, : h - 1]], axis=1)
+    h = STEPS + extra
+    hh = h - 1
+    last = jnp.concatenate([temp[:, rows - h:], heat[:, rows - hh:]], axis=1)
+    leading = jnp.concatenate([temp[:, :h], heat[:, :hh]], axis=1)
     before, after = exchange(last, leading, FLAT)
     ext = jnp.concatenate([before[:, :h], temp, after[:, :h]], axis=1)
     heat_ext = jnp.concatenate([before[:, h:], heat, after[:, h:]], axis=1)
     for step in range(1, STEPS + 1):
-        r = STEPS - step
-        heat_rows = heat_ext[:, h - 1 - r: h - 1 - r + rows + 2 * r]
+        r = STEPS - step + extra
+        heat_rows = heat_ext[:, hh - r: hh - r + rows + 2 * r]
         ext = thermal_step(ext, heat_rows, lateral, vertical)
-        if r > 0:
+        if step < STEPS:
             g = t * rows + jnp.arange(-r, rows + r)
             inside = (g >= 0) & (g < devices * rows)
             ext = jnp.where(inside[None, :, None], ext, 0.0)
     return ext
 
 
+def halo_2d(array, width):
+    n_gx, n_gy = lax.axis_size("gx"), lax.axis_size("gy")
+    rm, cm = array.shape[-2:]
+    w = width
+    pieces = {}
+    for di in (-1, 0, 1):
+        for dj in (-1, 0, 1):
+            if di == 0 and dj == 0:
+                continue
+            rs = slice(rm - w, rm) if di == 1 else (slice(0, w) if di == -1 else slice(0, rm))
+            cs = slice(cm - w, cm) if dj == 1 else (slice(0, w) if dj == -1 else slice(0, cm))
+            pairs = [
+                (i * n_gy + j, (i + di) * n_gy + (j + dj))
+                for i in range(n_gx)
+                for j in range(n_gy)
+                if 0 <= i + di < n_gx and 0 <= j + dj < n_gy
+            ]
+            pieces[(di, dj)] = lax.ppermute(array[..., rs, cs], FLAT, pairs)
+    top = jnp.concatenate([pieces[(1, 1)], pieces[(1, 0)], pieces[(1, -1)]], axis=-1)
+    mid = jnp.concatenate([pieces[(0, 1)], array, pieces[(0, -1)]], axis=-1)
+    bottom = jnp.concatenate([pieces[(-1, 1)], pieces[(-1, 0)], pieces[(-1, -1)]], axis=-1)
+    return jnp.concatenate([top, mid, bottom], axis=-2)
+
+
 def relay(load, top, width):
     n_gy = lax.axis_size("gy")
     rows, cols = load.shape
     cm = cols // n_gy
-    before, after = exchange(load[rows - width:], load[:width], FLAT)
-    load_ext = jnp.concatenate([before, load, after], axis=0)
-    lp = jnp.pad(load_ext, ((0, 0), (width, width)))
+    rows = rows - 2 * width
+    lp = jnp.pad(load, ((0, 0), (width, width)))
     tp = jnp.pad(top, ((width, width), (width, width)))
     both = jnp.stack([lp, tp])
     send = jnp.stack([both[:, :, k * cm: k * cm + cm + 2 * width] for k in range(n_gy)])
@@ -207,14 +231,15 @@
     gi, gj = lax.axis_index("gx"), lax.axis_index("gy")
     rm, cm = warp_prev.shape
 
-    wm = with_halo(jnp.stack([warp_prev, modulus]), (("gx", 1), ("gy", 2)), SWEEPS)
+    wm = halo_2d(jnp.stack([warp_prev, modulus]), SWEEPS)
     owners = joint_owner[:, 0]
     capacity = joint_resist.shape[1] // devices
     slots = owners * capacity + joint_ranks(owners, devices)
 
-    temp = thermal(temp_start, heat_input, lateral, vertical)
+    extra = SWEEPS - 1
+    temp = thermal(temp_start, heat_input, lateral, vertical, extra)
     load_t = moment_of(temp, weighting)
-    load, top = relay(load_t, temp[-1], SWEEPS - 1)
+    load, top = relay(load_t, temp[-1, extra: temp.shape[1] - extra], extra)
 
     warp = wm[0]
     mod_ext = wm[1]

time: 113 us -> 115 us (1.018)
  other arithmetic: 22 us -> 26.9 us
  blocking collectives: 15.7 us -> 11.7 us
  starting transfers between devices: 27.2 us -> 29.3 us
    ppermute x0 -> x8, starting transfers between devices: none -> 19 us  [halo_2d(): pieces[di, dj] = lax.ppermute(array[..., rs, cs], FLAT, pairs)]
    ppermute x8 -> x2, starting transfers between devices: 21.4 us -> 6.39 us  [exchange(): return (lax.ppermute(last, axis, up), lax.ppermute(leading, axis, down))]
    ppermute x8 -> x2, waiting for transfers between devices: 14.3 us -> 5.35 us  [exchange(): return (lax.ppermute(last, axis, up), lax.ppermute(leading, axis, down))]
    ppermute x0 -> x8, waiting for transfers between devices: none -> 7.61 us  [halo_2d(): pieces[di, dj] = lax.ppermute(array[..., rs, cs], FLAT, pairs)]
    concatenate x3 -> x4, other arithmetic: 0.56 us -> 5.7 us  [the longest x1 2.86 us: thermal(): heat_ext = jnp.concatenate([before[:, h:], heat, after[:, h:]], axis=1)]
    all_to_all x1, blocking collectives: 15.7 us -> 11.7 us  [body(): lax.all_to_all(outgoing, FLAT, split_axis=1, concat_axis=1, tiled=True)]
    select_n x1 -> x0, other arithmetic: 3.03 us -> none  [thermal(): ext = jnp.where(inside[None, :, None], ext, 0.0)]
    all_to_all x1, starting transfers between devices: 5.83 us -> 3.91 us  [relay(): recv = lax.all_to_all(send, 'gy', split_axis=0, concat_axis=0, tiled=True)]
  transfers between devices with their start and end apart: 9 -> 11, of which waited for: 4 -> 3; matrix products, arithmetic and copies ran while one was open for 19% -> 23% of each run, Pallas kernels for 0% -> 0%
where the time goes in v3:
time: 115 us; the launch traced here: 114 us
  starting transfers between devices  29.3 us (25%)
  other arithmetic  26.9 us (23%)
  local copies, waits for them, and re-layouts  18.5 us (16%)
  waiting for transfers between devices  17.6 us (15%)
  blocking collectives  11.7 us (10%)
  Pallas kernels  8.22 us (7%)
  between operations  1.25 us (1%)
    ppermute x8, starting transfers between devices, halo_2d(): pieces[di, dj] = lax.ppermute(array[..., rs, cs], FLAT, pairs)  19 us
    all_to_all x1, blocking collectives, body(): lax.all_to_all(outgoing, FLAT, split_axis=1, concat_axis=1, tiled=True)  11.7 us
    pallas_call x1, Pallas kernels, pick_cells(): pl.pallas_call(pick_kernel, grid=(count // block,), in_specs=[pl.BlockSpe...  8.22 us
    ppermute x8, waiting for transfers between devices, halo_2d(): pieces[di, dj] = lax.ppermute(array[..., rs, cs], FLAT, pairs)  7.61 us
    scatter x1, local copies, waits for them, and re-layouts, body(): jnp.zeros((3, devices * capacity), jnp.float32).at[:, slots].set(values)  6.8 us
    ppermute x2, starting transfers between devices, exchange(): return (lax.ppermute(last, axis, up), lax.ppermute(leading, axis, down))  6.39 us
    ppermute x2, waiting for transfers between devices, exchange(): return (lax.ppermute(last, axis, up), lax.ppermute(leading, axis, down))  5.35 us
    add x1, other arithmetic, moment_of(): total = total + weighting[layer] * field[layer]  5.14 us
  transfers between devices with their start and end apart: 11, of which 3 were waited for; matrix products, arithmetic and copies ran while one was open for 23% of the time, Pallas kernels for 0%

profile of v3, /device:TPU:0, one launch (start us, length us, event | category | flops | bytes accessed | tf_op | source)
XLA Modules:
  0.0 113.7 jit_solution(16327055577953614993)
XLA Ops:
  0.7 1.4 %fusion.92 = (f32[8,4,2048]{2,1,0:T(4,128)S(1)}, f32[8,4,2048]{2,1,0:T(4,128)S(1)}) fusion(f32[8,32,2048]{2,1,0:T(8,128)} %param.11), kind=kLoop, calls=%fused_computation.210 | loop fusion | bytes 1048576 | tf_op jit(solution)/shard_map/slice | solution.py:94
  2.0 1.3 %fusion.93 = (f32[8,3,2048]{2,1,0:T(4,128)S(1)}, f32[8,3,2048]{2,1,0:T(4,128)S(1)}) fusion(f32[8,32,2048]{2,1,0:T(8,128)} %param.12), kind=kLoop, calls=%fused_computation.211 | loop fusion | bytes 786432 | tf_op jit(solution)/shard_map/slice | solution.py:94
  4.3 5.1 %collective-permute-start = (f32[8,7,2048]{2,1,0:T(8,128)}, f32[8,7,2048]{2,1,0:T(8,128)S(1)}, u32[]{:S(2)}, u32[]{:S(2)}) collective-permute-start(f32[8,7,2048]{2,1,0:T(8,128)} %pad_maximum_fusion.4), channel_id=1, source_target_pairs={{0,1},{1,2},{2,3},{3,4},{4,5},{5,6},{6,7},{7,8},{8,9},{9,10},{10,1... | collective-permute-start | bytes 1376264 | tf_op jit(solution)/shard_map/ppermute | solution.py:25
  10.3 1.3 %collective-permute-start.1 = (f32[8,7,2048]{2,1,0:T(8,128)}, f32[8,7,2048]{2,1,0:T(8,128)}, u32[]{:S(2)}, u32[]{:S(2)}) collective-permute-start(f32[8,7,2048]{2,1,0:T(8,128)} %pad_maximum_fusion.5), channel_id=1, source_target_pairs={{1,0},{2,1},{3,2},{4,3},{5,4},{6,5},{7,6},{8,7},{9,8},{10,9},{11,1... | collective-permute-start | bytes 1376264 | tf_op jit(solution)/shard_map/ppermute | solution.py:25
  12.3 4.0 %collective-permute-start.2 = (f32[2,3,3]{2,1,0:T(4,128)}, f32[2,3,3]{2,1,0:T(4,128)}, u32[]{:S(2)}, u32[]{:S(2)}) collective-permute-start(f32[2,3,3]{2,1,0:T(4,128)} %get-tuple-element.34), channel_id=1, source_target_pairs={{0,5},{1,6},{2,7},{4,9},{5,10},{6,11},{8,13},{9,14},{10,15},{12,17... | collective-permute-start | bytes 224 | tf_op jit(solution)/shard_map/ppermute | solution.py:127
  16.3 1.2 %collective-permute-start.4 = (f32[2,3,3]{2,1,0:T(4,128)}, f32[2,3,3]{2,1,0:T(4,128)}, u32[]{:S(2)}, u32[]{:S(2)}) collective-permute-start(f32[2,3,3]{2,1,0:T(4,128)} %get-tuple-element.37), channel_id=1, source_target_pairs={{1,4},{2,5},{3,6},{5,8},{6,9},{7,10},{9,12},{10,13},{11,14},{13,16... | collective-permute-start | bytes 224 | tf_op jit(solution)/shard_map/ppermute | solution.py:127
  23.3 7.0 %collective-permute-start.5 = (f32[2,128,3]{2,1,0:T(8,128)}, f32[2,128,3]{2,1,0:T(8,128)S(1)}, u32[]{:S(2)}, u32[]{:S(2)}) collective-permute-start(f32[2,128,3]{2,1,0:T(8,128)} %get-tuple-element.40), channel_id=1, source_target_pairs={{0,1},{1,2},{2,3},{4,5},{5,6},{6,7},{8,9},{9,10},{10,11},{12,13},{... | collective-permute-start | bytes 9224 | tf_op jit(solution)/shard_map/ppermute | solution.py:127
  30.4 5.3 %collective-permute-done.1 = f32[8,7,2048]{2,1,0:T(8,128)} collective-permute-done((f32[8,7,2048]{2,1,0:T(8,128)}, f32[8,7,2048]{2,1,0:T(8,128)}, u32[]{:S(2)}, u32[]{:S(2)}) %collective-permute-start.1) | collective-permute-done | bytes 458784 | tf_op jit(solution)/shard_map/ppermute | solution.py:25
  35.8 1.3 %collective-permute-start.6 = (f32[2,128,3]{2,1,0:T(8,128)S(1)}, f32[2,128,3]{2,1,0:T(8,128)S(1)}, u32[]{:S(2)}, u32[]{:S(2)}) collective-permute-start(f32[2,128,3]{2,1,0:T(8,128)S(1)} %get-tuple-element.41), channel_id=1, source_target_pairs={{1,0},{2,1},{3,2},{5,4},{6,5},{7,6},{9,8},{10,9},{11,10},{13,12},{... | collective-permute-start | bytes 9224 | tf_op jit(solution)/shard_map/ppermute | solution.py:127
  40.6 2.9 %pad_maximum_fusion.1 = (f32[8,38,2048]{2,1,0:T(8,128)S(1)}, f32[8,38,2048]{2,1,0:T(8,128)S(1)}) fusion(f32[8,3,2048]{2,1,0:T(4,128)S(1)} %slice.427, f32[8,32,2048]{2,1,0:T(8,128)S(1)} %copy-done.3, f32[8,3,2048]{2,1,0:T(4,128)S(1)} %slice.426, f32[7,38,2048]{2,1,0:T(8,128)S(1)} %fusion.16, f32[8,40,2048]{2,1,0:T(8,128)S(1)} %pad_maximum_fusion, ...), kind=kLoop, calls=%fused_computation.23 | loop fusion | flops 8093696 | bytes 20382720 | tf_op jit(solution)/shard_map/concatenate | solution.py:98
  44.0 2.6 %fusion.14 = f32[8,36,2048]{2,1,0:T(8,128)S(1)} fusion(f32[8,38,2048]{2,1,0:T(8,128)S(1)} %get-tuple-element.12, f32[8,38,2048]{2,1,0:T(8,128)S(1)} %get-tuple-element.11, f32[7,36,2048]{2,1,0:T(8,128)S(1)} %fusion.15, f32[8]{0:T(128)S(1)} %copy-done.13), kind=kLoop, calls=%fused_computation.19 | loop fusion | flops 5898240 | bytes 17760768 | tf_op jit(solution)/shard_map/add | solution.py:44
  46.6 5.1 %fusion.43 = f32[36,2048]{1,0:T(8,128)S(1)} fusion(f32[8,36,2048]{2,1,0:T(8,128)S(1)} %fusion.14, f32[]{:T(128)} %bitcast.7, f32[]{:T(128)} %bitcast.6, f32[]{:T(128)} %bitcast.5, f32[]{:T(128)} %bitcast.4, f32[]{:T(128)} %bitcast.3, f32[]{:T(128)} %bitcast.2, f32[]{:T(128)} %bitcast.1, f32[]{:T(128)} %bitcast), kind=kLoop, calls=%fused_computation.100 | loop fusion | flops 1105920 | bytes 2654240 | tf_op jit(solution)/shard_map/add | solution.py:50
  54.5 3.9 %all-to-all-start = ((f32[4,2,36,516]{3,1,2,0:T(2,128)}), f32[4,2,36,516]{3,1,2,0:T(2,128)S(1)}, u32[]{:S(2)}, u32[]{:S(2)}) async-start(f32[4,2,36,516]{3,1,2,0:T(2,128)} %pad_maximum_fusion.3), calls=%async_computation | async-start | bytes 1474560 | tf_op jit(solution)/shard_map/all_to_all | solution.py:143
  58.5 1.5 %collective-permute-start.3 = (f32[2,3,512]{2,1,0:T(4,128)S(1)}, f32[2,3,512]{2,1,0:T(4,128)S(1)}, u32[]{:S(2)}, u32[]{:S(2)}) collective-permute-start(f32[2,3,512]{2,1,0:T(4,128)S(1)} %copy-done.9), channel_id=1, source_target_pairs={{0,4},{1,5},{2,6},{3,7},{4,8},{5,9},{6,10},{7,11},{8,12},{9,13},{1... | collective-permute-start | bytes 36872 | tf_op jit(solution)/shard_map/ppermute | solution.py:127
  60.0 1.3 %collective-permute-start.8 = (f32[2,3,512]{2,1,0:T(4,128)S(1)}, f32[2,3,512]{2,1,0:T(4,128)S(1)}, u32[]{:S(2)}, u32[]{:S(2)}) collective-permute-start(f32[2,3,512]{2,1,0:T(4,128)S(1)} %copy-done.8), channel_id=1, source_target_pairs={{4,0},{5,1},{6,2},{7,3},{8,4},{9,5},{10,6},{11,7},{12,8},{13,9},{1... | collective-permute-start | bytes 36872 | tf_op jit(solution)/shard_map/ppermute | solution.py:127
  61.4 1.5 %collective-permute-start.9 = (f32[2,3,3]{2,1,0:T(4,128)S(1)}, f32[2,3,3]{2,1,0:T(4,128)S(1)}, u32[]{:S(2)}, u32[]{:S(2)}) collective-permute-start(f32[2,3,3]{2,1,0:T(4,128)S(1)} %copy-done.11), channel_id=1, source_target_pairs={{5,0},{6,1},{7,2},{9,4},{10,5},{11,6},{13,8},{14,9},{15,10},{17,12... | collective-permute-start | bytes 224 | tf_op jit(solution)/shard_map/ppermute | solution.py:127
  62.9 1.4 %copy.26.rc_ref = s32[2048,2]{1,0:T(8,128)} copy(s32[2048,2]{0,1:T(2,128)S(1)} %pad_add_fusion) | data formatting | bytes 32768 | tf_op jit(solution)/shard_map/stack | solution.py:201
  64.2 7.6 %collective-permute-done.9 = f32[2,3,3]{2,1,0:T(4,128)S(1)} collective-permute-done((f32[2,3,3]{2,1,0:T(4,128)S(1)}, f32[2,3,3]{2,1,0:T(4,128)S(1)}, u32[]{:S(2)}, u32[]{:S(2)}) %collective-permute-start.9) | collective-permute-done | bytes 104 | tf_op jit(solution)/shard_map/ppermute | solution.py:127
  72.9 4.6 %all-to-all-done = f32[4,2,36,516]{3,1,2,0:T(2,128)S(1)} async-done(((f32[4,2,36,516]{3,1,2,0:T(2,128)}), f32[4,2,36,516]{3,1,2,0:T(2,128)S(1)}, u32[]{:S(2)}, u32[]{:S(2)}) %all-to-all-start) | async-done | bytes 594464 | tf_op jit(solution)/shard_map/all_to_all | solution.py:143
  79.5 1.4 %subtract_bitcast_fusion = (f32[1,128,512]{2,1,0:T(8,128)S(1)}, f32[128,512]{1,0:T(8,128)}) fusion(f32[128,512]{1,0:T(8,128)S(1)} %copy-done, f32[130,514]{1,0:T(8,128)S(1)} %fusion.24, f32[134,518]{1,0:T(8,128)S(1)} %get-tuple-element.25, f32[132,516]{1,0:T(8,128)S(1)} %get-tuple-element.10), kind=kLoop, calls=%fused_computation.134 | loop fusion | flops 1441792 | bytes 3407872 | tf_op jit(solution)/shard_map/concatenate | solution.py:195
  82.9 8.2 %shard_map.130 = f32[2048,2]{1,0:T(8,128)} custom-call(s32[2048,2]{1,0:T(8,128)} %copy.26.rc_ref, bf16[3,128,1024]{2,1,0:T(8,128)(2,1)} %pad_maximum_fusion.2.parts_ref), custom_call_target="tpu_custom_call" | custom-call | tf_op jit(solution)/shard_map/pallas_call | solution.py:203
  91.1 6.8 %scatter_custom_fusion = f32[3,6144]{0,1:T(8,128)S(1)} fusion(s32[2048]{0:T(1024)} %bitcast.98, f32[]{:T(128)} %constant.37.clone.1, f32[2,2048]{0,1:T(8,128)} %bitcast.88, f32[]{:T(128)} %constant.51.clone.1), kind=kCustom, calls=%fused_computation.28 | custom fusion | bytes 1123328 | tf_op jit(solution)/shard_map/scatter | solution.py:261
  97.9 1.5 %copy.27 = f32[3,32,192]{2,0,1:T(4,128)S(1)} copy(f32[3,32,192]{0,2,1:T(8,128)S(1)} %bitcast.83) | data formatting | bytes 147456 | tf_op jit(solution)/shard_map/all_to_all | solution.py:262
  99.4 11.7 %all_to_all.14 = f32[3,32,192]{2,0,1:T(4,128)S(1)} all-to-all(f32[3,32,192]{2,0,1:T(4,128)S(1)} %copy.27), channel_id=1, replica_groups=mesh['gx'=8,'gy'=4] {'gx','gy'}, dimensions={1} | all-to-all | bytes 147456 | tf_op jit(solution)/shard_map/all_to_all | solution.py:262
  (99 shorter events, 22.7 us)
Async XLA Ops:
  0.6 11.0 %copy-start = (f32[128,512]{1,0:T(8,128)S(1)}, f32[128,512]{1,0:T(8,128)}, u32[]{:S(2)}) copy-start(f32[128,512]{1,0:T(8,128)} %param.17) | copy-start | bytes 786436
  0.6 11.0 %copy-start.1 = (f32[128,512]{1,0:T(8,128)S(1)}, f32[128,512]{1,0:T(8,128)}, u32[]{:S(2)}) copy-start(f32[128,512]{1,0:T(8,128)} %param.16) | copy-start | bytes 786436
  2.0 18.1 %copy-start.6 = (f32[8]{0:T(128)S(1)}, f32[8]{0:T(128)}, u32[]{:S(2)}) copy-start(f32[8]{0:T(128)} %param.15) | copy-start | bytes 100
  2.0 19.3 %copy-start.10 = (s32[2048]{0:T(1024)S(1)}, s32[2048]{0:T(1024)}, u32[]{:S(2)}) copy-start(s32[2048]{0:T(1024)} %param.18) | copy-start | bytes 24580
  2.0 19.3 %copy-start.5 = (s32[2048,1]{0,1:T(1,128)S(1)}, s32[2048,1]{0,1:T(1,128)}, u32[]{:S(2)}) copy-start(s32[2048,1]{0,1:T(1,128)} %param.19) | copy-start | bytes 24580
  4.3 33.9 %copy-start.2 = (f32[8,32,2048]{2,1,0:T(8,128)S(1)}, f32[8,32,2048]{2,1,0:T(8,128)}, u32[]{:S(2)}) copy-start(f32[8,32,2048]{2,1,0:T(8,128)} %param.11) | copy-start | bytes 6291460
  4.3 19.1 %collective-permute-start = (f32[8,7,2048]{2,1,0:T(8,128)}, f32[8,7,2048]{2,1,0:T(8,128)S(1)}, u32[]{:S(2)}, u32[]{:S(2)}) collective-permute-start(f32[8,7,2048]{2,1,0:T(8,128)} %pad_maximum_fusion.4), channel_id=1, source_target_pairs={{0,1},{1,2},{2,3},{3,4},{4,5},{5,6},{6,7},{7,8},{8,9},{9,10},{10,1... | collective-permute-start | bytes 1376264 | tf_op jit(solution)/shard_map/ppermute | solution.py:25
  10.3 25.5 %collective-permute-start.1 = (f32[8,7,2048]{2,1,0:T(8,128)}, f32[8,7,2048]{2,1,0:T(8,128)}, u32[]{:S(2)}, u32[]{:S(2)}) collective-permute-start(f32[8,7,2048]{2,1,0:T(8,128)} %pad_maximum_fusion.5), channel_id=1, source_target_pairs={{1,0},{2,1},{3,2},{4,3},{5,4},{6,5},{7,6},{8,7},{9,8},{10,9},{11,1... | collective-permute-start | bytes 1376264 | tf_op jit(solution)/shard_map/ppermute | solution.py:25
  12.3 46.2 %collective-permute-start.2 = (f32[2,3,3]{2,1,0:T(4,128)}, f32[2,3,3]{2,1,0:T(4,128)}, u32[]{:S(2)}, u32[]{:S(2)}) collective-permute-start(f32[2,3,3]{2,1,0:T(4,128)} %get-tuple-element.34), channel_id=1, source_target_pairs={{0,5},{1,6},{2,7},{4,9},{5,10},{6,11},{8,13},{9,14},{10,15},{12,17... | collective-permute-start | bytes 224 | tf_op jit(solution)/shard_map/ppermute | solution.py:127
  16.3 43.8 %collective-permute-start.4 = (f32[2,3,3]{2,1,0:T(4,128)}, f32[2,3,3]{2,1,0:T(4,128)}, u32[]{:S(2)}, u32[]{:S(2)}) collective-permute-start(f32[2,3,3]{2,1,0:T(4,128)} %get-tuple-element.37), channel_id=1, source_target_pairs={{1,4},{2,5},{3,6},{5,8},{6,9},{7,10},{9,12},{10,13},{11,14},{13,16... | collective-permute-start | bytes 224 | tf_op jit(solution)/shard_map/ppermute | solution.py:127
  17.5 43.9 %collective-permute-start.7 = (f32[2,3,3]{2,1,0:T(4,128)}, f32[2,3,3]{2,1,0:T(4,128)}, u32[]{:S(2)}, u32[]{:S(2)}) collective-permute-start(f32[2,3,3]{2,1,0:T(4,128)} %get-tuple-element.35), channel_id=1, source_target_pairs={{4,1},{5,2},{6,3},{8,5},{9,6},{10,7},{12,9},{13,10},{14,11},{16,13... | collective-permute-start | bytes 224 | tf_op jit(solution)/shard_map/ppermute | solution.py:127
  23.3 48.5 %collective-permute-start.5 = (f32[2,128,3]{2,1,0:T(8,128)}, f32[2,128,3]{2,1,0:T(8,128)S(1)}, u32[]{:S(2)}, u32[]{:S(2)}) collective-permute-start(f32[2,128,3]{2,1,0:T(8,128)} %get-tuple-element.40), channel_id=1, source_target_pairs={{0,1},{1,2},{2,3},{4,5},{5,6},{6,7},{8,9},{9,10},{10,11},{12,13},{... | collective-permute-start | bytes 9224 | tf_op jit(solution)/shard_map/ppermute | solution.py:127
  35.8 36.1 %collective-permute-start.6 = (f32[2,128,3]{2,1,0:T(8,128)S(1)}, f32[2,128,3]{2,1,0:T(8,128)S(1)}, u32[]{:S(2)}, u32[]{:S(2)}) collective-permute-start(f32[2,128,3]{2,1,0:T(8,128)S(1)} %get-tuple-element.41), channel_id=1, source_target_pairs={{1,0},{2,1},{3,2},{5,4},{6,5},{7,6},{9,8},{10,9},{11,10},{13,12},{... | collective-permute-start | bytes 9224 | tf_op jit(solution)/shard_map/ppermute | solution.py:127
  38.8 1.8 %copy-start.15 = (pred[38]{0:T(512)(128)(4,1)S(1)}, pred[38]{0:T(512)(128)(4,1)}, u32[]{:S(2)}) copy-start(pred[38]{0:T(512)(128)(4,1)} %compare_and_fusion.2) | copy-start | bytes 118
  52.4 6.1 %copy-start.9 = (f32[2,3,512]{2,1,0:T(4,128)S(1)}, f32[2,3,512]{2,1,0:T(4,128)}, u32[]{:S(2)}) copy-start(f32[2,3,512]{2,1,0:T(4,128)} %get-tuple-element.38) | copy-start | bytes 36868
  52.4 7.6 %copy-start.8 = (f32[2,3,512]{2,1,0:T(4,128)S(1)}, f32[2,3,512]{2,1,0:T(4,128)}, u32[]{:S(2)}) copy-start(f32[2,3,512]{2,1,0:T(4,128)} %get-tuple-element.39) | copy-start | bytes 36868
  52.4 8.9 %copy-start.11 = (f32[2,3,3]{2,1,0:T(4,128)S(1)}, f32[2,3,3]{2,1,0:T(4,128)}, u32[]{:S(2)}) copy-start(f32[2,3,3]{2,1,0:T(4,128)} %get-tuple-element.36) | copy-start | bytes 220
  54.5 23.0 %all-to-all-start = ((f32[4,2,36,516]{3,1,2,0:T(2,128)}), f32[4,2,36,516]{3,1,2,0:T(2,128)S(1)}, u32[]{:S(2)}, u32[]{:S(2)}) async-start(f32[4,2,36,516]{3,1,2,0:T(2,128)} %pad_maximum_fusion.3), calls=%async_computation | async-start | bytes 1474560 | tf_op jit(solution)/shard_map/all_to_all | solution.py:143
  58.5 13.3 %collective-permute-start.3 = (f32[2,3,512]{2,1,0:T(4,128)S(1)}, f32[2,3,512]{2,1,0:T(4,128)S(1)}, u32[]{:S(2)}, u32[]{:S(2)}) collective-permute-start(f32[2,3,512]{2,1,0:T(4,128)S(1)} %copy-done.9), channel_id=1, source_target_pairs={{0,4},{1,5},{2,6},{3,7},{4,8},{5,9},{6,10},{7,11},{8,12},{9,13},{1... | collective-permute-start | bytes 36872 | tf_op jit(solution)/shard_map/ppermute | solution.py:127
  60.0 11.8 %collective-permute-start.8 = (f32[2,3,512]{2,1,0:T(4,128)S(1)}, f32[2,3,512]{2,1,0:T(4,128)S(1)}, u32[]{:S(2)}, u32[]{:S(2)}) collective-permute-start(f32[2,3,512]{2,1,0:T(4,128)S(1)} %copy-done.8), channel_id=1, source_target_pairs={{4,0},{5,1},{6,2},{7,3},{8,4},{9,5},{10,6},{11,7},{12,8},{13,9},{1... | collective-permute-start | bytes 36872 | tf_op jit(solution)/shard_map/ppermute | solution.py:127
  61.4 16.5 %copy-start.14 = (pred[516]{0:T(1024)(128)(4,1)S(1)}, pred[516]{0:T(1024)(128)(4,1)}, u32[]{:S(2)}) copy-start(pred[516]{0:T(1024)(128)(4,1)} %fusion.90) | copy-start | bytes 1552
  61.4 10.4 %collective-permute-start.9 = (f32[2,3,3]{2,1,0:T(4,128)S(1)}, f32[2,3,3]{2,1,0:T(4,128)S(1)}, u32[]{:S(2)}, u32[]{:S(2)}) collective-permute-start(f32[2,3,3]{2,1,0:T(4,128)S(1)} %copy-done.11), channel_id=1, source_target_pairs={{5,0},{6,1},{7,2},{9,4},{10,5},{11,6},{13,8},{14,9},{15,10},{17,12... | collective-permute-start | bytes 224 | tf_op jit(solution)/shard_map/ppermute | solution.py:127
  97.9 13.9 %copy-start.4 = (f32[2,1,6144]{2,1,0:T(1,128)S(1)}, f32[2,1,6144]{2,1,0:T(1,128)}, u32[]{:S(2)}) copy-start(f32[2,1,6144]{2,1,0:T(1,128)} %param.20) | copy-start | bytes 147460
  97.9 13.9 %copy-start.7 = (f32[1,6144]{1,0:T(1,128)S(1)}, f32[1,6144]{1,0:T(1,128)}, u32[]{:S(2)}) copy-start(f32[1,6144]{1,0:T(1,128)} %param.21) | copy-start | bytes 73732
  (3 other events, 4.2 us)

commit v4 on v2

--- a/solution.py
+++ b/solution.py
@@ -85,34 +85,53 @@
     return (strain_out, jnp.where(keep, resist_new, resist))
 
 
-def thermal(temp, heat, lateral, vertical):
+def as_slab(piece, layers, cols):
+    flat = piece.reshape(-1)
+    per = layers * cols
+    n = -(-flat.shape[0] // per)
+    return jnp.pad(flat, (0, n * per - flat.shape[0])).reshape(n, layers, cols).transpose(1, 0, 2)
+
+
+def from_slab(slab, shape):
+    size = 1
+    for d in shape:
+        size *= d
+    return slab.transpose(1, 0, 2).reshape(-1)[:size].reshape(shape)
+
+
+def thermal(temp, heat, lateral, vertical, extra, side_last, side_leading):
     devices = lax.axis_size(FLAT)
     t = lax.axis_index(FLAT)
-    rows = temp.shape[1]
-    h = STEPS
-    last = jnp.concatenate([temp[:, rows - h:], heat[:, rows - (h - 1):]], axis=1)
-    leading = jnp.concatenate([temp[:, :h], heat[:, : h - 1]], axis=1)
+    layers, rows, cols = temp.shape
+    h = STEPS + extra
+    hh = h - 1
+    last = jnp.concatenate(
+        [temp[:, rows - h:], heat[:, rows - hh:], as_slab(side_last, layers, cols)], axis=1)
+    leading = jnp.concatenate(
+        [temp[:, :h], heat[:, :hh], as_slab(side_leading, layers, cols)], axis=1)
     before, after = exchange(last, leading, FLAT)
+    side_before = from_slab(before[:, h + hh:], side_last.shape)
+    side_after = from_slab(after[:, h + hh:], side_leading.shape)
+    before, after = before[:, : h + hh], after[:, : h + hh]
     ext = jnp.concatenate([before[:, :h], temp, after[:, :h]], axis=1)
     heat_ext = jnp.concatenate([before[:, h:], heat, after[:, h:]], axis=1)
     for step in range(1, STEPS + 1):
-        r = STEPS - step
-        heat_rows = heat_ext[:, h - 1 - r: h - 1 - r + rows + 2 * r]
+        r = STEPS - step + extra
+        heat_rows = heat_ext[:, hh - r: hh - r + rows + 2 * r]
         ext = thermal_step(ext, heat_rows, lateral, vertical)
-        if r > 0:
+        if step < STEPS:
             g = t * rows + jnp.arange(-r, rows + r)
             inside = (g >= 0) & (g < devices * rows)
             ext = jnp.where(inside[None, :, None], ext, 0.0)
-    return ext
+    return ext, side_before, side_after
 
 
 def relay(load, top, width):
     n_gy = lax.axis_size("gy")
     rows, cols = load.shape
     cm = cols // n_gy
-    before, after = exchange(load[rows - width:], load[:width], FLAT)
-    load_ext = jnp.concatenate([before, load, after], axis=0)
-    lp = jnp.pad(load_ext, ((0, 0), (width, width)))
+    rows = rows - 2 * width
+    lp = jnp.pad(load, ((0, 0), (width, width)))
     tp = jnp.pad(top, ((width, width), (width, width)))
     both = jnp.stack([lp, tp])
     send = jnp.stack([both[:, :, k * cm: k * cm + cm + 2 * width] for k in range(n_gy)])
@@ -207,14 +226,20 @@
     gi, gj = lax.axis_index("gx"), lax.axis_index("gy")
     rm, cm = warp_prev.shape
 
-    wm = with_halo(jnp.stack([warp_prev, modulus]), (("gx", 1), ("gy", 2)), SWEEPS)
+    wm = jnp.stack([warp_prev, modulus])
     owners = joint_owner[:, 0]
     capacity = joint_resist.shape[1] // devices
     slots = owners * capacity + joint_ranks(owners, devices)
 
-    temp = thermal(temp_start, heat_input, lateral, vertical)
+    extra = SWEEPS - 1
+    g = SWEEPS
+    temp, left, right = thermal(
+        temp_start, heat_input, lateral, vertical, extra, wm[:, :, cm - g:], wm[:, :, :g])
+    left = jnp.where(gj > 0, left, 0.0)
+    right = jnp.where(gj < n_gy - 1, right, 0.0)
+    wm = with_halo(jnp.concatenate([left, wm, right], axis=2), (("gx", 1),), g)
     load_t = moment_of(temp, weighting)
-    load, top = relay(load_t, temp[-1], SWEEPS - 1)
+    load, top = relay(load_t, temp[-1, extra: temp.shape[1] - extra], extra)
 
     warp = wm[0]
     mod_ext = wm[1]

time: 113 us -> 114 us (level)
  starting transfers between devices: 27.2 us -> 24 us
  waiting for transfers between devices: 18.7 us -> 21.5 us
  other arithmetic: 22 us -> 23.8 us
    ppermute x8 -> x4, starting transfers between devices: 21.4 us -> 13.3 us  [exchange(): return (lax.ppermute(last, axis, up), lax.ppermute(leading, axis, down))]
    all_to_all x1, waiting for transfers between devices: 4.42 us -> 10.6 us  [relay(): recv = lax.all_to_all(send, 'gy', split_axis=0, concat_axis=0, tiled=True)]
    all_to_all x1, starting transfers between devices: 5.83 us -> 10.7 us  [relay(): recv = lax.all_to_all(send, 'gy', split_axis=0, concat_axis=0, tiled=True)]
    concatenate x2 -> x3, other arithmetic: 0.25 us -> 4.79 us  [the longest x1 2.84 us: thermal(): heat_ext = jnp.concatenate([before[:, h:], heat, after[:, h:]], axis=1)]
    ppermute x8 -> x4, waiting for transfers between devices: 14.3 us -> 10.9 us  [exchange(): return (lax.ppermute(last, axis, up), lax.ppermute(leading, axis, down))]
    select_n x1 -> x2, other arithmetic: 3.03 us -> 0.01 us  [the longest x1 0.01 us: body(): right = jnp.where(gj < n_gy - 1, right, 0.0)]
  transfers between devices with their start and end apart: 9 -> 5, of which waited for: 4 -> 3; matrix products, arithmetic and copies ran while one was open for 19% -> 4% of each run, Pallas kernels for 0% -> 0%
where the time goes in v4:
time: 114 us; the launch traced here: 113 us
  starting transfers between devices  24 us (21%)
  other arithmetic  23.8 us (21%)
  waiting for transfers between devices  21.5 us (19%)
  local copies, waits for them, and re-layouts  18.3 us (16%)
  blocking collectives  15.9 us (14%)
  Pallas kernels  8.2 us (7%)
  between operations  1.24 us (1%)
    all_to_all x1, blocking collectives, body(): lax.all_to_all(outgoing, FLAT, split_axis=1, concat_axis=1, tiled=True)  15.9 us
    ppermute x4, starting transfers between devices, exchange(): return (lax.ppermute(last, axis, up), lax.ppermute(leading, axis, down))  13.3 us
    ppermute x4, waiting for transfers between devices, exchange(): return (lax.ppermute(last, axis, up), lax.ppermute(leading, axis, down))  10.9 us
    all_to_all x1, starting transfers between devices, relay(): recv = lax.all_to_all(send, 'gy', split_axis=0, concat_axis=0, tiled=True)  10.7 us
    all_to_all x1, waiting for transfers between devices, relay(): recv = lax.all_to_all(send, 'gy', split_axis=0, concat_axis=0, tiled=True)  10.6 us
    pallas_call x1, Pallas kernels, pick_cells(): pl.pallas_call(pick_kernel, grid=(count // block,), in_specs=[pl.BlockSpe...  8.2 us
    scatter x1, local copies, waits for them, and re-layouts, body(): jnp.zeros((3, devices * capacity), jnp.float32).at[:, slots].set(values)  6.81 us
    add x1, other arithmetic, moment_of(): total = total + weighting[layer] * field[layer]  5.22 us
  transfers between devices with their start and end apart: 5, of which 3 were waited for; matrix products, arithmetic and copies ran while one was open for 4% of the time, Pallas kernels for 0%

profile of v4, /device:TPU:0, one launch (start us, length us, event | category | flops | bytes accessed | tf_op | source)
XLA Modules:
  0.0 113.4 jit_solution(2950231519190286768)
XLA Ops:
  0.7 1.0 pad_maximum_fusion.11
  1.9 1.3 %fusion.89 = (f32[8,3,2048]{2,1,0:T(4,128)S(1)}, f32[8,3,2048]{2,1,0:T(4,128)S(1)}) fusion(f32[8,32,2048]{2,1,0:T(8,128)} %param.12), kind=kLoop, calls=%fused_computation.203 | loop fusion | bytes 786432 | tf_op jit(solution)/shard_map/slice | solution.py:109
  3.2 1.4 %fusion.88 = (f32[8,4,2048]{2,1,0:T(4,128)S(1)}, f32[8,4,2048]{2,1,0:T(4,128)S(1)}) fusion(f32[8,32,2048]{2,1,0:T(8,128)} %param.11), kind=kLoop, calls=%fused_computation.202 | loop fusion | bytes 1048576 | tf_op jit(solution)/shard_map/slice | solution.py:109
  4.7 1.0 pad_maximum_fusion.6
  5.7 1.3 %collective-permute-start.1 = (f32[8,8,2048]{2,1,0:T(8,128)}, f32[8,8,2048]{2,1,0:T(8,128)S(1)}, u32[]{:S(2)}, u32[]{:S(2)}) collective-permute-start(f32[8,8,2048]{2,1,0:T(8,128)} %pad_maximum_fusion.6), channel_id=1, source_target_pairs={{1,0},{2,1},{3,2},{4,3},{5,4},{6,5},{7,6},{8,7},{9,8},{10,9},{11,1... | collective-permute-start | bytes 1572872 | tf_op jit(solution)/shard_map/ppermute | solution.py:25
  8.2 5.6 %collective-permute-start = (f32[8,8,2048]{2,1,0:T(8,128)}, f32[8,8,2048]{2,1,0:T(8,128)S(1)}, u32[]{:S(2)}, u32[]{:S(2)}) collective-permute-start(f32[8,8,2048]{2,1,0:T(8,128)} %pad_maximum_fusion.5), channel_id=1, source_target_pairs={{0,1},{1,2},{2,3},{3,4},{4,5},{5,6},{6,7},{7,8},{8,9},{9,10},{10,1... | collective-permute-start | bytes 1572872 | tf_op jit(solution)/shard_map/ppermute | solution.py:25
  15.4 7.4 %collective-permute-done.1 = f32[8,8,2048]{2,1,0:T(8,128)S(1)} collective-permute-done((f32[8,8,2048]{2,1,0:T(8,128)}, f32[8,8,2048]{2,1,0:T(8,128)S(1)}, u32[]{:S(2)}, u32[]{:S(2)}) %collective-permute-start.1) | collective-permute-done | bytes 524320 | tf_op jit(solution)/shard_map/ppermute | solution.py:25
  22.8 3.5 %collective-permute-done = f32[8,8,2048]{2,1,0:T(8,128)S(1)} collective-permute-done((f32[8,8,2048]{2,1,0:T(8,128)}, f32[8,8,2048]{2,1,0:T(8,128)S(1)}, u32[]{:S(2)}, u32[]{:S(2)}) %collective-permute-start) | collective-permute-done | bytes 524320 | tf_op jit(solution)/shard_map/ppermute | solution.py:25
  27.7 1.0 copy-done.2
  28.7 2.8 %pad_maximum_fusion.1 = (f32[8,38,2048]{2,1,0:T(8,128)S(1)}, f32[8,38,2048]{2,1,0:T(8,128)S(1)}) fusion(f32[8,3,2048]{2,1,0:T(4,128)S(1)} %slice.433, f32[8,32,2048]{2,1,0:T(8,128)S(1)} %copy-done.2, f32[8,3,2048]{2,1,0:T(4,128)S(1)} %slice.432, f32[7,38,2048]{2,1,0:T(8,128)S(1)} %fusion.16, f32[8,40,2048]{2,1,0:T(8,128)S(1)} %pad_maximum_fusion, ...), kind=kLoop, calls=%fused_computation.23 | loop fusion | flops 8093696 | bytes 20382720 | tf_op jit(solution)/shard_map/concatenate | solution.py:117
  32.0 2.6 %fusion.14 = f32[8,36,2048]{2,1,0:T(8,128)S(1)} fusion(f32[8,38,2048]{2,1,0:T(8,128)S(1)} %get-tuple-element.12, f32[8,38,2048]{2,1,0:T(8,128)S(1)} %get-tuple-element.11, f32[7,36,2048]{2,1,0:T(8,128)S(1)} %fusion.15, f32[8]{0:T(128)S(1)} %copy-done.10), kind=kLoop, calls=%fused_computation.19 | loop fusion | flops 5898240 | bytes 17760768 | tf_op jit(solution)/shard_map/add | solution.py:44
  35.0 5.2 %fusion.43 = f32[36,2048]{1,0:T(8,128)S(1)} fusion(f32[8,36,2048]{2,1,0:T(8,128)S(1)} %fusion.14, f32[]{:T(128)} %bitcast.11, f32[]{:T(128)} %bitcast.10, f32[]{:T(128)} %bitcast.9, f32[]{:T(128)} %bitcast.8, f32[]{:T(128)} %bitcast.7, f32[]{:T(128)} %bitcast.6, f32[]{:T(128)} %bitcast.5, f32[]{:T(128)} %bitcast), kind=kLoop, calls=%fused_computation.92 | loop fusion | flops 1105920 | bytes 2654240 | tf_op jit(solution)/shard_map/add | solution.py:50
  41.5 1.2 %pad_maximum_fusion.3 = f32[4,2,36,516]{3,1,2,0:T(2,128)} fusion(f32[1,2,36,516]{3,1,2,0:T(2,128)S(1)} %get-tuple-element.31, f32[1,2,36,516]{3,1,2,0:T(2,128)S(1)} %get-tuple-element.32, f32[1,2,36,516]{3,1,2,0:T(2,128)S(1)} %get-tuple-element.30, f32[1,2,36,516]{3,1,2,0:T(2,128)S(1)} %get-tuple-element.29), kind=kLoop, calls=%fused_computation.38 | loop fusion | flops 445824 | bytes 1188864 | tf_op jit(solution)/shard_map/stack | solution.py:137
  42.7 10.7 %all-to-all-start = ((f32[4,2,36,516]{3,1,2,0:T(2,128)}), f32[4,2,36,516]{3,1,2,0:T(2,128)S(1)}, u32[]{:S(2)}, u32[]{:S(2)}) async-start(f32[4,2,36,516]{3,1,2,0:T(2,128)} %pad_maximum_fusion.3), calls=%async_computation | async-start | bytes 1474560 | tf_op jit(solution)/shard_map/all_to_all | solution.py:138
  54.1 1.3 %collective-permute-start.3 = (f32[2,3,518]{2,1,0:T(4,128)S(1)}, f32[2,3,518]{2,1,0:T(4,128)S(1)}, u32[]{:S(2)}, u32[]{:S(2)}) collective-permute-start(f32[2,3,518]{2,1,0:T(4,128)S(1)} %get-tuple-element.18), channel_id=1, source_target_pairs={{4,0},{8,4},{12,8},{16,12},{20,16},{24,20},{28,24},{5,1},{9,5},{13... | collective-permute-start | bytes 37304 | tf_op jit(solution)/shard_map/ppermute | solution.py:25
  55.4 5.1 %collective-permute-start.2 = (f32[2,3,518]{2,1,0:T(4,128)S(1)}, f32[2,3,518]{2,1,0:T(4,128)S(1)}, u32[]{:S(2)}, u32[]{:S(2)}) collective-permute-start(f32[2,3,518]{2,1,0:T(4,128)S(1)} %get-tuple-element.17), channel_id=1, source_target_pairs={{0,4},{4,8},{8,12},{12,16},{16,20},{20,24},{24,28},{1,5},{5,9},{9,... | collective-permute-start | bytes 37304 | tf_op jit(solution)/shard_map/ppermute | solution.py:25
  60.6 1.4 %copy.26.rc_ref = s32[2048,2]{1,0:T(8,128)} copy(s32[2048,2]{0,1:T(2,128)S(1)} %pad_add_fusion) | data formatting | bytes 32768 | tf_op jit(solution)/shard_map/stack | solution.py:196
  62.3 10.6 %all-to-all-done = f32[4,2,36,516]{3,1,2,0:T(2,128)S(1)} async-done(((f32[4,2,36,516]{3,1,2,0:T(2,128)}), f32[4,2,36,516]{3,1,2,0:T(2,128)S(1)}, u32[]{:S(2)}, u32[]{:S(2)}) %all-to-all-start) | async-done | bytes 594464 | tf_op jit(solution)/shard_map/all_to_all | solution.py:138
  74.9 1.4 %subtract_bitcast_fusion = (f32[1,128,512]{2,1,0:T(8,128)S(1)}, f32[128,512]{1,0:T(8,128)}) fusion(f32[128,512]{1,0:T(8,128)S(1)} %copy-done, f32[130,514]{1,0:T(8,128)S(1)} %fusion.24, f32[134,518]{1,0:T(8,128)S(1)} %get-tuple-element.27, f32[132,516]{1,0:T(8,128)S(1)} %get-tuple-element.10), kind=kLoop, calls=%fused_computation.126 | loop fusion | flops 1441792 | bytes 3407872 | tf_op jit(solution)/shard_map/concatenate | solution.py:190
  78.3 8.2 %shard_map.130 = f32[2048,2]{1,0:T(8,128)} custom-call(s32[2048,2]{1,0:T(8,128)} %copy.26.rc_ref, bf16[3,128,1024]{2,1,0:T(8,128)(2,1)} %pad_maximum_fusion.2.parts_ref), custom_call_target="tpu_custom_call" | custom-call | tf_op jit(solution)/shard_map/pallas_call | solution.py:198
  86.5 6.8 %scatter_custom_fusion = f32[3,6144]{0,1:T(8,128)S(1)} fusion(s32[2048]{0:T(1024)S(1)} %bitcast.104, f32[]{:T(128)} %constant.38.clone.1, f32[2,2048]{0,1:T(8,128)} %bitcast.88, f32[]{:T(128)} %constant.53.clone.1), kind=kCustom, calls=%fused_computation.28 | custom fusion | bytes 90120 | tf_op jit(solution)/shard_map/scatter | solution.py:261
  93.3 1.5 %copy.27 = f32[3,32,192]{2,0,1:T(4,128)S(1)} copy(f32[3,32,192]{0,2,1:T(8,128)S(1)} %bitcast.87) | data formatting | bytes 147456 | tf_op jit(solution)/shard_map/all_to_all | solution.py:262
  94.8 15.9 %all_to_all.14 = f32[3,32,192]{2,0,1:T(4,128)S(1)} all-to-all(f32[3,32,192]{2,0,1:T(4,128)S(1)} %copy.27), channel_id=1, replica_groups=mesh['gx'=8,'gy'=4] {'gx','gy'}, dimensions={1} | all-to-all | bytes 147456 | tf_op jit(solution)/shard_map/all_to_all | solution.py:262
  111.5 1.1 add_select_fusion
  (86 shorter events, 12.6 us)
Async XLA Ops:
  0.6 13.2 %copy-start.6 = (f32[8]{0:T(128)S(1)}, f32[8]{0:T(128)}, u32[]{:S(2)}) copy-start(f32[8]{0:T(128)} %param.15) | copy-start | bytes 100
  0.6 13.9 %copy-start.5 = (s32[2048,1]{0,1:T(1,128)S(1)}, s32[2048,1]{0,1:T(1,128)}, u32[]{:S(2)}) copy-start(s32[2048,1]{0,1:T(1,128)} %param.19) | copy-start | bytes 24580
  1.9 13.4 %copy-start.8 = (s32[2048]{0:T(1024)S(1)}, s32[2048]{0:T(1024)}, u32[]{:S(2)}) copy-start(s32[2048]{0:T(1024)} %param.18) | copy-start | bytes 24580
  3.2 23.2 %copy-start.1 = (f32[8,32,2048]{2,1,0:T(8,128)S(1)}, f32[8,32,2048]{2,1,0:T(8,128)}, u32[]{:S(2)}) copy-start(f32[8,32,2048]{2,1,0:T(8,128)} %param.11) | copy-start | bytes 6291460
  5.7 17.1 %collective-permute-start.1 = (f32[8,8,2048]{2,1,0:T(8,128)}, f32[8,8,2048]{2,1,0:T(8,128)S(1)}, u32[]{:S(2)}, u32[]{:S(2)}) collective-permute-start(f32[8,8,2048]{2,1,0:T(8,128)} %pad_maximum_fusion.6), channel_id=1, source_target_pairs={{1,0},{2,1},{3,2},{4,3},{5,4},{6,5},{7,6},{8,7},{9,8},{10,9},{11,1... | collective-permute-start | bytes 1572872 | tf_op jit(solution)/shard_map/ppermute | solution.py:25
  8.2 18.2 %collective-permute-start = (f32[8,8,2048]{2,1,0:T(8,128)}, f32[8,8,2048]{2,1,0:T(8,128)S(1)}, u32[]{:S(2)}, u32[]{:S(2)}) collective-permute-start(f32[8,8,2048]{2,1,0:T(8,128)} %pad_maximum_fusion.5), channel_id=1, source_target_pairs={{0,1},{1,2},{2,3},{3,4},{4,5},{5,6},{6,7},{7,8},{8,9},{9,10},{10,1... | collective-permute-start | bytes 1572872 | tf_op jit(solution)/shard_map/ppermute | solution.py:25
  26.4 0.7 copy-start.9
  27.1 1.6 %copy-start.2 = (f32[8,32,2048]{2,1,0:T(8,128)S(1)}, f32[8,32,2048]{2,1,0:T(8,128)}, u32[]{:S(2)}) copy-start(f32[8,32,2048]{2,1,0:T(8,128)} %param.12) | copy-start | bytes 6291460
  27.1 1.6 %copy-start.10 = (f32[8]{0:T(128)S(1)}, f32[8]{0:T(128)}, u32[]{:S(2)}) copy-start(f32[8]{0:T(128)} %param.13) | copy-start | bytes 100
  40.4 13.6 %copy-start = (f32[128,512]{1,0:T(8,128)S(1)}, f32[128,512]{1,0:T(8,128)}, u32[]{:S(2)}) copy-start(f32[128,512]{1,0:T(8,128)} %param.17) | copy-start | bytes 786436
  40.4 13.6 %copy-start.3 = (f32[128,512]{1,0:T(8,128)S(1)}, f32[128,512]{1,0:T(8,128)}, u32[]{:S(2)}) copy-start(f32[128,512]{1,0:T(8,128)} %param.16) | copy-start | bytes 786436
  42.7 30.2 %all-to-all-start = ((f32[4,2,36,516]{3,1,2,0:T(2,128)}), f32[4,2,36,516]{3,1,2,0:T(2,128)S(1)}, u32[]{:S(2)}, u32[]{:S(2)}) async-start(f32[4,2,36,516]{3,1,2,0:T(2,128)} %pad_maximum_fusion.3), calls=%async_computation | async-start | bytes 1474560 | tf_op jit(solution)/shard_map/all_to_all | solution.py:138
  54.1 7.8 %collective-permute-start.3 = (f32[2,3,518]{2,1,0:T(4,128)S(1)}, f32[2,3,518]{2,1,0:T(4,128)S(1)}, u32[]{:S(2)}, u32[]{:S(2)}) collective-permute-start(f32[2,3,518]{2,1,0:T(4,128)S(1)} %get-tuple-element.18), channel_id=1, source_target_pairs={{4,0},{8,4},{12,8},{16,12},{20,16},{24,20},{28,24},{5,1},{9,5},{13... | collective-permute-start | bytes 37304 | tf_op jit(solution)/shard_map/ppermute | solution.py:25
  55.4 6.5 %collective-permute-start.2 = (f32[2,3,518]{2,1,0:T(4,128)S(1)}, f32[2,3,518]{2,1,0:T(4,128)S(1)}, u32[]{:S(2)}, u32[]{:S(2)}) collective-permute-start(f32[2,3,518]{2,1,0:T(4,128)S(1)} %get-tuple-element.17), channel_id=1, source_target_pairs={{0,4},{4,8},{8,12},{12,16},{16,20},{20,24},{24,28},{1,5},{5,9},{9,... | collective-permute-start | bytes 37304 | tf_op jit(solution)/shard_map/ppermute | solution.py:25
  93.3 18.2 %copy-start.4 = (f32[2,1,6144]{2,1,0:T(1,128)S(1)}, f32[2,1,6144]{2,1,0:T(1,128)}, u32[]{:S(2)}) copy-start(f32[2,1,6144]{2,1,0:T(1,128)} %param.20) | copy-start | bytes 147460
  93.3 18.2 %copy-start.7 = (f32[1,6144]{1,0:T(1,128)S(1)}, f32[1,6144]{1,0:T(1,128)}, u32[]{:S(2)}) copy-start(f32[1,6144]{1,0:T(1,128)} %param.21) | copy-start | bytes 73732

commit v5 on v4

--- a/solution.py
+++ b/solution.py
@@ -135,7 +135,12 @@
     tp = jnp.pad(top, ((width, width), (width, width)))
     both = jnp.stack([lp, tp])
     send = jnp.stack([both[:, :, k * cm: k * cm + cm + 2 * width] for k in range(n_gy)])
-    recv = lax.all_to_all(send, "gy", split_axis=0, concat_axis=0, tiled=True)
+    gj = lax.axis_index("gy")
+    got = [lax.dynamic_index_in_dim(send, gj, 0, keepdims=False)]
+    for shift in range(1, n_gy):
+        piece = lax.dynamic_index_in_dim(send, (gj + shift) % n_gy, 0, keepdims=False)
+        got.append(lax.ppermute(piece, "gy", [(j, (j + shift) % n_gy) for j in range(n_gy)]))
+    recv = jnp.take(jnp.stack(got), (gj - jnp.arange(n_gy)) % n_gy, axis=0)
     parts = []
     for k in range(n_gy):
         lo = 0 if k == 0 else width

time: 114 us -> 120 us (1.053)
  blocking collectives: 15.9 us -> 22.1 us
  local copies, waits for them, and re-layouts: 18.3 us -> 22.8 us
  waiting for transfers between devices: 21.5 us -> 18.9 us
  other arithmetic: 23.8 us -> 22.2 us
    ppermute x0 -> x3, waiting for transfers between devices: none -> 11.4 us  [relay(): lax.ppermute(piece, 'gy', [(j, (j + shift) % n_gy) for j in range(n_gy)])]
    all_to_all x1 -> x0, starting transfers between devices: 10.7 us -> none  [relay(): recv = lax.all_to_all(send, 'gy', split_axis=0, concat_axis=0, tiled=True)]
    all_to_all x1 -> x0, waiting for transfers between devices: 10.6 us -> none  [relay(): recv = lax.all_to_all(send, 'gy', split_axis=0, concat_axis=0, tiled=True)]
    ppermute x4, starting transfers between devices: 13.3 us -> 21.2 us  [exchange(): return (lax.ppermute(last, axis, up), lax.ppermute(leading, axis, down))]
    all_to_all x1, blocking collectives: 15.9 us -> 22.1 us  [body(): lax.all_to_all(outgoing, FLAT, split_axis=1, concat_axis=1, tiled=True)]
    ppermute x4, waiting for transfers between devices: 10.9 us -> 7.48 us  [exchange(): return (lax.ppermute(last, axis, up), lax.ppermute(leading, axis, down))]
    slice x2, local copies, waits for them, and re-layouts: 0.12 us -> 2.38 us  [thermal(): heat_ext = jnp.concatenate([before[:, h:], heat, after[:, h:]], axis=1)]
    slice x2, local copies, waits for them, and re-layouts: 0.07 us -> 2.15 us  [thermal(): ext = jnp.concatenate([before[:, :h], temp, after[:, :h]], axis=1)]
  transfers between devices with their start and end apart: 5 -> 7, of which waited for: 3 -> 5; matrix products, arithmetic and copies ran while one was open for 4% -> 19% of each run, Pallas kernels for 0% -> 0%
where the time goes in v5:
time: 120 us; the launch traced here: 119 us
  starting transfers between devices  23.3 us (19%)
  local copies, waits for them, and re-layouts  22.8 us (19%)
  other arithmetic  22.2 us (18%)
  blocking collectives  22.1 us (18%)
  waiting for transfers between devices  18.9 us (16%)
  Pallas kernels  8.2 us (7%)
  between operations  1.21 us (1%)
    all_to_all x1, blocking collectives, body(): lax.all_to_all(outgoing, FLAT, split_axis=1, concat_axis=1, tiled=True)  22.1 us
    ppermute x4, starting transfers between devices, exchange(): return (lax.ppermute(last, axis, up), lax.ppermute(leading, axis, down))  21.2 us
    ppermute x3, waiting for transfers between devices, relay(): lax.ppermute(piece, 'gy', [(j, (j + shift) % n_gy) for j in range(n_gy)])  11.4 us
    pallas_call x1, Pallas kernels, pick_cells(): pl.pallas_call(pick_kernel, grid=(count // block,), in_specs=[pl.BlockSpe...  8.2 us
    ppermute x4, waiting for transfers between devices, exchange(): return (lax.ppermute(last, axis, up), lax.ppermute(leading, axis, down))  7.48 us
    scatter x1, local copies, waits for them, and re-layouts, body(): jnp.zeros((3, devices * capacity), jnp.float32).at[:, slots].set(values)  6.81 us
    add x1, other arithmetic, moment_of(): total = total + weighting[layer] * field[layer]  5.2 us
    concatenate x1, other arithmetic, thermal(): heat_ext = jnp.concatenate([before[:, h:], heat, after[:, h:]], axis=1)  2.87 us
  transfers between devices with their start and end apart: 7, of which 5 were waited for; matrix products, arithmetic and copies ran while one was open for 19% of the time, Pallas kernels for 0%

profile of v5, /device:TPU:0, one launch (start us, length us, event | category | flops | bytes accessed | tf_op | source)
XLA Modules:
  0.0 119.0 jit_solution(3768639512305698038)
XLA Ops:
  1.9 1.3 %fusion.92 = (f32[8,3,2048]{2,1,0:T(4,128)S(1)}, f32[8,3,2048]{2,1,0:T(4,128)S(1)}) fusion(f32[8,32,2048]{2,1,0:T(8,128)} %param.12), kind=kLoop, calls=%fused_computation.224 | loop fusion | bytes 786432 | tf_op jit(solution)/shard_map/slice | solution.py:109
  3.2 1.3 %fusion.91 = (f32[8,4,2048]{2,1,0:T(4,128)S(1)}, f32[8,4,2048]{2,1,0:T(4,128)S(1)}) fusion(f32[8,32,2048]{2,1,0:T(8,128)} %param.11), kind=kLoop, calls=%fused_computation.223 | loop fusion | bytes 1048576 | tf_op jit(solution)/shard_map/slice | solution.py:109
  5.6 1.3 %collective-permute-start.1 = (f32[8,8,2048]{2,1,0:T(8,128)}, f32[8,8,2048]{2,1,0:T(8,128)}, u32[]{:S(2)}, u32[]{:S(2)}) collective-permute-start(f32[8,8,2048]{2,1,0:T(8,128)} %pad_maximum_fusion.7), channel_id=1, source_target_pairs={{1,0},{2,1},{3,2},{4,3},{5,4},{6,5},{7,6},{8,7},{9,8},{10,9},{11,1... | collective-permute-start | bytes 1572872 | tf_op jit(solution)/shard_map/ppermute | solution.py:25
  8.0 6.4 %collective-permute-start = (f32[8,8,2048]{2,1,0:T(8,128)}, f32[8,8,2048]{2,1,0:T(8,128)}, u32[]{:S(2)}, u32[]{:S(2)}) collective-permute-start(f32[8,8,2048]{2,1,0:T(8,128)} %pad_maximum_fusion.6), channel_id=1, source_target_pairs={{0,1},{1,2},{2,3},{3,4},{4,5},{5,6},{6,7},{7,8},{8,9},{9,10},{10,1... | collective-permute-start | bytes 1572872 | tf_op jit(solution)/shard_map/ppermute | solution.py:25
  16.1 1.4 %copy.17.rc_ref = s32[2048,2]{1,0:T(8,128)} copy(s32[2048,2]{0,1:T(2,128)S(1)} %pad_add_fusion) | data formatting | bytes 32768 | tf_op jit(solution)/shard_map/stack | solution.py:201
  17.5 5.3 %collective-permute-done.1 = f32[8,8,2048]{2,1,0:T(8,128)} collective-permute-done((f32[8,8,2048]{2,1,0:T(8,128)}, f32[8,8,2048]{2,1,0:T(8,128)}, u32[]{:S(2)}, u32[]{:S(2)}) %collective-permute-start.1) | collective-permute-done | bytes 524320 | tf_op jit(solution)/shard_map/ppermute | solution.py:25
  22.7 1.1 slice.464
  24.1 2.2 %collective-permute-done = f32[8,8,2048]{2,1,0:T(8,128)} collective-permute-done((f32[8,8,2048]{2,1,0:T(8,128)}, f32[8,8,2048]{2,1,0:T(8,128)}, u32[]{:S(2)}, u32[]{:S(2)}) %collective-permute-start) | collective-permute-done | bytes 524320 | tf_op jit(solution)/shard_map/ppermute | solution.py:25
  27.7 1.3 %collective-permute-start.6 = (f32[2,3,518]{2,1,0:T(4,128)S(1)}, f32[2,3,518]{2,1,0:T(4,128)S(1)}, u32[]{:S(2)}, u32[]{:S(2)}) collective-permute-start(f32[2,3,518]{2,1,0:T(4,128)S(1)} %get-tuple-element.30), channel_id=1, source_target_pairs={{4,0},{8,4},{12,8},{16,12},{20,16},{24,20},{28,24},{5,1},{9,5},{13... | collective-permute-start | bytes 37304 | tf_op jit(solution)/shard_map/ppermute | solution.py:25
  29.0 12.3 %collective-permute-start.5 = (f32[2,3,518]{2,1,0:T(4,128)S(1)}, f32[2,3,518]{2,1,0:T(4,128)S(1)}, u32[]{:S(2)}, u32[]{:S(2)}) collective-permute-start(f32[2,3,518]{2,1,0:T(4,128)S(1)} %get-tuple-element.29), channel_id=1, source_target_pairs={{0,4},{4,8},{8,12},{12,16},{16,20},{20,24},{24,28},{1,5},{5,9},{9,... | collective-permute-start | bytes 37304 | tf_op jit(solution)/shard_map/ppermute | solution.py:25
  44.5 1.3 %slice.435 = f32[8,3,2048]{2,1,0:T(4,128)S(1)} slice(f32[8,8,2048]{2,1,0:T(8,128)} %collective-permute-done.1), slice={[0:8], [4:7], [0:2048]} | slice | bytes 393216 | tf_op jit(solution)/shard_map/slice | solution.py:117
  45.8 1.1 slice.434
  47.0 2.9 %pad_maximum_fusion.1 = (f32[8,38,2048]{2,1,0:T(8,128)S(1)}, f32[8,38,2048]{2,1,0:T(8,128)S(1)}) fusion(f32[8,3,2048]{2,1,0:T(4,128)S(1)} %slice.435, f32[8,32,2048]{2,1,0:T(8,128)S(1)} %copy-done.2, f32[8,3,2048]{2,1,0:T(4,128)S(1)} %slice.434, f32[7,38,2048]{2,1,0:T(8,128)S(1)} %fusion.16, f32[8,40,2048]{2,1,0:T(8,128)S(1)} %pad_maximum_fusion, ...), kind=kLoop, calls=%fused_computation.24 | loop fusion | flops 8093696 | bytes 20382720 | tf_op jit(solution)/shard_map/concatenate | solution.py:117
  50.4 2.6 %fusion.14 = f32[8,36,2048]{2,1,0:T(8,128)S(1)} fusion(f32[8,38,2048]{2,1,0:T(8,128)S(1)} %get-tuple-element.12, f32[8,38,2048]{2,1,0:T(8,128)S(1)} %get-tuple-element.11, f32[7,36,2048]{2,1,0:T(8,128)S(1)} %fusion.15, f32[8]{0:T(128)S(1)} %copy-done.10), kind=kLoop, calls=%fused_computation.20 | loop fusion | flops 5898240 | bytes 17760768 | tf_op jit(solution)/shard_map/add | solution.py:44
  53.0 5.2 %fusion.43 = f32[36,2048]{1,0:T(8,128)S(1)} fusion(f32[8,36,2048]{2,1,0:T(8,128)S(1)} %fusion.14, f32[]{:T(128)} %bitcast.11, f32[]{:T(128)} %bitcast.10, f32[]{:T(128)} %bitcast.9, f32[]{:T(128)} %bitcast.8, f32[]{:T(128)} %bitcast.7, f32[]{:T(128)} %bitcast.6, f32[]{:T(128)} %bitcast.5, f32[]{:T(128)} %bitcast), kind=kLoop, calls=%fused_computation.96 | loop fusion | flops 1105920 | bytes 2654240 | tf_op jit(solution)/shard_map/add | solution.py:50
  58.9 1.8 %collective-permute-start.2 = (f32[2,36,516]{2,1,0:T(8,128)S(1)}, f32[2,36,516]{2,1,0:T(8,128)S(1)}, u32[]{:S(2)}, u32[]{:S(2)}) collective-permute-start(f32[2,36,516]{2,1,0:T(8,128)S(1)} %get-tuple-element.28), channel_id=1, source_target_pairs={{0,1},{1,2},{2,3},{3,0},{4,5},{5,6},{6,7},{7,4},{8,9},{9,10},{10,1... | collective-permute-start | bytes 445832 | tf_op jit(solution)/shard_map/ppermute | solution.py:142
  61.1 5.9 %collective-permute-done.4 = f32[2,36,516]{2,1,0:T(8,128)S(1)} collective-permute-done((f32[2,36,516]{2,1,0:T(8,128)S(1)}, f32[2,36,516]{2,1,0:T(8,128)S(1)}, u32[]{:S(2)}, u32[]{:S(2)}) %collective-permute-start.4) | collective-permute-done | bytes 148640 | tf_op jit(solution)/shard_map/ppermute | solution.py:142
  67.0 2.5 %collective-permute-done.3 = f32[2,36,516]{2,1,0:T(8,128)S(1)} collective-permute-done((f32[2,36,516]{2,1,0:T(8,128)S(1)}, f32[2,36,516]{2,1,0:T(8,128)S(1)}, u32[]{:S(2)}, u32[]{:S(2)}) %collective-permute-start.3) | collective-permute-done | bytes 148640 | tf_op jit(solution)/shard_map/ppermute | solution.py:142
  69.5 3.0 %collective-permute-done.2 = f32[2,36,516]{2,1,0:T(8,128)S(1)} collective-permute-done((f32[2,36,516]{2,1,0:T(8,128)S(1)}, f32[2,36,516]{2,1,0:T(8,128)S(1)}, u32[]{:S(2)}, u32[]{:S(2)}) %collective-permute-start.2) | collective-permute-done | bytes 148640 | tf_op jit(solution)/shard_map/ppermute | solution.py:142
  75.2 1.4 %subtract_bitcast_fusion = (f32[1,128,512]{2,1,0:T(8,128)S(1)}, f32[128,512]{1,0:T(8,128)}) fusion(f32[128,512]{1,0:T(8,128)S(1)} %copy-done, f32[130,514]{1,0:T(8,128)S(1)} %fusion.24, f32[134,518]{1,0:T(8,128)S(1)} %get-tuple-element.35, f32[132,516]{1,0:T(8,128)S(1)} %get-tuple-element.10), kind=kLoop, calls=%fused_computation.130 | loop fusion | flops 1441792 | bytes 3407872 | tf_op jit(solution)/shard_map/concatenate | solution.py:195
  77.7 8.2 %shard_map.130 = f32[2048,2]{1,0:T(8,128)} custom-call(s32[2048,2]{1,0:T(8,128)} %copy.17.rc_ref, bf16[3,128,1024]{2,1,0:T(8,128)(2,1)} %pad_maximum_fusion.4.parts_ref), custom_call_target="tpu_custom_call" | custom-call | tf_op jit(solution)/shard_map/pallas_call | solution.py:203
  85.9 6.8 %scatter_custom_fusion = f32[3,6144]{0,1:T(8,128)S(1)} fusion(s32[2048]{0:T(1024)S(1)} %bitcast.120, f32[]{:T(128)} %constant.134.clone.1, f32[2,2048]{0,1:T(8,128)} %bitcast.101, f32[]{:T(128)} %constant.150.clone.1), kind=kCustom, calls=%fused_computation.29 | custom fusion | bytes 90120 | tf_op jit(solution)/shard_map/scatter | solution.py:266
  92.8 1.5 %copy.18 = f32[3,32,192]{2,0,1:T(4,128)S(1)} copy(f32[3,32,192]{0,2,1:T(8,128)S(1)} %bitcast.100) | data formatting | bytes 147456 | tf_op jit(solution)/shard_map/all_to_all | solution.py:267
  94.2 22.1 %all_to_all.9 = f32[3,32,192]{2,0,1:T(4,128)S(1)} all-to-all(f32[3,32,192]{2,0,1:T(4,128)S(1)} %copy.18), channel_id=1, replica_groups=mesh['gx'=8,'gy'=4] {'gx','gy'}, dimensions={1} | all-to-all | bytes 147456 | tf_op jit(solution)/shard_map/all_to_all | solution.py:267
  (90 shorter events, 17.8 us)
Async XLA Ops:
  1.7 12.9 %copy-start.6 = (f32[8]{0:T(128)S(1)}, f32[8]{0:T(128)}, u32[]{:S(2)}) copy-start(f32[8]{0:T(128)} %param.15) | copy-start | bytes 100
  1.7 13.5 %copy-start.5 = (s32[2048,1]{0,1:T(1,128)S(1)}, s32[2048,1]{0,1:T(1,128)}, u32[]{:S(2)}) copy-start(s32[2048,1]{0,1:T(1,128)} %param.19) | copy-start | bytes 24580
  1.9 14.1 %copy-start.8 = (s32[2048]{0:T(1024)S(1)}, s32[2048]{0:T(1024)}, u32[]{:S(2)}) copy-start(s32[2048]{0:T(1024)} %param.18) | copy-start | bytes 24580
  4.5 23.0 %copy-start = (f32[128,512]{1,0:T(8,128)S(1)}, f32[128,512]{1,0:T(8,128)}, u32[]{:S(2)}) copy-start(f32[128,512]{1,0:T(8,128)} %param.17) | copy-start | bytes 786436
  4.5 23.0 %copy-start.3 = (f32[128,512]{1,0:T(8,128)S(1)}, f32[128,512]{1,0:T(8,128)}, u32[]{:S(2)}) copy-start(f32[128,512]{1,0:T(8,128)} %param.16) | copy-start | bytes 786436
  5.6 17.2 %collective-permute-start.1 = (f32[8,8,2048]{2,1,0:T(8,128)}, f32[8,8,2048]{2,1,0:T(8,128)}, u32[]{:S(2)}, u32[]{:S(2)}) collective-permute-start(f32[8,8,2048]{2,1,0:T(8,128)} %pad_maximum_fusion.7), channel_id=1, source_target_pairs={{1,0},{2,1},{3,2},{4,3},{5,4},{6,5},{7,6},{8,7},{9,8},{10,9},{11,1... | collective-permute-start | bytes 1572872 | tf_op jit(solution)/shard_map/ppermute | solution.py:25
  7.1 36.4 %copy-start.1 = (f32[8,32,2048]{2,1,0:T(8,128)S(1)}, f32[8,32,2048]{2,1,0:T(8,128)}, u32[]{:S(2)}) copy-start(f32[8,32,2048]{2,1,0:T(8,128)} %param.11) | copy-start | bytes 6291460
  8.0 18.2 %collective-permute-start = (f32[8,8,2048]{2,1,0:T(8,128)}, f32[8,8,2048]{2,1,0:T(8,128)}, u32[]{:S(2)}, u32[]{:S(2)}) collective-permute-start(f32[8,8,2048]{2,1,0:T(8,128)} %pad_maximum_fusion.6), channel_id=1, source_target_pairs={{0,1},{1,2},{2,3},{3,4},{4,5},{5,6},{6,7},{7,8},{8,9},{9,10},{10,1... | collective-permute-start | bytes 1572872 | tf_op jit(solution)/shard_map/ppermute | solution.py:25
  27.7 33.0 %collective-permute-start.6 = (f32[2,3,518]{2,1,0:T(4,128)S(1)}, f32[2,3,518]{2,1,0:T(4,128)S(1)}, u32[]{:S(2)}, u32[]{:S(2)}) collective-permute-start(f32[2,3,518]{2,1,0:T(4,128)S(1)} %get-tuple-element.30), channel_id=1, source_target_pairs={{4,0},{8,4},{12,8},{16,12},{20,16},{24,20},{28,24},{5,1},{9,5},{13... | collective-permute-start | bytes 37304 | tf_op jit(solution)/shard_map/ppermute | solution.py:25
  29.0 31.7 %collective-permute-start.5 = (f32[2,3,518]{2,1,0:T(4,128)S(1)}, f32[2,3,518]{2,1,0:T(4,128)S(1)}, u32[]{:S(2)}, u32[]{:S(2)}) collective-permute-start(f32[2,3,518]{2,1,0:T(4,128)S(1)} %get-tuple-element.29), channel_id=1, source_target_pairs={{0,4},{4,8},{8,12},{12,16},{16,20},{20,24},{24,28},{1,5},{5,9},{9,... | collective-permute-start | bytes 37304 | tf_op jit(solution)/shard_map/ppermute | solution.py:25
  43.4 0.7 copy-start.9
  44.1 2.9 %copy-start.2 = (f32[8,32,2048]{2,1,0:T(8,128)S(1)}, f32[8,32,2048]{2,1,0:T(8,128)}, u32[]{:S(2)}) copy-start(f32[8,32,2048]{2,1,0:T(8,128)} %param.12) | copy-start | bytes 6291460
  44.1 2.9 %copy-start.10 = (f32[8]{0:T(128)S(1)}, f32[8]{0:T(128)}, u32[]{:S(2)}) copy-start(f32[8]{0:T(128)} %param.13) | copy-start | bytes 100
  58.6 8.4 %collective-permute-start.4 = (f32[2,36,516]{2,1,0:T(8,128)S(1)}, f32[2,36,516]{2,1,0:T(8,128)S(1)}, u32[]{:S(2)}, u32[]{:S(2)}) collective-permute-start(f32[2,36,516]{2,1,0:T(8,128)S(1)} %get-tuple-element.26), channel_id=1, source_target_pairs={{0,3},{1,0},{2,1},{3,2},{4,7},{5,4},{6,5},{7,6},{8,11},{9,8},{10,9... | collective-permute-start | bytes 445832 | tf_op jit(solution)/shard_map/ppermute | solution.py:142
  58.9 10.5 %collective-permute-start.3 = (f32[2,36,516]{2,1,0:T(8,128)S(1)}, f32[2,36,516]{2,1,0:T(8,128)S(1)}, u32[]{:S(2)}, u32[]{:S(2)}) collective-permute-start(f32[2,36,516]{2,1,0:T(8,128)S(1)} %get-tuple-element.27), channel_id=1, source_target_pairs={{0,2},{1,3},{2,0},{3,1},{4,6},{5,7},{6,4},{7,5},{8,10},{9,11},{10,... | collective-permute-start | bytes 445832 | tf_op jit(solution)/shard_map/ppermute | solution.py:142
  58.9 13.6 %collective-permute-start.2 = (f32[2,36,516]{2,1,0:T(8,128)S(1)}, f32[2,36,516]{2,1,0:T(8,128)S(1)}, u32[]{:S(2)}, u32[]{:S(2)}) collective-permute-start(f32[2,36,516]{2,1,0:T(8,128)S(1)} %get-tuple-element.28), channel_id=1, source_target_pairs={{0,1},{1,2},{2,3},{3,0},{4,5},{5,6},{6,7},{7,4},{8,9},{9,10},{10,1... | collective-permute-start | bytes 445832 | tf_op jit(solution)/shard_map/ppermute | solution.py:142
  92.7 24.4 %copy-start.4 = (f32[2,1,6144]{2,1,0:T(1,128)S(1)}, f32[2,1,6144]{2,1,0:T(1,128)}, u32[]{:S(2)}) copy-start(f32[2,1,6144]{2,1,0:T(1,128)} %param.20) | copy-start | bytes 147460
  92.7 24.4 %copy-start.7 = (f32[1,6144]{1,0:T(1,128)S(1)}, f32[1,6144]{1,0:T(1,128)}, u32[]{:S(2)}) copy-start(f32[1,6144]{1,0:T(1,128)} %param.21) | copy-start | bytes 73732

commit v6 on v5

--- a/solution.py
+++ b/solution.py
@@ -99,20 +99,15 @@
     return slab.transpose(1, 0, 2).reshape(-1)[:size].reshape(shape)
 
 
-def thermal(temp, heat, lateral, vertical, extra, side_last, side_leading):
+def thermal(temp, heat, lateral, vertical, extra):
     devices = lax.axis_size(FLAT)
     t = lax.axis_index(FLAT)
-    layers, rows, cols = temp.shape
+    rows = temp.shape[1]
     h = STEPS + extra
     hh = h - 1
-    last = jnp.concatenate(
-        [temp[:, rows - h:], heat[:, rows - hh:], as_slab(side_last, layers, cols)], axis=1)
-    leading = jnp.concatenate(
-        [temp[:, :h], heat[:, :hh], as_slab(side_leading, layers, cols)], axis=1)
+    last = jnp.concatenate([temp[:, rows - h:], heat[:, rows - hh:]], axis=1)
+    leading = jnp.concatenate([temp[:, :h], heat[:, :hh]], axis=1)
     before, after = exchange(last, leading, FLAT)
-    side_before = from_slab(before[:, h + hh:], side_last.shape)
-    side_after = from_slab(after[:, h + hh:], side_leading.shape)
-    before, after = before[:, : h + hh], after[:, : h + hh]
     ext = jnp.concatenate([before[:, :h], temp, after[:, :h]], axis=1)
     heat_ext = jnp.concatenate([before[:, h:], heat, after[:, h:]], axis=1)
     for step in range(1, STEPS + 1):
@@ -123,11 +118,12 @@
             g = t * rows + jnp.arange(-r, rows + r)
             inside = (g >= 0) & (g < devices * rows)
             ext = jnp.where(inside[None, :, None], ext, 0.0)
-    return ext, side_before, side_after
-
-
-def relay(load, top, width):
+    return ext
+
+
+def relay(load, top, width, side_last, side_leading):
     n_gy = lax.axis_size("gy")
+    gj = lax.axis_index("gy")
     rows, cols = load.shape
     cm = cols // n_gy
     rows = rows - 2 * width
@@ -135,11 +131,32 @@
     tp = jnp.pad(top, ((width, width), (width, width)))
     both = jnp.stack([lp, tp])
     send = jnp.stack([both[:, :, k * cm: k * cm + cm + 2 * width] for k in range(n_gy)])
-    gj = lax.axis_index("gy")
+    depth = send.shape[2]
     got = [lax.dynamic_index_in_dim(send, gj, 0, keepdims=False)]
+    side_before = side_after = None
     for shift in range(1, n_gy):
         piece = lax.dynamic_index_in_dim(send, (gj + shift) % n_gy, 0, keepdims=False)
-        got.append(lax.ppermute(piece, "gy", [(j, (j + shift) % n_gy) for j in range(n_gy)]))
+        extras = []
+        if shift == 1:
+            extras.append(as_slab(side_last, 2, piece.shape[2]))
+        if shift == n_gy - 1:
+            extras.append(as_slab(side_leading, 2, piece.shape[2]))
+        piece = jnp.concatenate([piece] + extras, axis=1)
+        moved = lax.ppermute(piece, "gy", [(j, (j + shift) % n_gy) for j in range(n_gy)])
+        at = depth
+        if shift == 1:
+            slab = as_slab(side_last, 2, piece.shape[2])
+            side_before = from_slab(moved[:, at: at + slab.shape[1]], side_last.shape)
+            at += slab.shape[1]
+        if shift == n_gy - 1:
+            slab = as_slab(side_leading, 2, piece.shape[2])
+            side_after = from_slab(moved[:, at: at + slab.shape[1]], side_leading.shape)
+        got.append(moved[:, :depth])
+    if side_before is None:
+        side_before = jnp.zeros_like(side_last)
+        side_after = jnp.zeros_like(side_leading)
+    side_before = jnp.where(gj > 0, side_before, 0.0)
+    side_after = jnp.where(gj < n_gy - 1, side_after, 0.0)
     recv = jnp.take(jnp.stack(got), (gj - jnp.arange(n_gy)) % n_gy, axis=0)
     parts = []
     for k in range(n_gy):
@@ -150,7 +167,7 @@
     top_m = jnp.concatenate(
         [recv[k, 1, width: rows + width, width: cm + width] for k in range(n_gy)], axis=0
     )
-    return load_m, top_m
+    return load_m, top_m, side_before, side_after
 
 
 def joint_ranks(owners, devices):
@@ -238,13 +255,12 @@
 
     extra = SWEEPS - 1
     g = SWEEPS
-    temp, left, right = thermal(
-        temp_start, heat_input, lateral, vertical, extra, wm[:, :, cm - g:], wm[:, :, :g])
-    left = jnp.where(gj > 0, left, 0.0)
-    right = jnp.where(gj < n_gy - 1, right, 0.0)
-    wm = with_halo(jnp.concatenate([left, wm, right], axis=2), (("gx", 1),), g)
+    wm = with_halo(wm, (("gx", 1),), g)
+    temp = thermal(temp_start, heat_input, lateral, vertical, extra)
     load_t = moment_of(temp, weighting)
-    load, top = relay(load_t, temp[-1, extra: temp.shape[1] - extra], extra)
+    load, top, left, right = relay(
+        load_t, temp[-1, extra: temp.shape[1] - extra], extra, wm[:, :, cm - g:], wm[:, :, :g])
+    wm = jnp.concatenate([left, wm, right], axis=2)
 
     warp = wm[0]
     mod_ext = wm[1]

time: 120 us -> 109 us (0.908)
  waiting for transfers between devices: 18.9 us -> 32.1 us
  blocking collectives: 22.1 us -> 10.1 us
  starting transfers between devices: 23.3 us -> 16.4 us
  local copies, waits for them, and re-layouts: 22.8 us -> 18.9 us
    all_to_all x1, blocking collectives: 22.1 us -> 10.1 us  [body(): lax.all_to_all(outgoing, FLAT, split_axis=1, concat_axis=1, tiled=True)]
    ppermute x4, starting transfers between devices: 21.2 us -> 12.3 us  [exchange(): return (lax.ppermute(last, axis, up), lax.ppermute(leading, axis, down))]
    ppermute x4, waiting for transfers between devices: 7.48 us -> 15.9 us  [exchange(): return (lax.ppermute(last, axis, up), lax.ppermute(leading, axis, down))]
    ppermute x3, waiting for transfers between devices: 11.4 us -> 16.2 us  [relay(): lax.ppermute(piece, 'gy', [(j, (j + shift) % n_gy) for j in range(n_gy)])]
    slice x4, local copies, waits for them, and re-layouts: 4.8 us -> 2.71 us  [the longest x2 2.65 us: thermal(): last = jnp.concatenate([temp[:, rows - h:], heat[:, rows - hh:]], axis=1)]
    ppermute x3, starting transfers between devices: 2.08 us -> 4.11 us  [relay(): lax.ppermute(piece, 'gy', [(j, (j + shift) % n_gy) for j in range(n_gy)])]
  transfers between devices with their start and end apart: 7 -> 7, of which waited for: 5 -> 6; matrix products, arithmetic and copies ran while one was open for 19% -> 4% of each run, Pallas kernels for 0% -> 0%
where the time goes in v6:
time: 109 us
  waiting for transfers between devices  32.1 us (29%)
  other arithmetic  21.3 us (20%)
  local copies, waits for them, and re-layouts  18.9 us (17%)
  starting transfers between devices  16.4 us (15%)
  blocking collectives  10.1 us (9%)
  Pallas kernels  8.21 us (8%)
  between operations  1.26 us (1%)
    ppermute x3, waiting for transfers between devices, relay(): lax.ppermute(piece, 'gy', [(j, (j + shift) % n_gy) for j in range(n_gy)])  16.2 us
    ppermute x4, waiting for transfers between devices, exchange(): return (lax.ppermute(last, axis, up), lax.ppermute(leading, axis, down))  15.9 us
    ppermute x4, starting transfers between devices, exchange(): return (lax.ppermute(last, axis, up), lax.ppermute(leading, axis, down))  12.3 us
    all_to_all x1, blocking collectives, body(): lax.all_to_all(outgoing, FLAT, split_axis=1, concat_axis=1, tiled=True)  10.1 us
    pallas_call x1, Pallas kernels, pick_cells(): pl.pallas_call(pick_kernel, grid=(count // block,), in_specs=[pl.BlockSpe...  8.21 us
    scatter x1, local copies, waits for them, and re-layouts, body(): jnp.zeros((3, devices * capacity), jnp.float32).at[:, slots].set(values)  6.81 us
    add x1, other arithmetic, moment_of(): total = total + weighting[layer] * field[layer]  5.26 us
    ppermute x3, starting transfers between devices, relay(): lax.ppermute(piece, 'gy', [(j, (j + shift) % n_gy) for j in range(n_gy)])  4.11 us
  transfers between devices with their start and end apart: 7, of which 6 were waited for; matrix products, arithmetic and copies ran while one was open for 4% of the time, Pallas kernels for 0%

profile of v6, /device:TPU:0, one launch (start us, length us, event | category | flops | bytes accessed | tf_op | source)
XLA Modules:
  0.0 108.6 jit_solution(18316582416452664319)
XLA Ops:
  0.7 1.3 %fusion.91 = (f32[8,4,2048]{2,1,0:T(4,128)S(1)}, f32[8,4,2048]{2,1,0:T(4,128)S(1)}) fusion(f32[8,32,2048]{2,1,0:T(8,128)} %param.11), kind=kLoop, calls=%fused_computation.229 | loop fusion | bytes 1048576 | tf_op jit(solution)/shard_map/slice | solution.py:108
  2.0 1.3 %fusion.92 = (f32[8,3,2048]{2,1,0:T(4,128)S(1)}, f32[8,3,2048]{2,1,0:T(4,128)S(1)}) fusion(f32[8,32,2048]{2,1,0:T(8,128)} %param.12), kind=kLoop, calls=%fused_computation.230 | loop fusion | bytes 786432 | tf_op jit(solution)/shard_map/slice | solution.py:108
  4.3 5.1 %collective-permute-start = (f32[8,7,2048]{2,1,0:T(8,128)}, f32[8,7,2048]{2,1,0:T(8,128)S(1)}, u32[]{:S(2)}, u32[]{:S(2)}) collective-permute-start(f32[8,7,2048]{2,1,0:T(8,128)} %pad_maximum_fusion.6), channel_id=1, source_target_pairs={{0,1},{1,2},{2,3},{3,4},{4,5},{5,6},{6,7},{7,8},{8,9},{9,10},{10,1... | collective-permute-start | bytes 1376264 | tf_op jit(solution)/shard_map/ppermute | solution.py:25
  10.3 1.3 %collective-permute-start.1 = (f32[8,7,2048]{2,1,0:T(8,128)}, f32[8,7,2048]{2,1,0:T(8,128)}, u32[]{:S(2)}, u32[]{:S(2)}) collective-permute-start(f32[8,7,2048]{2,1,0:T(8,128)} %pad_maximum_fusion.7), channel_id=1, source_target_pairs={{1,0},{2,1},{3,2},{4,3},{5,4},{6,5},{7,6},{8,7},{9,8},{10,9},{11,1... | collective-permute-start | bytes 1376264 | tf_op jit(solution)/shard_map/ppermute | solution.py:25
  11.6 4.6 %collective-permute-start.2 = (f32[2,3,512]{2,1,0:T(4,128)S(1)}, f32[2,3,512]{2,1,0:T(4,128)S(1)}, u32[]{:S(2)}, u32[]{:S(2)}) collective-permute-start(f32[2,3,512]{2,1,0:T(4,128)S(1)} %get-tuple-element.40), channel_id=1, source_target_pairs={{0,4},{4,8},{8,12},{12,16},{16,20},{20,24},{24,28},{1,5},{5,9},{9,... | collective-permute-start | bytes 36872 | tf_op jit(solution)/shard_map/ppermute | solution.py:25
  16.3 1.3 %collective-permute-start.3 = (f32[2,3,512]{2,1,0:T(4,128)S(1)}, f32[2,3,512]{2,1,0:T(4,128)S(1)}, u32[]{:S(2)}, u32[]{:S(2)}) collective-permute-start(f32[2,3,512]{2,1,0:T(4,128)S(1)} %get-tuple-element.41), channel_id=1, source_target_pairs={{4,0},{8,4},{12,8},{16,12},{20,16},{24,20},{28,24},{5,1},{9,5},{13... | collective-permute-start | bytes 36872 | tf_op jit(solution)/shard_map/ppermute | solution.py:25
  19.3 1.9 %collective-permute-done.3 = f32[2,3,512]{2,1,0:T(4,128)S(1)} collective-permute-done((f32[2,3,512]{2,1,0:T(4,128)S(1)}, f32[2,3,512]{2,1,0:T(4,128)S(1)}, u32[]{:S(2)}, u32[]{:S(2)}) %collective-permute-start.3) | collective-permute-done | bytes 12320 | tf_op jit(solution)/shard_map/ppermute | solution.py:25
  22.0 13.7 %collective-permute-done.1 = f32[8,7,2048]{2,1,0:T(8,128)} collective-permute-done((f32[8,7,2048]{2,1,0:T(8,128)}, f32[8,7,2048]{2,1,0:T(8,128)}, u32[]{:S(2)}, u32[]{:S(2)}) %collective-permute-start.1) | collective-permute-done | bytes 458784 | tf_op jit(solution)/shard_map/ppermute | solution.py:25
  35.7 1.1 %slice.430 = f32[8,4,2048]{2,1,0:T(4,128)S(1)} slice(f32[8,7,2048]{2,1,0:T(8,128)} %collective-permute-done.1), slice={[0:8], [0:4], [0:2048]} | slice | bytes 524288 | tf_op jit(solution)/shard_map/slice | solution.py:111
  38.0 1.2 %slice.437 = f32[8,3,2048]{2,1,0:T(4,128)S(1)} slice(f32[8,7,2048]{2,1,0:T(8,128)} %collective-permute-done.1), slice={[0:8], [4:7], [0:2048]} | slice | bytes 393216 | tf_op jit(solution)/shard_map/slice | solution.py:112
  39.3 2.9 %pad_maximum_fusion.1 = (f32[8,38,2048]{2,1,0:T(8,128)S(1)}, f32[8,38,2048]{2,1,0:T(8,128)S(1)}) fusion(f32[8,3,2048]{2,1,0:T(4,128)S(1)} %slice.437, f32[8,32,2048]{2,1,0:T(8,128)S(1)} %copy-done.2, f32[8,3,2048]{2,1,0:T(4,128)S(1)} %slice.436, f32[7,38,2048]{2,1,0:T(8,128)S(1)} %fusion.16, f32[8,40,2048]{2,1,0:T(8,128)S(1)} %pad_maximum_fusion, ...), kind=kLoop, calls=%fused_computation.24 | loop fusion | flops 8093696 | bytes 20382720 | tf_op jit(solution)/shard_map/concatenate | solution.py:112
  42.6 2.6 %fusion.14 = f32[8,36,2048]{2,1,0:T(8,128)S(1)} fusion(f32[8,38,2048]{2,1,0:T(8,128)S(1)} %get-tuple-element.12, f32[8,38,2048]{2,1,0:T(8,128)S(1)} %get-tuple-element.11, f32[7,36,2048]{2,1,0:T(8,128)S(1)} %fusion.15, f32[8]{0:T(128)S(1)} %copy-done.10), kind=kLoop, calls=%fused_computation.20 | loop fusion | flops 5898240 | bytes 17760768 | tf_op jit(solution)/shard_map/add | solution.py:44
  45.3 5.3 %fusion.43 = f32[36,2048]{1,0:T(8,128)S(1)} fusion(f32[8,36,2048]{2,1,0:T(8,128)S(1)} %fusion.14, f32[]{:T(128)} %bitcast.7, f32[]{:T(128)} %bitcast.6, f32[]{:T(128)} %bitcast.5, f32[]{:T(128)} %bitcast.4, f32[]{:T(128)} %bitcast.3, f32[]{:T(128)} %bitcast.2, f32[]{:T(128)} %bitcast.1, f32[]{:T(128)} %bitcast), kind=kLoop, calls=%fused_computation.96 | loop fusion | flops 1105920 | bytes 2654240 | tf_op jit(solution)/shard_map/add | solution.py:50
  51.7 1.4 %copy.17.rc_ref = s32[2048,2]{1,0:T(8,128)} copy(s32[2048,2]{0,1:T(2,128)S(1)} %pad_add_fusion) | data formatting | bytes 32768 | tf_op jit(solution)/shard_map/stack | solution.py:218
  53.3 3.5 %collective-permute-start.6 = (f32[2,37,516]{2,1,0:T(8,128)S(1)}, f32[2,37,516]{2,1,0:T(8,128)S(1)}, u32[]{:S(2)}, u32[]{:S(2)}) collective-permute-start(f32[2,37,516]{2,1,0:T(8,128)S(1)} %pad_maximum_fusion.12), channel_id=1, source_target_pairs={{0,3},{1,0},{2,1},{3,2},{4,7},{5,4},{6,5},{7,6},{8,11},{9,8},{10,9... | collective-permute-start | bytes 458216 | tf_op jit(solution)/shard_map/ppermute | solution.py:145
  56.8 4.0 %collective-permute-done.4 = f32[2,37,516]{2,1,0:T(8,128)S(1)} collective-permute-done((f32[2,37,516]{2,1,0:T(8,128)S(1)}, f32[2,37,516]{2,1,0:T(8,128)S(1)}, u32[]{:S(2)}, u32[]{:S(2)}) %collective-permute-start.4) | collective-permute-done | bytes 152768 | tf_op jit(solution)/shard_map/ppermute | solution.py:145
  60.9 3.4 %collective-permute-done.6 = f32[2,37,516]{2,1,0:T(8,128)S(1)} collective-permute-done((f32[2,37,516]{2,1,0:T(8,128)S(1)}, f32[2,37,516]{2,1,0:T(8,128)S(1)}, u32[]{:S(2)}, u32[]{:S(2)}) %collective-permute-start.6) | collective-permute-done | bytes 152768 | tf_op jit(solution)/shard_map/ppermute | solution.py:145
  64.3 8.7 %collective-permute-done.5 = f32[2,36,516]{2,1,0:T(8,128)S(1)} collective-permute-done((f32[2,36,516]{2,1,0:T(8,128)S(1)}, f32[2,36,516]{2,1,0:T(8,128)S(1)}, u32[]{:S(2)}, u32[]{:S(2)}) %collective-permute-start.5) | collective-permute-done | bytes 148640 | tf_op jit(solution)/shard_map/ppermute | solution.py:145
  76.8 1.4 %subtract_bitcast_fusion = (f32[1,128,512]{2,1,0:T(8,128)S(1)}, f32[128,512]{1,0:T(8,128)}) fusion(f32[128,512]{1,0:T(8,128)S(1)} %copy-done, f32[130,514]{1,0:T(8,128)S(1)} %fusion.24, f32[134,518]{1,0:T(8,128)S(1)} %get-tuple-element.29, f32[132,516]{1,0:T(8,128)S(1)} %get-tuple-element.10), kind=kLoop, calls=%fused_computation.130 | loop fusion | flops 1441792 | bytes 3407872 | tf_op jit(solution)/shard_map/concatenate | solution.py:212
  79.3 8.2 %shard_map.130 = f32[2048,2]{1,0:T(8,128)} custom-call(s32[2048,2]{1,0:T(8,128)} %copy.17.rc_ref, bf16[3,128,1024]{2,1,0:T(8,128)(2,1)} %pad_maximum_fusion.4.parts_ref), custom_call_target="tpu_custom_call" | custom-call | tf_op jit(solution)/shard_map/pallas_call | solution.py:220
  87.5 6.8 %scatter_custom_fusion = f32[3,6144]{0,1:T(8,128)S(1)} fusion(s32[2048]{0:T(1024)S(1)} %bitcast.112, f32[]{:T(128)} %constant.134.clone.1, f32[2,2048]{0,1:T(8,128)} %bitcast.99, f32[]{:T(128)} %constant.150.clone.1), kind=kCustom, calls=%fused_computation.29 | custom fusion | bytes 90120 | tf_op jit(solution)/shard_map/scatter | solution.py:282
  94.4 1.5 %copy.18 = f32[3,32,192]{2,0,1:T(4,128)S(1)} copy(f32[3,32,192]{0,2,1:T(8,128)S(1)} %bitcast.98) | data formatting | bytes 147456 | tf_op jit(solution)/shard_map/all_to_all | solution.py:283
  95.8 10.1 %all_to_all.9 = f32[3,32,192]{2,0,1:T(4,128)S(1)} all-to-all(f32[3,32,192]{2,0,1:T(4,128)S(1)} %copy.18), channel_id=1, replica_groups=mesh['gx'=8,'gy'=4] {'gx','gy'}, dimensions={1} | all-to-all | bytes 147456 | tf_op jit(solution)/shard_map/all_to_all | solution.py:283
  106.7 1.1 add_select_fusion
  (98 shorter events, 13.7 us)
Async XLA Ops:
  0.6 11.0 %copy-start = (f32[128,512]{1,0:T(8,128)S(1)}, f32[128,512]{1,0:T(8,128)}, u32[]{:S(2)}) copy-start(f32[128,512]{1,0:T(8,128)} %param.17) | copy-start | bytes 786436
  0.6 11.0 %copy-start.3 = (f32[128,512]{1,0:T(8,128)S(1)}, f32[128,512]{1,0:T(8,128)}, u32[]{:S(2)}) copy-start(f32[128,512]{1,0:T(8,128)} %param.16) | copy-start | bytes 786436
  0.7 17.0 %copy-start.6 = (f32[8]{0:T(128)S(1)}, f32[8]{0:T(128)}, u32[]{:S(2)}) copy-start(f32[8]{0:T(128)} %param.15) | copy-start | bytes 100
  0.7 17.7 %copy-start.8 = (s32[2048]{0:T(1024)S(1)}, s32[2048]{0:T(1024)}, u32[]{:S(2)}) copy-start(s32[2048]{0:T(1024)} %param.18) | copy-start | bytes 24580
  0.7 17.8 %copy-start.5 = (s32[2048,1]{0,1:T(1,128)S(1)}, s32[2048,1]{0,1:T(1,128)}, u32[]{:S(2)}) copy-start(s32[2048,1]{0,1:T(1,128)} %param.19) | copy-start | bytes 24580
  4.3 32.5 %copy-start.1 = (f32[8,32,2048]{2,1,0:T(8,128)S(1)}, f32[8,32,2048]{2,1,0:T(8,128)}, u32[]{:S(2)}) copy-start(f32[8,32,2048]{2,1,0:T(8,128)} %param.11) | copy-start | bytes 6291460
  4.3 17.7 %collective-permute-start = (f32[8,7,2048]{2,1,0:T(8,128)}, f32[8,7,2048]{2,1,0:T(8,128)S(1)}, u32[]{:S(2)}, u32[]{:S(2)}) collective-permute-start(f32[8,7,2048]{2,1,0:T(8,128)} %pad_maximum_fusion.6), channel_id=1, source_target_pairs={{0,1},{1,2},{2,3},{3,4},{4,5},{5,6},{6,7},{7,8},{8,9},{9,10},{10,1... | collective-permute-start | bytes 1376264 | tf_op jit(solution)/shard_map/ppermute | solution.py:25
  10.3 25.4 %collective-permute-start.1 = (f32[8,7,2048]{2,1,0:T(8,128)}, f32[8,7,2048]{2,1,0:T(8,128)}, u32[]{:S(2)}, u32[]{:S(2)}) collective-permute-start(f32[8,7,2048]{2,1,0:T(8,128)} %pad_maximum_fusion.7), channel_id=1, source_target_pairs={{1,0},{2,1},{3,2},{4,3},{5,4},{6,5},{7,6},{8,7},{9,8},{10,9},{11,1... | collective-permute-start | bytes 1376264 | tf_op jit(solution)/shard_map/ppermute | solution.py:25
  11.6 7.7 %collective-permute-start.2 = (f32[2,3,512]{2,1,0:T(4,128)S(1)}, f32[2,3,512]{2,1,0:T(4,128)S(1)}, u32[]{:S(2)}, u32[]{:S(2)}) collective-permute-start(f32[2,3,512]{2,1,0:T(4,128)S(1)} %get-tuple-element.40), channel_id=1, source_target_pairs={{0,4},{4,8},{8,12},{12,16},{16,20},{20,24},{24,28},{1,5},{5,9},{9,... | collective-permute-start | bytes 36872 | tf_op jit(solution)/shard_map/ppermute | solution.py:25
  16.3 4.9 %collective-permute-start.3 = (f32[2,3,512]{2,1,0:T(4,128)S(1)}, f32[2,3,512]{2,1,0:T(4,128)S(1)}, u32[]{:S(2)}, u32[]{:S(2)}) collective-permute-start(f32[2,3,512]{2,1,0:T(4,128)S(1)} %get-tuple-element.41), channel_id=1, source_target_pairs={{4,0},{8,4},{12,8},{16,12},{20,16},{24,20},{28,24},{5,1},{9,5},{13... | collective-permute-start | bytes 36872 | tf_op jit(solution)/shard_map/ppermute | solution.py:25
  36.8 0.7 copy-start.9
  37.5 1.8 %copy-start.2 = (f32[8,32,2048]{2,1,0:T(8,128)S(1)}, f32[8,32,2048]{2,1,0:T(8,128)}, u32[]{:S(2)}) copy-start(f32[8,32,2048]{2,1,0:T(8,128)} %param.12) | copy-start | bytes 6291460
  37.5 1.8 %copy-start.10 = (f32[8]{0:T(128)S(1)}, f32[8]{0:T(128)}, u32[]{:S(2)}) copy-start(f32[8]{0:T(128)} %param.13) | copy-start | bytes 100
  51.0 9.8 %collective-permute-start.4 = (f32[2,37,516]{2,1,0:T(8,128)S(1)}, f32[2,37,516]{2,1,0:T(8,128)S(1)}, u32[]{:S(2)}, u32[]{:S(2)}) collective-permute-start(f32[2,37,516]{2,1,0:T(8,128)S(1)} %pad_maximum_fusion.11), channel_id=1, source_target_pairs={{0,1},{1,2},{2,3},{3,0},{4,5},{5,6},{6,7},{7,4},{8,9},{9,10},{10,1... | collective-permute-start | bytes 458216 | tf_op jit(solution)/shard_map/ppermute | solution.py:145
  53.3 10.9 %collective-permute-start.6 = (f32[2,37,516]{2,1,0:T(8,128)S(1)}, f32[2,37,516]{2,1,0:T(8,128)S(1)}, u32[]{:S(2)}, u32[]{:S(2)}) collective-permute-start(f32[2,37,516]{2,1,0:T(8,128)S(1)} %pad_maximum_fusion.12), channel_id=1, source_target_pairs={{0,3},{1,0},{2,1},{3,2},{4,7},{5,4},{6,5},{7,6},{8,11},{9,8},{10,9... | collective-permute-start | bytes 458216 | tf_op jit(solution)/shard_map/ppermute | solution.py:145
  56.8 16.2 %collective-permute-start.5 = (f32[2,36,516]{2,1,0:T(8,128)S(1)}, f32[2,36,516]{2,1,0:T(8,128)S(1)}, u32[]{:S(2)}, u32[]{:S(2)}) collective-permute-start(f32[2,36,516]{2,1,0:T(8,128)S(1)} %get-tuple-element.27), channel_id=1, source_target_pairs={{0,2},{1,3},{2,0},{3,1},{4,6},{5,7},{6,4},{7,5},{8,10},{9,11},{10,... | collective-permute-start | bytes 445832 | tf_op jit(solution)/shard_map/ppermute | solution.py:145
  94.3 12.4 %copy-start.4 = (f32[2,1,6144]{2,1,0:T(1,128)S(1)}, f32[2,1,6144]{2,1,0:T(1,128)}, u32[]{:S(2)}) copy-start(f32[2,1,6144]{2,1,0:T(1,128)} %param.20) | copy-start | bytes 147460
  94.4 12.4 %copy-start.7 = (f32[1,6144]{1,0:T(1,128)S(1)}, f32[1,6144]{1,0:T(1,128)}, u32[]{:S(2)}) copy-start(f32[1,6144]{1,0:T(1,128)} %param.21) | copy-start | bytes 73732

commit v7 on v6

--- a/solution.py
+++ b/solution.py
@@ -187,47 +187,43 @@
     return jnp.sum(cum * onehot, axis=1).astype(jnp.int32) - 1
 
 
-def pick_kernel(rc_ref, parts_ref, out_ref):
-    rc = rc_ref[...]
-    rows = rc[:, 0:1]
-    cols = rc[:, 1:2]
-    block = rc.shape[0]
-    _, rm, width = parts_ref.shape
-    fields = out_ref.shape[1]
-    cm = width // fields
-    hit = rows == lax.broadcasted_iota(jnp.int32, (block, rm), 1)
+def pick_kernel(rows_ref, cols_ref, parts_ref, out_ref):
+    rows = rows_ref[...]
+    cols = cols_ref[...]
+    block = rows.shape[1]
+    _, fields, rm, cm = parts_ref.shape
+    hit = lax.broadcasted_iota(jnp.int32, (cm, block), 0) == cols
     onehot = jnp.where(hit, 1.0, 0.0).astype(jnp.bfloat16)
-    acc = jnp.dot(onehot, parts_ref[0], preferred_element_type=jnp.float32)
-    acc = acc + jnp.dot(onehot, parts_ref[1], preferred_element_type=jnp.float32)
-    acc = acc + jnp.dot(onehot, parts_ref[2], preferred_element_type=jnp.float32)
-    lane = cols == lax.broadcasted_iota(jnp.int32, (block, cm), 1)
+    sel = lax.broadcasted_iota(jnp.int32, (rm, block), 0) == rows
     for f in range(fields):
-        seg = acc[:, f * cm: (f + 1) * cm]
-        out_ref[:, f: f + 1] = jnp.sum(jnp.where(lane, seg, 0.0), axis=1, keepdims=True)
+        acc = jnp.dot(parts_ref[0, f], onehot, preferred_element_type=jnp.float32)
+        acc = acc + jnp.dot(parts_ref[1, f], onehot, preferred_element_type=jnp.float32)
+        acc = acc + jnp.dot(parts_ref[2, f], onehot, preferred_element_type=jnp.float32)
+        out_ref[f: f + 1, :] = jnp.sum(jnp.where(sel, acc, 0.0), axis=0, keepdims=True)
 
 
 def pick_cells(fields, cells):
     count = cells.shape[0]
     nf, rm, cm = fields.shape
-    wide = jnp.concatenate(list(fields), axis=1)
-    hi = lax.reduce_precision(wide, exponent_bits=8, mantissa_bits=7)
-    rest = wide - hi
+    hi = lax.reduce_precision(fields, exponent_bits=8, mantissa_bits=7)
+    rest = fields - hi
     mid = lax.reduce_precision(rest, exponent_bits=8, mantissa_bits=7)
     lo = rest - mid
     parts = jnp.stack([hi, mid, lo]).astype(jnp.bfloat16)
-    rc = jnp.stack([cells // cm, cells % cm], axis=1).astype(jnp.int32)
-    block = 256 if count % 256 == 0 else count
-    picked = pl.pallas_call(
+    rows = (cells // cm).astype(jnp.int32)[None, :]
+    cols = (cells % cm).astype(jnp.int32)[None, :]
+    block = 512 if count % 512 == 0 else count
+    return pl.pallas_call(
         pick_kernel,
         grid=(count // block,),
         in_specs=[
-            pl.BlockSpec((block, 2), lambda i: (i, 0)),
-            pl.BlockSpec((3, rm, nf * cm), lambda i: (0, 0, 0)),
+            pl.BlockSpec((1, block), lambda i: (0, i)),
+            pl.BlockSpec((1, block), lambda i: (0, i)),
+            pl.BlockSpec((3, nf, rm, cm), lambda i: (0, 0, 0, 0)),
         ],
-        out_specs=pl.BlockSpec((block, nf), lambda i: (i, 0)),
-        out_shape=jax.ShapeDtypeStruct((count, nf), jnp.float32),
-    )(rc, parts)
-    return picked.T
+        out_specs=pl.BlockSpec((nf, block), lambda i: (0, i)),
+        out_shape=jax.ShapeDtypeStruct((nf, count), jnp.float32),
+    )(rows, cols, parts)
 
 
 def body(

time: 109 us -> 106 us (0.972)
  Pallas kernels: 8.21 us -> 4.37 us
    pallas_call x1, Pallas kernels: 8.21 us -> 4.37 us  [pick_cells(): pl.pallas_call(pick_kernel, grid=(count // block,), in_specs=[pl.BlockSpe...]
    concatenate x0 -> x2, local copies, waits for them, and re-layouts: none -> 2.08 us  [body(): values = jnp.concatenate([picked, jnp.ones_like(picked[:1])], axis=0)]
    concatenate x2 -> x0, other arithmetic: 1.43 us -> none  [pick_cells(): wide = jnp.concatenate(list(fields), axis=1)]
    another operation x2 -> x3, other arithmetic: 0.15 us -> 1.55 us  [the longest x2 1.43 us: body(): picked = pick_cells(jnp.stack([warp - warp_prev, top]), joint_cell)]
    another operation x1 -> x0, local copies, waits for them, and re-layouts: 1.36 us -> none  [pick_cells(): rc = jnp.stack([cells // cm, cells % cm], axis=1).astype(jnp.int32)]
where the time goes in v7:
time: 106 us
  waiting for transfers between devices  31.9 us (30%)
  other arithmetic  21.8 us (21%)
  local copies, waits for them, and re-layouts  19.6 us (18%)
  starting transfers between devices  16.4 us (15%)
  blocking collectives  10.1 us (10%)
  Pallas kernels  4.37 us (4%)
  between operations  1.19 us (1%)
    ppermute x3, waiting for transfers between devices, relay(): lax.ppermute(piece, 'gy', [(j, (j + shift) % n_gy) for j in range(n_gy)])  16.4 us
    ppermute x4, waiting for transfers between devices, exchange(): return (lax.ppermute(last, axis, up), lax.ppermute(leading, axis, down))  15.4 us
    ppermute x4, starting transfers between devices, exchange(): return (lax.ppermute(last, axis, up), lax.ppermute(leading, axis, down))  12.3 us
    all_to_all x1, blocking collectives, body(): lax.all_to_all(outgoing, FLAT, split_axis=1, concat_axis=1, tiled=True)  10.1 us
    scatter x1, local copies, waits for them, and re-layouts, body(): jnp.zeros((3, devices * capacity), jnp.float32).at[:, slots].set(values)  6.73 us
    add x1, other arithmetic, moment_of(): total = total + weighting[layer] * field[layer]  5.27 us
    pallas_call x1, Pallas kernels, pick_cells(): pl.pallas_call(pick_kernel, grid=(count // block,), in_specs=[pl.BlockSpe...  4.37 us
    ppermute x3, starting transfers between devices, relay(): lax.ppermute(piece, 'gy', [(j, (j + shift) % n_gy) for j in range(n_gy)])  4.11 us
  transfers between devices with their start and end apart: 7, of which 6 were waited for; matrix products, arithmetic and copies ran while one was open for 4% of the time, Pallas kernels for 0%

profile of v7, /device:TPU:0, one launch (start us, length us, event | category | flops | bytes accessed | tf_op | source)
XLA Modules:
  0.0 105.7 jit_solution(10624871022339628601)
XLA Ops:
  0.7 1.3 %fusion.89 = (f32[8,4,2048]{2,1,0:T(4,128)S(1)}, f32[8,4,2048]{2,1,0:T(4,128)S(1)}) fusion(f32[8,32,2048]{2,1,0:T(8,128)} %param.11), kind=kLoop, calls=%fused_computation.227 | loop fusion | bytes 1048576 | tf_op jit(solution)/shard_map/slice | solution.py:108
  2.0 1.3 %fusion.90 = (f32[8,3,2048]{2,1,0:T(4,128)S(1)}, f32[8,3,2048]{2,1,0:T(4,128)S(1)}) fusion(f32[8,32,2048]{2,1,0:T(8,128)} %param.12), kind=kLoop, calls=%fused_computation.228 | loop fusion | bytes 786432 | tf_op jit(solution)/shard_map/slice | solution.py:108
  4.3 5.1 %collective-permute-start = (f32[8,7,2048]{2,1,0:T(8,128)}, f32[8,7,2048]{2,1,0:T(8,128)S(1)}, u32[]{:S(2)}, u32[]{:S(2)}) collective-permute-start(f32[8,7,2048]{2,1,0:T(8,128)} %pad_maximum_fusion.6), channel_id=1, source_target_pairs={{0,1},{1,2},{2,3},{3,4},{4,5},{5,6},{6,7},{7,8},{8,9},{9,10},{10,1... | collective-permute-start | bytes 1376264 | tf_op jit(solution)/shard_map/ppermute | solution.py:25
  10.3 1.3 %collective-permute-start.1 = (f32[8,7,2048]{2,1,0:T(8,128)}, f32[8,7,2048]{2,1,0:T(8,128)}, u32[]{:S(2)}, u32[]{:S(2)}) collective-permute-start(f32[8,7,2048]{2,1,0:T(8,128)} %pad_maximum_fusion.7), channel_id=1, source_target_pairs={{1,0},{2,1},{3,2},{4,3},{5,4},{6,5},{7,6},{8,7},{9,8},{10,9},{11,1... | collective-permute-start | bytes 1376264 | tf_op jit(solution)/shard_map/ppermute | solution.py:25
  11.6 4.6 %collective-permute-start.2 = (f32[2,3,512]{2,1,0:T(4,128)S(1)}, f32[2,3,512]{2,1,0:T(4,128)S(1)}, u32[]{:S(2)}, u32[]{:S(2)}) collective-permute-start(f32[2,3,512]{2,1,0:T(4,128)S(1)} %get-tuple-element.40), channel_id=1, source_target_pairs={{0,4},{4,8},{8,12},{12,16},{16,20},{20,24},{24,28},{1,5},{5,9},{9,... | collective-permute-start | bytes 36872 | tf_op jit(solution)/shard_map/ppermute | solution.py:25
  16.3 1.3 %collective-permute-start.3 = (f32[2,3,512]{2,1,0:T(4,128)S(1)}, f32[2,3,512]{2,1,0:T(4,128)S(1)}, u32[]{:S(2)}, u32[]{:S(2)}) collective-permute-start(f32[2,3,512]{2,1,0:T(4,128)S(1)} %get-tuple-element.41), channel_id=1, source_target_pairs={{4,0},{8,4},{12,8},{16,12},{20,16},{24,20},{28,24},{5,1},{9,5},{13... | collective-permute-start | bytes 36872 | tf_op jit(solution)/shard_map/ppermute | solution.py:25
  19.8 1.4 %collective-permute-done.3 = f32[2,3,512]{2,1,0:T(4,128)S(1)} collective-permute-done((f32[2,3,512]{2,1,0:T(4,128)S(1)}, f32[2,3,512]{2,1,0:T(4,128)S(1)}, u32[]{:S(2)}, u32[]{:S(2)}) %collective-permute-start.3) | collective-permute-done | bytes 12320 | tf_op jit(solution)/shard_map/ppermute | solution.py:25
  22.0 13.7 %collective-permute-done.1 = f32[8,7,2048]{2,1,0:T(8,128)} collective-permute-done((f32[8,7,2048]{2,1,0:T(8,128)}, f32[8,7,2048]{2,1,0:T(8,128)}, u32[]{:S(2)}, u32[]{:S(2)}) %collective-permute-start.1) | collective-permute-done | bytes 458784 | tf_op jit(solution)/shard_map/ppermute | solution.py:25
  35.7 1.1 %slice.430 = f32[8,4,2048]{2,1,0:T(4,128)S(1)} slice(f32[8,7,2048]{2,1,0:T(8,128)} %collective-permute-done.1), slice={[0:8], [0:4], [0:2048]} | slice | bytes 524288 | tf_op jit(solution)/shard_map/slice | solution.py:111
  38.0 1.2 %slice.437 = f32[8,3,2048]{2,1,0:T(4,128)S(1)} slice(f32[8,7,2048]{2,1,0:T(8,128)} %collective-permute-done.1), slice={[0:8], [4:7], [0:2048]} | slice | bytes 393216 | tf_op jit(solution)/shard_map/slice | solution.py:112
  39.3 2.9 %pad_maximum_fusion.1 = (f32[8,38,2048]{2,1,0:T(8,128)S(1)}, f32[8,38,2048]{2,1,0:T(8,128)S(1)}) fusion(f32[8,3,2048]{2,1,0:T(4,128)S(1)} %slice.437, f32[8,32,2048]{2,1,0:T(8,128)S(1)} %copy-done.2, f32[8,3,2048]{2,1,0:T(4,128)S(1)} %slice.436, f32[7,38,2048]{2,1,0:T(8,128)S(1)} %fusion.16, f32[8,40,2048]{2,1,0:T(8,128)S(1)} %pad_maximum_fusion, ...), kind=kLoop, calls=%fused_computation.24 | loop fusion | flops 8093696 | bytes 20382720 | tf_op jit(solution)/shard_map/concatenate | solution.py:112
  42.6 2.6 %fusion.14 = f32[8,36,2048]{2,1,0:T(8,128)S(1)} fusion(f32[8,38,2048]{2,1,0:T(8,128)S(1)} %get-tuple-element.12, f32[8,38,2048]{2,1,0:T(8,128)S(1)} %get-tuple-element.11, f32[7,36,2048]{2,1,0:T(8,128)S(1)} %fusion.15, f32[8]{0:T(128)S(1)} %copy-done.10), kind=kLoop, calls=%fused_computation.20 | loop fusion | flops 5898240 | bytes 17760768 | tf_op jit(solution)/shard_map/add | solution.py:44
  45.3 5.3 %fusion.41 = f32[36,2048]{1,0:T(8,128)S(1)} fusion(f32[8,36,2048]{2,1,0:T(8,128)S(1)} %fusion.14, f32[]{:T(128)} %bitcast.7, f32[]{:T(128)} %bitcast.6, f32[]{:T(128)} %bitcast.5, f32[]{:T(128)} %bitcast.4, f32[]{:T(128)} %bitcast.3, f32[]{:T(128)} %bitcast.2, f32[]{:T(128)} %bitcast.1, f32[]{:T(128)} %bitcast), kind=kLoop, calls=%fused_computation.94 | loop fusion | flops 1105920 | bytes 2654240 | tf_op jit(solution)/shard_map/add | solution.py:50
  52.0 3.5 %collective-permute-start.6 = (f32[2,37,516]{2,1,0:T(8,128)S(1)}, f32[2,37,516]{2,1,0:T(8,128)S(1)}, u32[]{:S(2)}, u32[]{:S(2)}) collective-permute-start(f32[2,37,516]{2,1,0:T(8,128)S(1)} %pad_maximum_fusion.12), channel_id=1, source_target_pairs={{0,3},{1,0},{2,1},{3,2},{4,7},{5,4},{6,5},{7,6},{8,11},{9,8},{10,9... | collective-permute-start | bytes 458216 | tf_op jit(solution)/shard_map/ppermute | solution.py:145
  55.5 5.4 %collective-permute-done.4 = f32[2,37,516]{2,1,0:T(8,128)S(1)} collective-permute-done((f32[2,37,516]{2,1,0:T(8,128)S(1)}, f32[2,37,516]{2,1,0:T(8,128)S(1)}, u32[]{:S(2)}, u32[]{:S(2)}) %collective-permute-start.4) | collective-permute-done | bytes 152768 | tf_op jit(solution)/shard_map/ppermute | solution.py:145
  60.9 3.1 %collective-permute-done.6 = f32[2,37,516]{2,1,0:T(8,128)S(1)} collective-permute-done((f32[2,37,516]{2,1,0:T(8,128)S(1)}, f32[2,37,516]{2,1,0:T(8,128)S(1)}, u32[]{:S(2)}, u32[]{:S(2)}) %collective-permute-start.6) | collective-permute-done | bytes 152768 | tf_op jit(solution)/shard_map/ppermute | solution.py:145
  64.0 7.9 %collective-permute-done.5 = f32[2,36,516]{2,1,0:T(8,128)S(1)} collective-permute-done((f32[2,36,516]{2,1,0:T(8,128)S(1)}, f32[2,36,516]{2,1,0:T(8,128)S(1)}, u32[]{:S(2)}, u32[]{:S(2)}) %collective-permute-start.5) | collective-permute-done | bytes 148640 | tf_op jit(solution)/shard_map/ppermute | solution.py:145
  75.7 1.4 %subtract_bitcast_fusion = (f32[1,1,128,512]{3,2,1,0:T(8,128)S(1)}, f32[128,512]{1,0:T(8,128)}) fusion(f32[128,512]{1,0:T(8,128)S(1)} %copy-done, f32[130,514]{1,0:T(8,128)S(1)} %fusion.22, f32[134,518]{1,0:T(8,128)S(1)} %get-tuple-element.29, f32[132,516]{1,0:T(8,128)S(1)} %get-tuple-element.10), kind=kLoop, calls=%fused_computation.128 | loop fusion | flops 1441792 | bytes 3407872 | tf_op jit(solution)/shard_map/stack | solution.py:276
  78.2 4.4 %shard_map.130 = f32[2,2048]{1,0:T(2,128)} custom-call(s32[1,2048]{1,0:T(1,128)} %bitcast.107, s32[1,2048]{1,0:T(1,128)} %bitcast.106, bf16[3,2,128,512]{3,2,1,0:T(8,128)(2,1)} %pad_maximum_fusion.4.parts_ref), custom_call_target="tpu_custom_call" | custom-call | tf_op jit(solution)/shard_map/pallas_call | solution.py:216
  83.3 1.4 %copy.17 = f32[2048,3]{1,0:T(8,128)} copy(f32[2048,3]{0,1:T(4,128)S(1)} %pad_bitcast_fusion.2) | data formatting | bytes 49152 | tf_op jit(solution)/shard_map/concatenate | solution.py:277
  84.7 6.7 %scatter_custom_fusion = f32[3,6144]{0,1:T(8,128)S(1)} fusion(s32[2048]{0:T(1024)S(1)} %bitcast.109, f32[2048,3]{1,0:T(8,128)} %copy.17, f32[]{:T(128)} %constant.134.clone.1), kind=kCustom, calls=%fused_computation.29 | custom fusion | bytes 74240 | tf_op jit(solution)/shard_map/scatter | solution.py:278
  91.4 1.5 %copy.18 = f32[3,32,192]{2,0,1:T(4,128)S(1)} copy(f32[3,32,192]{0,2,1:T(8,128)S(1)} %bitcast.96) | data formatting | bytes 147456 | tf_op jit(solution)/shard_map/all_to_all | solution.py:279
  92.9 10.1 %all_to_all.9 = f32[3,32,192]{2,0,1:T(4,128)S(1)} all-to-all(f32[3,32,192]{2,0,1:T(4,128)S(1)} %copy.18), channel_id=1, replica_groups=mesh['gx'=8,'gy'=4] {'gx','gy'}, dimensions={1} | all-to-all | bytes 147456 | tf_op jit(solution)/shard_map/all_to_all | solution.py:279
  103.8 1.1 %add_select_fusion = (f32[1,6144]{1,0:T(1,128)}, f32[1,6144]{1,0:T(1,128)S(1)}) fusion(pred[1,6144]{1,0:T(4,128)(4,1)S(1)} %gt.46, f32[1,6144]{1,0:T(1,128)S(1)} %copy-done.7, f32[2,1,6144]{2,1,0:T(1,128)S(1)} %copy-done.4, f32[1,6144]{1,0:T(1,128)S(1)} %slice.426, f32[1,6144]{1,0:T(1,128)S(1)} %slice.425), kind=kLoop, calls=%fused_computation.165 | loop fusion | flops 202752 | bytes 178176 | tf_op jit(solution)/shard_map/jit(_where)/select_n | solution.py:85
  (98 shorter events, 15.0 us)
Async XLA Ops:
  0.6 11.0 %copy-start = (f32[128,512]{1,0:T(8,128)S(1)}, f32[128,512]{1,0:T(8,128)}, u32[]{:S(2)}) copy-start(f32[128,512]{1,0:T(8,128)} %param.17) | copy-start | bytes 786436
  0.6 11.0 %copy-start.3 = (f32[128,512]{1,0:T(8,128)S(1)}, f32[128,512]{1,0:T(8,128)}, u32[]{:S(2)}) copy-start(f32[128,512]{1,0:T(8,128)} %param.16) | copy-start | bytes 786436
  0.7 17.0 %copy-start.6 = (f32[8]{0:T(128)S(1)}, f32[8]{0:T(128)}, u32[]{:S(2)}) copy-start(f32[8]{0:T(128)} %param.15) | copy-start | bytes 100
  0.7 17.7 %copy-start.5 = (s32[2048,1]{0,1:T(1,128)S(1)}, s32[2048,1]{0,1:T(1,128)}, u32[]{:S(2)}) copy-start(s32[2048,1]{0,1:T(1,128)} %param.19) | copy-start | bytes 24580
  0.7 18.5 %copy-start.8 = (s32[2048]{0:T(1024)S(1)}, s32[2048]{0:T(1024)}, u32[]{:S(2)}) copy-start(s32[2048]{0:T(1024)} %param.18) | copy-start | bytes 24580
  4.3 32.5 %copy-start.1 = (f32[8,32,2048]{2,1,0:T(8,128)S(1)}, f32[8,32,2048]{2,1,0:T(8,128)}, u32[]{:S(2)}) copy-start(f32[8,32,2048]{2,1,0:T(8,128)} %param.11) | copy-start | bytes 6291460
  4.3 17.7 %collective-permute-start = (f32[8,7,2048]{2,1,0:T(8,128)}, f32[8,7,2048]{2,1,0:T(8,128)S(1)}, u32[]{:S(2)}, u32[]{:S(2)}) collective-permute-start(f32[8,7,2048]{2,1,0:T(8,128)} %pad_maximum_fusion.6), channel_id=1, source_target_pairs={{0,1},{1,2},{2,3},{3,4},{4,5},{5,6},{6,7},{7,8},{8,9},{9,10},{10,1... | collective-permute-start | bytes 1376264 | tf_op jit(solution)/shard_map/ppermute | solution.py:25
  10.3 25.4 %collective-permute-start.1 = (f32[8,7,2048]{2,1,0:T(8,128)}, f32[8,7,2048]{2,1,0:T(8,128)}, u32[]{:S(2)}, u32[]{:S(2)}) collective-permute-start(f32[8,7,2048]{2,1,0:T(8,128)} %pad_maximum_fusion.7), channel_id=1, source_target_pairs={{1,0},{2,1},{3,2},{4,3},{5,4},{6,5},{7,6},{8,7},{9,8},{10,9},{11,1... | collective-permute-start | bytes 1376264 | tf_op jit(solution)/shard_map/ppermute | solution.py:25
  11.6 8.2 %collective-permute-start.2 = (f32[2,3,512]{2,1,0:T(4,128)S(1)}, f32[2,3,512]{2,1,0:T(4,128)S(1)}, u32[]{:S(2)}, u32[]{:S(2)}) collective-permute-start(f32[2,3,512]{2,1,0:T(4,128)S(1)} %get-tuple-element.40), channel_id=1, source_target_pairs={{0,4},{4,8},{8,12},{12,16},{16,20},{20,24},{24,28},{1,5},{5,9},{9,... | collective-permute-start | bytes 36872 | tf_op jit(solution)/shard_map/ppermute | solution.py:25
  16.3 4.9 %collective-permute-start.3 = (f32[2,3,512]{2,1,0:T(4,128)S(1)}, f32[2,3,512]{2,1,0:T(4,128)S(1)}, u32[]{:S(2)}, u32[]{:S(2)}) collective-permute-start(f32[2,3,512]{2,1,0:T(4,128)S(1)} %get-tuple-element.41), channel_id=1, source_target_pairs={{4,0},{8,4},{12,8},{16,12},{20,16},{24,20},{28,24},{5,1},{9,5},{13... | collective-permute-start | bytes 36872 | tf_op jit(solution)/shard_map/ppermute | solution.py:25
  36.8 0.7 copy-start.9
  37.5 1.8 %copy-start.2 = (f32[8,32,2048]{2,1,0:T(8,128)S(1)}, f32[8,32,2048]{2,1,0:T(8,128)}, u32[]{:S(2)}) copy-start(f32[8,32,2048]{2,1,0:T(8,128)} %param.12) | copy-start | bytes 6291460
  37.5 1.8 %copy-start.10 = (f32[8]{0:T(128)S(1)}, f32[8]{0:T(128)}, u32[]{:S(2)}) copy-start(f32[8]{0:T(128)} %param.13) | copy-start | bytes 100
  51.0 9.9 %collective-permute-start.4 = (f32[2,37,516]{2,1,0:T(8,128)S(1)}, f32[2,37,516]{2,1,0:T(8,128)S(1)}, u32[]{:S(2)}, u32[]{:S(2)}) collective-permute-start(f32[2,37,516]{2,1,0:T(8,128)S(1)} %pad_maximum_fusion.11), channel_id=1, source_target_pairs={{0,1},{1,2},{2,3},{3,0},{4,5},{5,6},{6,7},{7,4},{8,9},{9,10},{10,1... | collective-permute-start | bytes 458216 | tf_op jit(solution)/shard_map/ppermute | solution.py:145
  52.0 12.0 %collective-permute-start.6 = (f32[2,37,516]{2,1,0:T(8,128)S(1)}, f32[2,37,516]{2,1,0:T(8,128)S(1)}, u32[]{:S(2)}, u32[]{:S(2)}) collective-permute-start(f32[2,37,516]{2,1,0:T(8,128)S(1)} %pad_maximum_fusion.12), channel_id=1, source_target_pairs={{0,3},{1,0},{2,1},{3,2},{4,7},{5,4},{6,5},{7,6},{8,11},{9,8},{10,9... | collective-permute-start | bytes 458216 | tf_op jit(solution)/shard_map/ppermute | solution.py:145
  55.5 16.5 %collective-permute-start.5 = (f32[2,36,516]{2,1,0:T(8,128)S(1)}, f32[2,36,516]{2,1,0:T(8,128)S(1)}, u32[]{:S(2)}, u32[]{:S(2)}) collective-permute-start(f32[2,36,516]{2,1,0:T(8,128)S(1)} %get-tuple-element.27), channel_id=1, source_target_pairs={{0,2},{1,3},{2,0},{3,1},{4,6},{5,7},{6,4},{7,5},{8,10},{9,11},{10,... | collective-permute-start | bytes 445832 | tf_op jit(solution)/shard_map/ppermute | solution.py:145
  91.4 12.4 %copy-start.4 = (f32[2,1,6144]{2,1,0:T(1,128)S(1)}, f32[2,1,6144]{2,1,0:T(1,128)}, u32[]{:S(2)}) copy-start(f32[2,1,6144]{2,1,0:T(1,128)} %param.20) | copy-start | bytes 147460
  91.4 12.4 %copy-start.7 = (f32[1,6144]{1,0:T(1,128)S(1)}, f32[1,6144]{1,0:T(1,128)}, u32[]{:S(2)}) copy-start(f32[1,6144]{1,0:T(1,128)} %param.21) | copy-start | bytes 73732

commit v8 on v7

--- a/solution.py
+++ b/solution.py
@@ -226,6 +226,38 @@
     )(rows, cols, parts)
 
 
+def place_kernel(owners_ref, ranks_ref, parts_ref, out_ref):
+    owners = owners_ref[...]
+    ranks = ranks_ref[...]
+    _, fields, count = parts_ref.shape
+    devices, cap = out_ref.shape[1:]
+    mine = lax.broadcasted_iota(jnp.int32, (devices, count), 0) == owners
+    slot = lax.broadcasted_iota(jnp.int32, (count, cap), 1) == ranks
+    at = jnp.where(slot, 1.0, 0.0).astype(jnp.bfloat16)
+    for f in range(fields):
+        acc = None
+        for p in range(3):
+            spread = jnp.where(mine, parts_ref[p, f: f + 1, :], 0.0).astype(jnp.bfloat16)
+            term = jnp.dot(spread, at, preferred_element_type=jnp.float32)
+            acc = term if acc is None else acc + term
+        out_ref[f] = acc
+    live = jnp.where(mine, 1.0, 0.0).astype(jnp.bfloat16)
+    out_ref[fields] = jnp.dot(live, at, preferred_element_type=jnp.float32)
+
+
+def place_joints(values, owners, ranks, devices, cap):
+    nf, count = values.shape
+    hi = lax.reduce_precision(values, exponent_bits=8, mantissa_bits=7)
+    rest = values - hi
+    mid = lax.reduce_precision(rest, exponent_bits=8, mantissa_bits=7)
+    lo = rest - mid
+    parts = jnp.stack([hi, mid, lo]).astype(jnp.float32)
+    return pl.pallas_call(
+        place_kernel,
+        out_shape=jax.ShapeDtypeStruct((nf + 1, devices, cap), jnp.float32),
+    )(owners[None, :].astype(jnp.int32), ranks[:, None].astype(jnp.int32), parts)
+
+
 def body(
     temp_start,
     heat_input,
@@ -247,7 +279,7 @@
     wm = jnp.stack([warp_prev, modulus])
     owners = joint_owner[:, 0]
     capacity = joint_resist.shape[1] // devices
-    slots = owners * capacity + joint_ranks(owners, devices)
+    ranks = joint_ranks(owners, devices)
 
     extra = SWEEPS - 1
     g = SWEEPS
@@ -274,9 +306,9 @@
             warp = jnp.where(inside, warp, 0.0)
 
     picked = pick_cells(jnp.stack([warp - warp_prev, top]), joint_cell)
-    values = jnp.concatenate([picked, jnp.ones_like(picked[:1])], axis=0)
-    outgoing = jnp.zeros((3, devices * capacity), jnp.float32).at[:, slots].set(values)
+    outgoing = place_joints(picked, owners, ranks, devices, capacity)
     incoming = lax.all_to_all(outgoing, FLAT, split_axis=1, concat_axis=1, tiled=True)
+    incoming = incoming.reshape(incoming.shape[0], devices * capacity)
     strain_next, resist_next = anand(joint_strain, joint_resist, incoming[:, None, :])
     return (warp, strain_next, resist_next)
 

time: 106 us -> 103 us (0.972)
  local copies, waits for them, and re-layouts: 19.6 us -> 11.6 us
  Pallas kernels: 4.37 us -> 7.74 us
  other arithmetic: 21.8 us -> 23.2 us
    scatter x1 -> x0, local copies, waits for them, and re-layouts: 6.73 us -> none  [body(): jnp.zeros((3, devices * capacity), jnp.float32).at[:, slots].set(values)]
    pallas_call x0 -> x1, Pallas kernels: none -> 3.37 us  [place_joints(): pl.pallas_call(place_kernel, out_shape=jax.ShapeDtypeStruct((nf + 1, devi...]
    concatenate x2 -> x0, local copies, waits for them, and re-layouts: 2.08 us -> none  [body(): values = jnp.concatenate([picked, jnp.ones_like(picked[:1])], axis=0)]
    all_to_all x1 -> x0, local copies, waits for them, and re-layouts: 1.47 us -> none  [body(): lax.all_to_all(outgoing, FLAT, split_axis=1, concat_axis=1, tiled=True)]
    another operation x1 -> x3, other arithmetic: 0.12 us -> 1.49 us  [the longest x2 1.38 us: place_joints(): parts = jnp.stack([hi, mid, lo]).astype(jnp.float32)]
    sub x0 -> x1, local copies, waits for them, and re-layouts: none -> 1.36 us  [joint_ranks(): return jnp.sum(cum * onehot, axis=1).astype(jnp.int32) - 1]
  transfers between devices with their start and end apart: 7 -> 7, of which waited for: 6 -> 6; matrix products, arithmetic and copies ran while one was open for 4% -> 5% of each run, Pallas kernels for 0% -> 0%
where the time goes in v8:
time: 103 us; the launch traced here: 102 us
  waiting for transfers between devices  31.6 us (31%)
  other arithmetic  23.2 us (23%)
  starting transfers between devices  16.3 us (16%)
  local copies, waits for them, and re-layouts  11.6 us (11%)
  blocking collectives  10.1 us (10%)
  Pallas kernels  7.74 us (8%)
  between operations  1.19 us (1%)
    ppermute x3, waiting for transfers between devices, relay(): lax.ppermute(piece, 'gy', [(j, (j + shift) % n_gy) for j in range(n_gy)])  16.2 us
    ppermute x4, waiting for transfers between devices, exchange(): return (lax.ppermute(last, axis, up), lax.ppermute(leading, axis, down))  15.5 us
    ppermute x4, starting transfers between devices, exchange(): return (lax.ppermute(last, axis, up), lax.ppermute(leading, axis, down))  12.2 us
    all_to_all x1, blocking collectives, body(): lax.all_to_all(outgoing, FLAT, split_axis=1, concat_axis=1, tiled=True)  10.1 us
    add x1, other arithmetic, moment_of(): total = total + weighting[layer] * field[layer]  5.25 us
    pallas_call x1, Pallas kernels, pick_cells(): pl.pallas_call(pick_kernel, grid=(count // block,), in_specs=[pl.BlockSpe...  4.37 us
    ppermute x3, starting transfers between devices, relay(): lax.ppermute(piece, 'gy', [(j, (j + shift) % n_gy) for j in range(n_gy)])  4.11 us
    pallas_call x1, Pallas kernels, place_joints(): pl.pallas_call(place_kernel, out_shape=jax.ShapeDtypeStruct((nf + 1, devi...  3.37 us
  transfers between devices with their start and end apart: 7, of which 6 were waited for; matrix products, arithmetic and copies ran while one was open for 5% of the time, Pallas kernels for 0%

profile of v8, /device:TPU:0, one launch (start us, length us, event | category | flops | bytes accessed | tf_op | source)
XLA Modules:
  0.0 102.1 jit_solution(9058047643778008793)
XLA Ops:
  0.7 1.3 %fusion.88 = (f32[8,4,2048]{2,1,0:T(4,128)S(1)}, f32[8,4,2048]{2,1,0:T(4,128)S(1)}) fusion(f32[8,32,2048]{2,1,0:T(8,128)} %param.11), kind=kLoop, calls=%fused_computation.228 | loop fusion | bytes 1048576 | tf_op jit(solution)/shard_map/slice | solution.py:108
  2.0 1.3 %fusion.89 = (f32[8,3,2048]{2,1,0:T(4,128)S(1)}, f32[8,3,2048]{2,1,0:T(4,128)S(1)}) fusion(f32[8,32,2048]{2,1,0:T(8,128)} %param.12), kind=kLoop, calls=%fused_computation.229 | loop fusion | bytes 786432 | tf_op jit(solution)/shard_map/slice | solution.py:108
  4.3 5.0 %collective-permute-start = (f32[8,7,2048]{2,1,0:T(8,128)}, f32[8,7,2048]{2,1,0:T(8,128)S(1)}, u32[]{:S(2)}, u32[]{:S(2)}) collective-permute-start(f32[8,7,2048]{2,1,0:T(8,128)} %pad_maximum_fusion.6), channel_id=1, source_target_pairs={{0,1},{1,2},{2,3},{3,4},{4,5},{5,6},{6,7},{7,8},{8,9},{9,10},{10,1... | collective-permute-start | bytes 1376264 | tf_op jit(solution)/shard_map/ppermute | solution.py:25
  10.2 1.3 %collective-permute-start.1 = (f32[8,7,2048]{2,1,0:T(8,128)}, f32[8,7,2048]{2,1,0:T(8,128)}, u32[]{:S(2)}, u32[]{:S(2)}) collective-permute-start(f32[8,7,2048]{2,1,0:T(8,128)} %pad_maximum_fusion.7), channel_id=1, source_target_pairs={{1,0},{2,1},{3,2},{4,3},{5,4},{6,5},{7,6},{8,7},{9,8},{10,9},{11,1... | collective-permute-start | bytes 1376264 | tf_op jit(solution)/shard_map/ppermute | solution.py:25
  11.5 4.6 %collective-permute-start.2 = (f32[2,3,512]{2,1,0:T(4,128)S(1)}, f32[2,3,512]{2,1,0:T(4,128)S(1)}, u32[]{:S(2)}, u32[]{:S(2)}) collective-permute-start(f32[2,3,512]{2,1,0:T(4,128)S(1)} %get-tuple-element.40), channel_id=1, source_target_pairs={{0,4},{4,8},{8,12},{12,16},{16,20},{20,24},{24,28},{1,5},{5,9},{9,... | collective-permute-start | bytes 36872 | tf_op jit(solution)/shard_map/ppermute | solution.py:25
  16.2 1.3 %collective-permute-start.3 = (f32[2,3,512]{2,1,0:T(4,128)S(1)}, f32[2,3,512]{2,1,0:T(4,128)S(1)}, u32[]{:S(2)}, u32[]{:S(2)}) collective-permute-start(f32[2,3,512]{2,1,0:T(4,128)S(1)} %get-tuple-element.41), channel_id=1, source_target_pairs={{4,0},{8,4},{12,8},{16,12},{20,16},{24,20},{28,24},{5,1},{9,5},{13... | collective-permute-start | bytes 36872 | tf_op jit(solution)/shard_map/ppermute | solution.py:25
  19.7 1.4 %collective-permute-done.3 = f32[2,3,512]{2,1,0:T(4,128)S(1)} collective-permute-done((f32[2,3,512]{2,1,0:T(4,128)S(1)}, f32[2,3,512]{2,1,0:T(4,128)S(1)}, u32[]{:S(2)}, u32[]{:S(2)}) %collective-permute-start.3) | collective-permute-done | bytes 12320 | tf_op jit(solution)/shard_map/ppermute | solution.py:25
  21.9 13.7 %collective-permute-done.1 = f32[8,7,2048]{2,1,0:T(8,128)} collective-permute-done((f32[8,7,2048]{2,1,0:T(8,128)}, f32[8,7,2048]{2,1,0:T(8,128)}, u32[]{:S(2)}, u32[]{:S(2)}) %collective-permute-start.1) | collective-permute-done | bytes 458784 | tf_op jit(solution)/shard_map/ppermute | solution.py:25
  35.6 1.1 %slice.418 = f32[8,4,2048]{2,1,0:T(4,128)S(1)} slice(f32[8,7,2048]{2,1,0:T(8,128)} %collective-permute-done.1), slice={[0:8], [0:4], [0:2048]} | slice | bytes 524288 | tf_op jit(solution)/shard_map/slice | solution.py:111
  37.9 1.2 %slice.425 = f32[8,3,2048]{2,1,0:T(4,128)S(1)} slice(f32[8,7,2048]{2,1,0:T(8,128)} %collective-permute-done.1), slice={[0:8], [4:7], [0:2048]} | slice | bytes 393216 | tf_op jit(solution)/shard_map/slice | solution.py:112
  39.1 2.9 %pad_maximum_fusion.1 = (f32[8,38,2048]{2,1,0:T(8,128)S(1)}, f32[8,38,2048]{2,1,0:T(8,128)S(1)}) fusion(f32[8,3,2048]{2,1,0:T(4,128)S(1)} %slice.425, f32[8,32,2048]{2,1,0:T(8,128)S(1)} %copy-done.2, f32[8,3,2048]{2,1,0:T(4,128)S(1)} %slice.424, f32[7,38,2048]{2,1,0:T(8,128)S(1)} %fusion.16, f32[8,40,2048]{2,1,0:T(8,128)S(1)} %pad_maximum_fusion, ...), kind=kLoop, calls=%fused_computation.23 | loop fusion | flops 8093696 | bytes 20382720 | tf_op jit(solution)/shard_map/concatenate | solution.py:112
  42.5 2.6 %fusion.14 = f32[8,36,2048]{2,1,0:T(8,128)S(1)} fusion(f32[8,38,2048]{2,1,0:T(8,128)S(1)} %get-tuple-element.12, f32[8,38,2048]{2,1,0:T(8,128)S(1)} %get-tuple-element.11, f32[7,36,2048]{2,1,0:T(8,128)S(1)} %fusion.15, f32[8]{0:T(128)S(1)} %copy-done.10), kind=kLoop, calls=%fused_computation.19 | loop fusion | flops 5898240 | bytes 17760768 | tf_op jit(solution)/shard_map/add | solution.py:44
  45.1 5.3 %fusion.39 = f32[36,2048]{1,0:T(8,128)S(1)} fusion(f32[8,36,2048]{2,1,0:T(8,128)S(1)} %fusion.14, f32[]{:T(128)} %bitcast.7, f32[]{:T(128)} %bitcast.6, f32[]{:T(128)} %bitcast.5, f32[]{:T(128)} %bitcast.4, f32[]{:T(128)} %bitcast.3, f32[]{:T(128)} %bitcast.2, f32[]{:T(128)} %bitcast.1, f32[]{:T(128)} %bitcast), kind=kLoop, calls=%fused_computation.91 | loop fusion | flops 1105920 | bytes 2654240 | tf_op jit(solution)/shard_map/add | solution.py:50
  51.5 1.4 %copy.17.ranks_ref = s32[2048,1]{1,0:T(8,128)} copy(s32[2048,1]{0,1:T(1,128)S(1)} %bitcast.111) | data formatting | bytes 16384 | tf_op jit(solution)/shard_map/sub | solution.py:187
  53.2 3.5 %collective-permute-start.6 = (f32[2,37,516]{2,1,0:T(8,128)S(1)}, f32[2,37,516]{2,1,0:T(8,128)S(1)}, u32[]{:S(2)}, u32[]{:S(2)}) collective-permute-start(f32[2,37,516]{2,1,0:T(8,128)S(1)} %pad_maximum_fusion.12), channel_id=1, source_target_pairs={{0,3},{1,0},{2,1},{3,2},{4,7},{5,4},{6,5},{7,6},{8,11},{9,8},{10,9... | collective-permute-start | bytes 458216 | tf_op jit(solution)/shard_map/ppermute | solution.py:145
  56.7 4.0 %collective-permute-done.4 = f32[2,37,516]{2,1,0:T(8,128)S(1)} collective-permute-done((f32[2,37,516]{2,1,0:T(8,128)S(1)}, f32[2,37,516]{2,1,0:T(8,128)S(1)}, u32[]{:S(2)}, u32[]{:S(2)}) %collective-permute-start.4) | collective-permute-done | bytes 152768 | tf_op jit(solution)/shard_map/ppermute | solution.py:145
  60.7 3.4 %collective-permute-done.6 = f32[2,37,516]{2,1,0:T(8,128)S(1)} collective-permute-done((f32[2,37,516]{2,1,0:T(8,128)S(1)}, f32[2,37,516]{2,1,0:T(8,128)S(1)}, u32[]{:S(2)}, u32[]{:S(2)}) %collective-permute-start.6) | collective-permute-done | bytes 152768 | tf_op jit(solution)/shard_map/ppermute | solution.py:145
  64.2 8.7 %collective-permute-done.5 = f32[2,36,516]{2,1,0:T(8,128)S(1)} collective-permute-done((f32[2,36,516]{2,1,0:T(8,128)S(1)}, f32[2,36,516]{2,1,0:T(8,128)S(1)}, u32[]{:S(2)}, u32[]{:S(2)}) %collective-permute-start.5) | collective-permute-done | bytes 148640 | tf_op jit(solution)/shard_map/ppermute | solution.py:145
  76.6 1.4 %subtract_bitcast_fusion = (f32[1,1,128,512]{3,2,1,0:T(8,128)S(1)}, f32[128,512]{1,0:T(8,128)}) fusion(f32[128,512]{1,0:T(8,128)S(1)} %copy-done, f32[130,514]{1,0:T(8,128)S(1)} %fusion.20, f32[134,518]{1,0:T(8,128)S(1)} %get-tuple-element.29, f32[132,516]{1,0:T(8,128)S(1)} %get-tuple-element.10), kind=kLoop, calls=%fused_computation.125 | loop fusion | flops 1441792 | bytes 3407872 | tf_op jit(solution)/shard_map/stack | solution.py:308
  78.2 1.0 pad_maximum_fusion.4.parts_ref
  79.2 4.4 %shard_map.130 = f32[2,2048]{1,0:T(2,128)} custom-call(s32[1,2048]{1,0:T(1,128)} %bitcast.110, s32[1,2048]{1,0:T(1,128)} %bitcast.109, bf16[3,2,128,512]{3,2,1,0:T(8,128)(2,1)} %pad_maximum_fusion.4.parts_ref), custom_call_target="tpu_custom_call" | custom-call | tf_op jit(solution)/shard_map/pallas_call | solution.py:216
  85.0 3.4 %shard_map.131 = f32[3,32,192]{2,1,0:T(8,128)} custom-call(s32[1,2048]{1,0:T(1,128)} %bitcast.106, s32[2048,1]{1,0:T(8,128)} %copy.17.ranks_ref, f32[3,2,2048]{2,1,0:T(2,128)} %pad_maximum_fusion.17.parts_ref), custom_call_target="tpu_custom_call" | custom-call | tf_op jit(solution)/shard_map/pallas_call | solution.py:255
  89.3 10.1 %all_to_all.5 = f32[3,32,192]{2,0,1:T(4,128)S(1)} all-to-all(f32[3,32,192]{2,0,1:T(4,128)S(1)} %copy.18), channel_id=1, replica_groups=mesh['gx'=8,'gy'=4] {'gx','gy'}, dimensions={1} | all-to-all | bytes 147456 | tf_op jit(solution)/shard_map/all_to_all | solution.py:310
  100.2 1.1 %add_select_fusion = (f32[1,6144]{1,0:T(1,128)}, f32[1,6144]{1,0:T(1,128)S(1)}) fusion(pred[1,6144]{1,0:T(4,128)(4,1)S(1)} %gt.47, f32[1,6144]{1,0:T(1,128)S(1)} %copy-done.7, f32[2,1,6144]{2,1,0:T(1,128)S(1)} %copy-done.4, f32[1,6144]{1,0:T(1,128)S(1)} %squeeze.121, f32[1,6144]{1,0:T(1,128)S(1)} %squeeze.119), kind=kLoop, calls=%fused_computation.162 | loop fusion | flops 202752 | bytes 178176 | tf_op jit(solution)/shard_map/jit(_where)/select_n | solution.py:85
  (98 shorter events, 15.6 us)
Async XLA Ops:
  0.6 10.8 %copy-start = (f32[128,512]{1,0:T(8,128)S(1)}, f32[128,512]{1,0:T(8,128)}, u32[]{:S(2)}) copy-start(f32[128,512]{1,0:T(8,128)} %param.17) | copy-start | bytes 786436
  0.6 10.8 %copy-start.3 = (f32[128,512]{1,0:T(8,128)S(1)}, f32[128,512]{1,0:T(8,128)}, u32[]{:S(2)}) copy-start(f32[128,512]{1,0:T(8,128)} %param.16) | copy-start | bytes 786436
  0.7 16.9 %copy-start.6 = (f32[8]{0:T(128)S(1)}, f32[8]{0:T(128)}, u32[]{:S(2)}) copy-start(f32[8]{0:T(128)} %param.15) | copy-start | bytes 100
  0.7 17.6 %copy-start.5 = (s32[2048,1]{0,1:T(1,128)S(1)}, s32[2048,1]{0,1:T(1,128)}, u32[]{:S(2)}) copy-start(s32[2048,1]{0,1:T(1,128)} %param.19) | copy-start | bytes 24580
  0.7 18.4 %copy-start.8 = (s32[2048]{0:T(1024)S(1)}, s32[2048]{0:T(1024)}, u32[]{:S(2)}) copy-start(s32[2048]{0:T(1024)} %param.18) | copy-start | bytes 24580
  3.3 33.3 %copy-start.1 = (f32[8,32,2048]{2,1,0:T(8,128)S(1)}, f32[8,32,2048]{2,1,0:T(8,128)}, u32[]{:S(2)}) copy-start(f32[8,32,2048]{2,1,0:T(8,128)} %param.11) | copy-start | bytes 6291460
  4.3 17.6 %collective-permute-start = (f32[8,7,2048]{2,1,0:T(8,128)}, f32[8,7,2048]{2,1,0:T(8,128)S(1)}, u32[]{:S(2)}, u32[]{:S(2)}) collective-permute-start(f32[8,7,2048]{2,1,0:T(8,128)} %pad_maximum_fusion.6), channel_id=1, source_target_pairs={{0,1},{1,2},{2,3},{3,4},{4,5},{5,6},{6,7},{7,8},{8,9},{9,10},{10,1... | collective-permute-start | bytes 1376264 | tf_op jit(solution)/shard_map/ppermute | solution.py:25
  10.2 25.4 %collective-permute-start.1 = (f32[8,7,2048]{2,1,0:T(8,128)}, f32[8,7,2048]{2,1,0:T(8,128)}, u32[]{:S(2)}, u32[]{:S(2)}) collective-permute-start(f32[8,7,2048]{2,1,0:T(8,128)} %pad_maximum_fusion.7), channel_id=1, source_target_pairs={{1,0},{2,1},{3,2},{4,3},{5,4},{6,5},{7,6},{8,7},{9,8},{10,9},{11,1... | collective-permute-start | bytes 1376264 | tf_op jit(solution)/shard_map/ppermute | solution.py:25
  11.5 8.2 %collective-permute-start.2 = (f32[2,3,512]{2,1,0:T(4,128)S(1)}, f32[2,3,512]{2,1,0:T(4,128)S(1)}, u32[]{:S(2)}, u32[]{:S(2)}) collective-permute-start(f32[2,3,512]{2,1,0:T(4,128)S(1)} %get-tuple-element.40), channel_id=1, source_target_pairs={{0,4},{4,8},{8,12},{12,16},{16,20},{20,24},{24,28},{1,5},{5,9},{9,... | collective-permute-start | bytes 36872 | tf_op jit(solution)/shard_map/ppermute | solution.py:25
  16.2 4.9 %collective-permute-start.3 = (f32[2,3,512]{2,1,0:T(4,128)S(1)}, f32[2,3,512]{2,1,0:T(4,128)S(1)}, u32[]{:S(2)}, u32[]{:S(2)}) collective-permute-start(f32[2,3,512]{2,1,0:T(4,128)S(1)} %get-tuple-element.41), channel_id=1, source_target_pairs={{4,0},{8,4},{12,8},{16,12},{20,16},{24,20},{28,24},{5,1},{9,5},{13... | collective-permute-start | bytes 36872 | tf_op jit(solution)/shard_map/ppermute | solution.py:25
  36.7 0.7 copy-start.9
  37.3 1.8 %copy-start.2 = (f32[8,32,2048]{2,1,0:T(8,128)S(1)}, f32[8,32,2048]{2,1,0:T(8,128)}, u32[]{:S(2)}) copy-start(f32[8,32,2048]{2,1,0:T(8,128)} %param.12) | copy-start | bytes 6291460
  37.3 1.8 %copy-start.10 = (f32[8]{0:T(128)S(1)}, f32[8]{0:T(128)}, u32[]{:S(2)}) copy-start(f32[8]{0:T(128)} %param.13) | copy-start | bytes 100
  50.9 9.8 %collective-permute-start.4 = (f32[2,37,516]{2,1,0:T(8,128)S(1)}, f32[2,37,516]{2,1,0:T(8,128)S(1)}, u32[]{:S(2)}, u32[]{:S(2)}) collective-permute-start(f32[2,37,516]{2,1,0:T(8,128)S(1)} %pad_maximum_fusion.11), channel_id=1, source_target_pairs={{0,1},{1,2},{2,3},{3,0},{4,5},{5,6},{6,7},{7,4},{8,9},{9,10},{10,1... | collective-permute-start | bytes 458216 | tf_op jit(solution)/shard_map/ppermute | solution.py:145
  53.2 10.9 %collective-permute-start.6 = (f32[2,37,516]{2,1,0:T(8,128)S(1)}, f32[2,37,516]{2,1,0:T(8,128)S(1)}, u32[]{:S(2)}, u32[]{:S(2)}) collective-permute-start(f32[2,37,516]{2,1,0:T(8,128)S(1)} %pad_maximum_fusion.12), channel_id=1, source_target_pairs={{0,3},{1,0},{2,1},{3,2},{4,7},{5,4},{6,5},{7,6},{8,11},{9,8},{10,9... | collective-permute-start | bytes 458216 | tf_op jit(solution)/shard_map/ppermute | solution.py:145
  56.7 16.2 %collective-permute-start.5 = (f32[2,36,516]{2,1,0:T(8,128)S(1)}, f32[2,36,516]{2,1,0:T(8,128)S(1)}, u32[]{:S(2)}, u32[]{:S(2)}) collective-permute-start(f32[2,36,516]{2,1,0:T(8,128)S(1)} %get-tuple-element.27), channel_id=1, source_target_pairs={{0,2},{1,3},{2,0},{3,1},{4,6},{5,7},{6,4},{7,5},{8,10},{9,11},{10,... | collective-permute-start | bytes 445832 | tf_op jit(solution)/shard_map/ppermute | solution.py:145
  78.2 22.0 %copy-start.4 = (f32[2,1,6144]{2,1,0:T(1,128)S(1)}, f32[2,1,6144]{2,1,0:T(1,128)}, u32[]{:S(2)}) copy-start(f32[2,1,6144]{2,1,0:T(1,128)} %param.20) | copy-start | bytes 147460
  78.2 22.0 %copy-start.7 = (f32[1,6144]{1,0:T(1,128)S(1)}, f32[1,6144]{1,0:T(1,128)}, u32[]{:S(2)}) copy-start(f32[1,6144]{1,0:T(1,128)} %param.21) | copy-start | bytes 73732

commit v9 on v8

--- a/solution.py
+++ b/solution.py
@@ -107,7 +107,11 @@
     hh = h - 1
     last = jnp.concatenate([temp[:, rows - h:], heat[:, rows - hh:]], axis=1)
     leading = jnp.concatenate([temp[:, :h], heat[:, :hh]], axis=1)
-    before, after = exchange(last, leading, FLAT)
+    half = last.shape[0] // 2
+    lo_b, lo_a = exchange(last[:half], leading[:half], FLAT)
+    hi_b, hi_a = exchange(last[half:], leading[half:], FLAT)
+    before = jnp.concatenate([lo_b, hi_b], axis=0)
+    after = jnp.concatenate([lo_a, hi_a], axis=0)
     ext = jnp.concatenate([before[:, :h], temp, after[:, :h]], axis=1)
     heat_ext = jnp.concatenate([before[:, h:], heat, after[:, h:]], axis=1)
     for step in range(1, STEPS + 1):

time: 103 us -> 105 us (1.019)
  waiting for transfers between devices: 31.6 us -> 25.8 us
  starting transfers between devices: 16.3 us -> 20.6 us
  blocking collectives: 10.1 us -> 12.7 us
    ppermute x4 -> x6, waiting for transfers between devices: 15.5 us -> 8.9 us  [exchange(): return (lax.ppermute(last, axis, up), lax.ppermute(leading, axis, down))]
    ppermute x4 -> x6, starting transfers between devices: 12.2 us -> 16.5 us  [exchange(): return (lax.ppermute(last, axis, up), lax.ppermute(leading, axis, down))]
    all_to_all x1, blocking collectives: 10.1 us -> 12.7 us  [body(): lax.all_to_all(outgoing, FLAT, split_axis=1, concat_axis=1, tiled=True)]
    unnamed x22 -> x24, local copies, waits for them, and re-layouts: 0.26 us -> 2.42 us
    slice x2, local copies, waits for them, and re-layouts: 1.29 us -> 0.14 us  [thermal(): heat_ext = jnp.concatenate([before[:, h:], heat, after[:, h:]], axis=1)]
  transfers between devices with their start and end apart: 7 -> 9, of which waited for: 6 -> 6; matrix products, arithmetic and copies ran while one was open for 5% -> 6% of each run, Pallas kernels for 0% -> 0%
where the time goes in v9:
time: 105 us; the launch traced here: 104 us
  waiting for transfers between devices  25.8 us (25%)
  other arithmetic  23 us (22%)
  starting transfers between devices  20.6 us (20%)
  blocking collectives  12.7 us (12%)
  local copies, waits for them, and re-layouts  12.6 us (12%)
  Pallas kernels  7.74 us (7%)
  between operations  1.28 us (1%)
    ppermute x3, waiting for transfers between devices, relay(): lax.ppermute(piece, 'gy', [(j, (j + shift) % n_gy) for j in range(n_gy)])  16.9 us
    ppermute x6, starting transfers between devices, exchange(): return (lax.ppermute(last, axis, up), lax.ppermute(leading, axis, down))  16.5 us
    all_to_all x1, blocking collectives, body(): lax.all_to_all(outgoing, FLAT, split_axis=1, concat_axis=1, tiled=True)  12.7 us
    ppermute x6, waiting for transfers between devices, exchange(): return (lax.ppermute(last, axis, up), lax.ppermute(leading, axis, down))  8.9 us
    add x1, other arithmetic, moment_of(): total = total + weighting[layer] * field[layer]  5.24 us
    pallas_call x1, Pallas kernels, pick_cells(): pl.pallas_call(pick_kernel, grid=(count // block,), in_specs=[pl.BlockSpe...  4.37 us
    ppermute x3, starting transfers between devices, relay(): lax.ppermute(piece, 'gy', [(j, (j + shift) % n_gy) for j in range(n_gy)])  4.11 us
    pallas_call x1, Pallas kernels, place_joints(): pl.pallas_call(place_kernel, out_shape=jax.ShapeDtypeStruct((nf + 1, devi...  3.37 us
  transfers between devices with their start and end apart: 9, of which 6 were waited for; matrix products, arithmetic and copies ran while one was open for 6% of the time, Pallas kernels for 0%

profile of v9, /device:TPU:0, one launch (start us, length us, event | category | flops | bytes accessed | tf_op | source)
XLA Modules:
  0.0 104.0 jit_solution(7275012328462605300)
XLA Ops:
  0.7 1.3 %fusion.90 = (f32[8,3,2048]{2,1,0:T(4,128)S(1)}, f32[8,3,2048]{2,1,0:T(4,128)S(1)}) fusion(f32[8,32,2048]{2,1,0:T(8,128)} %param.12), kind=kLoop, calls=%fused_computation.238 | loop fusion | bytes 786432 | tf_op jit(solution)/shard_map/slice | solution.py:108
  2.0 1.3 %fusion.91 = (f32[8,4,2048]{2,1,0:T(4,128)S(1)}, f32[8,4,2048]{2,1,0:T(4,128)S(1)}) fusion(f32[8,32,2048]{2,1,0:T(8,128)} %param.11), kind=kLoop, calls=%fused_computation.239 | loop fusion | bytes 1048576 | tf_op jit(solution)/shard_map/slice | solution.py:108
  4.2 5.0 %collective-permute-start = (f32[4,7,2048]{2,1,0:T(8,128)}, f32[4,7,2048]{2,1,0:T(8,128)S(1)}, u32[]{:S(2)}, u32[]{:S(2)}) collective-permute-start(f32[4,7,2048]{2,1,0:T(8,128)} %get-tuple-element.41), channel_id=1, source_target_pairs={{0,1},{1,2},{2,3},{3,4},{4,5},{5,6},{6,7},{7,8},{8,9},{9,10},{10,1... | collective-permute-start | bytes 688136 | tf_op jit(solution)/shard_map/ppermute | solution.py:25
  9.2 3.5 %collective-permute-start.1 = (f32[4,7,2048]{2,1,0:T(8,128)}, f32[4,7,2048]{2,1,0:T(8,128)S(1)}, u32[]{:S(2)}, u32[]{:S(2)}) collective-permute-start(f32[4,7,2048]{2,1,0:T(8,128)} %get-tuple-element.40), channel_id=1, source_target_pairs={{0,1},{1,2},{2,3},{3,4},{4,5},{5,6},{6,7},{7,8},{8,9},{9,10},{10,1... | collective-permute-start | bytes 688136 | tf_op jit(solution)/shard_map/ppermute | solution.py:25
  13.6 1.3 %collective-permute-start.2 = (f32[4,7,2048]{2,1,0:T(8,128)}, f32[4,7,2048]{2,1,0:T(8,128)}, u32[]{:S(2)}, u32[]{:S(2)}) collective-permute-start(f32[4,7,2048]{2,1,0:T(8,128)} %get-tuple-element.43), channel_id=1, source_target_pairs={{1,0},{2,1},{3,2},{4,3},{5,4},{6,5},{7,6},{8,7},{9,8},{10,9},{11,1... | collective-permute-start | bytes 688136 | tf_op jit(solution)/shard_map/ppermute | solution.py:25
  14.9 4.0 %collective-permute-start.4 = (f32[2,3,512]{2,1,0:T(4,128)S(1)}, f32[2,3,512]{2,1,0:T(4,128)S(1)}, u32[]{:S(2)}, u32[]{:S(2)}) collective-permute-start(f32[2,3,512]{2,1,0:T(4,128)S(1)} %get-tuple-element.44), channel_id=1, source_target_pairs={{0,4},{4,8},{8,12},{12,16},{16,20},{20,24},{24,28},{1,5},{5,9},{9,... | collective-permute-start | bytes 36872 | tf_op jit(solution)/shard_map/ppermute | solution.py:25
  19.0 1.3 %collective-permute-start.5 = (f32[2,3,512]{2,1,0:T(4,128)S(1)}, f32[2,3,512]{2,1,0:T(4,128)S(1)}, u32[]{:S(2)}, u32[]{:S(2)}) collective-permute-start(f32[2,3,512]{2,1,0:T(4,128)S(1)} %get-tuple-element.45), channel_id=1, source_target_pairs={{4,0},{8,4},{12,8},{16,12},{20,16},{24,20},{28,24},{5,1},{9,5},{13... | collective-permute-start | bytes 36872 | tf_op jit(solution)/shard_map/ppermute | solution.py:25
  22.5 1.4 %collective-permute-start.3 = (f32[4,7,2048]{2,1,0:T(8,128)}, f32[4,7,2048]{2,1,0:T(8,128)}, u32[]{:S(2)}, u32[]{:S(2)}) collective-permute-start(f32[4,7,2048]{2,1,0:T(8,128)} %get-tuple-element.42), channel_id=1, source_target_pairs={{1,0},{2,1},{3,2},{4,3},{5,4},{6,5},{7,6},{8,7},{9,8},{10,9},{11,1... | collective-permute-start | bytes 688136 | tf_op jit(solution)/shard_map/ppermute | solution.py:25
  25.1 4.8 %collective-permute-done.2 = f32[4,7,2048]{2,1,0:T(8,128)} collective-permute-done((f32[4,7,2048]{2,1,0:T(8,128)}, f32[4,7,2048]{2,1,0:T(8,128)}, u32[]{:S(2)}, u32[]{:S(2)}) %collective-permute-start.2) | collective-permute-done | bytes 229408 | tf_op jit(solution)/shard_map/ppermute | solution.py:25
  30.9 3.5 %collective-permute-done.3 = f32[4,7,2048]{2,1,0:T(8,128)} collective-permute-done((f32[4,7,2048]{2,1,0:T(8,128)}, f32[4,7,2048]{2,1,0:T(8,128)}, u32[]{:S(2)}, u32[]{:S(2)}) %collective-permute-start.3) | collective-permute-done | bytes 229408 | tf_op jit(solution)/shard_map/ppermute | solution.py:25
  36.7 1.1 %copy-done.2 = f32[8,32,2048]{2,1,0:T(8,128)S(1)} copy-done((f32[8,32,2048]{2,1,0:T(8,128)S(1)}, f32[8,32,2048]{2,1,0:T(8,128)}, u32[]{:S(2)}) %copy-start.2) | copy-done | bytes 2097176
  37.8 2.8 %pad_maximum_fusion.1 = (f32[8,38,2048]{2,1,0:T(8,128)S(1)}, f32[8,38,2048]{2,1,0:T(8,128)S(1)}) fusion(f32[8,3,2048]{2,1,0:T(4,128)S(1)} %slice.445, f32[8,32,2048]{2,1,0:T(8,128)S(1)} %copy-done.2, f32[8,3,2048]{2,1,0:T(4,128)S(1)} %slice.444, f32[7,38,2048]{2,1,0:T(8,128)S(1)} %fusion.16, f32[8,40,2048]{2,1,0:T(8,128)S(1)} %pad_maximum_fusion, ...), kind=kLoop, calls=%fused_computation.23 | loop fusion | flops 8093696 | bytes 20382720 | tf_op jit(solution)/shard_map/concatenate | solution.py:116
  41.1 2.6 %fusion.14 = f32[8,36,2048]{2,1,0:T(8,128)S(1)} fusion(f32[8,38,2048]{2,1,0:T(8,128)S(1)} %get-tuple-element.12, f32[8,38,2048]{2,1,0:T(8,128)S(1)} %get-tuple-element.11, f32[7,36,2048]{2,1,0:T(8,128)S(1)} %fusion.15, f32[8]{0:T(128)S(1)} %copy-done.10), kind=kLoop, calls=%fused_computation.19 | loop fusion | flops 5898240 | bytes 17760768 | tf_op jit(solution)/shard_map/add | solution.py:44
  43.7 5.2 %fusion.39 = f32[36,2048]{1,0:T(8,128)S(1)} fusion(f32[8,36,2048]{2,1,0:T(8,128)S(1)} %fusion.14, f32[]{:T(128)} %bitcast.7, f32[]{:T(128)} %bitcast.6, f32[]{:T(128)} %bitcast.5, f32[]{:T(128)} %bitcast.4, f32[]{:T(128)} %bitcast.3, f32[]{:T(128)} %bitcast.2, f32[]{:T(128)} %bitcast.1, f32[]{:T(128)} %bitcast), kind=kLoop, calls=%fused_computation.93 | loop fusion | flops 1105920 | bytes 2654240 | tf_op jit(solution)/shard_map/add | solution.py:50
  49.5 1.7 %collective-permute-start.6 = (f32[2,37,516]{2,1,0:T(8,128)S(1)}, f32[2,37,516]{2,1,0:T(8,128)S(1)}, u32[]{:S(2)}, u32[]{:S(2)}) collective-permute-start(f32[2,37,516]{2,1,0:T(8,128)S(1)} %pad_maximum_fusion.11), channel_id=1, source_target_pairs={{0,1},{1,2},{2,3},{3,0},{4,5},{5,6},{6,7},{7,4},{8,9},{9,10},{10,1... | collective-permute-start | bytes 458216 | tf_op jit(solution)/shard_map/ppermute | solution.py:149
  51.2 1.4 %copy.17.ranks_ref = s32[2048,1]{1,0:T(8,128)} copy(s32[2048,1]{0,1:T(1,128)S(1)} %bitcast.111) | data formatting | bytes 16384 | tf_op jit(solution)/shard_map/sub | solution.py:191
  52.9 2.4 %collective-permute-start.8 = (f32[2,37,516]{2,1,0:T(8,128)S(1)}, f32[2,37,516]{2,1,0:T(8,128)S(1)}, u32[]{:S(2)}, u32[]{:S(2)}) collective-permute-start(f32[2,37,516]{2,1,0:T(8,128)S(1)} %pad_maximum_fusion.12), channel_id=1, source_target_pairs={{0,3},{1,0},{2,1},{3,2},{4,7},{5,4},{6,5},{7,6},{8,11},{9,8},{10,9... | collective-permute-start | bytes 458216 | tf_op jit(solution)/shard_map/ppermute | solution.py:149
  55.3 2.8 %collective-permute-done.6 = f32[2,37,516]{2,1,0:T(8,128)S(1)} collective-permute-done((f32[2,37,516]{2,1,0:T(8,128)S(1)}, f32[2,37,516]{2,1,0:T(8,128)S(1)}, u32[]{:S(2)}, u32[]{:S(2)}) %collective-permute-start.6) | collective-permute-done | bytes 152768 | tf_op jit(solution)/shard_map/ppermute | solution.py:149
  58.1 5.6 %collective-permute-done.8 = f32[2,37,516]{2,1,0:T(8,128)S(1)} collective-permute-done((f32[2,37,516]{2,1,0:T(8,128)S(1)}, f32[2,37,516]{2,1,0:T(8,128)S(1)}, u32[]{:S(2)}, u32[]{:S(2)}) %collective-permute-start.8) | collective-permute-done | bytes 152768 | tf_op jit(solution)/shard_map/ppermute | solution.py:149
  63.7 8.5 %collective-permute-done.7 = f32[2,36,516]{2,1,0:T(8,128)S(1)} collective-permute-done((f32[2,36,516]{2,1,0:T(8,128)S(1)}, f32[2,36,516]{2,1,0:T(8,128)S(1)}, u32[]{:S(2)}, u32[]{:S(2)}) %collective-permute-start.7) | collective-permute-done | bytes 148640 | tf_op jit(solution)/shard_map/ppermute | solution.py:149
  75.9 1.4 %subtract_bitcast_fusion = (f32[1,1,128,512]{3,2,1,0:T(8,128)S(1)}, f32[128,512]{1,0:T(8,128)}) fusion(f32[128,512]{1,0:T(8,128)S(1)} %copy-done, f32[130,514]{1,0:T(8,128)S(1)} %fusion.20, f32[134,518]{1,0:T(8,128)S(1)} %get-tuple-element.29, f32[132,516]{1,0:T(8,128)S(1)} %get-tuple-element.10), kind=kLoop, calls=%fused_computation.131 | loop fusion | flops 1441792 | bytes 3407872 | tf_op jit(solution)/shard_map/stack | solution.py:312
  78.5 4.4 %shard_map.130 = f32[2,2048]{1,0:T(2,128)} custom-call(s32[1,2048]{1,0:T(1,128)} %bitcast.110, s32[1,2048]{1,0:T(1,128)} %bitcast.109, bf16[3,2,128,512]{3,2,1,0:T(8,128)(2,1)} %pad_maximum_fusion.4.parts_ref), custom_call_target="tpu_custom_call" | custom-call | tf_op jit(solution)/shard_map/pallas_call | solution.py:220
  84.3 3.4 %shard_map.131 = f32[3,32,192]{2,1,0:T(8,128)} custom-call(s32[1,2048]{1,0:T(1,128)} %bitcast.106, s32[2048,1]{1,0:T(8,128)} %copy.17.ranks_ref, f32[3,2,2048]{2,1,0:T(2,128)} %pad_maximum_fusion.17.parts_ref), custom_call_target="tpu_custom_call" | custom-call | tf_op jit(solution)/shard_map/pallas_call | solution.py:259
  88.6 12.7 %all_to_all.5 = f32[3,32,192]{2,0,1:T(4,128)S(1)} all-to-all(f32[3,32,192]{2,0,1:T(4,128)S(1)} %copy.18), channel_id=1, replica_groups=mesh['gx'=8,'gy'=4] {'gx','gy'}, dimensions={1} | all-to-all | bytes 147456 | tf_op jit(solution)/shard_map/all_to_all | solution.py:314
  (106 shorter events, 19.2 us)
Async XLA Ops:
  0.6 14.3 %copy-start = (f32[128,512]{1,0:T(8,128)S(1)}, f32[128,512]{1,0:T(8,128)}, u32[]{:S(2)}) copy-start(f32[128,512]{1,0:T(8,128)} %param.17) | copy-start | bytes 786436
  0.6 14.3 %copy-start.3 = (f32[128,512]{1,0:T(8,128)S(1)}, f32[128,512]{1,0:T(8,128)}, u32[]{:S(2)}) copy-start(f32[128,512]{1,0:T(8,128)} %param.16) | copy-start | bytes 786436
  0.7 19.7 %copy-start.6 = (f32[8]{0:T(128)S(1)}, f32[8]{0:T(128)}, u32[]{:S(2)}) copy-start(f32[8]{0:T(128)} %param.15) | copy-start | bytes 100
  0.7 20.4 %copy-start.8 = (s32[2048]{0:T(1024)S(1)}, s32[2048]{0:T(1024)}, u32[]{:S(2)}) copy-start(s32[2048]{0:T(1024)} %param.18) | copy-start | bytes 24580
  0.7 21.0 %copy-start.5 = (s32[2048,1]{0,1:T(1,128)S(1)}, s32[2048,1]{0,1:T(1,128)}, u32[]{:S(2)}) copy-start(s32[2048,1]{0,1:T(1,128)} %param.19) | copy-start | bytes 24580
  4.2 20.7 %collective-permute-start = (f32[4,7,2048]{2,1,0:T(8,128)}, f32[4,7,2048]{2,1,0:T(8,128)S(1)}, u32[]{:S(2)}, u32[]{:S(2)}) collective-permute-start(f32[4,7,2048]{2,1,0:T(8,128)} %get-tuple-element.41), channel_id=1, source_target_pairs={{0,1},{1,2},{2,3},{3,4},{4,5},{5,6},{6,7},{7,8},{8,9},{9,10},{10,1... | collective-permute-start | bytes 688136 | tf_op jit(solution)/shard_map/ppermute | solution.py:25
  9.2 15.7 %collective-permute-start.1 = (f32[4,7,2048]{2,1,0:T(8,128)}, f32[4,7,2048]{2,1,0:T(8,128)S(1)}, u32[]{:S(2)}, u32[]{:S(2)}) collective-permute-start(f32[4,7,2048]{2,1,0:T(8,128)} %get-tuple-element.40), channel_id=1, source_target_pairs={{0,1},{1,2},{2,3},{3,4},{4,5},{5,6},{6,7},{7,8},{8,9},{9,10},{10,1... | collective-permute-start | bytes 688136 | tf_op jit(solution)/shard_map/ppermute | solution.py:25
  13.6 16.3 %collective-permute-start.2 = (f32[4,7,2048]{2,1,0:T(8,128)}, f32[4,7,2048]{2,1,0:T(8,128)}, u32[]{:S(2)}, u32[]{:S(2)}) collective-permute-start(f32[4,7,2048]{2,1,0:T(8,128)} %get-tuple-element.43), channel_id=1, source_target_pairs={{1,0},{2,1},{3,2},{4,3},{5,4},{6,5},{7,6},{8,7},{9,8},{10,9},{11,1... | collective-permute-start | bytes 688136 | tf_op jit(solution)/shard_map/ppermute | solution.py:25
  14.9 7.6 %collective-permute-start.4 = (f32[2,3,512]{2,1,0:T(4,128)S(1)}, f32[2,3,512]{2,1,0:T(4,128)S(1)}, u32[]{:S(2)}, u32[]{:S(2)}) collective-permute-start(f32[2,3,512]{2,1,0:T(4,128)S(1)} %get-tuple-element.44), channel_id=1, source_target_pairs={{0,4},{4,8},{8,12},{12,16},{16,20},{20,24},{24,28},{1,5},{5,9},{9,... | collective-permute-start | bytes 36872 | tf_op jit(solution)/shard_map/ppermute | solution.py:25
  19.0 5.5 %collective-permute-start.5 = (f32[2,3,512]{2,1,0:T(4,128)S(1)}, f32[2,3,512]{2,1,0:T(4,128)S(1)}, u32[]{:S(2)}, u32[]{:S(2)}) collective-permute-start(f32[2,3,512]{2,1,0:T(4,128)S(1)} %get-tuple-element.45), channel_id=1, source_target_pairs={{4,0},{8,4},{12,8},{16,12},{20,16},{24,20},{28,24},{5,1},{9,5},{13... | collective-permute-start | bytes 36872 | tf_op jit(solution)/shard_map/ppermute | solution.py:25
  22.5 13.1 %copy-start.1 = (f32[8,32,2048]{2,1,0:T(8,128)S(1)}, f32[8,32,2048]{2,1,0:T(8,128)}, u32[]{:S(2)}) copy-start(f32[8,32,2048]{2,1,0:T(8,128)} %param.11) | copy-start | bytes 6291460
  22.5 11.9 %collective-permute-start.3 = (f32[4,7,2048]{2,1,0:T(8,128)}, f32[4,7,2048]{2,1,0:T(8,128)}, u32[]{:S(2)}, u32[]{:S(2)}) collective-permute-start(f32[4,7,2048]{2,1,0:T(8,128)} %get-tuple-element.42), channel_id=1, source_target_pairs={{1,0},{2,1},{3,2},{4,3},{5,4},{6,5},{7,6},{8,7},{9,8},{10,9},{11,1... | collective-permute-start | bytes 688136 | tf_op jit(solution)/shard_map/ppermute | solution.py:25
  35.5 0.7 copy-start.9
  36.2 1.6 %copy-start.2 = (f32[8,32,2048]{2,1,0:T(8,128)S(1)}, f32[8,32,2048]{2,1,0:T(8,128)}, u32[]{:S(2)}) copy-start(f32[8,32,2048]{2,1,0:T(8,128)} %param.12) | copy-start | bytes 6291460
  36.2 1.6 %copy-start.10 = (f32[8]{0:T(128)S(1)}, f32[8]{0:T(128)}, u32[]{:S(2)}) copy-start(f32[8]{0:T(128)} %param.13) | copy-start | bytes 100
  49.5 8.6 %collective-permute-start.6 = (f32[2,37,516]{2,1,0:T(8,128)S(1)}, f32[2,37,516]{2,1,0:T(8,128)S(1)}, u32[]{:S(2)}, u32[]{:S(2)}) collective-permute-start(f32[2,37,516]{2,1,0:T(8,128)S(1)} %pad_maximum_fusion.11), channel_id=1, source_target_pairs={{0,1},{1,2},{2,3},{3,0},{4,5},{5,6},{6,7},{7,4},{8,9},{9,10},{10,1... | collective-permute-start | bytes 458216 | tf_op jit(solution)/shard_map/ppermute | solution.py:149
  52.9 10.8 %collective-permute-start.8 = (f32[2,37,516]{2,1,0:T(8,128)S(1)}, f32[2,37,516]{2,1,0:T(8,128)S(1)}, u32[]{:S(2)}, u32[]{:S(2)}) collective-permute-start(f32[2,37,516]{2,1,0:T(8,128)S(1)} %pad_maximum_fusion.12), channel_id=1, source_target_pairs={{0,3},{1,0},{2,1},{3,2},{4,7},{5,4},{6,5},{7,6},{8,11},{9,8},{10,9... | collective-permute-start | bytes 458216 | tf_op jit(solution)/shard_map/ppermute | solution.py:149
  55.3 16.9 %collective-permute-start.7 = (f32[2,36,516]{2,1,0:T(8,128)S(1)}, f32[2,36,516]{2,1,0:T(8,128)S(1)}, u32[]{:S(2)}, u32[]{:S(2)}) collective-permute-start(f32[2,36,516]{2,1,0:T(8,128)S(1)} %get-tuple-element.27), channel_id=1, source_target_pairs={{0,2},{1,3},{2,0},{3,1},{4,6},{5,7},{6,4},{7,5},{8,10},{9,11},{10,... | collective-permute-start | bytes 445832 | tf_op jit(solution)/shard_map/ppermute | solution.py:149
  77.5 24.6 %copy-start.4 = (f32[2,1,6144]{2,1,0:T(1,128)S(1)}, f32[2,1,6144]{2,1,0:T(1,128)}, u32[]{:S(2)}) copy-start(f32[2,1,6144]{2,1,0:T(1,128)} %param.20) | copy-start | bytes 147460
  77.5 24.6 %copy-start.7 = (f32[1,6144]{1,0:T(1,128)S(1)}, f32[1,6144]{1,0:T(1,128)}, u32[]{:S(2)}) copy-start(f32[1,6144]{1,0:T(1,128)} %param.21) | copy-start | bytes 73732

commit v10 on v8

--- a/solution.py
+++ b/solution.py
@@ -105,9 +105,21 @@
     rows = temp.shape[1]
     h = STEPS + extra
     hh = h - 1
-    last = jnp.concatenate([temp[:, rows - h:], heat[:, rows - hh:]], axis=1)
-    leading = jnp.concatenate([temp[:, :h], heat[:, :hh]], axis=1)
+    n_gx, n_gy = lax.axis_size("gx"), lax.axis_size("gy")
+    bt, bh = STEPS, STEPS - 1
+    last = jnp.concatenate([temp[:, rows - bt:], heat[:, rows - bh:]], axis=1)
+    leading = jnp.concatenate([temp[:, :bt], heat[:, :bh]], axis=1)
     before, after = exchange(last, leading, FLAT)
+    far_last = jnp.concatenate([temp[:, rows - h: rows - bt], heat[:, rows - hh: rows - bh]], axis=1)
+    far_leading = jnp.concatenate([temp[:, bt:h], heat[:, bh:hh]], axis=1)
+    up = [(i * n_gy + n_gy - 1, (i + 1) * n_gy) for i in range(n_gx - 1)]
+    far_before = lax.ppermute(far_last, FLAT, up)
+    far_after = lax.ppermute(far_leading, FLAT, [(b, a) for a, b in up])
+    before = jnp.concatenate(
+        [far_before[:, :extra], before[:, :bt], far_before[:, extra:], before[:, bt:]], axis=1)
+    after = jnp.concatenate(
+        [after[:, :bt], far_after[:, :extra], after[:, bt:], far_after[:, extra:]], axis=1)
+    before, after = lax.optimization_barrier((before, after))
     ext = jnp.concatenate([before[:, :h], temp, after[:, :h]], axis=1)
     heat_ext = jnp.concatenate([before[:, h:], heat, after[:, h:]], axis=1)
     for step in range(1, STEPS + 1):

time: 103 us -> 109 us (1.058)
  waiting for transfers between devices: 31.6 us -> 16.7 us
  starting transfers between devices: 16.3 us -> 25.2 us
  other arithmetic: 23.2 us -> 28.2 us
  local copies, waits for them, and re-layouts: 11.6 us -> 16 us
  blocking collectives: 10.1 us -> 13.1 us
    ppermute x4, waiting for transfers between devices: 15.5 us -> 0.01 us  [exchange(): return (lax.ppermute(last, axis, up), lax.ppermute(leading, axis, down))]
    slice x2 -> x9, local copies, waits for them, and re-layouts: 2.65 us -> 8.01 us  [the longest x2 2.03 us: thermal(): leading = jnp.concatenate([temp[:, :bt], heat[:, :bh]], axis=1)]
    ppermute x3, starting transfers between devices: 4.11 us -> 7.66 us  [relay(): lax.ppermute(piece, 'gy', [(j, (j + shift) % n_gy) for j in range(n_gy)])]
    ppermute x4, starting transfers between devices: 12.2 us -> 15.5 us  [exchange(): return (lax.ppermute(last, axis, up), lax.ppermute(leading, axis, down))]
    all_to_all x1, blocking collectives: 10.1 us -> 13.1 us  [body(): lax.all_to_all(outgoing, FLAT, split_axis=1, concat_axis=1, tiled=True)]
    ppermute x0 -> x2, starting transfers between devices: none -> 2.04 us  [the longest x1 1.37 us: thermal(): far_before = lax.ppermute(far_last, FLAT, up)]
    concatenate x2 -> x6, other arithmetic: 1.83 us -> 2.19 us  [the longest x1 0.72 us: thermal(): jnp.concatenate([temp[:, rows - h:rows - bt], heat[:, rows - hh:rows - bh...]
  transfers between devices with their start and end apart: 7 -> 9, of which waited for: 6 -> 3; matrix products, arithmetic and copies ran while one was open for 5% -> 13% of each run, Pallas kernels for 0% -> 0%
where the time goes in v10:
time: 109 us
  other arithmetic  28.2 us (26%)
  starting transfers between devices  25.2 us (23%)
  waiting for transfers between devices  16.7 us (15%)
  local copies, waits for them, and re-layouts  16 us (15%)
  blocking collectives  13.1 us (12%)
  Pallas kernels  7.72 us (7%)
  between operations  1.33 us (1%)
    ppermute x3, waiting for transfers between devices, relay(): lax.ppermute(piece, 'gy', [(j, (j + shift) % n_gy) for j in range(n_gy)])  16.6 us
    ppermute x4, starting transfers between devices, exchange(): return (lax.ppermute(last, axis, up), lax.ppermute(leading, axis, down))  15.5 us
    all_to_all x1, blocking collectives, body(): lax.all_to_all(outgoing, FLAT, split_axis=1, concat_axis=1, tiled=True)  13.1 us
    ppermute x3, starting transfers between devices, relay(): lax.ppermute(piece, 'gy', [(j, (j + shift) % n_gy) for j in range(n_gy)])  7.66 us
    add x1, other arithmetic, moment_of(): total = total + weighting[layer] * field[layer]  5.06 us
    pallas_call x1, Pallas kernels, pick_cells(): pl.pallas_call(pick_kernel, grid=(count // block,), in_specs=[pl.BlockSpe...  4.35 us
    pallas_call x1, Pallas kernels, place_joints(): pl.pallas_call(place_kernel, out_shape=jax.ShapeDtypeStruct((nf + 1, devi...  3.37 us
    concatenate x1, other arithmetic, thermal(): heat_ext = jnp.concatenate([before[:, h:], heat, after[:, h:]], axis=1)  2.84 us
  transfers between devices with their start and end apart: 9, of which 3 were waited for; matrix products, arithmetic and copies ran while one was open for 13% of the time, Pallas kernels for 0%

profile of v10, /device:TPU:0, one launch (start us, length us, event | category | flops | bytes accessed | tf_op | source)
XLA Modules:
  0.0 108.6 jit_solution(6527116790728860287)
XLA Ops:
  0.7 1.9 %fusion.88 = (f32[8,2,2048]{2,1,0:T(2,128)S(1)}, f32[8,2,2048]{2,1,0:T(2,128)S(1)}, f32[8,2,2048]{2,1,0:T(2,128)S(1)}, f32[8,2,2048]{2,1,0:T(2,128)S(1)}) fusion(f32[8,32,2048]{2,1,0:T(8,128)} %param.11), kind=kLoop, calls=%fused_computation.232 | loop fusion | bytes 1048576 | tf_op jit(solution)/shard_map/slice | solution.py:111
  2.7 1.3 %fusion.90 = (f32[8,2,2048]{2,1,0:T(2,128)S(1)}, f32[8,2,2048]{2,1,0:T(2,128)S(1)}) fusion(f32[8,32,2048]{2,1,0:T(8,128)} %param.12), kind=kLoop, calls=%fused_computation.234 | loop fusion | bytes 524288 | tf_op jit(solution)/shard_map/slice | solution.py:114
  5.7 1.3 %collective-permute-start.2 = (f32[8,3,2048]{2,0,1:T(8,128)}, f32[8,3,2048]{2,0,1:T(8,128)}, u32[]{:S(2)}, u32[]{:S(2)}) collective-permute-start(f32[8,3,2048]{2,0,1:T(8,128)} %pad_maximum_fusion.16), channel_id=1, source_target_pairs={{1,0},{2,1},{3,2},{4,3},{5,4},{6,5},{7,6},{8,7},{9,8},{10,9},{11,1... | collective-permute-start | bytes 589832 | tf_op jit(solution)/shard_map/ppermute | solution.py:25
  7.9 6.3 %collective-permute-start.1 = (f32[8,3,2048]{2,0,1:T(8,128)}, f32[8,3,2048]{2,0,1:T(8,128)}, u32[]{:S(2)}, u32[]{:S(2)}) collective-permute-start(f32[8,3,2048]{2,0,1:T(8,128)} %pad_maximum_fusion.15), channel_id=1, source_target_pairs={{0,1},{1,2},{2,3},{3,4},{4,5},{5,6},{6,7},{7,8},{8,9},{9,10},{10,1... | collective-permute-start | bytes 589832 | tf_op jit(solution)/shard_map/ppermute | solution.py:25
  14.7 6.7 %collective-permute-start.4 = (f32[2,3,512]{2,1,0:T(4,128)}, f32[2,3,512]{2,1,0:T(4,128)}, u32[]{:S(2)}, u32[]{:S(2)}) collective-permute-start(f32[2,3,512]{2,1,0:T(4,128)} %get-tuple-element.48), channel_id=1, source_target_pairs={{0,4},{4,8},{8,12},{12,16},{16,20},{20,24},{24,28},{1,5},{5,9},{9,... | collective-permute-start | bytes 36872 | tf_op jit(solution)/shard_map/ppermute | solution.py:25
  21.4 1.3 %collective-permute-start.5 = (f32[2,3,512]{2,1,0:T(4,128)}, f32[2,3,512]{2,1,0:T(4,128)}, u32[]{:S(2)}, u32[]{:S(2)}) collective-permute-start(f32[2,3,512]{2,1,0:T(4,128)} %get-tuple-element.49), channel_id=1, source_target_pairs={{4,0},{8,4},{12,8},{16,12},{20,16},{24,20},{28,24},{5,1},{9,5},{13... | collective-permute-start | bytes 36872 | tf_op jit(solution)/shard_map/ppermute | solution.py:25
  25.9 1.3 %add_select_fusion.3 = (s32[2048]{0:T(1024)}, s32[2048]{0:T(1024)}) fusion(s32[2048]{0:T(1024)} %param.18), kind=kLoop, calls=%fused_computation.192 | loop fusion | flops 38912 | bytes 24576 | tf_op jit(solution)/shard_map/jit(remainder)/select_n | solution.py:226
  28.8 1.4 %collective-permute-start = (f32[8,4,2048]{2,0,1:T(8,128)}, f32[8,4,2048]{2,0,1:T(8,128)}, u32[]{:S(2)}, u32[]{:S(2)}) collective-permute-start(f32[8,4,2048]{2,0,1:T(8,128)} %pad_maximum_fusion.10), channel_id=1, source_target_pairs={{3,4},{7,8},{11,12},{15,16},{19,20},{23,24},{27,28}} | collective-permute-start | bytes 786440 | tf_op jit(solution)/shard_map/ppermute | solution.py:116
  34.9 1.1 %fusion.92 = (f32[8,2,2048]{2,0,1:T(8,128)S(1)}, f32[8,2,2048]{2,0,1:T(8,128)S(1)}) fusion(f32[8,4,2048]{2,0,1:T(8,128)} %collective-permute-done), kind=kLoop, calls=%fused_computation.236 | loop fusion | bytes 524288 | tf_op jit(solution)/shard_map/slice | solution.py:119
  38.1 2.8 %pad_maximum_fusion.1 = (f32[8,38,2048]{2,1,0:T(8,128)S(1)}, f32[8,38,2048]{2,1,0:T(8,128)S(1)}) fusion(f32[8,3,2048]{2,1,0:T(4,128)S(1)} %copy.40, f32[8,32,2048]{2,1,0:T(8,128)S(1)} %copy-done.2, f32[8,3,2048]{2,1,0:T(4,128)S(1)} %copy.39, f32[7,38,2048]{2,1,0:T(8,128)S(1)} %fusion.16, f32[8,40,2048]{2,1,0:T(8,128)S(1)} %pad_maximum_fusion, ...), kind=kLoop, calls=%fused_computation.23 | loop fusion | flops 8093696 | bytes 20382720 | tf_op jit(solution)/shard_map/concatenate | solution.py:124
  41.4 2.6 %fusion.14 = f32[8,36,2048]{2,1,0:T(8,128)S(1)} fusion(f32[8,38,2048]{2,1,0:T(8,128)S(1)} %get-tuple-element.16, f32[8,38,2048]{2,1,0:T(8,128)S(1)} %get-tuple-element.15, f32[7,36,2048]{2,1,0:T(8,128)S(1)} %fusion.15, f32[8]{0:T(128)S(1)} %copy-done.9), kind=kLoop, calls=%fused_computation.19 | loop fusion | flops 5898240 | bytes 17760768 | tf_op jit(solution)/shard_map/add | solution.py:44
  44.1 5.1 %fusion.39 = f32[36,2048]{1,0:T(8,128)S(1)} fusion(f32[8,36,2048]{2,1,0:T(8,128)S(1)} %fusion.14, f32[]{:T(128)} %bitcast.7, f32[]{:T(128)} %bitcast.6, f32[]{:T(128)} %bitcast.5, f32[]{:T(128)} %bitcast.4, f32[]{:T(128)} %bitcast.3, f32[]{:T(128)} %bitcast.2, f32[]{:T(128)} %bitcast.1, f32[]{:T(128)} %bitcast), kind=kLoop, calls=%fused_computation.91 | loop fusion | flops 1105920 | bytes 2654240 | tf_op jit(solution)/shard_map/add | solution.py:50
  50.0 1.4 %copy.41.ranks_ref = s32[2048,1]{1,0:T(8,128)} copy(s32[2048,1]{0,1:T(1,128)S(1)} %bitcast.111) | data formatting | bytes 16384 | tf_op jit(solution)/shard_map/sub | solution.py:199
  51.7 6.7 %collective-permute-start.8 = (f32[2,37,516]{2,1,0:T(8,128)S(1)}, f32[2,37,516]{2,1,0:T(8,128)S(1)}, u32[]{:S(2)}, u32[]{:S(2)}) collective-permute-start(f32[2,37,516]{2,1,0:T(8,128)S(1)} %pad_maximum_fusion.14), channel_id=1, source_target_pairs={{0,3},{1,0},{2,1},{3,2},{4,7},{5,4},{6,5},{7,6},{8,11},{9,8},{10,9... | collective-permute-start | bytes 458216 | tf_op jit(solution)/shard_map/ppermute | solution.py:157
  59.0 1.2 %collective-permute-done.6 = f32[2,37,516]{2,1,0:T(8,128)S(1)} collective-permute-done((f32[2,37,516]{2,1,0:T(8,128)S(1)}, f32[2,37,516]{2,1,0:T(8,128)S(1)}, u32[]{:S(2)}, u32[]{:S(2)}) %collective-permute-start.6) | collective-permute-done | bytes 152768 | tf_op jit(solution)/shard_map/ppermute | solution.py:157
  60.2 1.5 %collective-permute-done.8 = f32[2,37,516]{2,1,0:T(8,128)S(1)} collective-permute-done((f32[2,37,516]{2,1,0:T(8,128)S(1)}, f32[2,37,516]{2,1,0:T(8,128)S(1)}, u32[]{:S(2)}, u32[]{:S(2)}) %collective-permute-start.8) | collective-permute-done | bytes 152768 | tf_op jit(solution)/shard_map/ppermute | solution.py:157
  61.7 14.0 %collective-permute-done.7 = f32[2,36,516]{2,1,0:T(8,128)S(1)} collective-permute-done((f32[2,36,516]{2,1,0:T(8,128)S(1)}, f32[2,36,516]{2,1,0:T(8,128)S(1)}, u32[]{:S(2)}, u32[]{:S(2)}) %collective-permute-start.7) | collective-permute-done | bytes 148640 | tf_op jit(solution)/shard_map/ppermute | solution.py:157
  77.3 1.0 pad_maximum_fusion.5
  80.1 1.4 %subtract_bitcast_fusion = (f32[1,1,128,512]{3,2,1,0:T(8,128)S(1)}, f32[128,512]{1,0:T(8,128)}) fusion(f32[128,512]{1,0:T(8,128)S(1)} %copy-done, f32[130,514]{1,0:T(8,128)S(1)} %fusion.20, f32[134,518]{1,0:T(8,128)S(1)} %get-tuple-element.37, f32[132,516]{1,0:T(8,128)S(1)} %get-tuple-element.14), kind=kLoop, calls=%fused_computation.127 | loop fusion | flops 1441792 | bytes 3407872 | tf_op jit(solution)/shard_map/stack | solution.py:320
  81.7 1.0 pad_maximum_fusion.4.parts_ref
  82.7 4.4 %shard_map.130 = f32[2,2048]{1,0:T(2,128)} custom-call(s32[1,2048]{1,0:T(1,128)} %bitcast.110, s32[1,2048]{1,0:T(1,128)} %bitcast.109, bf16[3,2,128,512]{3,2,1,0:T(8,128)(2,1)} %pad_maximum_fusion.4.parts_ref), custom_call_target="tpu_custom_call" | custom-call | tf_op jit(solution)/shard_map/pallas_call | solution.py:228
  88.4 3.4 %shard_map.131 = f32[3,32,192]{2,1,0:T(8,128)} custom-call(s32[1,2048]{1,0:T(1,128)} %bitcast.106, s32[2048,1]{1,0:T(8,128)} %copy.41.ranks_ref, f32[3,2,2048]{2,1,0:T(2,128)} %pad_maximum_fusion.21.parts_ref), custom_call_target="tpu_custom_call" | custom-call | tf_op jit(solution)/shard_map/pallas_call | solution.py:267
  92.8 13.1 %all_to_all.5 = f32[3,32,192]{2,0,1:T(4,128)S(1)} all-to-all(f32[3,32,192]{2,0,1:T(4,128)S(1)} %copy.42), channel_id=1, replica_groups=mesh['gx'=8,'gy'=4] {'gx','gy'}, dimensions={1} | all-to-all | bytes 147456 | tf_op jit(solution)/shard_map/all_to_all | solution.py:322
  106.7 1.1 add_select_fusion
  (127 shorter events, 24.1 us)
Async XLA Ops:
  0.6 4.2 %copy-start.2 = (f32[8,32,2048]{2,1,0:T(8,128)S(1)}, f32[8,32,2048]{2,1,0:T(8,128)}, u32[]{:S(2)}) copy-start(f32[8,32,2048]{2,1,0:T(8,128)} %param.12) | copy-start | bytes 6291460
  0.6 13.5 %copy-start = (f32[128,512]{1,0:T(8,128)S(1)}, f32[128,512]{1,0:T(8,128)}, u32[]{:S(2)}) copy-start(f32[128,512]{1,0:T(8,128)} %param.17) | copy-start | bytes 786436
  0.7 13.5 %copy-start.3 = (f32[128,512]{1,0:T(8,128)S(1)}, f32[128,512]{1,0:T(8,128)}, u32[]{:S(2)}) copy-start(f32[128,512]{1,0:T(8,128)} %param.16) | copy-start | bytes 786436
  0.7 23.9 %copy-start.6 = (f32[8]{0:T(128)S(1)}, f32[8]{0:T(128)}, u32[]{:S(2)}) copy-start(f32[8]{0:T(128)} %param.15) | copy-start | bytes 100
  0.7 26.6 %copy-start.5 = (s32[2048,1]{0,1:T(1,128)S(1)}, s32[2048,1]{0,1:T(1,128)}, u32[]{:S(2)}) copy-start(s32[2048,1]{0,1:T(1,128)} %param.19) | copy-start | bytes 24580
  4.1 30.7 %collective-permute-start.3 = (f32[8,4,2048]{2,0,1:T(8,128)S(1)}, f32[8,4,2048]{2,0,1:T(8,128)S(1)}, u32[]{:S(2)}, u32[]{:S(2)}) collective-permute-start(f32[8,4,2048]{2,0,1:T(8,128)S(1)} %pad_maximum_fusion.11), channel_id=1, source_target_pairs={{4,3},{8,7},{12,11},{16,15},{20,19},{24,23},{28,27}} | collective-permute-start | bytes 786440 | tf_op jit(solution)/shard_map/ppermute | solution.py:117
  5.7 25.5 %collective-permute-start.2 = (f32[8,3,2048]{2,0,1:T(8,128)}, f32[8,3,2048]{2,0,1:T(8,128)}, u32[]{:S(2)}, u32[]{:S(2)}) collective-permute-start(f32[8,3,2048]{2,0,1:T(8,128)} %pad_maximum_fusion.16), channel_id=1, source_target_pairs={{1,0},{2,1},{3,2},{4,3},{5,4},{6,5},{7,6},{8,7},{9,8},{10,9},{11,1... | collective-permute-start | bytes 589832 | tf_op jit(solution)/shard_map/ppermute | solution.py:25
  7.9 25.2 %collective-permute-start.1 = (f32[8,3,2048]{2,0,1:T(8,128)}, f32[8,3,2048]{2,0,1:T(8,128)}, u32[]{:S(2)}, u32[]{:S(2)}) collective-permute-start(f32[8,3,2048]{2,0,1:T(8,128)} %pad_maximum_fusion.15), channel_id=1, source_target_pairs={{0,1},{1,2},{2,3},{3,4},{4,5},{5,6},{6,7},{7,8},{8,9},{9,10},{10,1... | collective-permute-start | bytes 589832 | tf_op jit(solution)/shard_map/ppermute | solution.py:25
  14.7 14.1 %collective-permute-start.4 = (f32[2,3,512]{2,1,0:T(4,128)}, f32[2,3,512]{2,1,0:T(4,128)}, u32[]{:S(2)}, u32[]{:S(2)}) collective-permute-start(f32[2,3,512]{2,1,0:T(4,128)} %get-tuple-element.48), channel_id=1, source_target_pairs={{0,4},{4,8},{8,12},{12,16},{16,20},{20,24},{24,28},{1,5},{5,9},{9,... | collective-permute-start | bytes 36872 | tf_op jit(solution)/shard_map/ppermute | solution.py:25
  21.4 8.8 %collective-permute-start.5 = (f32[2,3,512]{2,1,0:T(4,128)}, f32[2,3,512]{2,1,0:T(4,128)}, u32[]{:S(2)}, u32[]{:S(2)}) collective-permute-start(f32[2,3,512]{2,1,0:T(4,128)} %get-tuple-element.49), channel_id=1, source_target_pairs={{4,0},{8,4},{12,8},{16,12},{20,16},{24,20},{28,24},{5,1},{9,5},{13... | collective-permute-start | bytes 36872 | tf_op jit(solution)/shard_map/ppermute | solution.py:25
  28.8 6.1 %collective-permute-start = (f32[8,4,2048]{2,0,1:T(8,128)}, f32[8,4,2048]{2,0,1:T(8,128)}, u32[]{:S(2)}, u32[]{:S(2)}) collective-permute-start(f32[8,4,2048]{2,0,1:T(8,128)} %pad_maximum_fusion.10), channel_id=1, source_target_pairs={{3,4},{7,8},{11,12},{15,16},{19,20},{23,24},{27,28}} | collective-permute-start | bytes 786440 | tf_op jit(solution)/shard_map/ppermute | solution.py:116
  34.9 2.0 %copy-start.1 = (f32[8,32,2048]{2,1,0:T(8,128)S(1)}, f32[8,32,2048]{2,1,0:T(8,128)}, u32[]{:S(2)}) copy-start(f32[8,32,2048]{2,1,0:T(8,128)} %param.11) | copy-start | bytes 6291460
  36.8 0.7 copy-start.8
  37.5 0.7 copy-start.9
  49.6 10.5 %collective-permute-start.6 = (f32[2,37,516]{2,1,0:T(8,128)S(1)}, f32[2,37,516]{2,1,0:T(8,128)S(1)}, u32[]{:S(2)}, u32[]{:S(2)}) collective-permute-start(f32[2,37,516]{2,1,0:T(8,128)S(1)} %pad_maximum_fusion.13), channel_id=1, source_target_pairs={{0,1},{1,2},{2,3},{3,0},{4,5},{5,6},{6,7},{7,4},{8,9},{9,10},{10,1... | collective-permute-start | bytes 458216 | tf_op jit(solution)/shard_map/ppermute | solution.py:157
  50.0 26.4 %copy-start.11 = (pred[4]{0:T(512)(128)(4,1)S(1)}, pred[4]{0:T(512)(128)(4,1)}, u32[]{:S(2)}) copy-start(pred[4]{0:T(512)(128)(4,1)} %compare_and_fusion.3) | copy-start | bytes 16
  51.7 10.0 %collective-permute-start.8 = (f32[2,37,516]{2,1,0:T(8,128)S(1)}, f32[2,37,516]{2,1,0:T(8,128)S(1)}, u32[]{:S(2)}, u32[]{:S(2)}) collective-permute-start(f32[2,37,516]{2,1,0:T(8,128)S(1)} %pad_maximum_fusion.14), channel_id=1, source_target_pairs={{0,3},{1,0},{2,1},{3,2},{4,7},{5,4},{6,5},{7,6},{8,11},{9,8},{10,9... | collective-permute-start | bytes 458216 | tf_op jit(solution)/shard_map/ppermute | solution.py:157
  58.4 17.3 %collective-permute-start.7 = (f32[2,36,516]{2,1,0:T(8,128)S(1)}, f32[2,36,516]{2,1,0:T(8,128)S(1)}, u32[]{:S(2)}, u32[]{:S(2)}) collective-permute-start(f32[2,36,516]{2,1,0:T(8,128)S(1)} %get-tuple-element.35), channel_id=1, source_target_pairs={{0,2},{1,3},{2,0},{3,1},{4,6},{5,7},{6,4},{7,5},{8,10},{9,11},{10,... | collective-permute-start | bytes 445832 | tf_op jit(solution)/shard_map/ppermute | solution.py:157
  76.5 2.0 %copy-start.10 = (pred[516]{0:T(1024)(128)(4,1)S(1)}, pred[516]{0:T(1024)(128)(4,1)}, u32[]{:S(2)}) copy-start(pred[516]{0:T(1024)(128)(4,1)} %fusion.83) | copy-start | bytes 1552
  81.7 25.0 %copy-start.4 = (f32[2,1,6144]{2,1,0:T(1,128)S(1)}, f32[2,1,6144]{2,1,0:T(1,128)}, u32[]{:S(2)}) copy-start(f32[2,1,6144]{2,1,0:T(1,128)} %param.20) | copy-start | bytes 147460
  81.7 25.0 %copy-start.7 = (f32[1,6144]{1,0:T(1,128)S(1)}, f32[1,6144]{1,0:T(1,128)}, u32[]{:S(2)}) copy-start(f32[1,6144]{1,0:T(1,128)} %param.21) | copy-start | bytes 73732

commit v11 on v7

--- a/solution.py
+++ b/solution.py
@@ -187,43 +187,65 @@
     return jnp.sum(cum * onehot, axis=1).astype(jnp.int32) - 1
 
 
-def pick_kernel(rows_ref, cols_ref, parts_ref, out_ref):
-    rows = rows_ref[...]
-    cols = cols_ref[...]
-    block = rows.shape[1]
+def split3(x):
+    hi = x.astype(jnp.bfloat16).astype(jnp.float32)
+    rest = x - hi
+    mid = rest.astype(jnp.bfloat16).astype(jnp.float32)
+    return hi, mid, rest - mid
+
+
+def joints_kernel(rows_ref, cols_ref, parts_ref, owners_ref, ranks_ref, out_ref):
     _, fields, rm, cm = parts_ref.shape
-    hit = lax.broadcasted_iota(jnp.int32, (cm, block), 0) == cols
-    onehot = jnp.where(hit, 1.0, 0.0).astype(jnp.bfloat16)
-    sel = lax.broadcasted_iota(jnp.int32, (rm, block), 0) == rows
+    count = rows_ref.shape[1]
+    devices, cap = out_ref.shape[1:]
+    block = 512 if count % 512 == 0 else count
+    picked = []
+    for b in range(count // block):
+        rows = rows_ref[:, b * block: (b + 1) * block]
+        cols = cols_ref[:, b * block: (b + 1) * block]
+        hit = lax.broadcasted_iota(jnp.int32, (cm, block), 0) == cols
+        onehot = jnp.where(hit, 1.0, 0.0).astype(jnp.bfloat16)
+        sel = lax.broadcasted_iota(jnp.int32, (rm, block), 0) == rows
+        got = []
+        for f in range(fields):
+            acc = jnp.dot(parts_ref[0, f], onehot, preferred_element_type=jnp.float32)
+            acc = acc + jnp.dot(parts_ref[1, f], onehot, preferred_element_type=jnp.float32)
+            acc = acc + jnp.dot(parts_ref[2, f], onehot, preferred_element_type=jnp.float32)
+            got.append(jnp.sum(jnp.where(sel, acc, 0.0), axis=0, keepdims=True))
+        picked.append(jnp.concatenate(got, axis=0))
+    values = jnp.concatenate(picked, axis=1)
+    mine = lax.broadcasted_iota(jnp.int32, (devices, count), 0) == owners_ref[...]
+    slot = lax.broadcasted_iota(jnp.int32, (count, cap), 1) == ranks_ref[...]
+    at = jnp.where(slot, 1.0, 0.0).astype(jnp.bfloat16)
+    split = split3(values)
     for f in range(fields):
-        acc = jnp.dot(parts_ref[0, f], onehot, preferred_element_type=jnp.float32)
-        acc = acc + jnp.dot(parts_ref[1, f], onehot, preferred_element_type=jnp.float32)
-        acc = acc + jnp.dot(parts_ref[2, f], onehot, preferred_element_type=jnp.float32)
-        out_ref[f: f + 1, :] = jnp.sum(jnp.where(sel, acc, 0.0), axis=0, keepdims=True)
-
-
-def pick_cells(fields, cells):
-    count = cells.shape[0]
+        acc = None
+        for part in split:
+            spread = jnp.where(mine, part[f: f + 1, :], 0.0).astype(jnp.bfloat16)
+            term = jnp.dot(spread, at, preferred_element_type=jnp.float32)
+            acc = term if acc is None else acc + term
+        out_ref[f] = acc
+    live = jnp.where(mine, 1.0, 0.0).astype(jnp.bfloat16)
+    out_ref[fields] = jnp.dot(live, at, preferred_element_type=jnp.float32)
+
+
+def route_joints(fields, cells, owners, ranks, devices, cap):
     nf, rm, cm = fields.shape
     hi = lax.reduce_precision(fields, exponent_bits=8, mantissa_bits=7)
     rest = fields - hi
     mid = lax.reduce_precision(rest, exponent_bits=8, mantissa_bits=7)
     lo = rest - mid
     parts = jnp.stack([hi, mid, lo]).astype(jnp.bfloat16)
-    rows = (cells // cm).astype(jnp.int32)[None, :]
-    cols = (cells % cm).astype(jnp.int32)[None, :]
-    block = 512 if count % 512 == 0 else count
     return pl.pallas_call(
-        pick_kernel,
-        grid=(count // block,),
-        in_specs=[
-            pl.BlockSpec((1, block), lambda i: (0, i)),
-            pl.BlockSpec((1, block), lambda i: (0, i)),
-            pl.BlockSpec((3, nf, rm, cm), lambda i: (0, 0, 0, 0)),
-        ],
-        out_specs=pl.BlockSpec((nf, block), lambda i: (0, i)),
-        out_shape=jax.ShapeDtypeStruct((nf, count), jnp.float32),
-    )(rows, cols, parts)
+        joints_kernel,
+        out_shape=jax.ShapeDtypeStruct((nf + 1, devices, cap), jnp.float32),
+    )(
+        (cells // cm).astype(jnp.int32)[None, :],
+        (cells % cm).astype(jnp.int32)[None, :],
+        parts,
+        owners[None, :].astype(jnp.int32),
+        ranks[:, None].astype(jnp.int32),
+    )
 
 
 def body(
@@ -247,7 +269,7 @@
     wm = jnp.stack([warp_prev, modulus])
     owners = joint_owner[:, 0]
     capacity = joint_resist.shape[1] // devices
-    slots = owners * capacity + joint_ranks(owners, devices)
+    ranks = joint_ranks(owners, devices)
 
     extra = SWEEPS - 1
     g = SWEEPS
@@ -273,10 +295,10 @@
             inside = ((gr >= 0) & (gr < n_gx * rm))[:, None] & ((gc >= 0) & (gc < n_gy * cm))[None, :]
             warp = jnp.where(inside, warp, 0.0)
 
-    picked = pick_cells(jnp.stack([warp - warp_prev, top]), joint_cell)
-    values = jnp.concatenate([picked, jnp.ones_like(picked[:1])], axis=0)
-    outgoing = jnp.zeros((3, devices * capacity), jnp.float32).at[:, slots].set(values)
+    outgoing = route_joints(
+        jnp.stack([warp - warp_prev, top]), joint_cell, owners, ranks, devices, capacity)
     incoming = lax.all_to_all(outgoing, FLAT, split_axis=1, concat_axis=1, tiled=True)
+    incoming = incoming.reshape(incoming.shape[0], devices * capacity)
     strain_next, resist_next = anand(joint_strain, joint_resist, incoming[:, None, :])
     return (warp, strain_next, resist_next)
 

time: 106 us -> 98.7 us (0.931)
  local copies, waits for them, and re-layouts: 19.6 us -> 11.6 us
    scatter x1 -> x0, local copies, waits for them, and re-layouts: 6.73 us -> none  [body(): jnp.zeros((3, devices * capacity), jnp.float32).at[:, slots].set(values)]
    concatenate x2 -> x0, local copies, waits for them, and re-layouts: 2.08 us -> none  [body(): values = jnp.concatenate([picked, jnp.ones_like(picked[:1])], axis=0)]
    all_to_all x1 -> x0, local copies, waits for them, and re-layouts: 1.47 us -> none  [body(): lax.all_to_all(outgoing, FLAT, split_axis=1, concat_axis=1, tiled=True)]
    sub x0 -> x1, local copies, waits for them, and re-layouts: none -> 1.35 us  [joint_ranks(): return jnp.sum(cum * onehot, axis=1).astype(jnp.int32) - 1]
  transfers between devices with their start and end apart: 7 -> 7, of which waited for: 6 -> 6; matrix products, arithmetic and copies ran while one was open for 4% -> 5% of each run, Pallas kernels for 0% -> 0%
where the time goes in v11:
time: 98.7 us; the launch traced here: 98.2 us
  waiting for transfers between devices  31.6 us (32%)
  other arithmetic  21.9 us (22%)
  starting transfers between devices  16.3 us (17%)
  local copies, waits for them, and re-layouts  11.6 us (12%)
  blocking collectives  10.1 us (10%)
  Pallas kernels  5.22 us (5%)
  between operations  1.19 us (1%)
    ppermute x3, waiting for transfers between devices, relay(): lax.ppermute(piece, 'gy', [(j, (j + shift) % n_gy) for j in range(n_gy)])  16.2 us
    ppermute x4, waiting for transfers between devices, exchange(): return (lax.ppermute(last, axis, up), lax.ppermute(leading, axis, down))  15.5 us
    ppermute x4, starting transfers between devices, exchange(): return (lax.ppermute(last, axis, up), lax.ppermute(leading, axis, down))  12.2 us
    all_to_all x1, blocking collectives, body(): lax.all_to_all(outgoing, FLAT, split_axis=1, concat_axis=1, tiled=True)  10.1 us
    add x1, other arithmetic, moment_of(): total = total + weighting[layer] * field[layer]  5.29 us
    pallas_call x1, Pallas kernels, route_joints(): pl.pallas_call(joints_kernel, out_shape=jax.ShapeDtypeStruct((nf + 1, dev...  5.22 us
    ppermute x3, starting transfers between devices, relay(): lax.ppermute(piece, 'gy', [(j, (j + shift) % n_gy) for j in range(n_gy)])  4.11 us
    concatenate x1, other arithmetic, thermal(): heat_ext = jnp.concatenate([before[:, h:], heat, after[:, h:]], axis=1)  2.86 us
  transfers between devices with their start and end apart: 7, of which 6 were waited for; matrix products, arithmetic and copies ran while one was open for 5% of the time, Pallas kernels for 0%

profile of v11, /device:TPU:0, one launch (start us, length us, event | category | flops | bytes accessed | tf_op | source)
XLA Modules:
  0.0 98.2 jit_solution(10980432949469031890)
XLA Ops:
  0.7 1.3 %fusion.87 = (f32[8,4,2048]{2,1,0:T(4,128)S(1)}, f32[8,4,2048]{2,1,0:T(4,128)S(1)}) fusion(f32[8,32,2048]{2,1,0:T(8,128)} %param.11), kind=kLoop, calls=%fused_computation.222 | loop fusion | bytes 1048576 | tf_op jit(solution)/shard_map/slice | solution.py:108
  2.0 1.3 %fusion.88 = (f32[8,3,2048]{2,1,0:T(4,128)S(1)}, f32[8,3,2048]{2,1,0:T(4,128)S(1)}) fusion(f32[8,32,2048]{2,1,0:T(8,128)} %param.12), kind=kLoop, calls=%fused_computation.223 | loop fusion | bytes 786432 | tf_op jit(solution)/shard_map/slice | solution.py:108
  4.3 5.0 %collective-permute-start = (f32[8,7,2048]{2,1,0:T(8,128)}, f32[8,7,2048]{2,1,0:T(8,128)S(1)}, u32[]{:S(2)}, u32[]{:S(2)}) collective-permute-start(f32[8,7,2048]{2,1,0:T(8,128)} %pad_maximum_fusion.6), channel_id=1, source_target_pairs={{0,1},{1,2},{2,3},{3,4},{4,5},{5,6},{6,7},{7,8},{8,9},{9,10},{10,1... | collective-permute-start | bytes 1376264 | tf_op jit(solution)/shard_map/ppermute | solution.py:25
  10.2 1.3 %collective-permute-start.1 = (f32[8,7,2048]{2,1,0:T(8,128)}, f32[8,7,2048]{2,1,0:T(8,128)}, u32[]{:S(2)}, u32[]{:S(2)}) collective-permute-start(f32[8,7,2048]{2,1,0:T(8,128)} %pad_maximum_fusion.7), channel_id=1, source_target_pairs={{1,0},{2,1},{3,2},{4,3},{5,4},{6,5},{7,6},{8,7},{9,8},{10,9},{11,1... | collective-permute-start | bytes 1376264 | tf_op jit(solution)/shard_map/ppermute | solution.py:25
  11.5 4.6 %collective-permute-start.2 = (f32[2,3,512]{2,1,0:T(4,128)S(1)}, f32[2,3,512]{2,1,0:T(4,128)S(1)}, u32[]{:S(2)}, u32[]{:S(2)}) collective-permute-start(f32[2,3,512]{2,1,0:T(4,128)S(1)} %get-tuple-element.40), channel_id=1, source_target_pairs={{0,4},{4,8},{8,12},{12,16},{16,20},{20,24},{24,28},{1,5},{5,9},{9,... | collective-permute-start | bytes 36872 | tf_op jit(solution)/shard_map/ppermute | solution.py:25
  16.2 1.3 %collective-permute-start.3 = (f32[2,3,512]{2,1,0:T(4,128)S(1)}, f32[2,3,512]{2,1,0:T(4,128)S(1)}, u32[]{:S(2)}, u32[]{:S(2)}) collective-permute-start(f32[2,3,512]{2,1,0:T(4,128)S(1)} %get-tuple-element.41), channel_id=1, source_target_pairs={{4,0},{8,4},{12,8},{16,12},{20,16},{24,20},{28,24},{5,1},{9,5},{13... | collective-permute-start | bytes 36872 | tf_op jit(solution)/shard_map/ppermute | solution.py:25
  19.7 1.4 %collective-permute-done.3 = f32[2,3,512]{2,1,0:T(4,128)S(1)} collective-permute-done((f32[2,3,512]{2,1,0:T(4,128)S(1)}, f32[2,3,512]{2,1,0:T(4,128)S(1)}, u32[]{:S(2)}, u32[]{:S(2)}) %collective-permute-start.3) | collective-permute-done | bytes 12320 | tf_op jit(solution)/shard_map/ppermute | solution.py:25
  21.9 13.7 %collective-permute-done.1 = f32[8,7,2048]{2,1,0:T(8,128)} collective-permute-done((f32[8,7,2048]{2,1,0:T(8,128)}, f32[8,7,2048]{2,1,0:T(8,128)}, u32[]{:S(2)}, u32[]{:S(2)}) %collective-permute-start.1) | collective-permute-done | bytes 458784 | tf_op jit(solution)/shard_map/ppermute | solution.py:25
  35.6 1.1 %slice.418 = f32[8,4,2048]{2,1,0:T(4,128)S(1)} slice(f32[8,7,2048]{2,1,0:T(8,128)} %collective-permute-done.1), slice={[0:8], [0:4], [0:2048]} | slice | bytes 524288 | tf_op jit(solution)/shard_map/slice | solution.py:111
  37.9 1.2 %slice.425 = f32[8,3,2048]{2,1,0:T(4,128)S(1)} slice(f32[8,7,2048]{2,1,0:T(8,128)} %collective-permute-done.1), slice={[0:8], [4:7], [0:2048]} | slice | bytes 393216 | tf_op jit(solution)/shard_map/slice | solution.py:112
  39.1 2.9 %pad_maximum_fusion.1 = (f32[8,38,2048]{2,1,0:T(8,128)S(1)}, f32[8,38,2048]{2,1,0:T(8,128)S(1)}) fusion(f32[8,3,2048]{2,1,0:T(4,128)S(1)} %slice.425, f32[8,32,2048]{2,1,0:T(8,128)S(1)} %copy-done.2, f32[8,3,2048]{2,1,0:T(4,128)S(1)} %slice.424, f32[7,38,2048]{2,1,0:T(8,128)S(1)} %fusion.16, f32[8,40,2048]{2,1,0:T(8,128)S(1)} %pad_maximum_fusion, ...), kind=kLoop, calls=%fused_computation.23 | loop fusion | flops 8093696 | bytes 20382720 | tf_op jit(solution)/shard_map/concatenate | solution.py:112
  42.5 2.6 %fusion.14 = f32[8,36,2048]{2,1,0:T(8,128)S(1)} fusion(f32[8,38,2048]{2,1,0:T(8,128)S(1)} %get-tuple-element.12, f32[8,38,2048]{2,1,0:T(8,128)S(1)} %get-tuple-element.11, f32[7,36,2048]{2,1,0:T(8,128)S(1)} %fusion.15, f32[8]{0:T(128)S(1)} %copy-done.10), kind=kLoop, calls=%fused_computation.19 | loop fusion | flops 5898240 | bytes 17760768 | tf_op jit(solution)/shard_map/add | solution.py:44
  45.1 5.3 %fusion.39 = f32[36,2048]{1,0:T(8,128)S(1)} fusion(f32[8,36,2048]{2,1,0:T(8,128)S(1)} %fusion.14, f32[]{:T(128)} %bitcast.7, f32[]{:T(128)} %bitcast.6, f32[]{:T(128)} %bitcast.5, f32[]{:T(128)} %bitcast.4, f32[]{:T(128)} %bitcast.3, f32[]{:T(128)} %bitcast.2, f32[]{:T(128)} %bitcast.1, f32[]{:T(128)} %bitcast), kind=kLoop, calls=%fused_computation.91 | loop fusion | flops 1105920 | bytes 2654240 | tf_op jit(solution)/shard_map/add | solution.py:50
  51.6 1.4 %copy.17.ranks_ref = s32[2048,1]{1,0:T(8,128)} copy(s32[2048,1]{0,1:T(1,128)S(1)} %bitcast.105) | data formatting | bytes 16384 | tf_op jit(solution)/shard_map/sub | solution.py:187
  53.2 3.5 %collective-permute-start.6 = (f32[2,37,516]{2,1,0:T(8,128)S(1)}, f32[2,37,516]{2,1,0:T(8,128)S(1)}, u32[]{:S(2)}, u32[]{:S(2)}) collective-permute-start(f32[2,37,516]{2,1,0:T(8,128)S(1)} %pad_maximum_fusion.12), channel_id=1, source_target_pairs={{0,3},{1,0},{2,1},{3,2},{4,7},{5,4},{6,5},{7,6},{8,11},{9,8},{10,9... | collective-permute-start | bytes 458216 | tf_op jit(solution)/shard_map/ppermute | solution.py:145
  56.7 4.0 %collective-permute-done.4 = f32[2,37,516]{2,1,0:T(8,128)S(1)} collective-permute-done((f32[2,37,516]{2,1,0:T(8,128)S(1)}, f32[2,37,516]{2,1,0:T(8,128)S(1)}, u32[]{:S(2)}, u32[]{:S(2)}) %collective-permute-start.4) | collective-permute-done | bytes 152768 | tf_op jit(solution)/shard_map/ppermute | solution.py:145
  60.8 3.4 %collective-permute-done.6 = f32[2,37,516]{2,1,0:T(8,128)S(1)} collective-permute-done((f32[2,37,516]{2,1,0:T(8,128)S(1)}, f32[2,37,516]{2,1,0:T(8,128)S(1)}, u32[]{:S(2)}, u32[]{:S(2)}) %collective-permute-start.6) | collective-permute-done | bytes 152768 | tf_op jit(solution)/shard_map/ppermute | solution.py:145
  64.2 8.7 %collective-permute-done.5 = f32[2,36,516]{2,1,0:T(8,128)S(1)} collective-permute-done((f32[2,36,516]{2,1,0:T(8,128)S(1)}, f32[2,36,516]{2,1,0:T(8,128)S(1)}, u32[]{:S(2)}, u32[]{:S(2)}) %collective-permute-start.5) | collective-permute-done | bytes 148640 | tf_op jit(solution)/shard_map/ppermute | solution.py:145
  76.7 1.4 %subtract_bitcast_fusion = (f32[1,1,128,512]{3,2,1,0:T(8,128)S(1)}, f32[128,512]{1,0:T(8,128)}) fusion(f32[128,512]{1,0:T(8,128)S(1)} %copy-done, f32[130,514]{1,0:T(8,128)S(1)} %fusion.20, f32[134,518]{1,0:T(8,128)S(1)} %get-tuple-element.29, f32[132,516]{1,0:T(8,128)S(1)} %get-tuple-element.10), kind=kLoop, calls=%fused_computation.127 | loop fusion | flops 1441792 | bytes 3407872 | tf_op jit(solution)/shard_map/stack | solution.py:299
  78.2 1.0 %pad_maximum_fusion.4.parts_ref = bf16[3,2,128,512]{3,2,1,0:T(8,128)(2,1)} fusion(bf16[1,2,128,512]{3,2,1,0:T(8,128)(2,1)S(1)} %get-tuple-element.39, bf16[1,2,128,512]{3,2,1,0:T(8,128)(2,1)S(1)} %get-tuple-element.38, bf16[1,2,128,512]{3,2,1,0:T(8,128)(2,1)S(1)} %get-tuple-element.37), kind=kLoop, calls=%fused_computation.37 | loop fusion | flops 786432 | bytes 1572864 | tf_op jit(solution)/shard_map/stack | solution.py:238
  79.3 5.2 %shard_map.130 = f32[3,32,192]{2,1,0:T(8,128)} custom-call(s32[1,2048]{1,0:T(1,128)} %bitcast.104, s32[1,2048]{1,0:T(1,128)} %bitcast.103, bf16[3,2,128,512]{3,2,1,0:T(8,128)(2,1)} %pad_maximum_fusion.4.parts_ref, s32[1,2048]{1,0:T(1,128)} %bitcast.100, s32[2048,1]{1,0:T(8,128)} %copy.17.ranks_ref), custom_call_target="tpu_custom_call" | custom-call | tf_op jit(solution)/shard_map/pallas_call | solution.py:239
  84.5 1.0 copy.18
  85.5 10.1 %all_to_all.5 = f32[3,32,192]{2,0,1:T(4,128)S(1)} all-to-all(f32[3,32,192]{2,0,1:T(4,128)S(1)} %copy.18), channel_id=1, replica_groups=mesh['gx'=8,'gy'=4] {'gx','gy'}, dimensions={1} | all-to-all | bytes 147456 | tf_op jit(solution)/shard_map/all_to_all | solution.py:300
  96.3 1.1 %add_select_fusion = (f32[1,6144]{1,0:T(1,128)}, f32[1,6144]{1,0:T(1,128)S(1)}) fusion(pred[1,6144]{1,0:T(4,128)(4,1)S(1)} %gt.47, f32[1,6144]{1,0:T(1,128)S(1)} %copy-done.7, f32[2,1,6144]{2,1,0:T(1,128)S(1)} %copy-done.4, f32[1,6144]{1,0:T(1,128)S(1)} %squeeze.121, f32[1,6144]{1,0:T(1,128)S(1)} %squeeze.119), kind=kLoop, calls=%fused_computation.161 | loop fusion | flops 202752 | bytes 178176 | tf_op jit(solution)/shard_map/jit(_where)/select_n | solution.py:85
  (95 shorter events, 13.2 us)
Async XLA Ops:
  0.6 10.8 %copy-start = (f32[128,512]{1,0:T(8,128)S(1)}, f32[128,512]{1,0:T(8,128)}, u32[]{:S(2)}) copy-start(f32[128,512]{1,0:T(8,128)} %param.17) | copy-start | bytes 786436
  0.6 10.8 %copy-start.3 = (f32[128,512]{1,0:T(8,128)S(1)}, f32[128,512]{1,0:T(8,128)}, u32[]{:S(2)}) copy-start(f32[128,512]{1,0:T(8,128)} %param.16) | copy-start | bytes 786436
  0.7 16.9 %copy-start.6 = (f32[8]{0:T(128)S(1)}, f32[8]{0:T(128)}, u32[]{:S(2)}) copy-start(f32[8]{0:T(128)} %param.15) | copy-start | bytes 100
  0.7 17.6 %copy-start.5 = (s32[2048,1]{0,1:T(1,128)S(1)}, s32[2048,1]{0,1:T(1,128)}, u32[]{:S(2)}) copy-start(s32[2048,1]{0,1:T(1,128)} %param.19) | copy-start | bytes 24580
  0.7 18.4 %copy-start.8 = (s32[2048]{0:T(1024)S(1)}, s32[2048]{0:T(1024)}, u32[]{:S(2)}) copy-start(s32[2048]{0:T(1024)} %param.18) | copy-start | bytes 24580
  3.3 33.3 %copy-start.1 = (f32[8,32,2048]{2,1,0:T(8,128)S(1)}, f32[8,32,2048]{2,1,0:T(8,128)}, u32[]{:S(2)}) copy-start(f32[8,32,2048]{2,1,0:T(8,128)} %param.11) | copy-start | bytes 6291460
  4.3 17.6 %collective-permute-start = (f32[8,7,2048]{2,1,0:T(8,128)}, f32[8,7,2048]{2,1,0:T(8,128)S(1)}, u32[]{:S(2)}, u32[]{:S(2)}) collective-permute-start(f32[8,7,2048]{2,1,0:T(8,128)} %pad_maximum_fusion.6), channel_id=1, source_target_pairs={{0,1},{1,2},{2,3},{3,4},{4,5},{5,6},{6,7},{7,8},{8,9},{9,10},{10,1... | collective-permute-start | bytes 1376264 | tf_op jit(solution)/shard_map/ppermute | solution.py:25
  10.2 25.4 %collective-permute-start.1 = (f32[8,7,2048]{2,1,0:T(8,128)}, f32[8,7,2048]{2,1,0:T(8,128)}, u32[]{:S(2)}, u32[]{:S(2)}) collective-permute-start(f32[8,7,2048]{2,1,0:T(8,128)} %pad_maximum_fusion.7), channel_id=1, source_target_pairs={{1,0},{2,1},{3,2},{4,3},{5,4},{6,5},{7,6},{8,7},{9,8},{10,9},{11,1... | collective-permute-start | bytes 1376264 | tf_op jit(solution)/shard_map/ppermute | solution.py:25
  11.5 8.2 %collective-permute-start.2 = (f32[2,3,512]{2,1,0:T(4,128)S(1)}, f32[2,3,512]{2,1,0:T(4,128)S(1)}, u32[]{:S(2)}, u32[]{:S(2)}) collective-permute-start(f32[2,3,512]{2,1,0:T(4,128)S(1)} %get-tuple-element.40), channel_id=1, source_target_pairs={{0,4},{4,8},{8,12},{12,16},{16,20},{20,24},{24,28},{1,5},{5,9},{9,... | collective-permute-start | bytes 36872 | tf_op jit(solution)/shard_map/ppermute | solution.py:25
  16.2 4.9 %collective-permute-start.3 = (f32[2,3,512]{2,1,0:T(4,128)S(1)}, f32[2,3,512]{2,1,0:T(4,128)S(1)}, u32[]{:S(2)}, u32[]{:S(2)}) collective-permute-start(f32[2,3,512]{2,1,0:T(4,128)S(1)} %get-tuple-element.41), channel_id=1, source_target_pairs={{4,0},{8,4},{12,8},{16,12},{20,16},{24,20},{28,24},{5,1},{9,5},{13... | collective-permute-start | bytes 36872 | tf_op jit(solution)/shard_map/ppermute | solution.py:25
  36.7 0.7 copy-start.9
  37.4 1.8 %copy-start.2 = (f32[8,32,2048]{2,1,0:T(8,128)S(1)}, f32[8,32,2048]{2,1,0:T(8,128)}, u32[]{:S(2)}) copy-start(f32[8,32,2048]{2,1,0:T(8,128)} %param.12) | copy-start | bytes 6291460
  37.4 1.8 %copy-start.10 = (f32[8]{0:T(128)S(1)}, f32[8]{0:T(128)}, u32[]{:S(2)}) copy-start(f32[8]{0:T(128)} %param.13) | copy-start | bytes 100
  50.9 9.8 %collective-permute-start.4 = (f32[2,37,516]{2,1,0:T(8,128)S(1)}, f32[2,37,516]{2,1,0:T(8,128)S(1)}, u32[]{:S(2)}, u32[]{:S(2)}) collective-permute-start(f32[2,37,516]{2,1,0:T(8,128)S(1)} %pad_maximum_fusion.11), channel_id=1, source_target_pairs={{0,1},{1,2},{2,3},{3,0},{4,5},{5,6},{6,7},{7,4},{8,9},{9,10},{10,1... | collective-permute-start | bytes 458216 | tf_op jit(solution)/shard_map/ppermute | solution.py:145
  53.2 11.0 %collective-permute-start.6 = (f32[2,37,516]{2,1,0:T(8,128)S(1)}, f32[2,37,516]{2,1,0:T(8,128)S(1)}, u32[]{:S(2)}, u32[]{:S(2)}) collective-permute-start(f32[2,37,516]{2,1,0:T(8,128)S(1)} %pad_maximum_fusion.12), channel_id=1, source_target_pairs={{0,3},{1,0},{2,1},{3,2},{4,7},{5,4},{6,5},{7,6},{8,11},{9,8},{10,9... | collective-permute-start | bytes 458216 | tf_op jit(solution)/shard_map/ppermute | solution.py:145
  56.7 16.2 %collective-permute-start.5 = (f32[2,36,516]{2,1,0:T(8,128)S(1)}, f32[2,36,516]{2,1,0:T(8,128)S(1)}, u32[]{:S(2)}, u32[]{:S(2)}) collective-permute-start(f32[2,36,516]{2,1,0:T(8,128)S(1)} %get-tuple-element.27), channel_id=1, source_target_pairs={{0,2},{1,3},{2,0},{3,1},{4,6},{5,7},{6,4},{7,5},{8,10},{9,11},{10,... | collective-permute-start | bytes 445832 | tf_op jit(solution)/shard_map/ppermute | solution.py:145
  78.1 18.2 %copy-start.4 = (f32[2,1,6144]{2,1,0:T(1,128)S(1)}, f32[2,1,6144]{2,1,0:T(1,128)}, u32[]{:S(2)}) copy-start(f32[2,1,6144]{2,1,0:T(1,128)} %param.20) | copy-start | bytes 147460
  78.1 18.2 %copy-start.7 = (f32[1,6144]{1,0:T(1,128)S(1)}, f32[1,6144]{1,0:T(1,128)}, u32[]{:S(2)}) copy-start(f32[1,6144]{1,0:T(1,128)} %param.21) | copy-start | bytes 73732

commit v12 on v11

--- a/solution.py
+++ b/solution.py
@@ -215,18 +215,19 @@
         picked.append(jnp.concatenate(got, axis=0))
     values = jnp.concatenate(picked, axis=1)
     mine = lax.broadcasted_iota(jnp.int32, (devices, count), 0) == owners_ref[...]
-    slot = lax.broadcasted_iota(jnp.int32, (count, cap), 1) == ranks_ref[...]
+    slot = lax.broadcasted_iota(jnp.int32, (cap, count), 0) == ranks_ref[...]
     at = jnp.where(slot, 1.0, 0.0).astype(jnp.bfloat16)
+    over_joints = (((1,), (1,)), ((), ()))
     split = split3(values)
     for f in range(fields):
         acc = None
         for part in split:
             spread = jnp.where(mine, part[f: f + 1, :], 0.0).astype(jnp.bfloat16)
-            term = jnp.dot(spread, at, preferred_element_type=jnp.float32)
+            term = lax.dot_general(spread, at, over_joints, preferred_element_type=jnp.float32)
             acc = term if acc is None else acc + term
         out_ref[f] = acc
     live = jnp.where(mine, 1.0, 0.0).astype(jnp.bfloat16)
-    out_ref[fields] = jnp.dot(live, at, preferred_element_type=jnp.float32)
+    out_ref[fields] = lax.dot_general(live, at, over_joints, preferred_element_type=jnp.float32)
 
 
 def route_joints(fields, cells, owners, ranks, devices, cap):
@@ -244,7 +245,7 @@
         (cells % cm).astype(jnp.int32)[None, :],
         parts,
         owners[None, :].astype(jnp.int32),
-        ranks[:, None].astype(jnp.int32),
+        ranks[None, :].astype(jnp.int32),
     )
 
 

time: 98.7 us -> 97.7 us (0.990)
  local copies, waits for them, and re-layouts: 11.6 us -> 10.2 us
    sub x1 -> x0, local copies, waits for them, and re-layouts: 1.35 us -> none  [joint_ranks(): return jnp.sum(cum * onehot, axis=1).astype(jnp.int32) - 1]
where the time goes in v12:
time: 97.7 us; the launch traced here: 97.2 us
  waiting for transfers between devices  31.3 us (32%)
  other arithmetic  22.4 us (23%)
  starting transfers between devices  16.3 us (17%)
  local copies, waits for them, and re-layouts  10.2 us (10%)
  blocking collectives  10.1 us (10%)
  Pallas kernels  5.4 us (6%)
  between operations  1.16 us (1%)
    ppermute x3, waiting for transfers between devices, relay(): lax.ppermute(piece, 'gy', [(j, (j + shift) % n_gy) for j in range(n_gy)])  16.4 us
    ppermute x4, waiting for transfers between devices, exchange(): return (lax.ppermute(last, axis, up), lax.ppermute(leading, axis, down))  14.9 us
    ppermute x4, starting transfers between devices, exchange(): return (lax.ppermute(last, axis, up), lax.ppermute(leading, axis, down))  12.2 us
    all_to_all x1, blocking collectives, body(): lax.all_to_all(outgoing, FLAT, split_axis=1, concat_axis=1, tiled=True)  10.1 us
    pallas_call x1, Pallas kernels, route_joints(): pl.pallas_call(joints_kernel, out_shape=jax.ShapeDtypeStruct((nf + 1, dev...  5.4 us
    add x1, other arithmetic, moment_of(): total = total + weighting[layer] * field[layer]  5.24 us
    ppermute x3, starting transfers between devices, relay(): lax.ppermute(piece, 'gy', [(j, (j + shift) % n_gy) for j in range(n_gy)])  4.11 us
    concatenate x1, other arithmetic, thermal(): heat_ext = jnp.concatenate([before[:, h:], heat, after[:, h:]], axis=1)  2.86 us
  transfers between devices with their start and end apart: 7, of which 6 were waited for; matrix products, arithmetic and copies ran while one was open for 5% of the time, Pallas kernels for 0%

profile of v12, /device:TPU:0, one launch (start us, length us, event | category | flops | bytes accessed | tf_op | source)
XLA Modules:
  0.0 97.2 jit_solution(6200894319901161633)
XLA Ops:
  0.7 1.3 %fusion.87 = (f32[8,4,2048]{2,1,0:T(4,128)S(1)}, f32[8,4,2048]{2,1,0:T(4,128)S(1)}) fusion(f32[8,32,2048]{2,1,0:T(8,128)} %param.11), kind=kLoop, calls=%fused_computation.222 | loop fusion | bytes 1048576 | tf_op jit(solution)/shard_map/slice | solution.py:108
  2.0 1.3 %fusion.88 = (f32[8,3,2048]{2,1,0:T(4,128)S(1)}, f32[8,3,2048]{2,1,0:T(4,128)S(1)}) fusion(f32[8,32,2048]{2,1,0:T(8,128)} %param.12), kind=kLoop, calls=%fused_computation.223 | loop fusion | bytes 786432 | tf_op jit(solution)/shard_map/slice | solution.py:108
  3.4 0.9 pad_maximum_fusion.6
  4.3 5.0 %collective-permute-start = (f32[8,7,2048]{2,1,0:T(8,128)}, f32[8,7,2048]{2,1,0:T(8,128)S(1)}, u32[]{:S(2)}, u32[]{:S(2)}) collective-permute-start(f32[8,7,2048]{2,1,0:T(8,128)} %pad_maximum_fusion.6), channel_id=1, source_target_pairs={{0,1},{1,2},{2,3},{3,4},{4,5},{5,6},{6,7},{7,8},{8,9},{9,10},{10,1... | collective-permute-start | bytes 1376264 | tf_op jit(solution)/shard_map/ppermute | solution.py:25
  10.2 1.3 %collective-permute-start.1 = (f32[8,7,2048]{2,1,0:T(8,128)}, f32[8,7,2048]{2,1,0:T(8,128)}, u32[]{:S(2)}, u32[]{:S(2)}) collective-permute-start(f32[8,7,2048]{2,1,0:T(8,128)} %pad_maximum_fusion.7), channel_id=1, source_target_pairs={{1,0},{2,1},{3,2},{4,3},{5,4},{6,5},{7,6},{8,7},{9,8},{10,9},{11,1... | collective-permute-start | bytes 1376264 | tf_op jit(solution)/shard_map/ppermute | solution.py:25
  11.5 4.6 %collective-permute-start.2 = (f32[2,3,512]{2,1,0:T(4,128)S(1)}, f32[2,3,512]{2,1,0:T(4,128)S(1)}, u32[]{:S(2)}, u32[]{:S(2)}) collective-permute-start(f32[2,3,512]{2,1,0:T(4,128)S(1)} %get-tuple-element.40), channel_id=1, source_target_pairs={{0,4},{4,8},{8,12},{12,16},{16,20},{20,24},{24,28},{1,5},{5,9},{9,... | collective-permute-start | bytes 36872 | tf_op jit(solution)/shard_map/ppermute | solution.py:25
  16.2 1.3 %collective-permute-start.3 = (f32[2,3,512]{2,1,0:T(4,128)S(1)}, f32[2,3,512]{2,1,0:T(4,128)S(1)}, u32[]{:S(2)}, u32[]{:S(2)}) collective-permute-start(f32[2,3,512]{2,1,0:T(4,128)S(1)} %get-tuple-element.41), channel_id=1, source_target_pairs={{4,0},{8,4},{12,8},{16,12},{20,16},{24,20},{28,24},{5,1},{9,5},{13... | collective-permute-start | bytes 36872 | tf_op jit(solution)/shard_map/ppermute | solution.py:25
  21.9 13.7 %collective-permute-done.1 = f32[8,7,2048]{2,1,0:T(8,128)} collective-permute-done((f32[8,7,2048]{2,1,0:T(8,128)}, f32[8,7,2048]{2,1,0:T(8,128)}, u32[]{:S(2)}, u32[]{:S(2)}) %collective-permute-start.1) | collective-permute-done | bytes 458784 | tf_op jit(solution)/shard_map/ppermute | solution.py:25
  35.6 1.1 %slice.418 = f32[8,4,2048]{2,1,0:T(4,128)S(1)} slice(f32[8,7,2048]{2,1,0:T(8,128)} %collective-permute-done.1), slice={[0:8], [0:4], [0:2048]} | slice | bytes 524288 | tf_op jit(solution)/shard_map/slice | solution.py:111
  37.9 1.2 %slice.425 = f32[8,3,2048]{2,1,0:T(4,128)S(1)} slice(f32[8,7,2048]{2,1,0:T(8,128)} %collective-permute-done.1), slice={[0:8], [4:7], [0:2048]} | slice | bytes 393216 | tf_op jit(solution)/shard_map/slice | solution.py:112
  39.1 2.9 %pad_maximum_fusion.1 = (f32[8,38,2048]{2,1,0:T(8,128)S(1)}, f32[8,38,2048]{2,1,0:T(8,128)S(1)}) fusion(f32[8,3,2048]{2,1,0:T(4,128)S(1)} %slice.425, f32[8,32,2048]{2,1,0:T(8,128)S(1)} %copy-done.2, f32[8,3,2048]{2,1,0:T(4,128)S(1)} %slice.424, f32[7,38,2048]{2,1,0:T(8,128)S(1)} %fusion.16, f32[8,40,2048]{2,1,0:T(8,128)S(1)} %pad_maximum_fusion, ...), kind=kLoop, calls=%fused_computation.23 | loop fusion | flops 8093696 | bytes 20382720 | tf_op jit(solution)/shard_map/concatenate | solution.py:112
  42.5 2.6 %fusion.14 = f32[8,36,2048]{2,1,0:T(8,128)S(1)} fusion(f32[8,38,2048]{2,1,0:T(8,128)S(1)} %get-tuple-element.12, f32[8,38,2048]{2,1,0:T(8,128)S(1)} %get-tuple-element.11, f32[7,36,2048]{2,1,0:T(8,128)S(1)} %fusion.15, f32[8]{0:T(128)S(1)} %copy-done.10), kind=kLoop, calls=%fused_computation.19 | loop fusion | flops 5898240 | bytes 17760768 | tf_op jit(solution)/shard_map/add | solution.py:44
  45.1 5.2 %fusion.39 = f32[36,2048]{1,0:T(8,128)S(1)} fusion(f32[8,36,2048]{2,1,0:T(8,128)S(1)} %fusion.14, f32[]{:T(128)} %bitcast.7, f32[]{:T(128)} %bitcast.6, f32[]{:T(128)} %bitcast.5, f32[]{:T(128)} %bitcast.4, f32[]{:T(128)} %bitcast.3, f32[]{:T(128)} %bitcast.2, f32[]{:T(128)} %bitcast.1, f32[]{:T(128)} %bitcast), kind=kLoop, calls=%fused_computation.91 | loop fusion | flops 1105920 | bytes 2654240 | tf_op jit(solution)/shard_map/add | solution.py:50
  51.8 3.5 %collective-permute-start.6 = (f32[2,37,516]{2,1,0:T(8,128)S(1)}, f32[2,37,516]{2,1,0:T(8,128)S(1)}, u32[]{:S(2)}, u32[]{:S(2)}) collective-permute-start(f32[2,37,516]{2,1,0:T(8,128)S(1)} %pad_maximum_fusion.12), channel_id=1, source_target_pairs={{0,3},{1,0},{2,1},{3,2},{4,7},{5,4},{6,5},{7,6},{8,11},{9,8},{10,9... | collective-permute-start | bytes 458216 | tf_op jit(solution)/shard_map/ppermute | solution.py:145
  55.3 5.4 %collective-permute-done.4 = f32[2,37,516]{2,1,0:T(8,128)S(1)} collective-permute-done((f32[2,37,516]{2,1,0:T(8,128)S(1)}, f32[2,37,516]{2,1,0:T(8,128)S(1)}, u32[]{:S(2)}, u32[]{:S(2)}) %collective-permute-start.4) | collective-permute-done | bytes 152768 | tf_op jit(solution)/shard_map/ppermute | solution.py:145
  60.7 3.1 %collective-permute-done.6 = f32[2,37,516]{2,1,0:T(8,128)S(1)} collective-permute-done((f32[2,37,516]{2,1,0:T(8,128)S(1)}, f32[2,37,516]{2,1,0:T(8,128)S(1)}, u32[]{:S(2)}, u32[]{:S(2)}) %collective-permute-start.6) | collective-permute-done | bytes 152768 | tf_op jit(solution)/shard_map/ppermute | solution.py:145
  63.9 7.9 %collective-permute-done.5 = f32[2,36,516]{2,1,0:T(8,128)S(1)} collective-permute-done((f32[2,36,516]{2,1,0:T(8,128)S(1)}, f32[2,36,516]{2,1,0:T(8,128)S(1)}, u32[]{:S(2)}, u32[]{:S(2)}) %collective-permute-start.5) | collective-permute-done | bytes 148640 | tf_op jit(solution)/shard_map/ppermute | solution.py:145
  74.6 0.9 fusion.20
  75.5 1.4 %subtract_bitcast_fusion = (f32[1,1,128,512]{3,2,1,0:T(8,128)S(1)}, f32[128,512]{1,0:T(8,128)}) fusion(f32[128,512]{1,0:T(8,128)S(1)} %copy-done, f32[130,514]{1,0:T(8,128)S(1)} %fusion.20, f32[134,518]{1,0:T(8,128)S(1)} %get-tuple-element.29, f32[132,516]{1,0:T(8,128)S(1)} %get-tuple-element.10), kind=kLoop, calls=%fused_computation.127 | loop fusion | flops 1441792 | bytes 3407872 | tf_op jit(solution)/shard_map/stack | solution.py:300
  77.1 1.0 %pad_maximum_fusion.4.parts_ref = bf16[3,2,128,512]{3,2,1,0:T(8,128)(2,1)} fusion(bf16[1,2,128,512]{3,2,1,0:T(8,128)(2,1)S(1)} %get-tuple-element.39, bf16[1,2,128,512]{3,2,1,0:T(8,128)(2,1)S(1)} %get-tuple-element.38, bf16[1,2,128,512]{3,2,1,0:T(8,128)(2,1)S(1)} %get-tuple-element.37), kind=kLoop, calls=%fused_computation.37 | loop fusion | flops 786432 | bytes 1572864 | tf_op jit(solution)/shard_map/stack | solution.py:239
  78.1 5.4 %shard_map.130 = f32[3,32,192]{2,1,0:T(8,128)} custom-call(s32[1,2048]{1,0:T(1,128)} %bitcast.104, s32[1,2048]{1,0:T(1,128)} %bitcast.103, bf16[3,2,128,512]{3,2,1,0:T(8,128)(2,1)} %pad_maximum_fusion.4.parts_ref, s32[1,2048]{1,0:T(1,128)} %bitcast.100, s32[1,2048]{1,0:T(1,128)} %bitcast.105), custom_call_target="tpu_custom_call" | custom-call | tf_op jit(solution)/shard_map/pallas_call | solution.py:240
  83.5 1.0 copy.15
  84.4 10.1 %all_to_all.5 = f32[3,32,192]{2,0,1:T(4,128)S(1)} all-to-all(f32[3,32,192]{2,0,1:T(4,128)S(1)} %copy.15), channel_id=1, replica_groups=mesh['gx'=8,'gy'=4] {'gx','gy'}, dimensions={1} | all-to-all | bytes 147456 | tf_op jit(solution)/shard_map/all_to_all | solution.py:301
  95.4 1.1 %add_select_fusion = (f32[1,6144]{1,0:T(1,128)}, f32[1,6144]{1,0:T(1,128)S(1)}) fusion(pred[1,6144]{1,0:T(4,128)(4,1)S(1)} %gt.47, f32[1,6144]{1,0:T(1,128)S(1)} %copy-done.7, f32[2,1,6144]{2,1,0:T(1,128)S(1)} %copy-done.4, f32[1,6144]{1,0:T(1,128)S(1)} %squeeze.121, f32[1,6144]{1,0:T(1,128)S(1)} %squeeze.119), kind=kLoop, calls=%fused_computation.161 | loop fusion | flops 202752 | bytes 178176 | tf_op jit(solution)/shard_map/jit(_where)/select_n | solution.py:85
  (94 shorter events, 12.8 us)
Async XLA Ops:
  0.6 10.8 %copy-start = (f32[128,512]{1,0:T(8,128)S(1)}, f32[128,512]{1,0:T(8,128)}, u32[]{:S(2)}) copy-start(f32[128,512]{1,0:T(8,128)} %param.17) | copy-start | bytes 786436
  0.6 10.8 %copy-start.3 = (f32[128,512]{1,0:T(8,128)S(1)}, f32[128,512]{1,0:T(8,128)}, u32[]{:S(2)}) copy-start(f32[128,512]{1,0:T(8,128)} %param.16) | copy-start | bytes 786436
  0.7 16.9 %copy-start.6 = (f32[8]{0:T(128)S(1)}, f32[8]{0:T(128)}, u32[]{:S(2)}) copy-start(f32[8]{0:T(128)} %param.15) | copy-start | bytes 100
  0.7 17.6 %copy-start.5 = (s32[2048,1]{0,1:T(1,128)S(1)}, s32[2048,1]{0,1:T(1,128)}, u32[]{:S(2)}) copy-start(s32[2048,1]{0,1:T(1,128)} %param.19) | copy-start | bytes 24580
  0.7 18.9 %copy-start.8 = (s32[2048]{0:T(1024)S(1)}, s32[2048]{0:T(1024)}, u32[]{:S(2)}) copy-start(s32[2048]{0:T(1024)} %param.18) | copy-start | bytes 24580
  3.3 33.3 %copy-start.1 = (f32[8,32,2048]{2,1,0:T(8,128)S(1)}, f32[8,32,2048]{2,1,0:T(8,128)}, u32[]{:S(2)}) copy-start(f32[8,32,2048]{2,1,0:T(8,128)} %param.11) | copy-start | bytes 6291460
  4.3 17.6 %collective-permute-start = (f32[8,7,2048]{2,1,0:T(8,128)}, f32[8,7,2048]{2,1,0:T(8,128)S(1)}, u32[]{:S(2)}, u32[]{:S(2)}) collective-permute-start(f32[8,7,2048]{2,1,0:T(8,128)} %pad_maximum_fusion.6), channel_id=1, source_target_pairs={{0,1},{1,2},{2,3},{3,4},{4,5},{5,6},{6,7},{7,8},{8,9},{9,10},{10,1... | collective-permute-start | bytes 1376264 | tf_op jit(solution)/shard_map/ppermute | solution.py:25
  10.2 25.4 %collective-permute-start.1 = (f32[8,7,2048]{2,1,0:T(8,128)}, f32[8,7,2048]{2,1,0:T(8,128)}, u32[]{:S(2)}, u32[]{:S(2)}) collective-permute-start(f32[8,7,2048]{2,1,0:T(8,128)} %pad_maximum_fusion.7), channel_id=1, source_target_pairs={{1,0},{2,1},{3,2},{4,3},{5,4},{6,5},{7,6},{8,7},{9,8},{10,9},{11,1... | collective-permute-start | bytes 1376264 | tf_op jit(solution)/shard_map/ppermute | solution.py:25
  11.5 8.7 %collective-permute-start.2 = (f32[2,3,512]{2,1,0:T(4,128)S(1)}, f32[2,3,512]{2,1,0:T(4,128)S(1)}, u32[]{:S(2)}, u32[]{:S(2)}) collective-permute-start(f32[2,3,512]{2,1,0:T(4,128)S(1)} %get-tuple-element.40), channel_id=1, source_target_pairs={{0,4},{4,8},{8,12},{12,16},{16,20},{20,24},{24,28},{1,5},{5,9},{9,... | collective-permute-start | bytes 36872 | tf_op jit(solution)/shard_map/ppermute | solution.py:25
  16.2 4.9 %collective-permute-start.3 = (f32[2,3,512]{2,1,0:T(4,128)S(1)}, f32[2,3,512]{2,1,0:T(4,128)S(1)}, u32[]{:S(2)}, u32[]{:S(2)}) collective-permute-start(f32[2,3,512]{2,1,0:T(4,128)S(1)} %get-tuple-element.41), channel_id=1, source_target_pairs={{4,0},{8,4},{12,8},{16,12},{20,16},{24,20},{28,24},{5,1},{9,5},{13... | collective-permute-start | bytes 36872 | tf_op jit(solution)/shard_map/ppermute | solution.py:25
  36.7 0.7 copy-start.9
  37.4 1.8 %copy-start.2 = (f32[8,32,2048]{2,1,0:T(8,128)S(1)}, f32[8,32,2048]{2,1,0:T(8,128)}, u32[]{:S(2)}) copy-start(f32[8,32,2048]{2,1,0:T(8,128)} %param.12) | copy-start | bytes 6291460
  37.4 1.8 %copy-start.10 = (f32[8]{0:T(128)S(1)}, f32[8]{0:T(128)}, u32[]{:S(2)}) copy-start(f32[8]{0:T(128)} %param.13) | copy-start | bytes 100
  50.9 9.9 %collective-permute-start.4 = (f32[2,37,516]{2,1,0:T(8,128)S(1)}, f32[2,37,516]{2,1,0:T(8,128)S(1)}, u32[]{:S(2)}, u32[]{:S(2)}) collective-permute-start(f32[2,37,516]{2,1,0:T(8,128)S(1)} %pad_maximum_fusion.11), channel_id=1, source_target_pairs={{0,1},{1,2},{2,3},{3,0},{4,5},{5,6},{6,7},{7,4},{8,9},{9,10},{10,1... | collective-permute-start | bytes 458216 | tf_op jit(solution)/shard_map/ppermute | solution.py:145
  51.8 12.0 %collective-permute-start.6 = (f32[2,37,516]{2,1,0:T(8,128)S(1)}, f32[2,37,516]{2,1,0:T(8,128)S(1)}, u32[]{:S(2)}, u32[]{:S(2)}) collective-permute-start(f32[2,37,516]{2,1,0:T(8,128)S(1)} %pad_maximum_fusion.12), channel_id=1, source_target_pairs={{0,3},{1,0},{2,1},{3,2},{4,7},{5,4},{6,5},{7,6},{8,11},{9,8},{10,9... | collective-permute-start | bytes 458216 | tf_op jit(solution)/shard_map/ppermute | solution.py:145
  55.3 16.5 %collective-permute-start.5 = (f32[2,36,516]{2,1,0:T(8,128)S(1)}, f32[2,36,516]{2,1,0:T(8,128)S(1)}, u32[]{:S(2)}, u32[]{:S(2)}) collective-permute-start(f32[2,36,516]{2,1,0:T(8,128)S(1)} %get-tuple-element.27), channel_id=1, source_target_pairs={{0,2},{1,3},{2,0},{3,1},{4,6},{5,7},{6,4},{7,5},{8,10},{9,11},{10,... | collective-permute-start | bytes 445832 | tf_op jit(solution)/shard_map/ppermute | solution.py:145
  76.9 18.4 %copy-start.4 = (f32[2,1,6144]{2,1,0:T(1,128)S(1)}, f32[2,1,6144]{2,1,0:T(1,128)}, u32[]{:S(2)}) copy-start(f32[2,1,6144]{2,1,0:T(1,128)} %param.20) | copy-start | bytes 147460
  76.9 18.4 %copy-start.7 = (f32[1,6144]{1,0:T(1,128)S(1)}, f32[1,6144]{1,0:T(1,128)}, u32[]{:S(2)}) copy-start(f32[1,6144]{1,0:T(1,128)} %param.21) | copy-start | bytes 73732

commit v13 on v12

--- a/solution.py
+++ b/solution.py
@@ -128,10 +128,17 @@
     cm = cols // n_gy
     rows = rows - 2 * width
     lp = jnp.pad(load, ((0, 0), (width, width)))
-    tp = jnp.pad(top, ((width, width), (width, width)))
-    both = jnp.stack([lp, tp])
-    send = jnp.stack([both[:, :, k * cm: k * cm + cm + 2 * width] for k in range(n_gy)])
+    tp = jnp.pad(top, ((width, width), (0, 0)))
+    send = []
+    for k in range(n_gy):
+        main = jnp.stack([load[:, k * cm: (k + 1) * cm], tp[:, k * cm: (k + 1) * cm]])
+        halo = jnp.concatenate(
+            [lp[:, k * cm: k * cm + width], lp[:, (k + 1) * cm + width: (k + 1) * cm + 2 * width]],
+            axis=1)
+        send.append(jnp.concatenate([main, as_slab(halo, 2, cm)], axis=1))
+    send = jnp.stack(send)
     depth = send.shape[2]
+    full = load.shape[0]
     got = [lax.dynamic_index_in_dim(send, gj, 0, keepdims=False)]
     side_before = side_after = None
     for shift in range(1, n_gy):
@@ -160,13 +167,13 @@
     recv = jnp.take(jnp.stack(got), (gj - jnp.arange(n_gy)) % n_gy, axis=0)
     parts = []
     for k in range(n_gy):
+        halo = from_slab(recv[k, :, full:], (full, 2 * width))
+        window = jnp.concatenate([halo[:, :width], recv[k, 0, :full], halo[:, width:]], axis=1)
         lo = 0 if k == 0 else width
         hi = rows + 2 * width if k == n_gy - 1 else rows + width
-        parts.append(recv[k, 0, lo:hi])
+        parts.append(window[lo:hi])
     load_m = jnp.concatenate(parts, axis=0)
-    top_m = jnp.concatenate(
-        [recv[k, 1, width: rows + width, width: cm + width] for k in range(n_gy)], axis=0
-    )
+    top_m = jnp.concatenate([recv[k, 1, width: rows + width] for k in range(n_gy)], axis=0)
     return load_m, top_m, side_before, side_after
 
 

time: 97.7 us -> 97.1 us (level)
  waiting for transfers between devices: 31.3 us -> 27 us
  local copies, waits for them, and re-layouts: 10.2 us -> 12.3 us
  other arithmetic: 22.4 us -> 23.4 us
    ppermute x3, waiting for transfers between devices: 16.4 us -> 12 us  [relay(): lax.ppermute(piece, 'gy', [(j, (j + shift) % n_gy) for j in range(n_gy)])]
  transfers between devices with their start and end apart: 7 -> 7, of which waited for: 6 -> 6; matrix products, arithmetic and copies ran while one was open for 5% -> 4% of each run, Pallas kernels for 0% -> 0%
where the time goes in v13:
time: 97.1 us; the launch traced here: 96.6 us
  waiting for transfers between devices  27 us (28%)
  other arithmetic  23.4 us (24%)
  starting transfers between devices  16.3 us (17%)
  local copies, waits for them, and re-layouts  12.3 us (13%)
  blocking collectives  10.6 us (11%)
  Pallas kernels  5.4 us (6%)
  between operations  1.34 us (1%)
    ppermute x4, waiting for transfers between devices, exchange(): return (lax.ppermute(last, axis, up), lax.ppermute(leading, axis, down))  14.9 us
    ppermute x4, starting transfers between devices, exchange(): return (lax.ppermute(last, axis, up), lax.ppermute(leading, axis, down))  12.2 us
    ppermute x3, waiting for transfers between devices, relay(): lax.ppermute(piece, 'gy', [(j, (j + shift) % n_gy) for j in range(n_gy)])  12 us
    all_to_all x1, blocking collectives, body(): lax.all_to_all(outgoing, FLAT, split_axis=1, concat_axis=1, tiled=True)  10.6 us
    pallas_call x1, Pallas kernels, route_joints(): pl.pallas_call(joints_kernel, out_shape=jax.ShapeDtypeStruct((nf + 1, dev...  5.4 us
    add x1, other arithmetic, moment_of(): total = total + weighting[layer] * field[layer]  5.24 us
    ppermute x3, starting transfers between devices, relay(): lax.ppermute(piece, 'gy', [(j, (j + shift) % n_gy) for j in range(n_gy)])  4.11 us
    concatenate x1, other arithmetic, thermal(): heat_ext = jnp.concatenate([before[:, h:], heat, after[:, h:]], axis=1)  2.86 us
  transfers between devices with their start and end apart: 7, of which 6 were waited for; matrix products, arithmetic and copies ran while one was open for 4% of the time, Pallas kernels for 0%

profile of v13, /device:TPU:0, one launch (start us, length us, event | category | flops | bytes accessed | tf_op | source)
XLA Modules:
  0.0 96.6 jit_solution(15207097253766335260)
XLA Ops:
  0.7 1.3 %fusion.89 = (f32[8,4,2048]{2,1,0:T(4,128)S(1)}, f32[8,4,2048]{2,1,0:T(4,128)S(1)}) fusion(f32[8,32,2048]{2,1,0:T(8,128)} %param.11), kind=kLoop, calls=%fused_computation.245 | loop fusion | bytes 1048576 | tf_op jit(solution)/shard_map/slice | solution.py:108
  2.0 1.3 %fusion.90 = (f32[8,3,2048]{2,1,0:T(4,128)S(1)}, f32[8,3,2048]{2,1,0:T(4,128)S(1)}) fusion(f32[8,32,2048]{2,1,0:T(8,128)} %param.12), kind=kLoop, calls=%fused_computation.246 | loop fusion | bytes 786432 | tf_op jit(solution)/shard_map/slice | solution.py:108
  4.3 5.0 %collective-permute-start = (f32[8,7,2048]{2,1,0:T(8,128)}, f32[8,7,2048]{2,1,0:T(8,128)S(1)}, u32[]{:S(2)}, u32[]{:S(2)}) collective-permute-start(f32[8,7,2048]{2,1,0:T(8,128)} %pad_maximum_fusion.6), channel_id=1, source_target_pairs={{0,1},{1,2},{2,3},{3,4},{4,5},{5,6},{6,7},{7,8},{8,9},{9,10},{10,1... | collective-permute-start | bytes 1376264 | tf_op jit(solution)/shard_map/ppermute | solution.py:25
  10.2 1.3 %collective-permute-start.1 = (f32[8,7,2048]{2,1,0:T(8,128)}, f32[8,7,2048]{2,1,0:T(8,128)}, u32[]{:S(2)}, u32[]{:S(2)}) collective-permute-start(f32[8,7,2048]{2,1,0:T(8,128)} %pad_maximum_fusion.7), channel_id=1, source_target_pairs={{1,0},{2,1},{3,2},{4,3},{5,4},{6,5},{7,6},{8,7},{9,8},{10,9},{11,1... | collective-permute-start | bytes 1376264 | tf_op jit(solution)/shard_map/ppermute | solution.py:25
  11.5 4.6 %collective-permute-start.2 = (f32[2,3,512]{2,1,0:T(4,128)S(1)}, f32[2,3,512]{2,1,0:T(4,128)S(1)}, u32[]{:S(2)}, u32[]{:S(2)}) collective-permute-start(f32[2,3,512]{2,1,0:T(4,128)S(1)} %get-tuple-element.40), channel_id=1, source_target_pairs={{0,4},{4,8},{8,12},{12,16},{16,20},{20,24},{24,28},{1,5},{5,9},{9,... | collective-permute-start | bytes 36872 | tf_op jit(solution)/shard_map/ppermute | solution.py:25
  16.2 1.3 %collective-permute-start.3 = (f32[2,3,512]{2,1,0:T(4,128)S(1)}, f32[2,3,512]{2,1,0:T(4,128)S(1)}, u32[]{:S(2)}, u32[]{:S(2)}) collective-permute-start(f32[2,3,512]{2,1,0:T(4,128)S(1)} %get-tuple-element.41), channel_id=1, source_target_pairs={{4,0},{8,4},{12,8},{16,12},{20,16},{24,20},{28,24},{5,1},{9,5},{13... | collective-permute-start | bytes 36872 | tf_op jit(solution)/shard_map/ppermute | solution.py:25
  21.9 13.7 %collective-permute-done.1 = f32[8,7,2048]{2,1,0:T(8,128)} collective-permute-done((f32[8,7,2048]{2,1,0:T(8,128)}, f32[8,7,2048]{2,1,0:T(8,128)}, u32[]{:S(2)}, u32[]{:S(2)}) %collective-permute-start.1) | collective-permute-done | bytes 458784 | tf_op jit(solution)/shard_map/ppermute | solution.py:25
  35.6 1.1 %slice.558 = f32[8,4,2048]{2,1,0:T(4,128)S(1)} slice(f32[8,7,2048]{2,1,0:T(8,128)} %collective-permute-done.1), slice={[0:8], [0:4], [0:2048]} | slice | bytes 524288 | tf_op jit(solution)/shard_map/slice | solution.py:111
  37.9 1.2 %slice.565 = f32[8,3,2048]{2,1,0:T(4,128)S(1)} slice(f32[8,7,2048]{2,1,0:T(8,128)} %collective-permute-done.1), slice={[0:8], [4:7], [0:2048]} | slice | bytes 393216 | tf_op jit(solution)/shard_map/slice | solution.py:112
  39.1 2.9 %pad_maximum_fusion.1 = (f32[8,38,2048]{2,1,0:T(8,128)S(1)}, f32[8,38,2048]{2,1,0:T(8,128)S(1)}) fusion(f32[8,3,2048]{2,1,0:T(4,128)S(1)} %slice.565, f32[8,32,2048]{2,1,0:T(8,128)S(1)} %copy-done.2, f32[8,3,2048]{2,1,0:T(4,128)S(1)} %slice.564, f32[7,38,2048]{2,1,0:T(8,128)S(1)} %fusion.16, f32[8,40,2048]{2,1,0:T(8,128)S(1)} %pad_maximum_fusion, ...), kind=kLoop, calls=%fused_computation.23 | loop fusion | flops 8093696 | bytes 20382720 | tf_op jit(solution)/shard_map/concatenate | solution.py:112
  42.5 2.6 %fusion.14 = f32[8,36,2048]{2,1,0:T(8,128)S(1)} fusion(f32[8,38,2048]{2,1,0:T(8,128)S(1)} %get-tuple-element.16, f32[8,38,2048]{2,1,0:T(8,128)S(1)} %get-tuple-element.15, f32[7,36,2048]{2,1,0:T(8,128)S(1)} %fusion.15, f32[8]{0:T(128)S(1)} %copy-done.10), kind=kLoop, calls=%fused_computation.19 | loop fusion | flops 5898240 | bytes 17760768 | tf_op jit(solution)/shard_map/add | solution.py:44
  45.1 5.2 %fusion.44 = f32[36,2048]{1,0:T(8,128)S(1)} fusion(f32[8,36,2048]{2,1,0:T(8,128)S(1)} %fusion.14, f32[]{:T(128)} %bitcast.7, f32[]{:T(128)} %bitcast.6, f32[]{:T(128)} %bitcast.5, f32[]{:T(128)} %bitcast.4, f32[]{:T(128)} %bitcast.3, f32[]{:T(128)} %bitcast.2, f32[]{:T(128)} %bitcast.1, f32[]{:T(128)} %bitcast), kind=kLoop, calls=%fused_computation.105 | loop fusion | flops 1105920 | bytes 2654240 | tf_op jit(solution)/shard_map/add | solution.py:50
  53.5 3.5 %collective-permute-start.6 = (f32[2,38,512]{2,0,1:T(2,128)S(1)}, f32[2,38,512]{2,0,1:T(2,128)S(1)}, u32[]{:S(2)}, u32[]{:S(2)}) collective-permute-start(f32[2,38,512]{2,0,1:T(2,128)S(1)} %pad_maximum_fusion.10), channel_id=1, source_target_pairs={{0,3},{1,0},{2,1},{3,2},{4,7},{5,4},{6,5},{7,6},{8,11},{9,8},{10,9... | collective-permute-start | bytes 466952 | tf_op jit(solution)/shard_map/ppermute | solution.py:152
  57.0 4.4 %collective-permute-done.4 = f32[2,38,512]{2,0,1:T(2,128)S(1)} collective-permute-done((f32[2,38,512]{2,0,1:T(2,128)S(1)}, f32[2,38,512]{2,0,1:T(2,128)S(1)}, u32[]{:S(2)}, u32[]{:S(2)}) %collective-permute-start.4) | collective-permute-done | bytes 155680 | tf_op jit(solution)/shard_map/ppermute | solution.py:152
  61.3 2.0 %collective-permute-done.6 = f32[2,38,512]{2,0,1:T(2,128)S(1)} collective-permute-done((f32[2,38,512]{2,0,1:T(2,128)S(1)}, f32[2,38,512]{2,0,1:T(2,128)S(1)}, u32[]{:S(2)}, u32[]{:S(2)}) %collective-permute-start.6) | collective-permute-done | bytes 155680 | tf_op jit(solution)/shard_map/ppermute | solution.py:152
  63.4 5.6 %collective-permute-done.5 = f32[2,37,512]{2,0,1:T(2,128)S(1)} collective-permute-done((f32[2,37,512]{2,0,1:T(2,128)S(1)}, f32[2,37,512]{2,0,1:T(2,128)S(1)}, u32[]{:S(2)}, u32[]{:S(2)}) %collective-permute-start.5) | collective-permute-done | bytes 151584 | tf_op jit(solution)/shard_map/ppermute | solution.py:152
  69.4 1.2 %gather_fusion = f32[4,2,37,512]{3,1,2,0:T(2,128)S(1)} fusion(f32[4,2,37,512]{3,1,2,0:T(2,128)S(1)} %pad_maximum_fusion.5, s32[1024]{0:T(1024)S(1)} %pad_clamp_fusion), kind=kCustom, calls=%fused_computation | custom fusion | bytes 1212432 | tf_op jit(solution)/shard_map/jit(_take)/gather | solution.py:167
  73.5 0.9 fusion.20
  74.5 1.4 %subtract_bitcast_fusion = (f32[1,1,128,512]{3,2,1,0:T(8,128)S(1)}, f32[128,512]{1,0:T(8,128)}) fusion(f32[128,512]{1,0:T(8,128)S(1)} %copy-done, f32[130,514]{1,0:T(8,128)S(1)} %fusion.20, f32[134,518]{1,0:T(8,128)S(1)} %get-tuple-element.21, f32[132,516]{1,0:T(8,128)S(1)} %get-tuple-element.14), kind=kLoop, calls=%fused_computation.141 | loop fusion | flops 1441792 | bytes 3407872 | tf_op jit(solution)/shard_map/stack | solution.py:307
  76.0 1.0 %pad_maximum_fusion.2.parts_ref = bf16[3,2,128,512]{3,2,1,0:T(8,128)(2,1)} fusion(bf16[1,2,128,512]{3,2,1,0:T(8,128)(2,1)S(1)} %get-tuple-element.39, bf16[1,2,128,512]{3,2,1,0:T(8,128)(2,1)S(1)} %get-tuple-element.38, bf16[1,2,128,512]{3,2,1,0:T(8,128)(2,1)S(1)} %get-tuple-element.37), kind=kLoop, calls=%fused_computation.29 | loop fusion | flops 786432 | bytes 1572864 | tf_op jit(solution)/shard_map/stack | solution.py:246
  77.0 5.4 %shard_map.130 = f32[3,32,192]{2,1,0:T(8,128)} custom-call(s32[1,2048]{1,0:T(1,128)} %bitcast.125, s32[1,2048]{1,0:T(1,128)} %bitcast.124, bf16[3,2,128,512]{3,2,1,0:T(8,128)(2,1)} %pad_maximum_fusion.2.parts_ref, s32[1,2048]{1,0:T(1,128)} %bitcast.121, s32[1,2048]{1,0:T(1,128)} %bitcast.126), custom_call_target="tpu_custom_call" | custom-call | tf_op jit(solution)/shard_map/pallas_call | solution.py:247
  82.4 1.0 copy.48
  83.4 10.6 %all_to_all.5 = f32[3,32,192]{2,0,1:T(4,128)S(1)} all-to-all(f32[3,32,192]{2,0,1:T(4,128)S(1)} %copy.48), channel_id=1, replica_groups=mesh['gx'=8,'gy'=4] {'gx','gy'}, dimensions={1} | all-to-all | bytes 147456 | tf_op jit(solution)/shard_map/all_to_all | solution.py:308
  94.7 1.1 %add_select_fusion = (f32[1,6144]{1,0:T(1,128)}, f32[1,6144]{1,0:T(1,128)S(1)}) fusion(pred[1,6144]{1,0:T(4,128)(4,1)S(1)} %gt.47, f32[1,6144]{1,0:T(1,128)S(1)} %copy-done.7, f32[2,1,6144]{2,1,0:T(1,128)S(1)} %copy-done.4, f32[1,6144]{1,0:T(1,128)S(1)} %squeeze.121, f32[1,6144]{1,0:T(1,128)S(1)} %squeeze.119), kind=kLoop, calls=%fused_computation.178 | loop fusion | flops 202752 | bytes 178176 | tf_op jit(solution)/shard_map/jit(_where)/select_n | solution.py:85
  (124 shorter events, 15.6 us)
Async XLA Ops:
  0.6 10.8 %copy-start = (f32[128,512]{1,0:T(8,128)S(1)}, f32[128,512]{1,0:T(8,128)}, u32[]{:S(2)}) copy-start(f32[128,512]{1,0:T(8,128)} %param.17) | copy-start | bytes 786436
  0.6 10.8 %copy-start.3 = (f32[128,512]{1,0:T(8,128)S(1)}, f32[128,512]{1,0:T(8,128)}, u32[]{:S(2)}) copy-start(f32[128,512]{1,0:T(8,128)} %param.16) | copy-start | bytes 786436
  0.7 16.9 %copy-start.6 = (f32[8]{0:T(128)S(1)}, f32[8]{0:T(128)}, u32[]{:S(2)}) copy-start(f32[8]{0:T(128)} %param.15) | copy-start | bytes 100
  0.7 17.6 %copy-start.5 = (s32[2048,1]{0,1:T(1,128)S(1)}, s32[2048,1]{0,1:T(1,128)}, u32[]{:S(2)}) copy-start(s32[2048,1]{0,1:T(1,128)} %param.19) | copy-start | bytes 24580
  0.7 18.9 %copy-start.8 = (s32[2048]{0:T(1024)S(1)}, s32[2048]{0:T(1024)}, u32[]{:S(2)}) copy-start(s32[2048]{0:T(1024)} %param.18) | copy-start | bytes 24580
  3.3 33.3 %copy-start.1 = (f32[8,32,2048]{2,1,0:T(8,128)S(1)}, f32[8,32,2048]{2,1,0:T(8,128)}, u32[]{:S(2)}) copy-start(f32[8,32,2048]{2,1,0:T(8,128)} %param.11) | copy-start | bytes 6291460
  4.3 17.6 %collective-permute-start = (f32[8,7,2048]{2,1,0:T(8,128)}, f32[8,7,2048]{2,1,0:T(8,128)S(1)}, u32[]{:S(2)}, u32[]{:S(2)}) collective-permute-start(f32[8,7,2048]{2,1,0:T(8,128)} %pad_maximum_fusion.6), channel_id=1, source_target_pairs={{0,1},{1,2},{2,3},{3,4},{4,5},{5,6},{6,7},{7,8},{8,9},{9,10},{10,1... | collective-permute-start | bytes 1376264 | tf_op jit(solution)/shard_map/ppermute | solution.py:25
  10.2 25.4 %collective-permute-start.1 = (f32[8,7,2048]{2,1,0:T(8,128)}, f32[8,7,2048]{2,1,0:T(8,128)}, u32[]{:S(2)}, u32[]{:S(2)}) collective-permute-start(f32[8,7,2048]{2,1,0:T(8,128)} %pad_maximum_fusion.7), channel_id=1, source_target_pairs={{1,0},{2,1},{3,2},{4,3},{5,4},{6,5},{7,6},{8,7},{9,8},{10,9},{11,1... | collective-permute-start | bytes 1376264 | tf_op jit(solution)/shard_map/ppermute | solution.py:25
  11.5 8.7 %collective-permute-start.2 = (f32[2,3,512]{2,1,0:T(4,128)S(1)}, f32[2,3,512]{2,1,0:T(4,128)S(1)}, u32[]{:S(2)}, u32[]{:S(2)}) collective-permute-start(f32[2,3,512]{2,1,0:T(4,128)S(1)} %get-tuple-element.40), channel_id=1, source_target_pairs={{0,4},{4,8},{8,12},{12,16},{16,20},{20,24},{24,28},{1,5},{5,9},{9,... | collective-permute-start | bytes 36872 | tf_op jit(solution)/shard_map/ppermute | solution.py:25
  16.2 4.9 %collective-permute-start.3 = (f32[2,3,512]{2,1,0:T(4,128)S(1)}, f32[2,3,512]{2,1,0:T(4,128)S(1)}, u32[]{:S(2)}, u32[]{:S(2)}) collective-permute-start(f32[2,3,512]{2,1,0:T(4,128)S(1)} %get-tuple-element.41), channel_id=1, source_target_pairs={{4,0},{8,4},{12,8},{16,12},{20,16},{24,20},{28,24},{5,1},{9,5},{13... | collective-permute-start | bytes 36872 | tf_op jit(solution)/shard_map/ppermute | solution.py:25
  36.7 0.7 copy-start.9
  37.4 1.8 %copy-start.2 = (f32[8,32,2048]{2,1,0:T(8,128)S(1)}, f32[8,32,2048]{2,1,0:T(8,128)}, u32[]{:S(2)}) copy-start(f32[8,32,2048]{2,1,0:T(8,128)} %param.12) | copy-start | bytes 6291460
  37.4 1.8 %copy-start.10 = (f32[8]{0:T(128)S(1)}, f32[8]{0:T(128)}, u32[]{:S(2)}) copy-start(f32[8]{0:T(128)} %param.13) | copy-start | bytes 100
  52.5 8.8 %collective-permute-start.4 = (f32[2,38,512]{2,0,1:T(2,128)S(1)}, f32[2,38,512]{2,0,1:T(2,128)S(1)}, u32[]{:S(2)}, u32[]{:S(2)}) collective-permute-start(f32[2,38,512]{2,0,1:T(2,128)S(1)} %pad_maximum_fusion.9), channel_id=1, source_target_pairs={{0,1},{1,2},{2,3},{3,0},{4,5},{5,6},{6,7},{7,4},{8,9},{9,10},{10,1... | collective-permute-start | bytes 466952 | tf_op jit(solution)/shard_map/ppermute | solution.py:152
  53.5 9.9 %collective-permute-start.6 = (f32[2,38,512]{2,0,1:T(2,128)S(1)}, f32[2,38,512]{2,0,1:T(2,128)S(1)}, u32[]{:S(2)}, u32[]{:S(2)}) collective-permute-start(f32[2,38,512]{2,0,1:T(2,128)S(1)} %pad_maximum_fusion.10), channel_id=1, source_target_pairs={{0,3},{1,0},{2,1},{3,2},{4,7},{5,4},{6,5},{7,6},{8,11},{9,8},{10,9... | collective-permute-start | bytes 466952 | tf_op jit(solution)/shard_map/ppermute | solution.py:152
  57.0 12.1 %collective-permute-start.5 = (f32[2,37,512]{2,0,1:T(2,128)S(1)}, f32[2,37,512]{2,0,1:T(2,128)S(1)}, u32[]{:S(2)}, u32[]{:S(2)}) collective-permute-start(f32[2,37,512]{2,0,1:T(2,128)S(1)} %get-tuple-element.33), channel_id=1, source_target_pairs={{0,2},{1,3},{2,0},{3,1},{4,6},{5,7},{6,4},{7,5},{8,10},{9,11},{10,... | collective-permute-start | bytes 454664 | tf_op jit(solution)/shard_map/ppermute | solution.py:152
  75.9 18.9 %copy-start.4 = (f32[2,1,6144]{2,1,0:T(1,128)S(1)}, f32[2,1,6144]{2,1,0:T(1,128)}, u32[]{:S(2)}) copy-start(f32[2,1,6144]{2,1,0:T(1,128)} %param.20) | copy-start | bytes 147460
  75.9 18.9 %copy-start.7 = (f32[1,6144]{1,0:T(1,128)S(1)}, f32[1,6144]{1,0:T(1,128)}, u32[]{:S(2)}) copy-start(f32[1,6144]{1,0:T(1,128)} %param.21) | copy-start | bytes 73732

commit v14 on v13

--- a/solution.py
+++ b/solution.py
@@ -107,7 +107,8 @@
     hh = h - 1
     last = jnp.concatenate([temp[:, rows - h:], heat[:, rows - hh:]], axis=1)
     leading = jnp.concatenate([temp[:, :h], heat[:, :hh]], axis=1)
-    before, after = exchange(last, leading, FLAT)
+    before, after = exchange(last.transpose(1, 0, 2), leading.transpose(1, 0, 2), FLAT)
+    before, after = before.transpose(1, 0, 2), after.transpose(1, 0, 2)
     ext = jnp.concatenate([before[:, :h], temp, after[:, :h]], axis=1)
     heat_ext = jnp.concatenate([before[:, h:], heat, after[:, h:]], axis=1)
     for step in range(1, STEPS + 1):

time: 97.1 us -> 97.6 us (level)
  local copies, waits for them, and re-layouts: 12.3 us -> 15.4 us
  waiting for transfers between devices: 27 us -> 24.6 us
    ppermute x4, waiting for transfers between devices: 14.9 us -> 12.6 us  [exchange(): return (lax.ppermute(last, axis, up), lax.ppermute(leading, axis, down))]
    concatenate x2 -> x0, other arithmetic: 1.84 us -> none  [the longest x1 0.93 us: thermal(): last = jnp.concatenate([temp[:, rows - h:], heat[:, rows - hh:]], axis=1)]
    unnamed x26, local copies, waits for them, and re-layouts: 0.27 us -> 1.4 us
    slice x2, local copies, waits for them, and re-layouts: 1.13 us -> 2.18 us  [thermal(): ext = jnp.concatenate([before[:, :h], temp, after[:, :h]], axis=1)]
    transpose x0 -> x2, other arithmetic: none -> 1.02 us  [the longest x1 0.9 us: thermal(): leading.transpose(1, 0, 2)]
  transfers between devices with their start and end apart: 7 -> 7, of which waited for: 6 -> 6; matrix products, arithmetic and copies ran while one was open for 4% -> 7% of each run, Pallas kernels for 0% -> 0%
where the time goes in v14:
time: 97.6 us; the launch traced here: 97 us
  waiting for transfers between devices  24.6 us (25%)
  other arithmetic  22.5 us (23%)
  starting transfers between devices  16.3 us (17%)
  local copies, waits for them, and re-layouts  15.4 us (16%)
  blocking collectives  11.1 us (11%)
  Pallas kernels  5.4 us (6%)
  between operations  1.32 us (1%)
    ppermute x4, waiting for transfers between devices, exchange(): return (lax.ppermute(last, axis, up), lax.ppermute(leading, axis, down))  12.6 us
    ppermute x4, starting transfers between devices, exchange(): return (lax.ppermute(last, axis, up), lax.ppermute(leading, axis, down))  12.2 us
    ppermute x3, waiting for transfers between devices, relay(): lax.ppermute(piece, 'gy', [(j, (j + shift) % n_gy) for j in range(n_gy)])  12 us
    all_to_all x1, blocking collectives, body(): lax.all_to_all(outgoing, FLAT, split_axis=1, concat_axis=1, tiled=True)  11.1 us
    pallas_call x1, Pallas kernels, route_joints(): pl.pallas_call(joints_kernel, out_shape=jax.ShapeDtypeStruct((nf + 1, dev...  5.4 us
    add x1, other arithmetic, moment_of(): total = total + weighting[layer] * field[layer]  5.24 us
    ppermute x3, starting transfers between devices, relay(): lax.ppermute(piece, 'gy', [(j, (j + shift) % n_gy) for j in range(n_gy)])  4.11 us
    concatenate x1, other arithmetic, thermal(): heat_ext = jnp.concatenate([before[:, h:], heat, after[:, h:]], axis=1)  2.84 us
  transfers between devices with their start and end apart: 7, of which 6 were waited for; matrix products, arithmetic and copies ran while one was open for 7% of the time, Pallas kernels for 0%

profile of v14, /device:TPU:0, one launch (start us, length us, event | category | flops | bytes accessed | tf_op | source)
XLA Modules:
  0.0 97.0 jit_solution(15483590176999685029)
XLA Ops:
  0.7 1.3 %fusion.89 = (f32[8,4,2048]{2,1,0:T(4,128)S(1)}, f32[8,4,2048]{2,1,0:T(4,128)S(1)}) fusion(f32[8,32,2048]{2,1,0:T(8,128)} %param.11), kind=kLoop, calls=%fused_computation.245 | loop fusion | bytes 1048576 | tf_op jit(solution)/shard_map/slice | solution.py:108
  2.0 1.3 %fusion.90 = (f32[8,3,2048]{2,1,0:T(4,128)S(1)}, f32[8,3,2048]{2,1,0:T(4,128)S(1)}) fusion(f32[8,32,2048]{2,1,0:T(8,128)} %param.12), kind=kLoop, calls=%fused_computation.246 | loop fusion | bytes 786432 | tf_op jit(solution)/shard_map/slice | solution.py:108
  3.5 5.8 %collective-permute-start = (f32[7,8,2048]{2,0,1:T(8,128)S(1)}, f32[7,8,2048]{2,0,1:T(8,128)}, u32[]{:S(2)}, u32[]{:S(2)}) collective-permute-start(f32[7,8,2048]{2,0,1:T(8,128)S(1)} %maximum_bitcast_fusion), channel_id=1, source_target_pairs={{0,1},{1,2},{2,3},{3,4},{4,5},{5,6},{6,7},{7,8},{8,9},{9,10},{10,1... | collective-permute-start | bytes 1376264 | tf_op jit(solution)/shard_map/ppermute | solution.py:25
  10.2 1.3 %collective-permute-start.1 = (f32[7,8,2048]{2,0,1:T(8,128)}, f32[7,8,2048]{2,0,1:T(8,128)}, u32[]{:S(2)}, u32[]{:S(2)}) collective-permute-start(f32[7,8,2048]{2,0,1:T(8,128)} %maximum_bitcast_fusion.1), channel_id=1, source_target_pairs={{1,0},{2,1},{3,2},{4,3},{5,4},{6,5},{7,6},{8,7},{9,8},{10,9},{11,1... | collective-permute-start | bytes 1376264 | tf_op jit(solution)/shard_map/ppermute | solution.py:25
  11.5 3.9 %collective-permute-start.2 = (f32[2,3,512]{2,1,0:T(4,128)S(1)}, f32[2,3,512]{2,1,0:T(4,128)S(1)}, u32[]{:S(2)}, u32[]{:S(2)}) collective-permute-start(f32[2,3,512]{2,1,0:T(4,128)S(1)} %get-tuple-element.40), channel_id=1, source_target_pairs={{0,4},{4,8},{8,12},{12,16},{16,20},{20,24},{24,28},{1,5},{5,9},{9,... | collective-permute-start | bytes 36872 | tf_op jit(solution)/shard_map/ppermute | solution.py:25
  15.4 1.3 %collective-permute-start.3 = (f32[2,3,512]{2,1,0:T(4,128)S(1)}, f32[2,3,512]{2,1,0:T(4,128)S(1)}, u32[]{:S(2)}, u32[]{:S(2)}) collective-permute-start(f32[2,3,512]{2,1,0:T(4,128)S(1)} %get-tuple-element.41), channel_id=1, source_target_pairs={{4,0},{8,4},{12,8},{16,12},{20,16},{24,20},{28,24},{5,1},{9,5},{13... | collective-permute-start | bytes 36872 | tf_op jit(solution)/shard_map/ppermute | solution.py:25
  20.7 1.1 %slice.557 = f32[8,4,2048]{2,1,0:T(4,128)S(1)} slice(f32[8,7,2048]{2,1,0:T(8,128)} %bitcast.2), slice={[0:8], [0:4], [0:2048]} | slice | bytes 524288 | tf_op jit(solution)/shard_map/slice | solution.py:112
  21.8 1.1 %slice.564 = f32[8,3,2048]{2,1,0:T(4,128)S(1)} slice(f32[8,7,2048]{2,1,0:T(8,128)} %bitcast.2), slice={[0:8], [4:7], [0:2048]} | slice | bytes 393216 | tf_op jit(solution)/shard_map/slice | solution.py:113
  22.9 11.6 %collective-permute-done.1 = f32[7,8,2048]{2,0,1:T(8,128)} collective-permute-done((f32[7,8,2048]{2,0,1:T(8,128)}, f32[7,8,2048]{2,0,1:T(8,128)}, u32[]{:S(2)}, u32[]{:S(2)}) %collective-permute-start.1) | collective-permute-done | bytes 458784 | tf_op jit(solution)/shard_map/ppermute | solution.py:25
  34.6 1.1 %slice.558 = f32[8,4,2048]{2,1,0:T(4,128)S(1)} slice(f32[8,7,2048]{2,1,0:T(8,128)} %bitcast.4), slice={[0:8], [0:4], [0:2048]} | slice | bytes 524288 | tf_op jit(solution)/shard_map/slice | solution.py:112
  35.7 1.1 %slice.565 = f32[8,3,2048]{2,1,0:T(4,128)S(1)} slice(f32[8,7,2048]{2,1,0:T(8,128)} %bitcast.4), slice={[0:8], [4:7], [0:2048]} | slice | bytes 393216 | tf_op jit(solution)/shard_map/slice | solution.py:113
  37.9 1.1 %copy-done.2 = f32[8,32,2048]{2,1,0:T(8,128)S(1)} copy-done((f32[8,32,2048]{2,1,0:T(8,128)S(1)}, f32[8,32,2048]{2,1,0:T(8,128)}, u32[]{:S(2)}) %copy-start.2) | copy-done | bytes 2097176
  39.0 2.8 %pad_maximum_fusion.1 = (f32[8,38,2048]{2,1,0:T(8,128)S(1)}, f32[8,38,2048]{2,1,0:T(8,128)S(1)}) fusion(f32[8,3,2048]{2,1,0:T(4,128)S(1)} %slice.565, f32[8,32,2048]{2,1,0:T(8,128)S(1)} %copy-done.2, f32[8,3,2048]{2,1,0:T(4,128)S(1)} %slice.564, f32[7,38,2048]{2,1,0:T(8,128)S(1)} %fusion.16, f32[8,40,2048]{2,1,0:T(8,128)S(1)} %pad_maximum_fusion, ...), kind=kLoop, calls=%fused_computation.23 | loop fusion | flops 8093696 | bytes 20382720 | tf_op jit(solution)/shard_map/concatenate | solution.py:113
  42.3 2.6 %fusion.14 = f32[8,36,2048]{2,1,0:T(8,128)S(1)} fusion(f32[8,38,2048]{2,1,0:T(8,128)S(1)} %get-tuple-element.16, f32[8,38,2048]{2,1,0:T(8,128)S(1)} %get-tuple-element.15, f32[7,36,2048]{2,1,0:T(8,128)S(1)} %fusion.15, f32[8]{0:T(128)S(1)} %copy-done.10), kind=kLoop, calls=%fused_computation.19 | loop fusion | flops 5898240 | bytes 17760768 | tf_op jit(solution)/shard_map/add | solution.py:44
  44.9 5.2 %fusion.44 = f32[36,2048]{1,0:T(8,128)S(1)} fusion(f32[8,36,2048]{2,1,0:T(8,128)S(1)} %fusion.14, f32[]{:T(128)} %bitcast.11, f32[]{:T(128)} %bitcast.10, f32[]{:T(128)} %bitcast.9, f32[]{:T(128)} %bitcast.8, f32[]{:T(128)} %bitcast.7, f32[]{:T(128)} %bitcast.6, f32[]{:T(128)} %bitcast.5, f32[]{:T(128)} %bitcast), kind=kLoop, calls=%fused_computation.105 | loop fusion | flops 1105920 | bytes 2654240 | tf_op jit(solution)/shard_map/add | solution.py:50
  53.3 3.5 %collective-permute-start.6 = (f32[2,38,512]{2,0,1:T(2,128)S(1)}, f32[2,38,512]{2,0,1:T(2,128)S(1)}, u32[]{:S(2)}, u32[]{:S(2)}) collective-permute-start(f32[2,38,512]{2,0,1:T(2,128)S(1)} %pad_maximum_fusion.8), channel_id=1, source_target_pairs={{0,3},{1,0},{2,1},{3,2},{4,7},{5,4},{6,5},{7,6},{8,11},{9,8},{10,9... | collective-permute-start | bytes 466952 | tf_op jit(solution)/shard_map/ppermute | solution.py:153
  56.8 4.4 %collective-permute-done.4 = f32[2,38,512]{2,0,1:T(2,128)S(1)} collective-permute-done((f32[2,38,512]{2,0,1:T(2,128)S(1)}, f32[2,38,512]{2,0,1:T(2,128)S(1)}, u32[]{:S(2)}, u32[]{:S(2)}) %collective-permute-start.4) | collective-permute-done | bytes 155680 | tf_op jit(solution)/shard_map/ppermute | solution.py:153
  61.2 2.0 %collective-permute-done.6 = f32[2,38,512]{2,0,1:T(2,128)S(1)} collective-permute-done((f32[2,38,512]{2,0,1:T(2,128)S(1)}, f32[2,38,512]{2,0,1:T(2,128)S(1)}, u32[]{:S(2)}, u32[]{:S(2)}) %collective-permute-start.6) | collective-permute-done | bytes 155680 | tf_op jit(solution)/shard_map/ppermute | solution.py:153
  63.2 5.6 %collective-permute-done.5 = f32[2,37,512]{2,0,1:T(2,128)S(1)} collective-permute-done((f32[2,37,512]{2,0,1:T(2,128)S(1)}, f32[2,37,512]{2,0,1:T(2,128)S(1)}, u32[]{:S(2)}, u32[]{:S(2)}) %collective-permute-start.5) | collective-permute-done | bytes 151584 | tf_op jit(solution)/shard_map/ppermute | solution.py:153
  69.2 1.2 %gather_fusion = f32[4,2,37,512]{3,1,2,0:T(2,128)S(1)} fusion(f32[4,2,37,512]{3,1,2,0:T(2,128)S(1)} %pad_maximum_fusion.5, s32[1024]{0:T(1024)S(1)} %pad_clamp_fusion), kind=kCustom, calls=%fused_computation | custom fusion | bytes 1212432 | tf_op jit(solution)/shard_map/jit(_take)/gather | solution.py:168
  74.3 1.4 %subtract_bitcast_fusion = (f32[1,1,128,512]{3,2,1,0:T(8,128)S(1)}, f32[128,512]{1,0:T(8,128)}) fusion(f32[128,512]{1,0:T(8,128)S(1)} %copy-done, f32[130,514]{1,0:T(8,128)S(1)} %fusion.20, f32[134,518]{1,0:T(8,128)S(1)} %get-tuple-element.21, f32[132,516]{1,0:T(8,128)S(1)} %get-tuple-element.14), kind=kLoop, calls=%fused_computation.141 | loop fusion | flops 1441792 | bytes 3407872 | tf_op jit(solution)/shard_map/stack | solution.py:308
  76.8 5.4 %shard_map.130 = f32[3,32,192]{2,1,0:T(8,128)} custom-call(s32[1,2048]{1,0:T(1,128)} %bitcast.131, s32[1,2048]{1,0:T(1,128)} %bitcast.130, bf16[3,2,128,512]{3,2,1,0:T(8,128)(2,1)} %pad_maximum_fusion.2.parts_ref, s32[1,2048]{1,0:T(1,128)} %bitcast.127, s32[1,2048]{1,0:T(1,128)} %bitcast.132), custom_call_target="tpu_custom_call" | custom-call | tf_op jit(solution)/shard_map/pallas_call | solution.py:248
  83.2 11.1 %all_to_all.5 = f32[3,32,192]{2,0,1:T(4,128)S(1)} all-to-all(f32[3,32,192]{2,0,1:T(4,128)S(1)} %copy.48), channel_id=1, replica_groups=mesh['gx'=8,'gy'=4] {'gx','gy'}, dimensions={1} | all-to-all | bytes 147456 | tf_op jit(solution)/shard_map/all_to_all | solution.py:309
  95.1 1.1 %add_select_fusion = (f32[1,6144]{1,0:T(1,128)}, f32[1,6144]{1,0:T(1,128)S(1)}) fusion(pred[1,6144]{1,0:T(4,128)(4,1)S(1)} %gt.47, f32[1,6144]{1,0:T(1,128)S(1)} %copy-done.7, f32[2,1,6144]{2,1,0:T(1,128)S(1)} %copy-done.4, f32[1,6144]{1,0:T(1,128)S(1)} %squeeze.121, f32[1,6144]{1,0:T(1,128)S(1)} %squeeze.119), kind=kLoop, calls=%fused_computation.178 | loop fusion | flops 202752 | bytes 178176 | tf_op jit(solution)/shard_map/jit(_where)/select_n | solution.py:85
  (124 shorter events, 17.2 us)
Async XLA Ops:
  0.6 10.8 %copy-start = (f32[128,512]{1,0:T(8,128)S(1)}, f32[128,512]{1,0:T(8,128)}, u32[]{:S(2)}) copy-start(f32[128,512]{1,0:T(8,128)} %param.17) | copy-start | bytes 786436
  0.6 10.8 %copy-start.3 = (f32[128,512]{1,0:T(8,128)S(1)}, f32[128,512]{1,0:T(8,128)}, u32[]{:S(2)}) copy-start(f32[128,512]{1,0:T(8,128)} %param.16) | copy-start | bytes 786436
  0.7 16.1 %copy-start.6 = (f32[8]{0:T(128)S(1)}, f32[8]{0:T(128)}, u32[]{:S(2)}) copy-start(f32[8]{0:T(128)} %param.15) | copy-start | bytes 100
  0.7 16.8 %copy-start.5 = (s32[2048,1]{0,1:T(1,128)S(1)}, s32[2048,1]{0,1:T(1,128)}, u32[]{:S(2)}) copy-start(s32[2048,1]{0,1:T(1,128)} %param.19) | copy-start | bytes 24580
  0.7 17.5 %copy-start.8 = (s32[2048]{0:T(1024)S(1)}, s32[2048]{0:T(1024)}, u32[]{:S(2)}) copy-start(s32[2048]{0:T(1024)} %param.18) | copy-start | bytes 24580
  3.5 17.3 %collective-permute-start = (f32[7,8,2048]{2,0,1:T(8,128)S(1)}, f32[7,8,2048]{2,0,1:T(8,128)}, u32[]{:S(2)}, u32[]{:S(2)}) collective-permute-start(f32[7,8,2048]{2,0,1:T(8,128)S(1)} %maximum_bitcast_fusion), channel_id=1, source_target_pairs={{0,1},{1,2},{2,3},{3,4},{4,5},{5,6},{6,7},{7,8},{8,9},{9,10},{10,1... | collective-permute-start | bytes 1376264 | tf_op jit(solution)/shard_map/ppermute | solution.py:25
  9.3 27.5 %copy-start.1 = (f32[8,32,2048]{2,1,0:T(8,128)S(1)}, f32[8,32,2048]{2,1,0:T(8,128)}, u32[]{:S(2)}) copy-start(f32[8,32,2048]{2,1,0:T(8,128)} %param.11) | copy-start | bytes 6291460
  10.2 24.4 %collective-permute-start.1 = (f32[7,8,2048]{2,0,1:T(8,128)}, f32[7,8,2048]{2,0,1:T(8,128)}, u32[]{:S(2)}, u32[]{:S(2)}) collective-permute-start(f32[7,8,2048]{2,0,1:T(8,128)} %maximum_bitcast_fusion.1), channel_id=1, source_target_pairs={{1,0},{2,1},{3,2},{4,3},{5,4},{6,5},{7,6},{8,7},{9,8},{10,9},{11,1... | collective-permute-start | bytes 1376264 | tf_op jit(solution)/shard_map/ppermute | solution.py:25
  11.5 8.0 %collective-permute-start.2 = (f32[2,3,512]{2,1,0:T(4,128)S(1)}, f32[2,3,512]{2,1,0:T(4,128)S(1)}, u32[]{:S(2)}, u32[]{:S(2)}) collective-permute-start(f32[2,3,512]{2,1,0:T(4,128)S(1)} %get-tuple-element.40), channel_id=1, source_target_pairs={{0,4},{4,8},{8,12},{12,16},{16,20},{20,24},{24,28},{1,5},{5,9},{9,... | collective-permute-start | bytes 36872 | tf_op jit(solution)/shard_map/ppermute | solution.py:25
  15.4 4.9 %collective-permute-start.3 = (f32[2,3,512]{2,1,0:T(4,128)S(1)}, f32[2,3,512]{2,1,0:T(4,128)S(1)}, u32[]{:S(2)}, u32[]{:S(2)}) collective-permute-start(f32[2,3,512]{2,1,0:T(4,128)S(1)} %get-tuple-element.41), channel_id=1, source_target_pairs={{4,0},{8,4},{12,8},{16,12},{20,16},{24,20},{28,24},{5,1},{9,5},{13... | collective-permute-start | bytes 36872 | tf_op jit(solution)/shard_map/ppermute | solution.py:25
  36.8 0.7 copy-start.9
  37.4 1.6 %copy-start.2 = (f32[8,32,2048]{2,1,0:T(8,128)S(1)}, f32[8,32,2048]{2,1,0:T(8,128)}, u32[]{:S(2)}) copy-start(f32[8,32,2048]{2,1,0:T(8,128)} %param.12) | copy-start | bytes 6291460
  37.4 1.6 %copy-start.10 = (f32[8]{0:T(128)S(1)}, f32[8]{0:T(128)}, u32[]{:S(2)}) copy-start(f32[8]{0:T(128)} %param.13) | copy-start | bytes 100
  52.4 8.8 %collective-permute-start.4 = (f32[2,38,512]{2,0,1:T(2,128)S(1)}, f32[2,38,512]{2,0,1:T(2,128)S(1)}, u32[]{:S(2)}, u32[]{:S(2)}) collective-permute-start(f32[2,38,512]{2,0,1:T(2,128)S(1)} %pad_maximum_fusion.7), channel_id=1, source_target_pairs={{0,1},{1,2},{2,3},{3,0},{4,5},{5,6},{6,7},{7,4},{8,9},{9,10},{10,1... | collective-permute-start | bytes 466952 | tf_op jit(solution)/shard_map/ppermute | solution.py:153
  53.3 9.9 %collective-permute-start.6 = (f32[2,38,512]{2,0,1:T(2,128)S(1)}, f32[2,38,512]{2,0,1:T(2,128)S(1)}, u32[]{:S(2)}, u32[]{:S(2)}) collective-permute-start(f32[2,38,512]{2,0,1:T(2,128)S(1)} %pad_maximum_fusion.8), channel_id=1, source_target_pairs={{0,3},{1,0},{2,1},{3,2},{4,7},{5,4},{6,5},{7,6},{8,11},{9,8},{10,9... | collective-permute-start | bytes 466952 | tf_op jit(solution)/shard_map/ppermute | solution.py:153
  56.8 12.1 %collective-permute-start.5 = (f32[2,37,512]{2,0,1:T(2,128)S(1)}, f32[2,37,512]{2,0,1:T(2,128)S(1)}, u32[]{:S(2)}, u32[]{:S(2)}) collective-permute-start(f32[2,37,512]{2,0,1:T(2,128)S(1)} %get-tuple-element.33), channel_id=1, source_target_pairs={{0,2},{1,3},{2,0},{3,1},{4,6},{5,7},{6,4},{7,5},{8,10},{9,11},{10,... | collective-permute-start | bytes 454664 | tf_op jit(solution)/shard_map/ppermute | solution.py:153
  75.7 19.4 %copy-start.4 = (f32[2,1,6144]{2,1,0:T(1,128)S(1)}, f32[2,1,6144]{2,1,0:T(1,128)}, u32[]{:S(2)}) copy-start(f32[2,1,6144]{2,1,0:T(1,128)} %param.20) | copy-start | bytes 147460
  75.7 19.4 %copy-start.7 = (f32[1,6144]{1,0:T(1,128)S(1)}, f32[1,6144]{1,0:T(1,128)}, u32[]{:S(2)}) copy-start(f32[1,6144]{1,0:T(1,128)} %param.21) | copy-start | bytes 73732

commit v15 on v13

--- a/solution.py
+++ b/solution.py
@@ -128,37 +128,37 @@
     cm = cols // n_gy
     rows = rows - 2 * width
     lp = jnp.pad(load, ((0, 0), (width, width)))
-    tp = jnp.pad(top, ((width, width), (0, 0)))
+    full = load.shape[0]
     send = []
     for k in range(n_gy):
-        main = jnp.stack([load[:, k * cm: (k + 1) * cm], tp[:, k * cm: (k + 1) * cm]])
         halo = jnp.concatenate(
             [lp[:, k * cm: k * cm + width], lp[:, (k + 1) * cm + width: (k + 1) * cm + 2 * width]],
             axis=1)
-        send.append(jnp.concatenate([main, as_slab(halo, 2, cm)], axis=1))
+        send.append(jnp.concatenate(
+            [load[:, k * cm: (k + 1) * cm], top[:, k * cm: (k + 1) * cm], as_slab(halo, 1, cm)[0]],
+            axis=0))
     send = jnp.stack(send)
-    depth = send.shape[2]
-    full = load.shape[0]
+    depth = send.shape[1]
     got = [lax.dynamic_index_in_dim(send, gj, 0, keepdims=False)]
     side_before = side_after = None
     for shift in range(1, n_gy):
         piece = lax.dynamic_index_in_dim(send, (gj + shift) % n_gy, 0, keepdims=False)
         extras = []
         if shift == 1:
-            extras.append(as_slab(side_last, 2, piece.shape[2]))
+            extras.append(as_slab(side_last, 1, cm)[0])
         if shift == n_gy - 1:
-            extras.append(as_slab(side_leading, 2, piece.shape[2]))
-        piece = jnp.concatenate([piece] + extras, axis=1)
+            extras.append(as_slab(side_leading, 1, cm)[0])
+        piece = jnp.concatenate([piece] + extras, axis=0)
         moved = lax.ppermute(piece, "gy", [(j, (j + shift) % n_gy) for j in range(n_gy)])
         at = depth
         if shift == 1:
-            slab = as_slab(side_last, 2, piece.shape[2])
-            side_before = from_slab(moved[:, at: at + slab.shape[1]], side_last.shape)
-            at += slab.shape[1]
+            n = as_slab(side_last, 1, cm).shape[1]
+            side_before = from_slab(moved[None, at: at + n], side_last.shape)
+            at += n
         if shift == n_gy - 1:
-            slab = as_slab(side_leading, 2, piece.shape[2])
-            side_after = from_slab(moved[:, at: at + slab.shape[1]], side_leading.shape)
-        got.append(moved[:, :depth])
+            n = as_slab(side_leading, 1, cm).shape[1]
+            side_after = from_slab(moved[None, at: at + n], side_leading.shape)
+        got.append(moved[:depth])
     if side_before is None:
         side_before = jnp.zeros_like(side_last)
         side_after = jnp.zeros_like(side_leading)
@@ -167,13 +167,13 @@
     recv = jnp.take(jnp.stack(got), (gj - jnp.arange(n_gy)) % n_gy, axis=0)
     parts = []
     for k in range(n_gy):
-        halo = from_slab(recv[k, :, full:], (full, 2 * width))
-        window = jnp.concatenate([halo[:, :width], recv[k, 0, :full], halo[:, width:]], axis=1)
+        halo = from_slab(recv[k, None, full + rows:], (full, 2 * width))
+        window = jnp.concatenate([halo[:, :width], recv[k, :full], halo[:, width:]], axis=1)
         lo = 0 if k == 0 else width
         hi = rows + 2 * width if k == n_gy - 1 else rows + width
         parts.append(window[lo:hi])
     load_m = jnp.concatenate(parts, axis=0)
-    top_m = jnp.concatenate([recv[k, 1, width: rows + width] for k in range(n_gy)], axis=0)
+    top_m = jnp.concatenate([recv[k, full: full + rows] for k in range(n_gy)], axis=0)
     return load_m, top_m, side_before, side_after
 
 

time: 97.1 us -> 94.3 us (0.971)
  local copies, waits for them, and re-layouts: 12.3 us -> 10.9 us
where the time goes in v15:
time: 94.3 us; the launch traced here: 93.9 us
  waiting for transfers between devices  26.5 us (28%)
  other arithmetic  22.5 us (24%)
  starting transfers between devices  16.3 us (17%)
  local copies, waits for them, and re-layouts  10.9 us (12%)
  blocking collectives  10.7 us (11%)
  Pallas kernels  5.39 us (6%)
  between operations  1.31 us (1%)
    ppermute x4, waiting for transfers between devices, exchange(): return (lax.ppermute(last, axis, up), lax.ppermute(leading, axis, down))  15 us
    ppermute x4, starting transfers between devices, exchange(): return (lax.ppermute(last, axis, up), lax.ppermute(leading, axis, down))  12.2 us
    ppermute x3, waiting for transfers between devices, relay(): lax.ppermute(piece, 'gy', [(j, (j + shift) % n_gy) for j in range(n_gy)])  11.5 us
    all_to_all x1, blocking collectives, body(): lax.all_to_all(outgoing, FLAT, split_axis=1, concat_axis=1, tiled=True)  10.7 us
    pallas_call x1, Pallas kernels, route_joints(): pl.pallas_call(joints_kernel, out_shape=jax.ShapeDtypeStruct((nf + 1, dev...  5.39 us
    add x1, other arithmetic, moment_of(): total = total + weighting[layer] * field[layer]  5.18 us
    ppermute x3, starting transfers between devices, relay(): lax.ppermute(piece, 'gy', [(j, (j + shift) % n_gy) for j in range(n_gy)])  4.11 us
    concatenate x1, other arithmetic, thermal(): heat_ext = jnp.concatenate([before[:, h:], heat, after[:, h:]], axis=1)  2.86 us
  transfers between devices with their start and end apart: 7, of which 6 were waited for; matrix products, arithmetic and copies ran while one was open for 4% of the time, Pallas kernels for 0%

profile of v15, /device:TPU:0, one launch (start us, length us, event | category | flops | bytes accessed | tf_op | source)
XLA Modules:
  0.0 93.9 jit_solution(18153353179154602439)
XLA Ops:
  0.7 1.3 %fusion.86 = (f32[8,4,2048]{2,1,0:T(4,128)S(1)}, f32[8,4,2048]{2,1,0:T(4,128)S(1)}) fusion(f32[8,32,2048]{2,1,0:T(8,128)} %param.11), kind=kLoop, calls=%fused_computation.234 | loop fusion | bytes 1048576 | tf_op jit(solution)/shard_map/slice | solution.py:108
  2.0 1.3 %fusion.87 = (f32[8,3,2048]{2,1,0:T(4,128)S(1)}, f32[8,3,2048]{2,1,0:T(4,128)S(1)}) fusion(f32[8,32,2048]{2,1,0:T(8,128)} %param.12), kind=kLoop, calls=%fused_computation.235 | loop fusion | bytes 786432 | tf_op jit(solution)/shard_map/slice | solution.py:108
  3.4 0.9 pad_maximum_fusion.6
  4.3 5.0 %collective-permute-start = (f32[8,7,2048]{2,1,0:T(8,128)}, f32[8,7,2048]{2,1,0:T(8,128)S(1)}, u32[]{:S(2)}, u32[]{:S(2)}) collective-permute-start(f32[8,7,2048]{2,1,0:T(8,128)} %pad_maximum_fusion.6), channel_id=1, source_target_pairs={{0,1},{1,2},{2,3},{3,4},{4,5},{5,6},{6,7},{7,8},{8,9},{9,10},{10,1... | collective-permute-start | bytes 1376264 | tf_op jit(solution)/shard_map/ppermute | solution.py:25
  10.2 1.3 %collective-permute-start.1 = (f32[8,7,2048]{2,1,0:T(8,128)}, f32[8,7,2048]{2,1,0:T(8,128)}, u32[]{:S(2)}, u32[]{:S(2)}) collective-permute-start(f32[8,7,2048]{2,1,0:T(8,128)} %pad_maximum_fusion.7), channel_id=1, source_target_pairs={{1,0},{2,1},{3,2},{4,3},{5,4},{6,5},{7,6},{8,7},{9,8},{10,9},{11,1... | collective-permute-start | bytes 1376264 | tf_op jit(solution)/shard_map/ppermute | solution.py:25
  11.5 4.6 %collective-permute-start.2 = (f32[2,3,512]{2,1,0:T(4,128)S(1)}, f32[2,3,512]{2,1,0:T(4,128)S(1)}, u32[]{:S(2)}, u32[]{:S(2)}) collective-permute-start(f32[2,3,512]{2,1,0:T(4,128)S(1)} %get-tuple-element.40), channel_id=1, source_target_pairs={{0,4},{4,8},{8,12},{12,16},{16,20},{20,24},{24,28},{1,5},{5,9},{9,... | collective-permute-start | bytes 36872 | tf_op jit(solution)/shard_map/ppermute | solution.py:25
  16.2 1.3 %collective-permute-start.3 = (f32[2,3,512]{2,1,0:T(4,128)S(1)}, f32[2,3,512]{2,1,0:T(4,128)S(1)}, u32[]{:S(2)}, u32[]{:S(2)}) collective-permute-start(f32[2,3,512]{2,1,0:T(4,128)S(1)} %get-tuple-element.41), channel_id=1, source_target_pairs={{4,0},{8,4},{12,8},{16,12},{20,16},{24,20},{28,24},{5,1},{9,5},{13... | collective-permute-start | bytes 36872 | tf_op jit(solution)/shard_map/ppermute | solution.py:25
  21.9 13.7 %collective-permute-done.1 = f32[8,7,2048]{2,1,0:T(8,128)} collective-permute-done((f32[8,7,2048]{2,1,0:T(8,128)}, f32[8,7,2048]{2,1,0:T(8,128)}, u32[]{:S(2)}, u32[]{:S(2)}) %collective-permute-start.1) | collective-permute-done | bytes 458784 | tf_op jit(solution)/shard_map/ppermute | solution.py:25
  35.6 1.1 %slice.542 = f32[8,4,2048]{2,1,0:T(4,128)S(1)} slice(f32[8,7,2048]{2,1,0:T(8,128)} %collective-permute-done.1), slice={[0:8], [0:4], [0:2048]} | slice | bytes 524288 | tf_op jit(solution)/shard_map/slice | solution.py:111
  37.9 1.2 %slice.549 = f32[8,3,2048]{2,1,0:T(4,128)S(1)} slice(f32[8,7,2048]{2,1,0:T(8,128)} %collective-permute-done.1), slice={[0:8], [4:7], [0:2048]} | slice | bytes 393216 | tf_op jit(solution)/shard_map/slice | solution.py:112
  39.1 2.9 %pad_maximum_fusion.1 = (f32[8,38,2048]{2,1,0:T(8,128)S(1)}, f32[8,38,2048]{2,1,0:T(8,128)S(1)}) fusion(f32[8,3,2048]{2,1,0:T(4,128)S(1)} %slice.549, f32[8,32,2048]{2,1,0:T(8,128)S(1)} %copy-done.2, f32[8,3,2048]{2,1,0:T(4,128)S(1)} %slice.548, f32[7,38,2048]{2,1,0:T(8,128)S(1)} %fusion.16, f32[8,40,2048]{2,1,0:T(8,128)S(1)} %pad_maximum_fusion, ...), kind=kLoop, calls=%fused_computation.23 | loop fusion | flops 8093696 | bytes 20382720 | tf_op jit(solution)/shard_map/concatenate | solution.py:112
  42.5 2.6 %fusion.14 = f32[8,36,2048]{2,1,0:T(8,128)S(1)} fusion(f32[8,38,2048]{2,1,0:T(8,128)S(1)} %get-tuple-element.16, f32[8,38,2048]{2,1,0:T(8,128)S(1)} %get-tuple-element.15, f32[7,36,2048]{2,1,0:T(8,128)S(1)} %fusion.15, f32[8]{0:T(128)S(1)} %copy-done.10), kind=kLoop, calls=%fused_computation.19 | loop fusion | flops 5898240 | bytes 17760768 | tf_op jit(solution)/shard_map/add | solution.py:44
  45.1 5.2 %fusion.44 = f32[36,2048]{1,0:T(8,128)S(1)} fusion(f32[8,36,2048]{2,1,0:T(8,128)S(1)} %fusion.14, f32[]{:T(128)} %bitcast.7, f32[]{:T(128)} %bitcast.6, f32[]{:T(128)} %bitcast.5, f32[]{:T(128)} %bitcast.4, f32[]{:T(128)} %bitcast.3, f32[]{:T(128)} %bitcast.2, f32[]{:T(128)} %bitcast.1, f32[]{:T(128)} %bitcast), kind=kLoop, calls=%fused_computation.100 | loop fusion | flops 1105920 | bytes 2654240 | tf_op jit(solution)/shard_map/add | solution.py:50
  52.2 3.5 %collective-permute-start.6 = (f32[71,512]{1,0:T(8,128)S(1)}, f32[71,512]{1,0:T(8,128)S(1)}, u32[]{:S(2)}, u32[]{:S(2)}) collective-permute-start(f32[71,512]{1,0:T(8,128)S(1)} %pad_maximum_fusion.10), channel_id=1, source_target_pairs={{0,3},{1,0},{2,1},{3,2},{4,7},{5,4},{6,5},{7,6},{8,11},{9,8},{10,9... | collective-permute-start | bytes 436232 | tf_op jit(solution)/shard_map/ppermute | solution.py:152
  55.7 4.3 %collective-permute-done.4 = f32[71,512]{1,0:T(8,128)S(1)} collective-permute-done((f32[71,512]{1,0:T(8,128)S(1)}, f32[71,512]{1,0:T(8,128)S(1)}, u32[]{:S(2)}, u32[]{:S(2)}) %collective-permute-start.4) | collective-permute-done | bytes 145440 | tf_op jit(solution)/shard_map/ppermute | solution.py:152
  60.0 1.8 %collective-permute-done.6 = f32[71,512]{1,0:T(8,128)S(1)} collective-permute-done((f32[71,512]{1,0:T(8,128)S(1)}, f32[71,512]{1,0:T(8,128)S(1)}, u32[]{:S(2)}, u32[]{:S(2)}) %collective-permute-start.6) | collective-permute-done | bytes 145440 | tf_op jit(solution)/shard_map/ppermute | solution.py:152
  61.8 5.4 %collective-permute-done.5 = f32[69,512]{1,0:T(8,128)S(1)} collective-permute-done((f32[69,512]{1,0:T(8,128)S(1)}, f32[69,512]{1,0:T(8,128)S(1)}, u32[]{:S(2)}, u32[]{:S(2)}) %collective-permute-start.5) | collective-permute-done | bytes 141344 | tf_op jit(solution)/shard_map/ppermute | solution.py:152
  70.6 0.9 %fusion.20 = f32[130,514]{1,0:T(8,128)S(1)} fusion(f32[132,516]{1,0:T(8,128)S(1)} %get-tuple-element.13, f32[132,516]{1,0:T(8,128)S(1)} %get-tuple-element.14, f32[134,518]{1,0:T(8,128)S(1)} %get-tuple-element.21, pred[514]{0:T(1024)(128)(4,1)S(1)} %fusion.79, pred[130]{0:T(512)(128)(4,1)S(1)} %compare_and_fusion.1), kind=kLoop, calls=%fused_computation.48 | loop fusion | flops 1536860 | bytes 2940724 | tf_op jit(solution)/shard_map/jit(_where)/select_n | solution.py:304
  71.5 1.4 %subtract_bitcast_fusion = (f32[1,1,128,512]{3,2,1,0:T(8,128)S(1)}, f32[128,512]{1,0:T(8,128)}) fusion(f32[128,512]{1,0:T(8,128)S(1)} %copy-done, f32[130,514]{1,0:T(8,128)S(1)} %fusion.20, f32[134,518]{1,0:T(8,128)S(1)} %get-tuple-element.21, f32[132,516]{1,0:T(8,128)S(1)} %get-tuple-element.14), kind=kLoop, calls=%fused_computation.137 | loop fusion | flops 1441792 | bytes 3407872 | tf_op jit(solution)/shard_map/stack | solution.py:307
  73.1 1.0 %pad_maximum_fusion.2.parts_ref = bf16[3,2,128,512]{3,2,1,0:T(8,128)(2,1)} fusion(bf16[1,2,128,512]{3,2,1,0:T(8,128)(2,1)S(1)} %get-tuple-element.39, bf16[1,2,128,512]{3,2,1,0:T(8,128)(2,1)S(1)} %get-tuple-element.38, bf16[1,2,128,512]{3,2,1,0:T(8,128)(2,1)S(1)} %get-tuple-element.37), kind=kLoop, calls=%fused_computation.29 | loop fusion | flops 786432 | bytes 1572864 | tf_op jit(solution)/shard_map/stack | solution.py:246
  74.1 5.4 %shard_map.130 = f32[3,32,192]{2,1,0:T(8,128)} custom-call(s32[1,2048]{1,0:T(1,128)} %bitcast.110, s32[1,2048]{1,0:T(1,128)} %bitcast.109, bf16[3,2,128,512]{3,2,1,0:T(8,128)(2,1)} %pad_maximum_fusion.2.parts_ref, s32[1,2048]{1,0:T(1,128)} %bitcast.106, s32[1,2048]{1,0:T(1,128)} %bitcast.111), custom_call_target="tpu_custom_call" | custom-call | tf_op jit(solution)/shard_map/pallas_call | solution.py:247
  79.5 1.0 %copy.32 = f32[3,32,192]{2,0,1:T(4,128)S(1)} copy(f32[3,32,192]{2,1,0:T(8,128)} %shard_map.130) | data formatting | bytes 147456 | tf_op jit(solution)/shard_map/pallas_call | solution.py:247
  80.5 10.7 %all_to_all.5 = f32[3,32,192]{2,0,1:T(4,128)S(1)} all-to-all(f32[3,32,192]{2,0,1:T(4,128)S(1)} %copy.32), channel_id=1, replica_groups=mesh['gx'=8,'gy'=4] {'gx','gy'}, dimensions={1} | all-to-all | bytes 147456 | tf_op jit(solution)/shard_map/all_to_all | solution.py:308
  92.0 1.1 %add_select_fusion = (f32[1,6144]{1,0:T(1,128)}, f32[1,6144]{1,0:T(1,128)S(1)}) fusion(pred[1,6144]{1,0:T(4,128)(4,1)S(1)} %gt.47, f32[1,6144]{1,0:T(1,128)S(1)} %copy-done.7, f32[2,1,6144]{2,1,0:T(1,128)S(1)} %copy-done.4, f32[1,6144]{1,0:T(1,128)S(1)} %squeeze.121, f32[1,6144]{1,0:T(1,128)S(1)} %squeeze.119), kind=kLoop, calls=%fused_computation.167 | loop fusion | flops 202752 | bytes 178176 | tf_op jit(solution)/shard_map/jit(_where)/select_n | solution.py:85
  (117 shorter events, 13.6 us)
Async XLA Ops:
  0.6 10.8 %copy-start = (f32[128,512]{1,0:T(8,128)S(1)}, f32[128,512]{1,0:T(8,128)}, u32[]{:S(2)}) copy-start(f32[128,512]{1,0:T(8,128)} %param.17) | copy-start | bytes 786436
  0.6 10.8 %copy-start.3 = (f32[128,512]{1,0:T(8,128)S(1)}, f32[128,512]{1,0:T(8,128)}, u32[]{:S(2)}) copy-start(f32[128,512]{1,0:T(8,128)} %param.16) | copy-start | bytes 786436
  0.7 16.9 %copy-start.6 = (f32[8]{0:T(128)S(1)}, f32[8]{0:T(128)}, u32[]{:S(2)}) copy-start(f32[8]{0:T(128)} %param.15) | copy-start | bytes 100
  0.7 17.6 %copy-start.5 = (s32[2048,1]{0,1:T(1,128)S(1)}, s32[2048,1]{0,1:T(1,128)}, u32[]{:S(2)}) copy-start(s32[2048,1]{0,1:T(1,128)} %param.19) | copy-start | bytes 24580
  0.7 18.9 %copy-start.8 = (s32[2048]{0:T(1024)S(1)}, s32[2048]{0:T(1024)}, u32[]{:S(2)}) copy-start(s32[2048]{0:T(1024)} %param.18) | copy-start | bytes 24580
  3.3 33.3 %copy-start.1 = (f32[8,32,2048]{2,1,0:T(8,128)S(1)}, f32[8,32,2048]{2,1,0:T(8,128)}, u32[]{:S(2)}) copy-start(f32[8,32,2048]{2,1,0:T(8,128)} %param.11) | copy-start | bytes 6291460
  4.3 17.6 %collective-permute-start = (f32[8,7,2048]{2,1,0:T(8,128)}, f32[8,7,2048]{2,1,0:T(8,128)S(1)}, u32[]{:S(2)}, u32[]{:S(2)}) collective-permute-start(f32[8,7,2048]{2,1,0:T(8,128)} %pad_maximum_fusion.6), channel_id=1, source_target_pairs={{0,1},{1,2},{2,3},{3,4},{4,5},{5,6},{6,7},{7,8},{8,9},{9,10},{10,1... | collective-permute-start | bytes 1376264 | tf_op jit(solution)/shard_map/ppermute | solution.py:25
  10.2 25.4 %collective-permute-start.1 = (f32[8,7,2048]{2,1,0:T(8,128)}, f32[8,7,2048]{2,1,0:T(8,128)}, u32[]{:S(2)}, u32[]{:S(2)}) collective-permute-start(f32[8,7,2048]{2,1,0:T(8,128)} %pad_maximum_fusion.7), channel_id=1, source_target_pairs={{1,0},{2,1},{3,2},{4,3},{5,4},{6,5},{7,6},{8,7},{9,8},{10,9},{11,1... | collective-permute-start | bytes 1376264 | tf_op jit(solution)/shard_map/ppermute | solution.py:25
  11.5 8.7 %collective-permute-start.2 = (f32[2,3,512]{2,1,0:T(4,128)S(1)}, f32[2,3,512]{2,1,0:T(4,128)S(1)}, u32[]{:S(2)}, u32[]{:S(2)}) collective-permute-start(f32[2,3,512]{2,1,0:T(4,128)S(1)} %get-tuple-element.40), channel_id=1, source_target_pairs={{0,4},{4,8},{8,12},{12,16},{16,20},{20,24},{24,28},{1,5},{5,9},{9,... | collective-permute-start | bytes 36872 | tf_op jit(solution)/shard_map/ppermute | solution.py:25
  16.2 4.9 %collective-permute-start.3 = (f32[2,3,512]{2,1,0:T(4,128)S(1)}, f32[2,3,512]{2,1,0:T(4,128)S(1)}, u32[]{:S(2)}, u32[]{:S(2)}) collective-permute-start(f32[2,3,512]{2,1,0:T(4,128)S(1)} %get-tuple-element.41), channel_id=1, source_target_pairs={{4,0},{8,4},{12,8},{16,12},{20,16},{24,20},{28,24},{5,1},{9,5},{13... | collective-permute-start | bytes 36872 | tf_op jit(solution)/shard_map/ppermute | solution.py:25
  36.7 0.7 copy-start.9
  37.3 1.8 %copy-start.2 = (f32[8,32,2048]{2,1,0:T(8,128)S(1)}, f32[8,32,2048]{2,1,0:T(8,128)}, u32[]{:S(2)}) copy-start(f32[8,32,2048]{2,1,0:T(8,128)} %param.12) | copy-start | bytes 6291460
  37.3 1.8 %copy-start.10 = (f32[8]{0:T(128)S(1)}, f32[8]{0:T(128)}, u32[]{:S(2)}) copy-start(f32[8]{0:T(128)} %param.13) | copy-start | bytes 100
  51.3 8.6 %collective-permute-start.4 = (f32[71,512]{1,0:T(8,128)S(1)}, f32[71,512]{1,0:T(8,128)S(1)}, u32[]{:S(2)}, u32[]{:S(2)}) collective-permute-start(f32[71,512]{1,0:T(8,128)S(1)} %pad_maximum_fusion.9), channel_id=1, source_target_pairs={{0,1},{1,2},{2,3},{3,0},{4,5},{5,6},{6,7},{7,4},{8,9},{9,10},{10,1... | collective-permute-start | bytes 436232 | tf_op jit(solution)/shard_map/ppermute | solution.py:152
  52.2 9.6 %collective-permute-start.6 = (f32[71,512]{1,0:T(8,128)S(1)}, f32[71,512]{1,0:T(8,128)S(1)}, u32[]{:S(2)}, u32[]{:S(2)}) collective-permute-start(f32[71,512]{1,0:T(8,128)S(1)} %pad_maximum_fusion.10), channel_id=1, source_target_pairs={{0,3},{1,0},{2,1},{3,2},{4,7},{5,4},{6,5},{7,6},{8,11},{9,8},{10,9... | collective-permute-start | bytes 436232 | tf_op jit(solution)/shard_map/ppermute | solution.py:152
  55.7 11.6 %collective-permute-start.5 = (f32[69,512]{1,0:T(8,128)S(1)}, f32[69,512]{1,0:T(8,128)S(1)}, u32[]{:S(2)}, u32[]{:S(2)}) collective-permute-start(f32[69,512]{1,0:T(8,128)S(1)} %get-tuple-element.33), channel_id=1, source_target_pairs={{0,2},{1,3},{2,0},{3,1},{4,6},{5,7},{6,4},{7,5},{8,10},{9,11},{10,... | collective-permute-start | bytes 423944 | tf_op jit(solution)/shard_map/ppermute | solution.py:152
  73.0 19.0 %copy-start.4 = (f32[2,1,6144]{2,1,0:T(1,128)S(1)}, f32[2,1,6144]{2,1,0:T(1,128)}, u32[]{:S(2)}) copy-start(f32[2,1,6144]{2,1,0:T(1,128)} %param.20) | copy-start | bytes 147460
  73.0 19.0 %copy-start.7 = (f32[1,6144]{1,0:T(1,128)S(1)}, f32[1,6144]{1,0:T(1,128)}, u32[]{:S(2)}) copy-start(f32[1,6144]{1,0:T(1,128)} %param.21) | copy-start | bytes 73732
